TPU v7x, 32 devices: a whole 2x2x4 slice. The times are simulated.
32 devices in a mesh: dp: 8 (over y, x, core), tensor: 4 (over z).
Axes of the slice: x: 2, y: 2, z: 4, core: 2. Of those that a mesh axis runs over, the one named last changes fastest.
Arguments:
- residual_in: bfloat16 [64, 2560], P(('dp', 'tensor')), may hold values from -6 to 6
- norm_gain: bfloat16 [2560], replicated, may hold values from 0.099609375 to 1.8984375
- w_query: bfloat16 [2560, 2560], P(None, 'tensor'), may hold values from -0.125 to 0.125
- key_weight: bfloat16 [2560, 640], P(None, 'tensor'), may hold values from -0.125 to 0.125
- value_weight: bfloat16 [2560, 640], P(None, 'tensor'), may hold values from -0.125 to 0.125
- key_page_pool: bfloat16 [256, 8, 80, 128], P('dp', 'tensor')
- value_page_pool: bfloat16 [256, 8, 80, 128], P('dp', 'tensor'), may hold values from -6 to 6
- lengths: int32 [64], replicated, may hold values from 1 to 512, as said below
- page_table: int32 [64, 4], replicated, may hold values from 0 to 255, as said below
- w_output: bfloat16 [2560, 2560], P('tensor'), may hold values from -0.125 to 0.125
- mlp_gain: bfloat16 [2560], replicated, may hold values from 0.099609375 to 1.8984375
- w_gate: bfloat16 [2560, 3584], P(None, 'tensor'), may hold values from -0.125 to 0.125
- w_up: bfloat16 [2560, 3584], P(None, 'tensor'), may hold values from -0.125 to 0.125
- w_down: bfloat16 [3584, 2560], P('tensor'), may hold values from -0.09375 to 0.09375
Outputs:
- residual_out: bfloat16 [64, 2560], P(('dp', 'tensor'))
Inputs may be any that keep to these rules, and one draw needn't show every extreme that they name: `lengths`: every value from 1 to 512 can occur; 512 and 1 occur in every draw. `page_table`: all entries are distinct. Requests are ranked by lengths[r] * 64 + r, rising; rank k goes to serving index s = k % N where N = 8 is the number of indices of dp, or N - 1 - k % N when k // N is odd, as its (k // N)-th served request; all pages of a request lie in pool pages s * 32 to (s + 1) * 32 - 1 of its serving index; pages past a request's length hold unused data.
All inputs are finite; a program needn't handle non-finite values.
Results may differ from a plain program's by a relative error of at most 0.0096.
Values may be sent and summed in bfloat16 or wider, within the bound.
No kernel may reach another device: no remote copies, remote signals or barrier semaphores. Data moves between devices by JAX's collectives and lax.ppermute only.
A program may use at most 64 MiB of HBM per device.

v0:
```python
import jax
import jax.numpy as jnp
from jax import lax
from jax.sharding import PartitionSpec as P

HEAD_SIZE = 80


def norm_rows(value_rows, gain):
    value_rows = value_rows.astype(jnp.float32)
    return (
        value_rows
        * lax.rsqrt(jnp.mean(value_rows * value_rows, axis=-1, keepdims=True) + 1e-05)
        * gain.astype(jnp.float32)
    )


def apply_rotation(tensor, positions):
    half_dim = tensor.shape[-1] // 2
    inverse_freq = 1000000.0 ** (
        -(jnp.arange(half_dim, dtype=jnp.float32) * 2.0 / tensor.shape[-1])
    )
    angles = positions.astype(jnp.float32)[:, None] * inverse_freq[None, :]
    cosine = jnp.cos(angles)[:, None, :]
    sines = jnp.sin(angles)[:, None, :]
    first_half = tensor[..., :half_dim]
    second_half = tensor[..., half_dim:]
    return jnp.concatenate(
        [first_half * cosine - second_half * sines, second_half * cosine + first_half * sines],
        axis=-1,
    )


def local(
    residual_in,
    norm_gain,
    w_query,
    key_weight,
    value_weight,
    key_page_pool,
    value_page_pool,
    lengths,
    page_table,
    w_output,
    mlp_gain,
    w_gate,
    w_up,
    w_down,
):
    dp_count = lax.axis_size("dp")
    tp_count = lax.axis_size("tensor")
    rows_loc = residual_in.shape[0]
    req_loc = rows_loc * tp_count
    kv_loc = key_page_pool.shape[1]
    q_loc = w_query.shape[1] // HEAD_SIZE
    group_width = q_loc // kv_loc
    pool_size = key_page_pool.shape[0]
    page_len = key_page_pool.shape[3]
    per_req = page_table.shape[1]
    total_reqs = page_table.shape[0]
    score_scale = 1.0 / HEAD_SIZE**0.5
    dp_index = lax.axis_index("dp")
    rows_all = lax.all_gather(residual_in, "tensor", axis=0, tiled=True)
    scaled_input = norm_rows(rows_all, norm_gain).astype(jnp.bfloat16)
    first_row = dp_index * req_loc
    own_len = lax.dynamic_slice_in_dim(lengths, first_row, req_loc, 0)
    query_heads = apply_rotation(
        jnp.dot(scaled_input, w_query, preferred_element_type=jnp.float32).reshape(
            req_loc, q_loc, HEAD_SIZE
        ),
        own_len,
    ).astype(jnp.bfloat16)
    fresh_key = apply_rotation(
        jnp.dot(scaled_input, key_weight, preferred_element_type=jnp.float32).reshape(
            req_loc, kv_loc, HEAD_SIZE
        ),
        own_len,
    ).astype(jnp.bfloat16)
    fresh_value = (
        jnp.dot(scaled_input, value_weight, preferred_element_type=jnp.float32)
        .astype(jnp.bfloat16)
        .reshape(req_loc, kv_loc, HEAD_SIZE)
    )
    request_ids = jnp.arange(total_reqs, dtype=jnp.int32)
    ranking = lengths * total_reqs + request_ids
    order = jnp.argsort(ranking, stable=True)
    rank = jnp.argsort(order, stable=True)
    round_no = rank // dp_count
    column = rank % dp_count
    server = jnp.where(round_no % 2 == 0, column, dp_count - 1 - column)
    slot_of = server * req_loc + round_no
    my_slots = first_row + jnp.arange(req_loc, dtype=jnp.int32)
    hits = (slot_of[None, :] == my_slots[:, None]).astype(jnp.int32)
    served = jnp.sum(hits * request_ids[None, :], axis=1)
    query_all, key_all, value_all = (
        lax.all_gather(query_heads.reshape(req_loc, q_loc * HEAD_SIZE), "dp", axis=0, tiled=True),
        lax.all_gather(fresh_key.reshape(req_loc, kv_loc * HEAD_SIZE), "dp", axis=0, tiled=True),
        lax.all_gather(fresh_value.reshape(req_loc, kv_loc * HEAD_SIZE), "dp", axis=0, tiled=True),
    )
    query_srv = query_all[served].reshape(req_loc, kv_loc, group_width, HEAD_SIZE)
    key_srv = key_all[served].reshape(req_loc, kv_loc, HEAD_SIZE)
    value_srv = value_all[served].reshape(req_loc, kv_loc, HEAD_SIZE)
    page_list = page_table[served] - dp_index * pool_size
    key_rows = key_page_pool[page_list]
    value_rows = value_page_pool[page_list]
    scores = (
        jnp.einsum("rhgd,rphdc->rhgpc", query_srv, key_rows, preferred_element_type=jnp.float32)
        * score_scale
    )
    positions = (
        jnp.arange(per_req, dtype=jnp.int32)[:, None] * page_len
        + jnp.arange(page_len, dtype=jnp.int32)[None, :]
    )
    valid_pos = (positions[None, :, :] < lengths[served][:, None, None])[:, None, None, :, :]
    own_score = (
        jnp.einsum("rhgd,rhd->rhg", query_srv, key_srv, preferred_element_type=jnp.float32)
        * score_scale
    )
    best = jnp.maximum(jnp.max(jnp.where(valid_pos, scores, -1e30), axis=(-2, -1)), own_score)
    weights = jnp.where(valid_pos, jnp.exp(scores - best[..., None, None]), 0.0)
    own_weight = jnp.exp(own_score - best)
    numer = (
        jnp.einsum("rhgpc,rphdc->rhgd", weights, value_rows.astype(jnp.float32))
        + own_weight[..., None] * value_srv.astype(jnp.float32)[:, :, None, :]
    )
    denom = jnp.sum(weights, axis=(-2, -1)) + own_weight
    served_out = (numer / denom[..., None]).reshape(req_loc, q_loc * HEAD_SIZE).astype(jnp.bfloat16)
    every_out = lax.all_gather(served_out, "dp", axis=0, tiled=True)
    attended = every_out[lax.dynamic_slice_in_dim(slot_of, first_row, req_loc, 0)]
    summed = lax.psum(jnp.dot(attended, w_output, preferred_element_type=jnp.float32), "tensor")
    mixed_all = rows_all.astype(jnp.float32) + summed
    normed_mlp = norm_rows(mixed_all, mlp_gain).astype(jnp.bfloat16)
    mixed = lax.dynamic_slice_in_dim(mixed_all, lax.axis_index("tensor") * rows_loc, rows_loc, 0)
    gate_act = jnp.dot(normed_mlp, w_gate, preferred_element_type=jnp.float32)
    up_act = jnp.dot(normed_mlp, w_up, preferred_element_type=jnp.float32)
    hidden = (jax.nn.silu(gate_act) * up_act).astype(jnp.bfloat16)
    down_part = lax.psum_scatter(
        jnp.dot(hidden, w_down, preferred_element_type=jnp.float32),
        "tensor",
        scatter_dimension=0,
        tiled=True,
    )
    return (mixed + down_part).astype(jnp.bfloat16)


def solution(mesh):
    return jax.shard_map(
        local,
        mesh=mesh,
        in_specs=(
            P(("dp", "tensor"), None),
            P(),
            P(None, "tensor"),
            P(None, "tensor"),
            P(None, "tensor"),
            P("dp", "tensor", None, None),
            P("dp", "tensor", None, None),
            P(),
            P(),
            P("tensor", None),
            P(),
            P(None, "tensor"),
            P(None, "tensor"),
            P("tensor", None),
        ),
        out_specs=P(("dp", "tensor"), None),
        check_vma=False,
    )
```

profile of v0, /device:TPU:0, one launch (start us, length us, event | category | flops | bytes accessed | tf_op | source)
XLA Modules:
  0.0 175.6 jit_solution(13523892685238837358)
XLA Ops:
  6.6 0.8 iota_add_fusion.2
  7.4 0.9 dynamic-slice_convert_fusion
  8.3 15.0 %all-gather = bf16[4,2,2560]{2,1,0:T(2,128)(2,1)S(1)} all-gather(bf16[1,2,2560]{2,1,0:T(2,128)(2,1)} %bitcast.45), channel_id=1, replica_groups=mesh['dp'=8,'tensor'=4] {'tensor'}, dimensions={0}, use_global_device_ids=true | all-gather | bytes 51200 | tf_op jit(solution)/shard_map/all_gather | solution.py:63
  23.4 0.7 convert_element_type.58
  24.2 2.5 %fusion.39 = f32[8,640]{1,0:T(8,128)S(1)} fusion(bf16[8,2560]{1,0:T(8,128)(2,1)S(1)} %multiply_convert_fusion.1, bf16[2560,640]{1,0:T(8,128)(2,1)} %param.16), kind=kOutput, calls=%fused_computation.83 | convolution fusion | flops 26214400 | bytes 3338240 | tf_op jit(solution)/shard_map/dot_general | solution.py:68
  27.1 9.3 %all_gather.16 = bf16[64,640]{1,0:T(8,128)(2,1)S(1)} all-gather(bf16[8,640]{1,0:T(8,128)(2,1)S(1)} %convert_element_type.61), channel_id=1, replica_groups=mesh['dp'=8,'tensor'=4] {'dp'}, dimensions={0}, use_global_device_ids=true | all-gather | bytes 92160 | tf_op jit(solution)/shard_map/all_gather | solution.py:96
  36.4 2.0 %sort.31 = (s32[64]{0:T(128)}, s32[64]{0:T(128)S(1)}) sort(s32[64]{0:T(128)S(1)} %iota_add_fusion.2, s32[64]{0:T(128)S(1)} %iota.39), dimensions={0}, to_apply=%region_0.0 | sort | flops 384 | bytes 1024 | tf_op jit(solution)/shard_map/jit(argsort)/sort | solution.py:86
  38.4 2.0 %sort.32 = (s32[64]{0:T(128)}, s32[64]{0:T(128)S(1)}) sort(s32[64]{0:T(128)S(1)} %get-tuple-element.7, s32[64]{0:T(128)S(1)} %iota.40), dimensions={0}, to_apply=%region_1.0 | sort | flops 384 | bytes 1024 | tf_op jit(solution)/shard_map/jit(argsort)/sort | solution.py:87
  41.4 0.7 reshape.237
  42.1 0.6 gather_fusion
  42.7 0.7 compare_select_fusion.1
  43.4 1.4 fusion.40
  45.2 9.0 %all_gather.17 = bf16[64,160]{1,0:T(8,128)(2,1)S(1)} all-gather(bf16[8,160]{1,0:T(8,128)(2,1)S(1)} %convert_element_type.62), channel_id=1, replica_groups=mesh['dp'=8,'tensor'=4] {'dp'}, dimensions={0}, use_global_device_ids=true | all-gather | bytes 23040 | tf_op jit(solution)/shard_map/all_gather | solution.py:97
  56.0 3.1 %gather_fusion.3 = bf16[32,2,80,128]{3,2,1,0:T(8,128)(2,1)} fusion(bf16[32,2,80,128]{3,2,1,0:T(8,128)(2,1)} %param.19, s32[1024]{0:T(1024)S(1)} %pad_clamp_fusion.1), kind=kCustom, calls=%fused_computation.3 | custom fusion | bytes 2621568 | tf_op jit(solution)/shard_map/gather | solution.py:104
  59.2 1.7 select_reduce_fusion
  61.1 0.6 fusion.38
  61.8 1.5 convolution_convert_fusion
  63.2 8.1 %all_gather.18 = bf16[64,160]{1,0:T(8,128)(2,1)S(1)} all-gather(bf16[8,160]{1,0:T(8,128)(2,1)S(1)} %convolution_convert_fusion), channel_id=1, replica_groups=mesh['dp'=8,'tensor'=4] {'dp'}, dimensions={0}, use_global_device_ids=true | all-gather | bytes 23040 | tf_op jit(solution)/shard_map/all_gather | solution.py:98
  71.3 0.7 gather_fusion.6
  72.1 3.1 %gather_fusion.5 = bf16[32,2,80,128]{3,2,1,0:T(8,128)(2,1)} fusion(bf16[32,2,80,128]{3,2,1,0:T(8,128)(2,1)} %param.20, s32[1024]{0:T(1024)S(1)} %pad_clamp_fusion.1), kind=kCustom, calls=%fused_computation.5 | custom fusion | bytes 2621568 | tf_op jit(solution)/shard_map/gather | solution.py:105
  75.2 1.8 %fusion.16 = bf16[8,2,4,80]{3,2,1,0:T(4,128)(2,1)S(1)} fusion(bf16[8,4,2,80,128]{4,3,2,1,0:T(8,128)(2,1)} %bitcast.41, f32[8,2,4,4,128]{4,2,3,1,0:T(4,128)S(1)} %get-tuple-element.20, f32[8,2,4]{2,1,0:T(2,128)S(1)} %multiply_maximum_fusion, pred[8,4,128]{2,1,0:T(4,128)(4,1)S(1)} %broadcast_compare_fusion, f32[8,2,4]{2,1,0:T(2,128)S(1)} %copy-done.3, ...), kind=kOutput, calls=%fused_computation.17 | convolution fusion | flops 5328896 | bytes 1462016 | tf_op jit(solution)/shard_map/rhgpc,rphdc->rhgd/dot_general | solution.py:123
  77.1 9.2 %all_gather.19 = bf16[64,640]{1,0:T(8,128)(2,1)S(1)} all-gather(bf16[8,640]{1,0:T(8,128)(2,1)S(1)} %convert_element_type.67), channel_id=1, replica_groups=mesh['dp'=8,'tensor'=4] {'dp'}, dimensions={0}, use_global_device_ids=true | all-gather | bytes 92160 | tf_op jit(solution)/shard_map/all_gather | solution.py:128
  86.4 0.7 pad_clamp_fusion
  87.6 1.2 fusion.42
  88.9 0.7 convert_element_type.68
  89.6 33.5 %all-reduce.4.cloned.1.call-done = f32[8,2560]{1,0:T(8,128)} async-done(((f32[8,2560]{1,0:T(8,128)}), f32[8,2560]{1,0:T(8,128)}) %all-reduce.4.cloned.1.call-update) | async-done | bytes 81936 | tf_op jit(solution)/shard_map/psum | solution.py:130
  123.1 1.0 multiply_reduce_fusion
  124.1 3.0 %fusion.37 = f32[8,896]{1,0:T(8,128)S(1)} fusion(bf16[2560,896]{1,0:T(8,128)(2,1)} %param.25, f32[8,2560]{1,0:T(8,128)S(1)} %get-tuple-element.10, f32[2560]{0:T(1024)S(1)} %convert_element_type.68, f32[8]{0:T(128)S(1)} %add_rsqrt_fusion), kind=kOutput, calls=%fused_computation.81 | convolution fusion | flops 36761600 | bytes 4708384 | tf_op jit(solution)/shard_map/dot_general | solution.py:134
  127.2 5.9 %fusion.20 = f32[8,2560]{1,0:T(8,128)} fusion(bf16[896,2560]{1,0:T(8,128)(2,1)} %param.27, bf16[2560,896]{1,0:T(8,128)(2,1)} %param.26, f32[8,896]{1,0:T(8,128)S(1)} %fusion.37, f32[8,2560]{1,0:T(8,128)S(1)} %get-tuple-element.10, f32[2560]{0:T(1024)S(1)} %convert_element_type.68, f32[8]{0:T(128)S(1)} %add_rsqrt_fusion), kind=kOutput, calls=%fused_computation.19 | convolution fusion | flops 73504768 | bytes 9377824 | tf_op jit(solution)/shard_map/dot_general | solution.py:138
  133.1 0.6 dynamic-slice
  134.4 32.9 %all-reduce.6.cloned.1.call-done = f32[8,2560]{1,0:T(8,128)} async-done(((f32[8,2560]{1,0:T(8,128)}), f32[8,2560]{1,0:T(8,128)}) %all-reduce.6.cloned.1.call-update) | async-done | bytes 81936
  167.2 1.5 fusion.30
  (59 shorter events, 4.9 us)
Async XLA Ops:
  6.5 81.1 %copy-start = (bf16[640,2560]{1,0:T(8,128)(2,1)S(1)}, bf16[640,2560]{1,0:T(8,128)(2,1)}, u32[]{:S(2)}) copy-start(bf16[640,2560]{1,0:T(8,128)(2,1)} %param.23) | copy-start | bytes 9830404
  6.5 35.5 %copy-start.1 = (s32[64]{0:T(128)S(1)}, s32[64]{0:T(128)}, u32[]{:S(2)}) copy-start(s32[64]{0:T(128)} %param.21) | copy-start | bytes 772
  6.5 48.3 %copy-start.4 = (s32[64,4]{0,1:T(4,128)S(1)}, s32[64,4]{0,1:T(4,128)}, u32[]{:S(2)}) copy-start(s32[64,4]{0,1:T(4,128)} %param.22) | copy-start | bytes 3076
  6.5 116.5 %all-reduce.4.cloned.1.call-start = ((), (), s32[]{:S(2)}) async-start(), calls=%async_computation | async-start | bytes 163840 | tf_op jit(solution)/shard_map/psum | solution.py:130
  40.7 18.5 %copy-start.2 = (s32[1024]{0:T(1024)}, s32[1024]{0:T(1024)S(1)}, u32[]{:S(2)}) copy-start(s32[1024]{0:T(1024)S(1)} %pad_clamp_fusion.2) | copy-start | bytes 12292
  61.8 13.4 %copy-start.3 = (f32[8,2,4]{2,1,0:T(2,128)S(1)}, f32[8,2,4]{2,1,0:T(2,128)}, u32[]{:S(2)}) copy-start(f32[8,2,4]{2,1,0:T(2,128)} %get-tuple-element.11) | copy-start | bytes 772
  88.8 78.4 %all-reduce.6.cloned.1.call-start = ((), (), s32[]{:S(2)}) async-start(), calls=%async_computation.1 | async-start | bytes 163840
  127.1 6.0 %copy-start.5 = (u32[32]{0:T(128)S(1)}, u32[32]{0:T(128)}, u32[]{:S(2)}) copy-start(u32[32]{0:T(128)} %constant.93) | copy-start | bytes 388
Sparse Core Ops, SparseCore 0:
  88.9 34.0 all-reduce.3
  133.2 33.9 all-reduce.5
where the time goes:
time: 176 us
  waiting for transfers between devices  66.4 us (38%)
  blocking collectives  50.7 us (29%)
  matrix products  19.1 us (11%)
  between operations  14.2 us (8%)
  other arithmetic  13 us (7%)
  local copies, waits for them, and re-layouts  12.2 us (7%)
    psum x1, waiting for transfers between devices, local(): lax.psum(jnp.dot(attended, w_output, preferred_element_type=jnp.float32),...  33.5 us
    unnamed x3, waiting for transfers between devices  32.9 us
    all_gather x1, blocking collectives, local(): rows_all = lax.all_gather(residual_in, 'tensor', axis=0, tiled=True)  15 us
    all_gather x1, blocking collectives, local(): lax.all_gather(query_heads.reshape(req_loc, q_loc * HEAD_SIZE), 'dp', axi...  9.27 us
    all_gather x1, blocking collectives, local(): every_out = lax.all_gather(served_out, 'dp', axis=0, tiled=True)  9.24 us
    all_gather x1, blocking collectives, local(): lax.all_gather(fresh_key.reshape(req_loc, kv_loc * HEAD_SIZE), 'dp', axis...  9.03 us
    all_gather x1, blocking collectives, local(): lax.all_gather(fresh_value.reshape(req_loc, kv_loc * HEAD_SIZE), 'dp', ax...  8.12 us
    dot_general x1, matrix products, local(): jnp.dot(hidden, w_down, preferred_element_type=jnp.float32)  5.93 us
  transfers between devices with their start and end apart: 2, of which 2 were waited for; matrix products, arithmetic and copies ran while one was open for 1% of the time, Pallas kernels for 0%

commit v1 on v0

v1 whole, which is shorter than its diff:
```python
import jax
import jax.numpy as jnp
from jax import lax
from jax.sharding import PartitionSpec as P

HEAD_SIZE = 80


def norm_rows(value_rows, gain):
    value_rows = value_rows.astype(jnp.float32)
    return (
        value_rows
        * lax.rsqrt(jnp.mean(value_rows * value_rows, axis=-1, keepdims=True) + 1e-05)
        * gain.astype(jnp.float32)
    )


def apply_rotation(tensor, positions):
    half_dim = tensor.shape[-1] // 2
    inverse_freq = 1000000.0 ** (
        -(jnp.arange(half_dim, dtype=jnp.float32) * 2.0 / tensor.shape[-1])
    )
    angles = positions.astype(jnp.float32)[:, None] * inverse_freq[None, :]
    cosine = jnp.cos(angles)[:, None, :]
    sines = jnp.sin(angles)[:, None, :]
    first_half = tensor[..., :half_dim]
    second_half = tensor[..., half_dim:]
    return jnp.concatenate(
        [first_half * cosine - second_half * sines, second_half * cosine + first_half * sines],
        axis=-1,
    )


def tensor_allreduce(part, tp_count):
    step = 1
    while step < tp_count:
        pairs = [(i, i ^ step) for i in range(tp_count)]
        part = part + lax.ppermute(part, "tensor", pairs)
        step *= 2
    return part


def local(
    residual_in,
    norm_gain,
    w_query,
    key_weight,
    value_weight,
    key_page_pool,
    value_page_pool,
    lengths,
    page_table,
    w_output,
    mlp_gain,
    w_gate,
    w_up,
    w_down,
):
    dp_count = lax.axis_size("dp")
    tp_count = lax.axis_size("tensor")
    rows_loc = residual_in.shape[0]
    req_loc = rows_loc * tp_count
    kv_loc = key_page_pool.shape[1]
    q_loc = w_query.shape[1] // HEAD_SIZE
    group_width = q_loc // kv_loc
    pool_size = key_page_pool.shape[0]
    page_len = key_page_pool.shape[3]
    per_req = page_table.shape[1]
    total_reqs = page_table.shape[0]
    score_scale = 1.0 / HEAD_SIZE**0.5
    dp_index = lax.axis_index("dp")
    tp_index = lax.axis_index("tensor")

    rows_all = lax.all_to_all(
        jnp.tile(residual_in, (dp_count * tp_count, 1)),
        ("dp", "tensor"),
        0,
        0,
        tiled=True,
    )

    request_ids = jnp.arange(total_reqs, dtype=jnp.int32)
    ranking = lengths * total_reqs + request_ids
    rank = jnp.sum((ranking[None, :] < ranking[:, None]).astype(jnp.int32), axis=1)
    round_no = rank // dp_count
    column = rank % dp_count
    server = jnp.where(round_no % 2 == 0, column, dp_count - 1 - column)
    slots = jnp.arange(req_loc, dtype=jnp.int32)
    hits = (server[None, :] == dp_index) & (round_no[None, :] == slots[:, None])
    served = jnp.sum(jnp.where(hits, request_ids[None, :], 0), axis=1)
    served_len = lengths[served]

    rows_srv = rows_all[served]
    scaled_input = norm_rows(rows_srv, norm_gain).astype(jnp.bfloat16)
    query_srv = (
        apply_rotation(
            jnp.dot(scaled_input, w_query, preferred_element_type=jnp.float32).reshape(
                req_loc, q_loc, HEAD_SIZE
            ),
            served_len,
        )
        .astype(jnp.bfloat16)
        .reshape(req_loc, kv_loc, group_width, HEAD_SIZE)
    )
    key_srv = apply_rotation(
        jnp.dot(scaled_input, key_weight, preferred_element_type=jnp.float32).reshape(
            req_loc, kv_loc, HEAD_SIZE
        ),
        served_len,
    ).astype(jnp.bfloat16)
    value_srv = (
        jnp.dot(scaled_input, value_weight, preferred_element_type=jnp.float32)
        .astype(jnp.bfloat16)
        .reshape(req_loc, kv_loc, HEAD_SIZE)
    )

    page_list = page_table[served] - dp_index * pool_size
    key_rows = key_page_pool[page_list]
    value_rows = value_page_pool[page_list]
    scores = (
        jnp.einsum("rhgd,rphdc->rhgpc", query_srv, key_rows, preferred_element_type=jnp.float32)
        * score_scale
    )
    positions = (
        jnp.arange(per_req, dtype=jnp.int32)[:, None] * page_len
        + jnp.arange(page_len, dtype=jnp.int32)[None, :]
    )
    valid_pos = (positions[None, :, :] < served_len[:, None, None])[:, None, None, :, :]
    own_score = (
        jnp.einsum("rhgd,rhd->rhg", query_srv, key_srv, preferred_element_type=jnp.float32)
        * score_scale
    )
    best = jnp.maximum(jnp.max(jnp.where(valid_pos, scores, -1e30), axis=(-2, -1)), own_score)
    weights = jnp.where(valid_pos, jnp.exp(scores - best[..., None, None]), 0.0)
    own_weight = jnp.exp(own_score - best)
    numer = (
        jnp.einsum("rhgpc,rphdc->rhgd", weights, value_rows.astype(jnp.float32))
        + own_weight[..., None] * value_srv.astype(jnp.float32)[:, :, None, :]
    )
    denom = jnp.sum(weights, axis=(-2, -1)) + own_weight
    attended = (numer / denom[..., None]).reshape(req_loc, q_loc * HEAD_SIZE).astype(jnp.bfloat16)

    summed = tensor_allreduce(
        jnp.dot(attended, w_output, preferred_element_type=jnp.float32), tp_count
    )
    mixed = rows_srv.astype(jnp.float32) + summed
    normed_mlp = norm_rows(mixed, mlp_gain).astype(jnp.bfloat16)
    gate_act = jnp.dot(normed_mlp, w_gate, preferred_element_type=jnp.float32)
    up_act = jnp.dot(normed_mlp, w_up, preferred_element_type=jnp.float32)
    hidden = (jax.nn.silu(gate_act) * up_act).astype(jnp.bfloat16)
    down_sum = tensor_allreduce(
        jnp.dot(hidden, w_down, preferred_element_type=jnp.float32), tp_count
    )
    final = (mixed + down_sum).astype(jnp.bfloat16)

    dest_rows = (
        jnp.arange(dp_count, dtype=jnp.int32)[:, None] * req_loc
        + tp_index * rows_loc
        + jnp.arange(rows_loc, dtype=jnp.int32)[None, :]
    ).reshape(-1)
    outgoing = final[round_no[dest_rows]]
    incoming = lax.all_to_all(outgoing, "dp", 0, 0, tiled=True)
    mine = dp_index * req_loc + tp_index * rows_loc + jnp.arange(rows_loc, dtype=jnp.int32)
    pick = server[mine] * rows_loc + jnp.arange(rows_loc, dtype=jnp.int32)
    return incoming[pick]


def solution(mesh):
    return jax.shard_map(
        local,
        mesh=mesh,
        in_specs=(
            P(("dp", "tensor"), None),
            P(),
            P(None, "tensor"),
            P(None, "tensor"),
            P(None, "tensor"),
            P("dp", "tensor", None, None),
            P("dp", "tensor", None, None),
            P(),
            P(),
            P("tensor", None),
            P(),
            P(None, "tensor"),
            P(None, "tensor"),
            P("tensor", None),
        ),
        out_specs=P(("dp", "tensor"), None),
        check_vma=False,
    )
```

time: 176 us -> 78.9 us (0.45)
  blocking collectives: 50.7 us -> 0 us
  waiting for transfers between devices: 66.4 us -> 19.7 us
  starting transfers between devices: 0.04 us -> 17.8 us
  between operations: 14.2 us -> 0.19 us
  other arithmetic: 13 us -> 3.82 us
  local copies, waits for them, and re-layouts: 12.2 us -> 18.5 us
    all_gather x5 -> x0, blocking collectives: 50.7 us -> none  [the longest x1 15 us: local(): rows_all = lax.all_gather(residual_in, 'tensor', axis=0, tiled=True)]
    psum x1 -> x0, waiting for transfers between devices: 33.5 us -> none  [local(): lax.psum(jnp.dot(attended, w_output, preferred_element_type=jnp.float32),...]
    unnamed x3 -> x0, waiting for transfers between devices: 32.9 us -> none
    ppermute x0 -> x4, waiting for transfers between devices: none -> 14.6 us  [tensor_allreduce(): part = part + lax.ppermute(part, 'tensor', pairs)]
    all_to_all x0 -> x2, starting transfers between devices: none -> 11.1 us  [the longest x1 7.41 us: local(): lax.all_to_all(jnp.tile(residual_in, (dp_count * tp_count, 1)), ('dp', 't...]
    ppermute x0 -> x4, starting transfers between devices: none -> 6.78 us  [tensor_allreduce(): part = part + lax.ppermute(part, 'tensor', pairs)]
    all_to_all x0 -> x2, waiting for transfers between devices: none -> 5.1 us  [the longest x1 5.1 us: local(): incoming = lax.all_to_all(outgoing, 'dp', 0, 0, tiled=True)]
    sort x2 -> x0, other arithmetic: 4.07 us -> none  [the longest x1 2.04 us: local(): rank = jnp.argsort(order, stable=True)]
  transfers between devices with their start and end apart: 2 -> 6, of which waited for: 2 -> 5; matrix products, arithmetic and copies ran while one was open for 1% -> 16% of each run, Pallas kernels for 0% -> 0%
where the time goes in v1:
time: 78.9 us; the launch traced here: 78.1 us
  waiting for transfers between devices  19.7 us (25%)
  local copies, waits for them, and re-layouts  18.5 us (23%)
  matrix products  18.1 us (23%)
  starting transfers between devices  17.8 us (23%)
  other arithmetic  3.82 us (5%)
    ppermute x4, waiting for transfers between devices, tensor_allreduce(): part = part + lax.ppermute(part, 'tensor', pairs)  14.6 us
    all_to_all x1, starting transfers between devices, local(): lax.all_to_all(jnp.tile(residual_in, (dp_count * tp_count, 1)), ('dp', 't...  7.41 us
    ppermute x4, starting transfers between devices, tensor_allreduce(): part = part + lax.ppermute(part, 'tensor', pairs)  6.78 us
    dot_general x1, matrix products, local(): jnp.dot(hidden, w_down, preferred_element_type=jnp.float32)  5.29 us
    all_to_all x1, waiting for transfers between devices, local(): incoming = lax.all_to_all(outgoing, 'dp', 0, 0, tiled=True)  5.1 us
    all_to_all x1, starting transfers between devices, local(): incoming = lax.all_to_all(outgoing, 'dp', 0, 0, tiled=True)  3.64 us
    gather x1, local copies, waits for them, and re-layouts, local(): key_rows = key_page_pool[page_list]  3.11 us
    gather x1, local copies, waits for them, and re-layouts, local(): value_rows = value_page_pool[page_list]  3.09 us
  transfers between devices with their start and end apart: 6, of which 5 were waited for; matrix products, arithmetic and copies ran while one was open for 16% of the time, Pallas kernels for 0%

profile of v1, /device:TPU:0, one launch (start us, length us, event | category | flops | bytes accessed | tf_op | source)
XLA Modules:
  0.0 78.1 jit_solution(331174364111790595)
XLA Ops:
  0.0 1.8 %tile.2 = bf16[32,2,2560]{2,1,0:T(2,128)(2,1)} broadcast(bf16[2,2560]{1,0:T(2,128)(2,1)} %param.14), dimensions={1,2} | broadcast | bytes 337920 | tf_op jit(solution)/shard_map/tile | solution.py:75
  1.8 7.4 %all-to-all-start = ((bf16[32,2,2560]{2,1,0:T(2,128)(2,1)}), bf16[32,2,2560]{2,1,0:T(2,128)(2,1)}, u32[]{:S(2)}, u32[]{:S(2)}) async-start(bf16[32,2,2560]{2,1,0:T(2,128)(2,1)} %tile.2), calls=%async_computation | async-start | bytes 655360 | tf_op jit(solution)/shard_map/all_to_all | solution.py:74
  9.2 0.7 iota_add_fusion.2
  10.2 0.7 convert_element_type.58
  10.9 1.3 %gather_fusion.1 = s32[8]{0:T(128)S(1)} fusion(s32[64]{0:T(128)} %param.21, s32[1024]{0:T(1024)S(1)} %pad_clamp_fusion.5), kind=kCustom, calls=%fused_computation.1 | custom fusion | bytes 96 | tf_op jit(solution)/shard_map/gather | solution.py:91
  12.2 0.8 copy.25
  13.9 3.1 %gather_fusion.3 = bf16[32,2,80,128]{3,2,1,0:T(8,128)(2,1)} fusion(bf16[32,2,80,128]{3,2,1,0:T(8,128)(2,1)} %param.19, s32[1024]{0:T(1024)S(1)} %pad_clamp_fusion.4), kind=kCustom, calls=%fused_computation.3 | custom fusion | bytes 2621568 | tf_op jit(solution)/shard_map/gather | solution.py:118
  17.0 3.1 %gather_fusion.4 = bf16[32,2,80,128]{3,2,1,0:T(8,128)(2,1)} fusion(bf16[32,2,80,128]{3,2,1,0:T(8,128)(2,1)} %param.20, s32[1024]{0:T(1024)S(1)} %pad_clamp_fusion.4), kind=kCustom, calls=%fused_computation.4 | custom fusion | bytes 2621568 | tf_op jit(solution)/shard_map/gather | solution.py:119
  20.3 0.7 gather_fusion.5
  21.2 1.8 %all_to_all.15 = bf16[64,2560]{1,0:T(8,128)(2,1)} reshape(bf16[32,2,2560]{2,1,0:T(2,128)(2,1)} %all-to-all-done) | data formatting | bytes 655360 | tf_op jit(solution)/shard_map/all_to_all | solution.py:74
  23.0 1.6 %gather_fusion = bf16[8,2560]{1,0:T(8,128)(2,1)S(1)} fusion(bf16[64,2560]{1,0:T(8,128)(2,1)} %all_to_all.15, s32[1024]{0:T(1024)S(1)} %pad_clamp_fusion.5), kind=kCustom, calls=%fused_computation | custom fusion | bytes 81952 | tf_op jit(solution)/shard_map/gather | solution.py:93
  24.8 1.5 %fusion.49 = f32[8,160]{1,0:T(8,128)S(1)} fusion(bf16[2560,160]{0,1:T(8,128)(2,1)} %param.17, bf16[8,2560]{1,0:T(8,128)(2,1)S(1)} %gather_fusion, f32[2560]{0:T(1024)S(1)} %convert_element_type.58, f32[8]{0:T(128)S(1)} %add_rsqrt_fusion.1), kind=kOutput, calls=%fused_computation.103 | convolution fusion | flops 6635520 | bytes 875552 | tf_op jit(solution)/shard_map/dot_general | solution.py:106
  26.4 2.5 %fusion.51 = f32[8,640]{1,0:T(8,128)S(1)} fusion(bf16[2560,640]{1,0:T(8,128)(2,1)} %param.16, bf16[8,2560]{1,0:T(8,128)(2,1)S(1)} %gather_fusion, f32[2560]{0:T(1024)S(1)} %convert_element_type.58, f32[8]{0:T(128)S(1)} %add_rsqrt_fusion.1), kind=kOutput, calls=%fused_computation.104 | convolution fusion | flops 26296320 | bytes 3348512 | tf_op jit(solution)/shard_map/dot_general | solution.py:97
  29.4 1.8 %select_reduce_fusion = (f32[8,2,4]{2,1,0:T(2,128)S(1)}, f32[8,2,4,4,128]{4,2,3,1,0:T(4,128)S(1)}) fusion(pred[8,4,128]{2,1,0:T(4,128)(4,1)S(1)} %broadcast_compare_fusion, bf16[8,4,2,80,128]{4,3,2,1,0:T(8,128)(2,1)} %bitcast.55, bf16[8,2,4,40]{3,2,1,0:T(4,128)(2,1)S(1)} %bitcast.61, bf16[8,2,4,40]{3,2,1,0:T(4,128)(2,1)S(1)} %bitcast.59), kind=kOutput, calls=%fused_computation.24 | convolution fusion | flops 5361600 | bytes 1456384 | tf_op jit(solution)/shard_map/rhgd,rphdc->rhgpc/dot_general | solution.py:121
  31.4 1.5 %fusion.21 = f32[8,160]{1,0:T(8,128)S(1)} fusion(bf16[2560,160]{0,1:T(8,128)(2,1)} %param.18, bf16[8,2560]{1,0:T(8,128)(2,1)S(1)} %gather_fusion, f32[2560]{0:T(1024)S(1)} %convert_element_type.58, f32[8]{0:T(128)S(1)} %add_rsqrt_fusion.1), kind=kOutput, calls=%fused_computation.22 | convolution fusion | flops 6638080 | bytes 875552 | tf_op jit(solution)/shard_map/dot_general | solution.py:112
  33.0 1.8 %fusion.16 = bf16[8,2,4,80]{3,2,1,0:T(4,128)(2,1)S(1)} fusion(bf16[8,4,2,80,128]{4,3,2,1,0:T(8,128)(2,1)} %bitcast.54, f32[8,2,4,4,128]{4,2,3,1,0:T(4,128)S(1)} %get-tuple-element.19, f32[8,2,4]{2,1,0:T(2,128)S(1)} %multiply_maximum_fusion, pred[8,4,128]{2,1,0:T(4,128)(4,1)S(1)} %broadcast_compare_fusion, f32[8,2,4]{2,1,0:T(2,128)S(1)} %get-tuple-element.7, ...), kind=kOutput, calls=%fused_computation.18 | convolution fusion | flops 5328896 | bytes 1462016 | tf_op jit(solution)/shard_map/rhgpc,rphdc->rhgd/dot_general | solution.py:137
  35.5 1.7 %collective-permute-start = (f32[8,2560]{1,0:T(8,128)S(1)}, f32[8,2560]{1,0:T(8,128)S(1)}, u32[]{:S(2)}, u32[]{:S(2)}) collective-permute-start(f32[8,2560]{1,0:T(8,128)S(1)} %fusion.54), channel_id=1, source_target_pairs={{0,1},{1,0},{2,3},{3,2},{4,5},{5,4},{6,7},{7,6},{8,9},{9,8},{10,11... | collective-permute-start | bytes 245768 | tf_op jit(solution)/shard_map/ppermute | solution.py:38
  37.2 2.8 %collective-permute-done = f32[8,2560]{1,0:T(8,128)S(1)} collective-permute-done((f32[8,2560]{1,0:T(8,128)S(1)}, f32[8,2560]{1,0:T(8,128)S(1)}, u32[]{:S(2)}, u32[]{:S(2)}) %collective-permute-start) | collective-permute-done | bytes 81952 | tf_op jit(solution)/shard_map/ppermute | solution.py:38
  40.0 2.6 %collective-permute-start.1 = (f32[8,2560]{1,0:T(8,128)S(1)}, f32[8,2560]{1,0:T(8,128)}, u32[]{:S(2)}, u32[]{:S(2)}) collective-permute-start(f32[8,2560]{1,0:T(8,128)S(1)} %add.233), channel_id=1, source_target_pairs={{0,2},{1,3},{2,0},{3,1},{4,6},{5,7},{6,4},{7,5},{8,10},{9,11},{10,... | collective-permute-start | bytes 245768 | tf_op jit(solution)/shard_map/ppermute | solution.py:38
  42.7 0.6 gather_fusion.7
  43.3 3.4 %collective-permute-done.1 = f32[8,2560]{1,0:T(8,128)} collective-permute-done((f32[8,2560]{1,0:T(8,128)S(1)}, f32[8,2560]{1,0:T(8,128)}, u32[]{:S(2)}, u32[]{:S(2)}) %collective-permute-start.1) | collective-permute-done | bytes 81952 | tf_op jit(solution)/shard_map/ppermute | solution.py:38
  46.8 1.0 %multiply_reduce_fusion = (f32[8]{0:T(128)S(1)}, f32[8,2560]{1,0:T(8,128)S(1)}) fusion(f32[8,2560]{1,0:T(8,128)S(1)} %add.233, f32[8,2560]{1,0:T(8,128)} %collective-permute-done.1, bf16[8,2560]{1,0:T(8,128)(2,1)S(1)} %gather_fusion), kind=kLoop, calls=%fused_computation.34 | loop fusion | flops 102392 | bytes 286752 | tf_op jit(solution)/shard_map/reduce_sum | solution.py:13
  47.8 3.0 %fusion.47 = f32[8,896]{1,0:T(8,128)S(1)} fusion(bf16[2560,896]{1,0:T(8,128)(2,1)} %param.25, f32[8,2560]{1,0:T(8,128)S(1)} %get-tuple-element.6, f32[2560]{0:T(1024)S(1)} %convert_element_type.66, f32[8]{0:T(128)S(1)} %add_rsqrt_fusion), kind=kOutput, calls=%fused_computation.102 | convolution fusion | flops 36761600 | bytes 4708384 | tf_op jit(solution)/shard_map/dot_general | solution.py:148
  50.8 5.3 %fusion.20 = f32[8,2560]{1,0:T(8,128)S(1)} fusion(bf16[896,2560]{1,0:T(8,128)(2,1)} %param.27, bf16[2560,896]{1,0:T(8,128)(2,1)} %param.26, f32[8,896]{1,0:T(8,128)S(1)} %fusion.47, f32[8,2560]{1,0:T(8,128)S(1)} %get-tuple-element.6, f32[2560]{0:T(1024)S(1)} %convert_element_type.66, f32[8]{0:T(128)S(1)} %add_rsqrt_fusion), kind=kOutput, calls=%fused_computation.20 | convolution fusion | flops 73504768 | bytes 9377824 | tf_op jit(solution)/shard_map/dot_general | solution.py:152
  56.7 3.9 %collective-permute-done.2 = f32[8,2560]{1,0:T(8,128)S(1)} collective-permute-done((f32[8,2560]{1,0:T(8,128)S(1)}, f32[8,2560]{1,0:T(8,128)S(1)}, u32[]{:S(2)}, u32[]{:S(2)}) %collective-permute-start.2) | collective-permute-done | bytes 81952 | tf_op jit(solution)/shard_map/ppermute | solution.py:38
  60.6 1.9 %collective-permute-start.3 = (f32[8,2560]{1,0:T(8,128)S(1)}, f32[8,2560]{1,0:T(8,128)S(1)}, u32[]{:S(2)}, u32[]{:S(2)}) collective-permute-start(f32[8,2560]{1,0:T(8,128)S(1)} %add.238), channel_id=1, source_target_pairs={{0,2},{1,3},{2,0},{3,1},{4,6},{5,7},{6,4},{7,5},{8,10},{9,11},{10,... | collective-permute-start | bytes 245768 | tf_op jit(solution)/shard_map/ppermute | solution.py:38
  62.5 4.4 %collective-permute-done.3 = f32[8,2560]{1,0:T(8,128)S(1)} collective-permute-done((f32[8,2560]{1,0:T(8,128)S(1)}, f32[8,2560]{1,0:T(8,128)S(1)}, u32[]{:S(2)}, u32[]{:S(2)}) %collective-permute-start.3) | collective-permute-done | bytes 81952 | tf_op jit(solution)/shard_map/ppermute | solution.py:38
  66.9 0.6 gather_fusion.6
  67.5 0.7 all_to_all.16
  68.2 3.6 %all-to-all-start.1 = ((bf16[8,2,2560]{2,1,0:T(2,128)(2,1)}), bf16[8,2,2560]{2,1,0:T(2,128)(2,1)S(1)}, u32[]{:S(2)}, u32[]{:S(2)}) async-start(bf16[8,2,2560]{2,1,0:T(2,128)(2,1)} %all_to_all.16), calls=%async_computation.1 | async-start | bytes 163840 | tf_op jit(solution)/shard_map/all_to_all | solution.py:162
  71.8 5.1 %all-to-all-done.1 = bf16[8,2,2560]{2,1,0:T(2,128)(2,1)S(1)} async-done(((bf16[8,2,2560]{2,1,0:T(2,128)(2,1)}), bf16[8,2,2560]{2,1,0:T(2,128)(2,1)S(1)}, u32[]{:S(2)}, u32[]{:S(2)}) %all-to-all-start.1) | async-done | bytes 81952 | tf_op jit(solution)/shard_map/all_to_all | solution.py:162
  77.0 1.2 %gather_fusion.8 = bf16[2,2560]{1,0:T(2,128)(2,1)} fusion(bf16[16,2560]{1,0:T(8,128)(2,1)S(1)} %all_to_all.18, s32[1024]{0:T(1024)S(1)} %pad_clamp_fusion), kind=kCustom, calls=%fused_computation.8 | custom fusion | bytes 20488 | tf_op jit(solution)/shard_map/gather | solution.py:165
  (55 shorter events, 4.0 us)
Async XLA Ops:
  0.0 34.9 %copy-start = (bf16[640,2560]{1,0:T(8,128)(2,1)S(1)}, bf16[640,2560]{1,0:T(8,128)(2,1)}, u32[]{:S(2)}) copy-start(bf16[640,2560]{1,0:T(8,128)(2,1)} %param.23) | copy-start | bytes 9830404
  1.8 18.4 %copy-start.1 = (bf16[2560]{0:T(1024)(128)(2,1)S(1)}, bf16[2560]{0:T(1024)(128)(2,1)}, u32[]{:S(2)}) copy-start(bf16[2560]{0:T(1024)(128)(2,1)} %param.24) | copy-start | bytes 15364
  1.8 19.4 %all-to-all-start = ((bf16[32,2,2560]{2,1,0:T(2,128)(2,1)}), bf16[32,2,2560]{2,1,0:T(2,128)(2,1)}, u32[]{:S(2)}, u32[]{:S(2)}) async-start(bf16[32,2,2560]{2,1,0:T(2,128)(2,1)} %tile.2), calls=%async_computation | async-start | bytes 655360 | tf_op jit(solution)/shard_map/all_to_all | solution.py:74
  35.5 4.5 %collective-permute-start = (f32[8,2560]{1,0:T(8,128)S(1)}, f32[8,2560]{1,0:T(8,128)S(1)}, u32[]{:S(2)}, u32[]{:S(2)}) collective-permute-start(f32[8,2560]{1,0:T(8,128)S(1)} %fusion.54), channel_id=1, source_target_pairs={{0,1},{1,0},{2,3},{3,2},{4,5},{5,4},{6,7},{7,6},{8,9},{9,8},{10,11... | collective-permute-start | bytes 245768 | tf_op jit(solution)/shard_map/ppermute | solution.py:38
  40.0 6.7 %collective-permute-start.1 = (f32[8,2560]{1,0:T(8,128)S(1)}, f32[8,2560]{1,0:T(8,128)}, u32[]{:S(2)}, u32[]{:S(2)}) collective-permute-start(f32[8,2560]{1,0:T(8,128)S(1)} %add.233), channel_id=1, source_target_pairs={{0,2},{1,3},{2,0},{3,1},{4,6},{5,7},{6,4},{7,5},{8,10},{9,11},{10,... | collective-permute-start | bytes 245768 | tf_op jit(solution)/shard_map/ppermute | solution.py:38
  56.1 4.5 %collective-permute-start.2 = (f32[8,2560]{1,0:T(8,128)S(1)}, f32[8,2560]{1,0:T(8,128)S(1)}, u32[]{:S(2)}, u32[]{:S(2)}) collective-permute-start(f32[8,2560]{1,0:T(8,128)S(1)} %fusion.20), channel_id=1, source_target_pairs={{0,1},{1,0},{2,3},{3,2},{4,5},{5,4},{6,7},{7,6},{8,9},{9,8},{10,11... | collective-permute-start | bytes 245768 | tf_op jit(solution)/shard_map/ppermute | solution.py:38
  60.6 6.3 %collective-permute-start.3 = (f32[8,2560]{1,0:T(8,128)S(1)}, f32[8,2560]{1,0:T(8,128)S(1)}, u32[]{:S(2)}, u32[]{:S(2)}) collective-permute-start(f32[8,2560]{1,0:T(8,128)S(1)} %add.238), channel_id=1, source_target_pairs={{0,2},{1,3},{2,0},{3,1},{4,6},{5,7},{6,4},{7,5},{8,10},{9,11},{10,... | collective-permute-start | bytes 245768 | tf_op jit(solution)/shard_map/ppermute | solution.py:38
  68.2 8.7 %all-to-all-start.1 = ((bf16[8,2,2560]{2,1,0:T(2,128)(2,1)}), bf16[8,2,2560]{2,1,0:T(2,128)(2,1)S(1)}, u32[]{:S(2)}, u32[]{:S(2)}) async-start(bf16[8,2,2560]{2,1,0:T(2,128)(2,1)} %all_to_all.16), calls=%async_computation.1 | async-start | bytes 163840 | tf_op jit(solution)/shard_map/all_to_all | solution.py:162

commit v2 on v1

--- a/solution.py
+++ b/solution.py
@@ -71,8 +71,11 @@
     dp_index = lax.axis_index("dp")
     tp_index = lax.axis_index("tensor")
 
+    width = residual_in.shape[1]
+    dev_count = dp_count * tp_count
+    packed = residual_in.reshape(1, rows_loc * width)
     rows_all = lax.all_to_all(
-        jnp.tile(residual_in, (dp_count * tp_count, 1)),
+        jnp.broadcast_to(packed, (dev_count, rows_loc * width)),
         ("dp", "tensor"),
         0,
         0,
@@ -90,7 +93,11 @@
     served = jnp.sum(jnp.where(hits, request_ids[None, :], 0), axis=1)
     served_len = lengths[served]
 
-    rows_srv = rows_all[served]
+    src_hot = (served[:, None] // rows_loc == jnp.arange(dev_count, dtype=jnp.int32)[None, :])
+    picked = jnp.dot(src_hot.astype(jnp.bfloat16), rows_all, preferred_element_type=jnp.float32)
+    picked = picked.reshape(req_loc, rows_loc, width)
+    seg_hot = served[:, None] % rows_loc == jnp.arange(rows_loc, dtype=jnp.int32)[None, :]
+    rows_srv = jnp.sum(jnp.where(seg_hot[:, :, None], picked, 0.0), axis=1).astype(jnp.bfloat16)
     scaled_input = norm_rows(rows_srv, norm_gain).astype(jnp.bfloat16)
     query_srv = (
         apply_rotation(
@@ -158,11 +165,17 @@
         + tp_index * rows_loc
         + jnp.arange(rows_loc, dtype=jnp.int32)[None, :]
     ).reshape(-1)
-    outgoing = final[round_no[dest_rows]]
+    out_hot = round_no[dest_rows][:, None] == slots[None, :]
+    outgoing = jnp.dot(
+        out_hot.astype(jnp.bfloat16), final, preferred_element_type=jnp.float32
+    ).astype(jnp.bfloat16)
     incoming = lax.all_to_all(outgoing, "dp", 0, 0, tiled=True)
     mine = dp_index * req_loc + tp_index * rows_loc + jnp.arange(rows_loc, dtype=jnp.int32)
     pick = server[mine] * rows_loc + jnp.arange(rows_loc, dtype=jnp.int32)
-    return incoming[pick]
+    in_hot = pick[:, None] == jnp.arange(dp_count * rows_loc, dtype=jnp.int32)[None, :]
+    return jnp.dot(
+        in_hot.astype(jnp.bfloat16), incoming, preferred_element_type=jnp.float32
+    ).astype(jnp.bfloat16)
 
 
 def solution(mesh):

time: 78.9 us -> 86 us (1.090)
  other arithmetic: 3.82 us -> 8.07 us
  starting transfers between devices: 17.8 us -> 15.3 us
  matrix products: 18.1 us -> 20.2 us
  waiting for transfers between devices: 19.7 us -> 21.7 us
  local copies, waits for them, and re-layouts: 18.5 us -> 19.6 us
    unnamed x5 -> x14, local copies, waits for them, and re-layouts: 0.79 us -> 6.47 us
    broadcast_in_dim x0 -> x1, other arithmetic: none -> 4.27 us  [local(): jnp.broadcast_to(packed, (dev_count, rows_loc * width))]
    gather x4 -> x1, local copies, waits for them, and re-layouts: 4.05 us -> 0.66 us  [local(): out_hot = round_no[dest_rows][:, None] == slots[None, :]]
    broadcast_in_dim x0 -> x3, local copies, waits for them, and re-layouts: none -> 2.55 us  [local(): jnp.broadcast_to(packed, (dev_count, rows_loc * width))]
    ppermute x4, starting transfers between devices: 6.78 us -> 4.56 us  [tensor_allreduce(): part = part + lax.ppermute(part, 'tensor', pairs)]
    dot_general x0 -> x3, matrix products: none -> 2.11 us  [the longest x1 1.1 us: local(): jnp.dot(out_hot.astype(jnp.bfloat16), final, preferred_element_type=jnp.f...]
    all_to_all x1 -> x0, local copies, waits for them, and re-layouts: 1.83 us -> none  [local(): lax.all_to_all(jnp.tile(residual_in, (dp_count * tp_count, 1)), ('dp', 't...]
    another operation x1 -> x0, local copies, waits for them, and re-layouts: 1.76 us -> none  [local(): jnp.tile(residual_in, (dp_count * tp_count, 1))]
  transfers between devices with their start and end apart: 6 -> 6, of which waited for: 5 -> 6; matrix products, arithmetic and copies ran while one was open for 16% -> 14% of each run, Pallas kernels for 0% -> 0%
where the time goes in v2:
time: 86 us; the launch traced here: 85.1 us
  waiting for transfers between devices  21.7 us (25%)
  matrix products  20.2 us (23%)
  local copies, waits for them, and re-layouts  19.6 us (23%)
  starting transfers between devices  15.3 us (18%)
  other arithmetic  8.07 us (9%)
    ppermute x4, waiting for transfers between devices, tensor_allreduce(): part = part + lax.ppermute(part, 'tensor', pairs)  16.2 us
    all_to_all x1, starting transfers between devices, local(): lax.all_to_all(jnp.broadcast_to(packed, (dev_count, rows_loc * width)), (...  7.42 us
    unnamed x14, local copies, waits for them, and re-layouts  6.47 us
    dot_general x1, matrix products, local(): jnp.dot(hidden, w_down, preferred_element_type=jnp.float32)  5.29 us
    all_to_all x1, waiting for transfers between devices, local(): incoming = lax.all_to_all(outgoing, 'dp', 0, 0, tiled=True)  5.02 us
    ppermute x4, starting transfers between devices, tensor_allreduce(): part = part + lax.ppermute(part, 'tensor', pairs)  4.56 us
    broadcast_in_dim x1, other arithmetic, local(): jnp.broadcast_to(packed, (dev_count, rows_loc * width))  4.27 us
    all_to_all x1, starting transfers between devices, local(): incoming = lax.all_to_all(outgoing, 'dp', 0, 0, tiled=True)  3.36 us
  transfers between devices with their start and end apart: 6, of which 6 were waited for; matrix products, arithmetic and copies ran while one was open for 14% of the time, Pallas kernels for 0%

profile of v2, /device:TPU:0, one launch (start us, length us, event | category | flops | bytes accessed | tf_op | source)
XLA Modules:
  0.0 85.1 jit_solution(5829598026609471288)
XLA Ops:
  0.0 0.9 %broadcast_in_dim.45 = bf16[5120]{0:T(1024)(128)(2,1)S(1)} reshape(bf16[2,2560]{1,0:T(2,128)(2,1)} %param.14) | data formatting | bytes 20480 | tf_op jit(solution)/shard_map/broadcast_in_dim | solution.py:78
  0.9 1.2 %broadcast_in_dim.46 = bf16[32,1,5120]{2,1,0:T(2,128)(2,1)} broadcast(bf16[5120]{0:T(1024)(128)(2,1)S(1)} %broadcast_in_dim.45), dimensions={2} | broadcast | bytes 337920 | tf_op jit(solution)/shard_map/broadcast_in_dim | solution.py:78
  2.6 4.3 %reduce = bf16[32,5120]{1,0:T(8,128)(2,1)} reduce(bf16[32,1,5120]{2,1,0:T(2,128)(2,1)} %broadcast_in_dim.46, bf16[]{:T(256)} %broadcast.501), dimensions={1}, to_apply=%broadcast_in_dim.46.reduce_sub_computation | reduce | bytes 655362 | tf_op jit(solution)/shard_map/broadcast_in_dim | solution.py:78
  6.8 1.9 %reshape.408 = bf16[32,2,2560]{2,1,0:T(2,128)(2,1)} reshape(bf16[32,5120]{1,0:T(8,128)(2,1)} %reduce) | data formatting | bytes 655360
  8.8 7.4 %all-to-all-start = ((bf16[32,2,2560]{2,1,0:T(2,128)(2,1)}), bf16[32,2,2560]{2,1,0:T(2,128)(2,1)}, u32[]{:S(2)}, u32[]{:S(2)}) async-start(bf16[32,2,2560]{2,1,0:T(2,128)(2,1)} %reshape.408), calls=%async_computation | async-start | bytes 655360 | tf_op jit(solution)/shard_map/all_to_all | solution.py:77
  16.2 0.7 iota_add_fusion.3
  17.2 0.7 convert_element_type.71
  19.6 3.1 %gather_fusion.4 = bf16[32,2,80,128]{3,2,1,0:T(8,128)(2,1)} fusion(bf16[32,2,80,128]{3,2,1,0:T(8,128)(2,1)} %param.19, s32[1024]{0:T(1024)S(1)} %pad_clamp_fusion), kind=kCustom, calls=%fused_computation.4 | custom fusion | bytes 2621568 | tf_op jit(solution)/shard_map/gather | solution.py:125
  22.7 3.1 %gather_fusion.5 = bf16[32,2,80,128]{3,2,1,0:T(8,128)(2,1)} fusion(bf16[32,2,80,128]{3,2,1,0:T(8,128)(2,1)} %param.20, s32[1024]{0:T(1024)S(1)} %pad_clamp_fusion), kind=kCustom, calls=%fused_computation.5 | custom fusion | bytes 2621568 | tf_op jit(solution)/shard_map/gather | solution.py:126
  27.2 3.2 %reshape.409 = bf16[32,1,5120]{2,1,0:T(2,128)(2,1)} reshape(bf16[32,2,2560]{2,1,0:T(2,128)(2,1)} %all-to-all-done) | data formatting | bytes 655360
  30.4 1.2 %copy.42 = bf16[32,1,5120]{2,0,1:T(8,128)(2,1)S(1)} copy(bf16[32,1,5120]{2,1,0:T(2,128)(2,1)} %reshape.409) | data formatting | bytes 655360
  32.0 1.5 %fusion.58 = f32[8,160]{1,0:T(8,128)S(1)} fusion(bf16[2560,160]{0,1:T(8,128)(2,1)} %param.17, f32[2560]{0:T(1024)S(1)} %convert_element_type.71, f32[8]{0:T(128)S(1)} %add_rsqrt_fusion.1, bf16[8,2560]{1,0:T(8,128)(2,1)S(1)} %fusion.7), kind=kOutput, calls=%fused_computation.115 | convolution fusion | flops 6635520 | bytes 875552 | tf_op jit(solution)/shard_map/dot_general | solution.py:113
  33.5 2.5 %fusion.60 = f32[8,640]{1,0:T(8,128)S(1)} fusion(bf16[2560,640]{1,0:T(8,128)(2,1)} %param.16, f32[2560]{0:T(1024)S(1)} %convert_element_type.71, f32[8]{0:T(128)S(1)} %add_rsqrt_fusion.1, bf16[8,2560]{1,0:T(8,128)(2,1)S(1)} %fusion.7), kind=kOutput, calls=%fused_computation.116 | convolution fusion | flops 26296320 | bytes 3348512 | tf_op jit(solution)/shard_map/dot_general | solution.py:104
  36.6 1.8 %select_reduce_fusion = (f32[8,2,4]{2,1,0:T(2,128)S(1)}, f32[8,2,4,4,128]{4,2,3,1,0:T(4,128)S(1)}) fusion(pred[8,4,128]{2,1,0:T(4,128)(4,1)S(1)} %broadcast_compare_fusion, bf16[8,4,2,80,128]{4,3,2,1,0:T(8,128)(2,1)} %bitcast.56, bf16[8,2,4,40]{3,2,1,0:T(4,128)(2,1)S(1)} %bitcast.63, bf16[8,2,4,40]{3,2,1,0:T(4,128)(2,1)S(1)} %bitcast.61), kind=kOutput, calls=%fused_computation.27 | convolution fusion | flops 5361600 | bytes 1456384 | tf_op jit(solution)/shard_map/rhgd,rphdc->rhgpc/dot_general | solution.py:128
  38.6 1.5 %fusion.22 = f32[8,160]{1,0:T(8,128)S(1)} fusion(bf16[2560,160]{0,1:T(8,128)(2,1)} %param.18, f32[2560]{0:T(1024)S(1)} %convert_element_type.71, f32[8]{0:T(128)S(1)} %add_rsqrt_fusion.1, bf16[8,2560]{1,0:T(8,128)(2,1)S(1)} %fusion.7), kind=kOutput, calls=%fused_computation.23 | convolution fusion | flops 6638080 | bytes 875552 | tf_op jit(solution)/shard_map/dot_general | solution.py:119
  40.2 1.8 %fusion.17 = bf16[8,2,4,80]{3,2,1,0:T(4,128)(2,1)S(1)} fusion(bf16[8,4,2,80,128]{4,3,2,1,0:T(8,128)(2,1)} %bitcast.55, f32[8,2,4,4,128]{4,2,3,1,0:T(4,128)S(1)} %get-tuple-element.21, f32[8,2,4]{2,1,0:T(2,128)S(1)} %multiply_maximum_fusion, pred[8,4,128]{2,1,0:T(4,128)(4,1)S(1)} %broadcast_compare_fusion, f32[8,2,4]{2,1,0:T(2,128)S(1)} %get-tuple-element.7, ...), kind=kOutput, calls=%fused_computation.19 | convolution fusion | flops 5328896 | bytes 1462016 | tf_op jit(solution)/shard_map/rhgpc,rphdc->rhgd/dot_general | solution.py:144
  42.7 1.7 %collective-permute-start = (f32[8,2560]{1,0:T(8,128)S(1)}, f32[8,2560]{1,0:T(8,128)S(1)}, u32[]{:S(2)}, u32[]{:S(2)}) collective-permute-start(f32[8,2560]{1,0:T(8,128)S(1)} %fusion.62), channel_id=1, source_target_pairs={{0,1},{1,0},{2,3},{3,2},{4,5},{5,4},{6,7},{7,6},{8,9},{9,8},{10,11... | collective-permute-start | bytes 245768 | tf_op jit(solution)/shard_map/ppermute | solution.py:38
  44.4 3.4 %collective-permute-done = f32[8,2560]{1,0:T(8,128)S(1)} collective-permute-done((f32[8,2560]{1,0:T(8,128)S(1)}, f32[8,2560]{1,0:T(8,128)S(1)}, u32[]{:S(2)}, u32[]{:S(2)}) %collective-permute-start) | collective-permute-done | bytes 81952 | tf_op jit(solution)/shard_map/ppermute | solution.py:38
  47.9 1.5 %collective-permute-start.1 = (f32[8,2560]{1,0:T(8,128)S(1)}, f32[8,2560]{1,0:T(8,128)}, u32[]{:S(2)}, u32[]{:S(2)}) collective-permute-start(f32[8,2560]{1,0:T(8,128)S(1)} %add.242), channel_id=1, source_target_pairs={{0,2},{1,3},{2,0},{3,1},{4,6},{5,7},{6,4},{7,5},{8,10},{9,11},{10,... | collective-permute-start | bytes 245768 | tf_op jit(solution)/shard_map/ppermute | solution.py:38
  49.4 0.7 gather_fusion.1
  50.1 4.2 %collective-permute-done.1 = f32[8,2560]{1,0:T(8,128)} collective-permute-done((f32[8,2560]{1,0:T(8,128)S(1)}, f32[8,2560]{1,0:T(8,128)}, u32[]{:S(2)}, u32[]{:S(2)}) %collective-permute-start.1) | collective-permute-done | bytes 81952 | tf_op jit(solution)/shard_map/ppermute | solution.py:38
  54.3 1.0 %multiply_reduce_fusion = (f32[8]{0:T(128)S(1)}, f32[8,2560]{1,0:T(8,128)S(1)}) fusion(f32[8,2560]{1,0:T(8,128)S(1)} %add.242, f32[8,2560]{1,0:T(8,128)} %collective-permute-done.1, bf16[8,2560]{1,0:T(8,128)(2,1)S(1)} %fusion.7), kind=kLoop, calls=%fused_computation.37 | loop fusion | flops 102392 | bytes 286752 | tf_op jit(solution)/shard_map/reduce_sum | solution.py:13
  55.3 3.0 %fusion.55 = f32[8,896]{1,0:T(8,128)S(1)} fusion(bf16[2560,896]{1,0:T(8,128)(2,1)} %param.25, f32[8,2560]{1,0:T(8,128)S(1)} %get-tuple-element.6, f32[2560]{0:T(1024)S(1)} %convert_element_type.79, f32[8]{0:T(128)S(1)} %add_rsqrt_fusion), kind=kOutput, calls=%fused_computation.113 | convolution fusion | flops 36761600 | bytes 4708384 | tf_op jit(solution)/shard_map/dot_general | solution.py:155
  58.4 5.3 %fusion.21 = f32[8,2560]{1,0:T(8,128)S(1)} fusion(bf16[896,2560]{1,0:T(8,128)(2,1)} %param.27, bf16[2560,896]{1,0:T(8,128)(2,1)} %param.26, f32[8,896]{1,0:T(8,128)S(1)} %fusion.55, f32[8,2560]{1,0:T(8,128)S(1)} %get-tuple-element.6, f32[2560]{0:T(1024)S(1)} %convert_element_type.79, f32[8]{0:T(128)S(1)} %add_rsqrt_fusion), kind=kOutput, calls=%fused_computation.21 | convolution fusion | flops 73504768 | bytes 9377824 | tf_op jit(solution)/shard_map/dot_general | solution.py:159
  63.9 4.2 %collective-permute-done.2 = f32[8,2560]{1,0:T(8,128)S(1)} collective-permute-done((f32[8,2560]{1,0:T(8,128)S(1)}, f32[8,2560]{1,0:T(8,128)S(1)}, u32[]{:S(2)}, u32[]{:S(2)}) %collective-permute-start.2) | collective-permute-done | bytes 81952 | tf_op jit(solution)/shard_map/ppermute | solution.py:38
  68.1 1.1 %collective-permute-start.3 = (f32[8,2560]{1,0:T(8,128)S(1)}, f32[8,2560]{1,0:T(8,128)}, u32[]{:S(2)}, u32[]{:S(2)}) collective-permute-start(f32[8,2560]{1,0:T(8,128)S(1)} %add.247), channel_id=1, source_target_pairs={{0,2},{1,3},{2,0},{3,1},{4,6},{5,7},{6,4},{7,5},{8,10},{9,11},{10,... | collective-permute-start | bytes 245768 | tf_op jit(solution)/shard_map/ppermute | solution.py:38
  69.8 4.3 %collective-permute-done.3 = f32[8,2560]{1,0:T(8,128)} collective-permute-done((f32[8,2560]{1,0:T(8,128)S(1)}, f32[8,2560]{1,0:T(8,128)}, u32[]{:S(2)}, u32[]{:S(2)}) %collective-permute-start.3) | collective-permute-done | bytes 81952 | tf_op jit(solution)/shard_map/ppermute | solution.py:38
  74.1 1.1 %convolution_convert_fusion = bf16[16,2560]{1,0:T(8,128)(2,1)S(1)} fusion(f32[8,2560]{1,0:T(8,128)S(1)} %get-tuple-element.6, f32[8,2560]{1,0:T(8,128)S(1)} %add.247, f32[8,2560]{1,0:T(8,128)} %collective-permute-done.3, s32[16]{0:T(128)S(1)} %gather_fusion.1), kind=kOutput, calls=%fused_computation.7 | convolution fusion | flops 757888 | bytes 327744 | tf_op jit(solution)/shard_map/dot_general | solution.py:169
  75.2 0.7 all_to_all.16
  75.9 3.4 %all-to-all-start.1 = ((bf16[8,2,2560]{2,1,0:T(2,128)(2,1)}), bf16[8,2,2560]{2,1,0:T(2,128)(2,1)S(1)}, u32[]{:S(2)}, u32[]{:S(2)}) async-start(bf16[8,2,2560]{2,1,0:T(2,128)(2,1)} %all_to_all.16), calls=%async_computation.1 | async-start | bytes 163840 | tf_op jit(solution)/shard_map/all_to_all | solution.py:172
  79.3 5.0 %all-to-all-done.1 = bf16[8,2,2560]{2,1,0:T(2,128)(2,1)S(1)} async-done(((bf16[8,2,2560]{2,1,0:T(2,128)(2,1)}), bf16[8,2,2560]{2,1,0:T(2,128)(2,1)S(1)}, u32[]{:S(2)}, u32[]{:S(2)}) %all-to-all-start.1) | async-done | bytes 81952 | tf_op jit(solution)/shard_map/all_to_all | solution.py:172
  84.3 0.8 convolution_convert_fusion.1
  (64 shorter events, 6.8 us)
Async XLA Ops:
  0.0 42.2 %copy-start = (bf16[640,2560]{1,0:T(8,128)(2,1)S(1)}, bf16[640,2560]{1,0:T(8,128)(2,1)}, u32[]{:S(2)}) copy-start(bf16[640,2560]{1,0:T(8,128)(2,1)} %param.23) | copy-start | bytes 9830404
  0.0 17.9 %copy-start.1 = (s32[64]{0:T(128)S(1)}, s32[64]{0:T(128)}, u32[]{:S(2)}) copy-start(s32[64]{0:T(128)} %param.21) | copy-start | bytes 772
  0.0 18.6 %copy-start.3 = (s32[64,4]{0,1:T(4,128)S(1)}, s32[64,4]{0,1:T(4,128)}, u32[]{:S(2)}) copy-start(s32[64,4]{0,1:T(4,128)} %param.22) | copy-start | bytes 3076
  8.8 18.4 %all-to-all-start = ((bf16[32,2,2560]{2,1,0:T(2,128)(2,1)}), bf16[32,2,2560]{2,1,0:T(2,128)(2,1)}, u32[]{:S(2)}, u32[]{:S(2)}) async-start(bf16[32,2,2560]{2,1,0:T(2,128)(2,1)} %reshape.408), calls=%async_computation | async-start | bytes 655360 | tf_op jit(solution)/shard_map/all_to_all | solution.py:77
  38.6 5.8 %copy-start.4 = (s32[16,1]{0,1:T(1,128)S(1)}, s32[16,1]{0,1:T(1,128)}, u32[]{:S(2)}) copy-start(s32[16,1]{0,1:T(1,128)} %add.228) | copy-start | bytes 196
  38.6 5.8 %copy-start.2 = (bf16[2560]{0:T(1024)(128)(2,1)S(1)}, bf16[2560]{0:T(1024)(128)(2,1)}, u32[]{:S(2)}) copy-start(bf16[2560]{0:T(1024)(128)(2,1)} %param.24) | copy-start | bytes 15364
  42.7 5.2 %collective-permute-start = (f32[8,2560]{1,0:T(8,128)S(1)}, f32[8,2560]{1,0:T(8,128)S(1)}, u32[]{:S(2)}, u32[]{:S(2)}) collective-permute-start(f32[8,2560]{1,0:T(8,128)S(1)} %fusion.62), channel_id=1, source_target_pairs={{0,1},{1,0},{2,3},{3,2},{4,5},{5,4},{6,7},{7,6},{8,9},{9,8},{10,11... | collective-permute-start | bytes 245768 | tf_op jit(solution)/shard_map/ppermute | solution.py:38
  47.9 6.4 %collective-permute-start.1 = (f32[8,2560]{1,0:T(8,128)S(1)}, f32[8,2560]{1,0:T(8,128)}, u32[]{:S(2)}, u32[]{:S(2)}) collective-permute-start(f32[8,2560]{1,0:T(8,128)S(1)} %add.242), channel_id=1, source_target_pairs={{0,2},{1,3},{2,0},{3,1},{4,6},{5,7},{6,4},{7,5},{8,10},{9,11},{10,... | collective-permute-start | bytes 245768 | tf_op jit(solution)/shard_map/ppermute | solution.py:38
  63.6 4.5 %collective-permute-start.2 = (f32[8,2560]{1,0:T(8,128)S(1)}, f32[8,2560]{1,0:T(8,128)S(1)}, u32[]{:S(2)}, u32[]{:S(2)}) collective-permute-start(f32[8,2560]{1,0:T(8,128)S(1)} %fusion.21), channel_id=1, source_target_pairs={{0,1},{1,0},{2,3},{3,2},{4,5},{5,4},{6,7},{7,6},{8,9},{9,8},{10,11... | collective-permute-start | bytes 245768 | tf_op jit(solution)/shard_map/ppermute | solution.py:38
  68.1 6.0 %collective-permute-start.3 = (f32[8,2560]{1,0:T(8,128)S(1)}, f32[8,2560]{1,0:T(8,128)}, u32[]{:S(2)}, u32[]{:S(2)}) collective-permute-start(f32[8,2560]{1,0:T(8,128)S(1)} %add.247), channel_id=1, source_target_pairs={{0,2},{1,3},{2,0},{3,1},{4,6},{5,7},{6,4},{7,5},{8,10},{9,11},{10,... | collective-permute-start | bytes 245768 | tf_op jit(solution)/shard_map/ppermute | solution.py:38
  75.9 8.4 %all-to-all-start.1 = ((bf16[8,2,2560]{2,1,0:T(2,128)(2,1)}), bf16[8,2,2560]{2,1,0:T(2,128)(2,1)S(1)}, u32[]{:S(2)}, u32[]{:S(2)}) async-start(bf16[8,2,2560]{2,1,0:T(2,128)(2,1)} %all_to_all.16), calls=%async_computation.1 | async-start | bytes 163840 | tf_op jit(solution)/shard_map/all_to_all | solution.py:172

commit v3 on v1

--- a/solution.py
+++ b/solution.py
@@ -1,6 +1,8 @@
 import jax
 import jax.numpy as jnp
 from jax import lax
+from jax.experimental import pallas as pl
+from jax.experimental.pallas import tpu as pltpu
 from jax.sharding import PartitionSpec as P
 
 HEAD_SIZE = 80
@@ -29,6 +31,74 @@
         [first_half * cosine - second_half * sines, second_half * cosine + first_half * sines],
         axis=-1,
     )
+
+
+def _contract_k_kernel(x_ref, *refs):
+    count = len(refs) // 2
+    w_refs, o_refs = refs[:count], refs[count:]
+
+    @pl.when(pl.program_id(0) == 0)
+    def _():
+        for o_ref in o_refs:
+            o_ref[...] = jnp.zeros_like(o_ref)
+
+    x = x_ref[...]
+    for w_ref, o_ref in zip(w_refs, o_refs):
+        o_ref[...] += jnp.dot(x, w_ref[...], preferred_element_type=jnp.float32)
+
+
+def contract_k(x, weights, block_k):
+    rows, depth = x.shape
+    steps = depth // block_k
+    out_bytes = sum(rows * w.shape[1] * 4 for w in weights)
+    w_bytes = sum(w.size * w.dtype.itemsize for w in weights)
+    return pl.pallas_call(
+        _contract_k_kernel,
+        grid=(steps,),
+        in_specs=[pl.BlockSpec((rows, block_k), lambda k: (0, k))]
+        + [pl.BlockSpec((block_k, w.shape[1]), lambda k: (k, 0)) for w in weights],
+        out_specs=[pl.BlockSpec((rows, w.shape[1]), lambda k: (0, 0)) for w in weights],
+        out_shape=[jax.ShapeDtypeStruct((rows, w.shape[1]), jnp.float32) for w in weights],
+        compiler_params=pltpu.CompilerParams(dimension_semantics=("arbitrary",)),
+        cost_estimate=pl.CostEstimate(
+            flops=2 * rows * depth * sum(w.shape[1] for w in weights),
+            bytes_accessed=w_bytes + x.size * x.dtype.itemsize + out_bytes,
+            transcendentals=0,
+        ),
+    )(x, *weights)
+
+
+def _contract_n_kernel(x_ref, w_ref, o_ref):
+    o_ref[...] = jnp.dot(x_ref[...], w_ref[...], preferred_element_type=jnp.float32)
+
+
+def contract_n(x, weight, block_n):
+    rows, depth = x.shape
+    width = weight.shape[1]
+    steps = width // block_n
+    return pl.pallas_call(
+        _contract_n_kernel,
+        grid=(steps,),
+        in_specs=[
+            pl.BlockSpec((rows, depth), lambda j: (0, 0)),
+            pl.BlockSpec((depth, block_n), lambda j: (0, j)),
+        ],
+        out_specs=pl.BlockSpec((rows, block_n), lambda j: (0, j)),
+        out_shape=jax.ShapeDtypeStruct((rows, width), jnp.float32),
+        compiler_params=pltpu.CompilerParams(dimension_semantics=("arbitrary",)),
+        cost_estimate=pl.CostEstimate(
+            flops=2 * rows * depth * width,
+            bytes_accessed=weight.size * weight.dtype.itemsize + x.size * 2 + rows * width * 4,
+            transcendentals=0,
+        ),
+    )(x, weight)
+
+
+def pick_block(size, target):
+    block = target
+    while size % block:
+        block //= 2
+    return block
 
 
 def tensor_allreduce(part, tp_count):
@@ -92,27 +162,17 @@
 
     rows_srv = rows_all[served]
     scaled_input = norm_rows(rows_srv, norm_gain).astype(jnp.bfloat16)
+    block_k = pick_block(scaled_input.shape[1], 512)
+    q_acc, k_acc, v_acc = contract_k(scaled_input, [w_query, key_weight, value_weight], block_k)
     query_srv = (
-        apply_rotation(
-            jnp.dot(scaled_input, w_query, preferred_element_type=jnp.float32).reshape(
-                req_loc, q_loc, HEAD_SIZE
-            ),
-            served_len,
-        )
+        apply_rotation(q_acc.reshape(req_loc, q_loc, HEAD_SIZE), served_len)
         .astype(jnp.bfloat16)
         .reshape(req_loc, kv_loc, group_width, HEAD_SIZE)
     )
-    key_srv = apply_rotation(
-        jnp.dot(scaled_input, key_weight, preferred_element_type=jnp.float32).reshape(
-            req_loc, kv_loc, HEAD_SIZE
-        ),
-        served_len,
-    ).astype(jnp.bfloat16)
-    value_srv = (
-        jnp.dot(scaled_input, value_weight, preferred_element_type=jnp.float32)
-        .astype(jnp.bfloat16)
-        .reshape(req_loc, kv_loc, HEAD_SIZE)
-    )
+    key_srv = apply_rotation(k_acc.reshape(req_loc, kv_loc, HEAD_SIZE), served_len).astype(
+        jnp.bfloat16
+    )
+    value_srv = v_acc.astype(jnp.bfloat16).reshape(req_loc, kv_loc, HEAD_SIZE)
 
     page_list = page_table[served] - dp_index * pool_size
     key_rows = key_page_pool[page_list]
@@ -145,11 +205,10 @@
     )
     mixed = rows_srv.astype(jnp.float32) + summed
     normed_mlp = norm_rows(mixed, mlp_gain).astype(jnp.bfloat16)
-    gate_act = jnp.dot(normed_mlp, w_gate, preferred_element_type=jnp.float32)
-    up_act = jnp.dot(normed_mlp, w_up, preferred_element_type=jnp.float32)
+    gate_act, up_act = contract_k(normed_mlp, [w_gate, w_up], block_k)
     hidden = (jax.nn.silu(gate_act) * up_act).astype(jnp.bfloat16)
     down_sum = tensor_allreduce(
-        jnp.dot(hidden, w_down, preferred_element_type=jnp.float32), tp_count
+        contract_n(hidden, w_down, pick_block(w_down.shape[1], 512)), tp_count
     )
     final = (mixed + down_sum).astype(jnp.bfloat16)
 

time: 78.9 us -> 90.4 us (1.15)
  Pallas kernels: 0 us -> 16.3 us
  matrix products: 18.1 us -> 4.3 us
  local copies, waits for them, and re-layouts: 18.5 us -> 23.3 us
  other arithmetic: 3.82 us -> 7.47 us
    pallas_call x0 -> x3, Pallas kernels: none -> 16.3 us  [the longest x2 11.4 us: contract_k(): pl.pallas_call(_contract_k_kernel, grid=(steps,), in_specs=[pl.BlockSpec(...]
    dot_general x5 -> x0, matrix products: 13.8 us -> none  [the longest x1 5.29 us: local(): jnp.dot(hidden, w_down, preferred_element_type=jnp.float32)]
    unnamed x5 -> x13, local copies, waits for them, and re-layouts: 0.79 us -> 4.82 us
    convert_element_type x0 -> x4, other arithmetic: none -> 2.77 us  [the longest x1 1.38 us: local(): hidden = (jax.nn.silu(gate_act) * up_act).astype(jnp.bfloat16)]
    reshape x2, local copies, waits for them, and re-layouts: 0.16 us -> 1.59 us  [the longest x1 0.8 us: local(): q_acc.reshape(req_loc, q_loc, HEAD_SIZE)]
  transfers between devices with their start and end apart: 6 -> 6, of which waited for: 5 -> 5; matrix products, arithmetic and copies ran while one was open for 16% -> 18% of each run, Pallas kernels for 0% -> 0%
where the time goes in v3:
time: 90.4 us; the launch traced here: 89.3 us
  local copies, waits for them, and re-layouts  23.3 us (26%)
  waiting for transfers between devices  19.9 us (22%)
  starting transfers between devices  17.8 us (20%)
  Pallas kernels  16.3 us (18%)
  other arithmetic  7.47 us (8%)
  matrix products  4.3 us (5%)
    ppermute x4, waiting for transfers between devices, tensor_allreduce(): part = part + lax.ppermute(part, 'tensor', pairs)  14.8 us
    pallas_call x2, Pallas kernels, contract_k(): pl.pallas_call(_contract_k_kernel, grid=(steps,), in_specs=[pl.BlockSpec(...  11.4 us
    all_to_all x1, starting transfers between devices, local(): lax.all_to_all(jnp.tile(residual_in, (dp_count * tp_count, 1)), ('dp', 't...  7.41 us
    ppermute x4, starting transfers between devices, tensor_allreduce(): part = part + lax.ppermute(part, 'tensor', pairs)  6.76 us
    all_to_all x1, waiting for transfers between devices, local(): incoming = lax.all_to_all(outgoing, 'dp', 0, 0, tiled=True)  5.1 us
    pallas_call x1, Pallas kernels, contract_n(): pl.pallas_call(_contract_n_kernel, grid=(steps,), in_specs=[pl.BlockSpec(...  4.93 us
    unnamed x13, local copies, waits for them, and re-layouts  4.82 us
    all_to_all x1, starting transfers between devices, local(): incoming = lax.all_to_all(outgoing, 'dp', 0, 0, tiled=True)  3.64 us
  transfers between devices with their start and end apart: 6, of which 5 were waited for; matrix products, arithmetic and copies ran while one was open for 18% of the time, Pallas kernels for 0%

profile of v3, /device:TPU:0, one launch (start us, length us, event | category | flops | bytes accessed | tf_op | source)
XLA Modules:
  0.0 89.3 jit_solution(2790608676200334998)
XLA Ops:
  0.0 1.8 %tile.2 = bf16[32,2,2560]{2,1,0:T(2,128)(2,1)} broadcast(bf16[2,2560]{1,0:T(2,128)(2,1)} %param.14), dimensions={1,2} | broadcast | bytes 337920 | tf_op jit(solution)/shard_map/tile | solution.py:145
  1.8 7.4 %all-to-all-start = ((bf16[32,2,2560]{2,1,0:T(2,128)(2,1)}), bf16[32,2,2560]{2,1,0:T(2,128)(2,1)}, u32[]{:S(2)}, u32[]{:S(2)}) async-start(bf16[32,2,2560]{2,1,0:T(2,128)(2,1)} %tile.2), calls=%async_computation | async-start | bytes 655360 | tf_op jit(solution)/shard_map/all_to_all | solution.py:144
  9.2 0.7 iota_add_fusion.2
  10.2 0.7 convert_element_type.58
  10.9 2.3 %copy.29.refs_1_ = bf16[2560,160]{1,0:T(8,128)(2,1)} copy(bf16[2560,160]{0,1:T(8,128)(2,1)} %param.17) | data formatting | bytes 1638400 | tf_op args[3]
  13.3 2.4 %copy.30.refs_2_ = bf16[2560,160]{1,0:T(8,128)(2,1)} copy(bf16[2560,160]{0,1:T(8,128)(2,1)} %param.18) | data formatting | bytes 1638400 | tf_op args[4]
  17.3 3.1 %gather_fusion.3 = bf16[32,2,80,128]{3,2,1,0:T(8,128)(2,1)} fusion(bf16[32,2,80,128]{3,2,1,0:T(8,128)(2,1)} %param.19, s32[1024]{0:T(1024)S(1)} %pad_clamp_fusion.4), kind=kCustom, calls=%fused_computation.3 | custom fusion | bytes 2621568 | tf_op jit(solution)/shard_map/gather | solution.py:178
  20.4 3.1 %gather_fusion.4 = bf16[32,2,80,128]{3,2,1,0:T(8,128)(2,1)} fusion(bf16[32,2,80,128]{3,2,1,0:T(8,128)(2,1)} %param.20, s32[1024]{0:T(1024)S(1)} %pad_clamp_fusion.4), kind=kCustom, calls=%fused_computation.4 | custom fusion | bytes 2621568 | tf_op jit(solution)/shard_map/gather | solution.py:179
  24.6 1.8 %all_to_all.15 = bf16[64,2560]{1,0:T(8,128)(2,1)} reshape(bf16[32,2,2560]{2,1,0:T(2,128)(2,1)} %all-to-all-done) | data formatting | bytes 655360 | tf_op jit(solution)/shard_map/all_to_all | solution.py:144
  26.4 1.6 %gather_fusion = bf16[8,2560]{1,0:T(8,128)(2,1)S(1)} fusion(bf16[64,2560]{1,0:T(8,128)(2,1)} %all_to_all.15, s32[1024]{0:T(1024)S(1)} %pad_clamp_fusion.5), kind=kCustom, calls=%fused_computation | custom fusion | bytes 81952 | tf_op jit(solution)/shard_map/gather | solution.py:163
  28.2 0.7 fusion.22.x_ref
  28.9 5.2 %shard_map.136 = (f32[8,640]{1,0:T(8,128)}, f32[8,160]{1,0:T(8,128)}, f32[8,160]{1,0:T(8,128)}) custom-call(bf16[8,2560]{1,0:T(8,128)(2,1)} %fusion.22.x_ref, bf16[2560,640]{1,0:T(8,128)(2,1)} %refs_0_.2, bf16[2560,160]{1,0:T(8,128)(2,1)} %copy.29.refs_1_, bf16[2560,160]{1,0:T(8,128)(2,1)} %copy.30.refs_2_), custom_call_target="tpu_custom_call" | custom-call | flops 39321600 | bytes 4986880 | tf_op jit(solution)/shard_map/pallas_call | solution.py:55
  34.1 0.8 reshape.304
  34.9 0.8 reshape.303
  36.1 1.8 %select_reduce_fusion = (f32[8,2,4]{2,1,0:T(2,128)S(1)}, f32[8,2,4,4,128]{4,2,3,1,0:T(4,128)S(1)}) fusion(pred[8,4,128]{2,1,0:T(4,128)(4,1)S(1)} %broadcast_compare_fusion, bf16[8,4,2,80,128]{4,3,2,1,0:T(8,128)(2,1)} %bitcast.49, bf16[8,2,4,40]{3,2,1,0:T(4,128)(2,1)S(1)} %bitcast.55, bf16[8,2,4,40]{3,2,1,0:T(4,128)(2,1)S(1)} %bitcast.53), kind=kOutput, calls=%fused_computation.19 | convolution fusion | flops 5361600 | bytes 1456384 | tf_op jit(solution)/shard_map/rhgd,rphdc->rhgpc/dot_general | solution.py:181
  38.2 1.8 %fusion.16 = bf16[8,2,4,80]{3,2,1,0:T(4,128)(2,1)S(1)} fusion(bf16[8,4,2,80,128]{4,3,2,1,0:T(8,128)(2,1)} %bitcast.48, f32[8,2,4,4,128]{4,2,3,1,0:T(4,128)S(1)} %get-tuple-element.29, f32[8,2,4]{2,1,0:T(2,128)S(1)} %multiply_maximum_fusion, pred[8,4,128]{2,1,0:T(4,128)(4,1)S(1)} %broadcast_compare_fusion, f32[8,2,4]{2,1,0:T(2,128)S(1)} %get-tuple-element.17, ...), kind=kOutput, calls=%fused_computation.17 | convolution fusion | flops 5328896 | bytes 1462016 | tf_op jit(solution)/shard_map/rhgpc,rphdc->rhgd/dot_general | solution.py:197
  40.7 1.7 %collective-permute-start = (f32[8,2560]{1,0:T(8,128)S(1)}, f32[8,2560]{1,0:T(8,128)S(1)}, u32[]{:S(2)}, u32[]{:S(2)}) collective-permute-start(f32[8,2560]{1,0:T(8,128)S(1)} %fusion.38), channel_id=1, source_target_pairs={{0,1},{1,0},{2,3},{3,2},{4,5},{5,4},{6,7},{7,6},{8,9},{9,8},{10,11... | collective-permute-start | bytes 245768 | tf_op jit(solution)/shard_map/ppermute | solution.py:108
  42.4 2.8 %collective-permute-done = f32[8,2560]{1,0:T(8,128)S(1)} collective-permute-done((f32[8,2560]{1,0:T(8,128)S(1)}, f32[8,2560]{1,0:T(8,128)S(1)}, u32[]{:S(2)}, u32[]{:S(2)}) %collective-permute-start) | collective-permute-done | bytes 81952 | tf_op jit(solution)/shard_map/ppermute | solution.py:108
  45.3 2.6 %collective-permute-start.1 = (f32[8,2560]{1,0:T(8,128)S(1)}, f32[8,2560]{1,0:T(8,128)}, u32[]{:S(2)}, u32[]{:S(2)}) collective-permute-start(f32[8,2560]{1,0:T(8,128)S(1)} %add.233), channel_id=1, source_target_pairs={{0,2},{1,3},{2,0},{3,1},{4,6},{5,7},{6,4},{7,5},{8,10},{9,11},{10,... | collective-permute-start | bytes 245768 | tf_op jit(solution)/shard_map/ppermute | solution.py:108
  48.6 3.4 %collective-permute-done.1 = f32[8,2560]{1,0:T(8,128)} collective-permute-done((f32[8,2560]{1,0:T(8,128)S(1)}, f32[8,2560]{1,0:T(8,128)}, u32[]{:S(2)}, u32[]{:S(2)}) %collective-permute-start.1) | collective-permute-done | bytes 81952 | tf_op jit(solution)/shard_map/ppermute | solution.py:108
  52.0 1.0 %multiply_reduce_fusion = (f32[8]{0:T(128)S(1)}, f32[8,2560]{1,0:T(8,128)S(1)}) fusion(f32[8,2560]{1,0:T(8,128)S(1)} %add.233, f32[8,2560]{1,0:T(8,128)} %collective-permute-done.1, bf16[8,2560]{1,0:T(8,128)(2,1)S(1)} %gather_fusion), kind=kLoop, calls=%fused_computation.29 | loop fusion | flops 102392 | bytes 286752 | tf_op jit(solution)/shard_map/reduce_sum | solution.py:15
  53.0 0.7 multiply_convert_fusion.x_ref
  53.7 6.2 %shard_map.137 = (f32[8,896]{1,0:T(8,128)}, f32[8,896]{1,0:T(8,128)}) custom-call(bf16[8,2560]{1,0:T(8,128)(2,1)} %multiply_convert_fusion.x_ref, bf16[2560,896]{1,0:T(8,128)(2,1)} %refs_0_.3, bf16[2560,896]{1,0:T(8,128)(2,1)} %refs_1_.2), custom_call_target="tpu_custom_call" | custom-call | flops 73400320 | bytes 9273344 | tf_op jit(solution)/shard_map/pallas_call | solution.py:55
  59.9 1.4 %multiply_convert_fusion.1.x_ref = bf16[8,896]{1,0:T(8,128)(2,1)} fusion(f32[8,896]{1,0:T(8,128)} %get-tuple-element.14, f32[8,896]{1,0:T(8,128)} %get-tuple-element.13), kind=kLoop, calls=%fused_computation.36 | loop fusion | flops 43008 | bytes 71680 | tf_op jit(solution)/shard_map/convert_element_type | solution.py:209
  61.3 4.9 %shard_map.138 = f32[8,2560]{1,0:T(8,128)} custom-call(bf16[8,896]{1,0:T(8,128)(2,1)} %multiply_convert_fusion.1.x_ref, bf16[896,2560]{1,0:T(8,128)(2,1)} %w_ref.1), custom_call_target="tpu_custom_call" | custom-call | flops 36700160 | bytes 4683776 | tf_op jit(solution)/shard_map/pallas_call | solution.py:79
  66.8 4.1 %collective-permute-done.2 = f32[8,2560]{1,0:T(8,128)S(1)} collective-permute-done((f32[8,2560]{1,0:T(8,128)}, f32[8,2560]{1,0:T(8,128)S(1)}, u32[]{:S(2)}, u32[]{:S(2)}) %collective-permute-start.2) | collective-permute-done | bytes 81952 | tf_op jit(solution)/shard_map/ppermute | solution.py:108
  70.9 0.9 %add.238 = f32[8,2560]{1,0:T(8,128)S(1)} add(f32[8,2560]{1,0:T(8,128)} %shard_map.138, f32[8,2560]{1,0:T(8,128)S(1)} %collective-permute-done.2) | non-fusion elementwise | flops 20480 | bytes 245760 | tf_op jit(solution)/shard_map/add | solution.py:108
  71.8 1.8 %collective-permute-start.3 = (f32[8,2560]{1,0:T(8,128)S(1)}, f32[8,2560]{1,0:T(8,128)S(1)}, u32[]{:S(2)}, u32[]{:S(2)}) collective-permute-start(f32[8,2560]{1,0:T(8,128)S(1)} %add.238), channel_id=1, source_target_pairs={{0,2},{1,3},{2,0},{3,1},{4,6},{5,7},{6,4},{7,5},{8,10},{9,11},{10,... | collective-permute-start | bytes 245768 | tf_op jit(solution)/shard_map/ppermute | solution.py:108
  73.7 4.4 %collective-permute-done.3 = f32[8,2560]{1,0:T(8,128)S(1)} collective-permute-done((f32[8,2560]{1,0:T(8,128)S(1)}, f32[8,2560]{1,0:T(8,128)S(1)}, u32[]{:S(2)}, u32[]{:S(2)}) %collective-permute-start.3) | collective-permute-done | bytes 81952 | tf_op jit(solution)/shard_map/ppermute | solution.py:108
  79.4 3.6 %all-to-all-start.1 = ((bf16[8,2,2560]{2,1,0:T(2,128)(2,1)}), bf16[8,2,2560]{2,1,0:T(2,128)(2,1)S(1)}, u32[]{:S(2)}, u32[]{:S(2)}) async-start(bf16[8,2,2560]{2,1,0:T(2,128)(2,1)} %all_to_all.16), calls=%async_computation.1 | async-start | bytes 163840 | tf_op jit(solution)/shard_map/all_to_all | solution.py:221
  83.0 5.1 %all-to-all-done.1 = bf16[8,2,2560]{2,1,0:T(2,128)(2,1)S(1)} async-done(((bf16[8,2,2560]{2,1,0:T(2,128)(2,1)}), bf16[8,2,2560]{2,1,0:T(2,128)(2,1)S(1)}, u32[]{:S(2)}, u32[]{:S(2)}) %all-to-all-start.1) | async-done | bytes 81952 | tf_op jit(solution)/shard_map/all_to_all | solution.py:221
  88.2 1.2 %gather_fusion.8 = bf16[2,2560]{1,0:T(2,128)(2,1)} fusion(bf16[16,2560]{1,0:T(8,128)(2,1)S(1)} %all_to_all.18, s32[1024]{0:T(1024)S(1)} %pad_clamp_fusion), kind=kCustom, calls=%fused_computation.8 | custom fusion | bytes 20488 | tf_op jit(solution)/shard_map/gather | solution.py:224
  (65 shorter events, 7.1 us)
Async XLA Ops:
  0.0 40.2 %copy-start = (bf16[640,2560]{1,0:T(8,128)(2,1)S(1)}, bf16[640,2560]{1,0:T(8,128)(2,1)}, u32[]{:S(2)}) copy-start(bf16[640,2560]{1,0:T(8,128)(2,1)} %param.23) | copy-start | bytes 9830404
  1.8 22.8 %all-to-all-start = ((bf16[32,2,2560]{2,1,0:T(2,128)(2,1)}), bf16[32,2,2560]{2,1,0:T(2,128)(2,1)}, u32[]{:S(2)}, u32[]{:S(2)}) async-start(bf16[32,2,2560]{2,1,0:T(2,128)(2,1)} %tile.2), calls=%async_computation | async-start | bytes 655360 | tf_op jit(solution)/shard_map/all_to_all | solution.py:144
  13.3 2.4 %copy-start.1 = (s32[64]{0:T(128)S(1)}, s32[64]{0:T(128)}, u32[]{:S(2)}) copy-start(s32[64]{0:T(128)} %param.21) | copy-start | bytes 772
  13.3 3.0 %copy-start.4 = (s32[64,4]{0,1:T(4,128)S(1)}, s32[64,4]{0,1:T(4,128)}, u32[]{:S(2)}) copy-start(s32[64,4]{0,1:T(4,128)} %param.22) | copy-start | bytes 3076
  20.4 3.1 %copy-start.3 = (bf16[2560]{0:T(1024)(128)(2,1)S(1)}, bf16[2560]{0:T(1024)(128)(2,1)}, u32[]{:S(2)}) copy-start(bf16[2560]{0:T(1024)(128)(2,1)} %param.24) | copy-start | bytes 15364
  34.1 4.1 %copy-start.2 = (f32[8,160]{1,0:T(8,128)S(1)}, f32[8,160]{1,0:T(8,128)}, u32[]{:S(2)}) copy-start(f32[8,160]{1,0:T(8,128)} %get-tuple-element.12) | copy-start | bytes 15364
  40.7 4.5 %collective-permute-start = (f32[8,2560]{1,0:T(8,128)S(1)}, f32[8,2560]{1,0:T(8,128)S(1)}, u32[]{:S(2)}, u32[]{:S(2)}) collective-permute-start(f32[8,2560]{1,0:T(8,128)S(1)} %fusion.38), channel_id=1, source_target_pairs={{0,1},{1,0},{2,3},{3,2},{4,5},{5,4},{6,7},{7,6},{8,9},{9,8},{10,11... | collective-permute-start | bytes 245768 | tf_op jit(solution)/shard_map/ppermute | solution.py:108
  45.3 6.7 %collective-permute-start.1 = (f32[8,2560]{1,0:T(8,128)S(1)}, f32[8,2560]{1,0:T(8,128)}, u32[]{:S(2)}, u32[]{:S(2)}) collective-permute-start(f32[8,2560]{1,0:T(8,128)S(1)} %add.233), channel_id=1, source_target_pairs={{0,2},{1,3},{2,0},{3,1},{4,6},{5,7},{6,4},{7,5},{8,10},{9,11},{10,... | collective-permute-start | bytes 245768 | tf_op jit(solution)/shard_map/ppermute | solution.py:108
  66.3 4.7 %collective-permute-start.2 = (f32[8,2560]{1,0:T(8,128)}, f32[8,2560]{1,0:T(8,128)S(1)}, u32[]{:S(2)}, u32[]{:S(2)}) collective-permute-start(f32[8,2560]{1,0:T(8,128)} %shard_map.138), channel_id=1, source_target_pairs={{0,1},{1,0},{2,3},{3,2},{4,5},{5,4},{6,7},{7,6},{8,9},{9,8},{10,11... | collective-permute-start | bytes 245768 | tf_op jit(solution)/shard_map/ppermute | solution.py:108
  71.8 6.3 %collective-permute-start.3 = (f32[8,2560]{1,0:T(8,128)S(1)}, f32[8,2560]{1,0:T(8,128)S(1)}, u32[]{:S(2)}, u32[]{:S(2)}) collective-permute-start(f32[8,2560]{1,0:T(8,128)S(1)} %add.238), channel_id=1, source_target_pairs={{0,2},{1,3},{2,0},{3,1},{4,6},{5,7},{6,4},{7,5},{8,10},{9,11},{10,... | collective-permute-start | bytes 245768 | tf_op jit(solution)/shard_map/ppermute | solution.py:108
  79.4 8.7 %all-to-all-start.1 = ((bf16[8,2,2560]{2,1,0:T(2,128)(2,1)}), bf16[8,2,2560]{2,1,0:T(2,128)(2,1)S(1)}, u32[]{:S(2)}, u32[]{:S(2)}) async-start(bf16[8,2,2560]{2,1,0:T(2,128)(2,1)} %all_to_all.16), calls=%async_computation.1 | async-start | bytes 163840 | tf_op jit(solution)/shard_map/all_to_all | solution.py:221

commit v4 on v1

--- a/solution.py
+++ b/solution.py
@@ -71,12 +71,12 @@
     dp_index = lax.axis_index("dp")
     tp_index = lax.axis_index("tensor")
 
+    dev_count = dp_count * tp_count
     rows_all = lax.all_to_all(
-        jnp.tile(residual_in, (dp_count * tp_count, 1)),
+        jnp.broadcast_to(residual_in[None], (dev_count,) + residual_in.shape),
         ("dp", "tensor"),
         0,
         0,
-        tiled=True,
     )
 
     request_ids = jnp.arange(total_reqs, dtype=jnp.int32)
@@ -90,7 +90,7 @@
     served = jnp.sum(jnp.where(hits, request_ids[None, :], 0), axis=1)
     served_len = lengths[served]
 
-    rows_srv = rows_all[served]
+    rows_srv = rows_all[served // rows_loc, served % rows_loc]
     scaled_input = norm_rows(rows_srv, norm_gain).astype(jnp.bfloat16)
     query_srv = (
         apply_rotation(
@@ -158,11 +158,10 @@
         + tp_index * rows_loc
         + jnp.arange(rows_loc, dtype=jnp.int32)[None, :]
     ).reshape(-1)
-    outgoing = final[round_no[dest_rows]]
-    incoming = lax.all_to_all(outgoing, "dp", 0, 0, tiled=True)
+    outgoing = final[round_no[dest_rows]].reshape(dp_count, rows_loc, final.shape[1])
+    incoming = lax.all_to_all(outgoing, "dp", 0, 0)
     mine = dp_index * req_loc + tp_index * rows_loc + jnp.arange(rows_loc, dtype=jnp.int32)
-    pick = server[mine] * rows_loc + jnp.arange(rows_loc, dtype=jnp.int32)
-    return incoming[pick]
+    return incoming[server[mine], jnp.arange(rows_loc, dtype=jnp.int32)]
 
 
 def solution(mesh):

time: 78.9 us -> 77 us (0.976)
  local copies, waits for them, and re-layouts: 18.5 us -> 16.7 us
    all_to_all x3 -> x0, local copies, waits for them, and re-layouts: 2.52 us -> none  [the longest x1 1.83 us: local(): lax.all_to_all(jnp.tile(residual_in, (dp_count * tp_count, 1)), ('dp', 't...]
    another operation x1 -> x0, local copies, waits for them, and re-layouts: 1.76 us -> none  [local(): jnp.tile(residual_in, (dp_count * tp_count, 1))]
    broadcast_in_dim x0 -> x1, local copies, waits for them, and re-layouts: none -> 1.75 us  [local(): jnp.broadcast_to(residual_in[None], (dev_count,) + residual_in.shape)]
    add x2, other arithmetic: 0.02 us -> 0.91 us  [tensor_allreduce(): part = part + lax.ppermute(part, 'tensor', pairs)]
    reduce_sum x2, other arithmetic: 1.16 us -> 0.28 us  [norm_rows(): jnp.mean(value_rows * value_rows, axis=-1, keepdims=True) + 1e-05]
  transfers between devices with their start and end apart: 6 -> 6, of which waited for: 5 -> 5; matrix products, arithmetic and copies ran while one was open for 16% -> 17% of each run, Pallas kernels for 0% -> 0%
where the time goes in v4:
time: 77 us; the launch traced here: 76.3 us
  waiting for transfers between devices  19.7 us (26%)
  matrix products  18.1 us (24%)
  starting transfers between devices  17.8 us (23%)
  local copies, waits for them, and re-layouts  16.7 us (22%)
  other arithmetic  3.83 us (5%)
    ppermute x4, waiting for transfers between devices, tensor_allreduce(): part = part + lax.ppermute(part, 'tensor', pairs)  14.6 us
    all_to_all x1, starting transfers between devices, local(): lax.all_to_all(jnp.broadcast_to(residual_in[None], (dev_count,) + residua...  7.41 us
    ppermute x4, starting transfers between devices, tensor_allreduce(): part = part + lax.ppermute(part, 'tensor', pairs)  6.78 us
    dot_general x1, matrix products, local(): jnp.dot(hidden, w_down, preferred_element_type=jnp.float32)  5.29 us
    all_to_all x1, waiting for transfers between devices, local(): incoming = lax.all_to_all(outgoing, 'dp', 0, 0)  5.1 us
    all_to_all x1, starting transfers between devices, local(): incoming = lax.all_to_all(outgoing, 'dp', 0, 0)  3.64 us
    gather x1, local copies, waits for them, and re-layouts, local(): key_rows = key_page_pool[page_list]  3.13 us
    gather x1, local copies, waits for them, and re-layouts, local(): value_rows = value_page_pool[page_list]  3.1 us
  transfers between devices with their start and end apart: 6, of which 5 were waited for; matrix products, arithmetic and copies ran while one was open for 17% of the time, Pallas kernels for 0%

profile of v4, /device:TPU:0, one launch (start us, length us, event | category | flops | bytes accessed | tf_op | source)
XLA Modules:
  0.0 76.3 jit_solution(3504369467579778809)
XLA Ops:
  0.0 1.8 %broadcast_in_dim.28 = bf16[32,2,2560]{2,1,0:T(2,128)(2,1)} broadcast(bf16[2,2560]{1,0:T(2,128)(2,1)} %param.14), dimensions={1,2} | broadcast | bytes 337920 | tf_op jit(solution)/shard_map/broadcast_in_dim | solution.py:76
  1.8 7.4 %all-to-all-start = ((bf16[32,2,2560]{2,1,0:T(2,128)(2,1)}), bf16[32,2,2560]{2,1,0:T(2,128)(2,1)}, u32[]{:S(2)}, u32[]{:S(2)}) async-start(bf16[32,2,2560]{2,1,0:T(2,128)(2,1)} %broadcast_in_dim.28), calls=%async_computation | async-start | bytes 655360 | tf_op jit(solution)/shard_map/all_to_all | solution.py:75
  9.2 0.7 iota_add_fusion.2
  10.2 0.7 convert_element_type.58
  10.9 1.3 %gather_fusion.1 = s32[8]{0:T(128)S(1)} fusion(s32[64]{0:T(128)} %param.21, s32[1024]{0:T(1024)S(1)} %pad_clamp_fusion.4), kind=kCustom, calls=%fused_computation.1 | custom fusion | bytes 96 | tf_op jit(solution)/shard_map/gather | solution.py:91
  12.2 0.8 %copy.25 = s32[64,4]{1,0:T(8,128)S(1)} copy(s32[64,4]{0,1:T(4,128)} %param.22) | data formatting | bytes 2048 | tf_op args[8]
  13.8 3.1 %gather_fusion.3 = bf16[32,2,80,128]{3,2,1,0:T(8,128)(2,1)} fusion(bf16[32,2,80,128]{3,2,1,0:T(8,128)(2,1)} %param.19, s32[1024]{0:T(1024)S(1)} %pad_clamp_fusion.3), kind=kCustom, calls=%fused_computation.3 | custom fusion | bytes 2621568 | tf_op jit(solution)/shard_map/gather | solution.py:118
  17.0 3.1 %gather_fusion.4 = bf16[32,2,80,128]{3,2,1,0:T(8,128)(2,1)} fusion(bf16[32,2,80,128]{3,2,1,0:T(8,128)(2,1)} %param.20, s32[1024]{0:T(1024)S(1)} %pad_clamp_fusion.3), kind=kCustom, calls=%fused_computation.4 | custom fusion | bytes 2621568 | tf_op jit(solution)/shard_map/gather | solution.py:119
  20.3 0.7 gather_fusion.5
  21.2 1.6 %gather_fusion = bf16[8,2560]{1,0:T(8,128)(2,1)S(1)} fusion(bf16[32,2,2560]{2,1,0:T(2,128)(2,1)} %all-to-all-done, s32[8]{0:T(128)S(1)} %get-tuple-element.18), kind=kCustom, calls=%fused_computation | custom fusion | bytes 81984 | tf_op jit(solution)/shard_map/gather | solution.py:93
  22.9 1.5 %fusion.58 = f32[8,160]{1,0:T(8,128)S(1)} fusion(bf16[2560,160]{0,1:T(8,128)(2,1)} %param.17, bf16[8,2560]{1,0:T(8,128)(2,1)S(1)} %gather_fusion, f32[2560]{0:T(1024)S(1)} %convert_element_type.58, f32[8]{0:T(128)S(1)} %add_rsqrt_fusion.1), kind=kOutput, calls=%fused_computation.118 | convolution fusion | flops 6635520 | bytes 875552 | tf_op jit(solution)/shard_map/dot_general | solution.py:106
  24.5 2.5 %fusion.60 = f32[8,640]{1,0:T(8,128)S(1)} fusion(bf16[2560,640]{1,0:T(8,128)(2,1)} %param.16, bf16[8,2560]{1,0:T(8,128)(2,1)S(1)} %gather_fusion, f32[2560]{0:T(1024)S(1)} %convert_element_type.58, f32[8]{0:T(128)S(1)} %add_rsqrt_fusion.1), kind=kOutput, calls=%fused_computation.119 | convolution fusion | flops 26296320 | bytes 3348512 | tf_op jit(solution)/shard_map/dot_general | solution.py:97
  27.6 1.8 %select_reduce_fusion = (f32[8,2,4]{2,1,0:T(2,128)S(1)}, f32[8,2,4,4,128]{4,2,3,1,0:T(4,128)S(1)}) fusion(pred[8,4,128]{2,1,0:T(4,128)(4,1)S(1)} %broadcast_compare_fusion, bf16[8,4,2,80,128]{4,3,2,1,0:T(8,128)(2,1)} %bitcast.71, bf16[8,2,4,40]{3,2,1,0:T(4,128)(2,1)S(1)} %bitcast.77, bf16[8,2,4,40]{3,2,1,0:T(4,128)(2,1)S(1)} %bitcast.75), kind=kOutput, calls=%fused_computation.24 | convolution fusion | flops 5361600 | bytes 1456384 | tf_op jit(solution)/shard_map/rhgd,rphdc->rhgpc/dot_general | solution.py:121
  29.6 1.5 %fusion.21 = f32[8,160]{1,0:T(8,128)S(1)} fusion(bf16[2560,160]{0,1:T(8,128)(2,1)} %param.18, bf16[8,2560]{1,0:T(8,128)(2,1)S(1)} %gather_fusion, f32[2560]{0:T(1024)S(1)} %convert_element_type.58, f32[8]{0:T(128)S(1)} %add_rsqrt_fusion.1), kind=kOutput, calls=%fused_computation.22 | convolution fusion | flops 6638080 | bytes 875552 | tf_op jit(solution)/shard_map/dot_general | solution.py:112
  31.2 1.8 %fusion.16 = bf16[8,2,4,80]{3,2,1,0:T(4,128)(2,1)S(1)} fusion(bf16[8,4,2,80,128]{4,3,2,1,0:T(8,128)(2,1)} %bitcast.70, f32[8,2,4,4,128]{4,2,3,1,0:T(4,128)S(1)} %get-tuple-element.21, f32[8,2,4]{2,1,0:T(2,128)S(1)} %multiply_maximum_fusion, pred[8,4,128]{2,1,0:T(4,128)(4,1)S(1)} %broadcast_compare_fusion, f32[8,2,4]{2,1,0:T(2,128)S(1)} %get-tuple-element.7, ...), kind=kOutput, calls=%fused_computation.18 | convolution fusion | flops 5328896 | bytes 1462016 | tf_op jit(solution)/shard_map/rhgpc,rphdc->rhgd/dot_general | solution.py:137
  33.7 1.7 %collective-permute-start = (f32[8,2560]{1,0:T(8,128)S(1)}, f32[8,2560]{1,0:T(8,128)S(1)}, u32[]{:S(2)}, u32[]{:S(2)}) collective-permute-start(f32[8,2560]{1,0:T(8,128)S(1)} %fusion.63), channel_id=1, source_target_pairs={{0,1},{1,0},{2,3},{3,2},{4,5},{5,4},{6,7},{7,6},{8,9},{9,8},{10,11... | collective-permute-start | bytes 245768 | tf_op jit(solution)/shard_map/ppermute | solution.py:38
  35.4 2.8 %collective-permute-done = f32[8,2560]{1,0:T(8,128)S(1)} collective-permute-done((f32[8,2560]{1,0:T(8,128)S(1)}, f32[8,2560]{1,0:T(8,128)S(1)}, u32[]{:S(2)}, u32[]{:S(2)}) %collective-permute-start) | collective-permute-done | bytes 81952 | tf_op jit(solution)/shard_map/ppermute | solution.py:38
  38.2 2.6 %collective-permute-start.1 = (f32[8,2560]{1,0:T(8,128)S(1)}, f32[8,2560]{1,0:T(8,128)S(1)}, u32[]{:S(2)}, u32[]{:S(2)}) collective-permute-start(f32[8,2560]{1,0:T(8,128)S(1)} %add.267), channel_id=1, source_target_pairs={{0,2},{1,3},{2,0},{3,1},{4,6},{5,7},{6,4},{7,5},{8,10},{9,11},{10,... | collective-permute-start | bytes 245768 | tf_op jit(solution)/shard_map/ppermute | solution.py:38
  40.9 4.0 %collective-permute-done.1 = f32[8,2560]{1,0:T(8,128)S(1)} collective-permute-done((f32[8,2560]{1,0:T(8,128)S(1)}, f32[8,2560]{1,0:T(8,128)S(1)}, u32[]{:S(2)}, u32[]{:S(2)}) %collective-permute-start.1) | collective-permute-done | bytes 81952 | tf_op jit(solution)/shard_map/ppermute | solution.py:38
  45.0 3.0 %fusion.56 = f32[8,896]{1,0:T(8,128)S(1)} fusion(bf16[2560,896]{1,0:T(8,128)(2,1)} %param.25, f32[8,2560]{1,0:T(8,128)S(1)} %get-tuple-element.6, f32[2560]{0:T(1024)S(1)} %convert_element_type.66, f32[8]{0:T(128)S(1)} %add_rsqrt_fusion), kind=kOutput, calls=%fused_computation.117 | convolution fusion | flops 36761600 | bytes 4708384 | tf_op jit(solution)/shard_map/dot_general | solution.py:148
  48.0 5.3 %fusion.20 = f32[8,2560]{1,0:T(8,128)S(1)} fusion(bf16[896,2560]{1,0:T(8,128)(2,1)} %param.27, bf16[2560,896]{1,0:T(8,128)(2,1)} %param.26, f32[8,896]{1,0:T(8,128)S(1)} %fusion.56, f32[8,2560]{1,0:T(8,128)S(1)} %get-tuple-element.6, f32[2560]{0:T(1024)S(1)} %convert_element_type.66, f32[8]{0:T(128)S(1)} %add_rsqrt_fusion), kind=kOutput, calls=%fused_computation.20 | convolution fusion | flops 73504768 | bytes 9377824 | tf_op jit(solution)/shard_map/dot_general | solution.py:152
  53.3 0.6 collective-permute-start.2
  53.9 0.6 gather_fusion.7
  54.5 3.3 %collective-permute-done.2 = f32[8,2560]{1,0:T(8,128)} collective-permute-done((f32[8,2560]{1,0:T(8,128)S(1)}, f32[8,2560]{1,0:T(8,128)}, u32[]{:S(2)}, u32[]{:S(2)}) %collective-permute-start.2) | collective-permute-done | bytes 81952 | tf_op jit(solution)/shard_map/ppermute | solution.py:38
  57.9 0.9 %add.272 = f32[8,2560]{1,0:T(8,128)S(1)} add(f32[8,2560]{1,0:T(8,128)S(1)} %fusion.20, f32[8,2560]{1,0:T(8,128)} %collective-permute-done.2) | non-fusion elementwise | flops 20480 | bytes 245760 | tf_op jit(solution)/shard_map/add | solution.py:38
  58.8 1.9 %collective-permute-start.3 = (f32[8,2560]{1,0:T(8,128)S(1)}, f32[8,2560]{1,0:T(8,128)S(1)}, u32[]{:S(2)}, u32[]{:S(2)}) collective-permute-start(f32[8,2560]{1,0:T(8,128)S(1)} %add.272), channel_id=1, source_target_pairs={{0,2},{1,3},{2,0},{3,1},{4,6},{5,7},{6,4},{7,5},{8,10},{9,11},{10,... | collective-permute-start | bytes 245768 | tf_op jit(solution)/shard_map/ppermute | solution.py:38
  60.6 4.4 %collective-permute-done.3 = f32[8,2560]{1,0:T(8,128)S(1)} collective-permute-done((f32[8,2560]{1,0:T(8,128)S(1)}, f32[8,2560]{1,0:T(8,128)S(1)}, u32[]{:S(2)}, u32[]{:S(2)}) %collective-permute-start.3) | collective-permute-done | bytes 81952 | tf_op jit(solution)/shard_map/ppermute | solution.py:38
  65.1 0.6 gather_fusion.6
  65.7 0.7 reshape.375
  66.3 3.6 %all-to-all-start.1 = ((bf16[8,2,2560]{2,1,0:T(2,128)(2,1)}), bf16[8,2,2560]{2,1,0:T(2,128)(2,1)S(1)}, u32[]{:S(2)}, u32[]{:S(2)}) async-start(bf16[8,2,2560]{2,1,0:T(2,128)(2,1)} %reshape.375), calls=%async_computation.1 | async-start | bytes 163840 | tf_op jit(solution)/shard_map/all_to_all | solution.py:162
  70.0 5.1 %all-to-all-done.1 = bf16[8,2,2560]{2,1,0:T(2,128)(2,1)S(1)} async-done(((bf16[8,2,2560]{2,1,0:T(2,128)(2,1)}), bf16[8,2,2560]{2,1,0:T(2,128)(2,1)S(1)}, u32[]{:S(2)}, u32[]{:S(2)}) %all-to-all-start.1) | async-done | bytes 81952 | tf_op jit(solution)/shard_map/all_to_all | solution.py:162
  75.1 1.2 %gather_fusion.8 = bf16[2,2560]{1,0:T(2,128)(2,1)} fusion(bf16[8,2,2560]{2,1,0:T(2,128)(2,1)S(1)} %all-to-all-done.1, s32[2]{0:T(128)S(1)} %fusion.52), kind=kCustom, calls=%fused_computation.8 | custom fusion | bytes 20496 | tf_op jit(solution)/shard_map/gather | solution.py:164
  (52 shorter events, 3.5 us)
Async XLA Ops:
  0.0 33.1 %copy-start = (bf16[640,2560]{1,0:T(8,128)(2,1)S(1)}, bf16[640,2560]{1,0:T(8,128)(2,1)}, u32[]{:S(2)}) copy-start(bf16[640,2560]{1,0:T(8,128)(2,1)} %param.23) | copy-start | bytes 9830404
  1.8 19.4 %all-to-all-start = ((bf16[32,2,2560]{2,1,0:T(2,128)(2,1)}), bf16[32,2,2560]{2,1,0:T(2,128)(2,1)}, u32[]{:S(2)}, u32[]{:S(2)}) async-start(bf16[32,2,2560]{2,1,0:T(2,128)(2,1)} %broadcast_in_dim.28), calls=%async_computation | async-start | bytes 655360 | tf_op jit(solution)/shard_map/all_to_all | solution.py:75
  29.6 5.8 %copy-start.1 = (bf16[2560]{0:T(1024)(128)(2,1)S(1)}, bf16[2560]{0:T(1024)(128)(2,1)}, u32[]{:S(2)}) copy-start(bf16[2560]{0:T(1024)(128)(2,1)} %param.24) | copy-start | bytes 15364
  33.7 4.5 %collective-permute-start = (f32[8,2560]{1,0:T(8,128)S(1)}, f32[8,2560]{1,0:T(8,128)S(1)}, u32[]{:S(2)}, u32[]{:S(2)}) collective-permute-start(f32[8,2560]{1,0:T(8,128)S(1)} %fusion.63), channel_id=1, source_target_pairs={{0,1},{1,0},{2,3},{3,2},{4,5},{5,4},{6,7},{7,6},{8,9},{9,8},{10,11... | collective-permute-start | bytes 245768 | tf_op jit(solution)/shard_map/ppermute | solution.py:38
  38.2 6.6 %collective-permute-start.1 = (f32[8,2560]{1,0:T(8,128)S(1)}, f32[8,2560]{1,0:T(8,128)S(1)}, u32[]{:S(2)}, u32[]{:S(2)}) collective-permute-start(f32[8,2560]{1,0:T(8,128)S(1)} %add.267), channel_id=1, source_target_pairs={{0,2},{1,3},{2,0},{3,1},{4,6},{5,7},{6,4},{7,5},{8,10},{9,11},{10,... | collective-permute-start | bytes 245768 | tf_op jit(solution)/shard_map/ppermute | solution.py:38
  53.3 4.6 %collective-permute-start.2 = (f32[8,2560]{1,0:T(8,128)S(1)}, f32[8,2560]{1,0:T(8,128)}, u32[]{:S(2)}, u32[]{:S(2)}) collective-permute-start(f32[8,2560]{1,0:T(8,128)S(1)} %fusion.20), channel_id=1, source_target_pairs={{0,1},{1,0},{2,3},{3,2},{4,5},{5,4},{6,7},{7,6},{8,9},{9,8},{10,11... | collective-permute-start | bytes 245768 | tf_op jit(solution)/shard_map/ppermute | solution.py:38
  58.8 6.3 %collective-permute-start.3 = (f32[8,2560]{1,0:T(8,128)S(1)}, f32[8,2560]{1,0:T(8,128)S(1)}, u32[]{:S(2)}, u32[]{:S(2)}) collective-permute-start(f32[8,2560]{1,0:T(8,128)S(1)} %add.272), channel_id=1, source_target_pairs={{0,2},{1,3},{2,0},{3,1},{4,6},{5,7},{6,4},{7,5},{8,10},{9,11},{10,... | collective-permute-start | bytes 245768 | tf_op jit(solution)/shard_map/ppermute | solution.py:38
  66.3 8.7 %all-to-all-start.1 = ((bf16[8,2,2560]{2,1,0:T(2,128)(2,1)}), bf16[8,2,2560]{2,1,0:T(2,128)(2,1)S(1)}, u32[]{:S(2)}, u32[]{:S(2)}) async-start(bf16[8,2,2560]{2,1,0:T(2,128)(2,1)} %reshape.375), calls=%async_computation.1 | async-start | bytes 163840 | tf_op jit(solution)/shard_map/all_to_all | solution.py:162

commit v5 on v4

--- a/solution.py
+++ b/solution.py
@@ -158,10 +158,12 @@
         + tp_index * rows_loc
         + jnp.arange(rows_loc, dtype=jnp.int32)[None, :]
     ).reshape(-1)
-    outgoing = final[round_no[dest_rows]].reshape(dp_count, rows_loc, final.shape[1])
+    outgoing = final[round_no[dest_rows].reshape(dp_count, rows_loc)]
     incoming = lax.all_to_all(outgoing, "dp", 0, 0)
     mine = dp_index * req_loc + tp_index * rows_loc + jnp.arange(rows_loc, dtype=jnp.int32)
-    return incoming[server[mine], jnp.arange(rows_loc, dtype=jnp.int32)]
+    from_src = jnp.arange(dp_count, dtype=jnp.int32)[:, None] == server[mine][None, :]
+    picked = jnp.where(from_src[:, :, None], incoming.astype(jnp.float32), 0.0)
+    return jnp.sum(picked, axis=0).astype(jnp.bfloat16)
 
 
 def solution(mesh):

time: 77 us -> 76.6 us (level)
  local copies, waits for them, and re-layouts: 16.7 us -> 15.6 us
where the time goes in v5:
time: 76.6 us; the launch traced here: 75.9 us
  waiting for transfers between devices  19.6 us (26%)
  matrix products  18.1 us (24%)
  starting transfers between devices  17.8 us (23%)
  local copies, waits for them, and re-layouts  15.6 us (20%)
  other arithmetic  4.59 us (6%)
    ppermute x4, waiting for transfers between devices, tensor_allreduce(): part = part + lax.ppermute(part, 'tensor', pairs)  14.5 us
    all_to_all x1, starting transfers between devices, local(): lax.all_to_all(jnp.broadcast_to(residual_in[None], (dev_count,) + residua...  7.41 us
    ppermute x4, starting transfers between devices, tensor_allreduce(): part = part + lax.ppermute(part, 'tensor', pairs)  6.77 us
    dot_general x1, matrix products, local(): jnp.dot(hidden, w_down, preferred_element_type=jnp.float32)  5.29 us
    all_to_all x1, waiting for transfers between devices, local(): incoming = lax.all_to_all(outgoing, 'dp', 0, 0)  5.1 us
    all_to_all x1, starting transfers between devices, local(): incoming = lax.all_to_all(outgoing, 'dp', 0, 0)  3.64 us
    gather x1, local copies, waits for them, and re-layouts, local(): key_rows = key_page_pool[page_list]  3.11 us
    gather x1, local copies, waits for them, and re-layouts, local(): value_rows = value_page_pool[page_list]  3.09 us
  transfers between devices with their start and end apart: 6, of which 5 were waited for; matrix products, arithmetic and copies ran while one was open for 17% of the time, Pallas kernels for 0%

profile of v5, /device:TPU:0, one launch (start us, length us, event | category | flops | bytes accessed | tf_op | source)
XLA Modules:
  0.0 75.9 jit_solution(16767803724385760299)
XLA Ops:
  0.0 1.8 %broadcast_in_dim.37 = bf16[32,2,2560]{2,1,0:T(2,128)(2,1)} broadcast(bf16[2,2560]{1,0:T(2,128)(2,1)} %param.14), dimensions={1,2} | broadcast | bytes 337920 | tf_op jit(solution)/shard_map/broadcast_in_dim | solution.py:76
  1.8 7.4 %all-to-all-start = ((bf16[32,2,2560]{2,1,0:T(2,128)(2,1)}), bf16[32,2,2560]{2,1,0:T(2,128)(2,1)}, u32[]{:S(2)}, u32[]{:S(2)}) async-start(bf16[32,2,2560]{2,1,0:T(2,128)(2,1)} %broadcast_in_dim.37), calls=%async_computation | async-start | bytes 655360 | tf_op jit(solution)/shard_map/all_to_all | solution.py:75
  9.2 0.7 iota_add_fusion.2
  10.2 0.7 convert_element_type.64
  10.9 1.3 %gather_fusion.2 = s32[8]{0:T(128)S(1)} fusion(s32[64]{0:T(128)} %param.21, s32[1024]{0:T(1024)S(1)} %pad_clamp_fusion.3), kind=kCustom, calls=%fused_computation.2 | custom fusion | bytes 96 | tf_op jit(solution)/shard_map/gather | solution.py:91
  12.2 0.8 %copy.25 = s32[64,4]{1,0:T(8,128)S(1)} copy(s32[64,4]{0,1:T(4,128)} %param.22) | data formatting | bytes 2048 | tf_op args[8]
  13.8 3.1 %gather_fusion.4 = bf16[32,2,80,128]{3,2,1,0:T(8,128)(2,1)} fusion(bf16[32,2,80,128]{3,2,1,0:T(8,128)(2,1)} %param.19, s32[1024]{0:T(1024)S(1)} %pad_clamp_fusion.2), kind=kCustom, calls=%fused_computation.4 | custom fusion | bytes 2621568 | tf_op jit(solution)/shard_map/gather | solution.py:118
  17.0 3.1 %gather_fusion.5 = bf16[32,2,80,128]{3,2,1,0:T(8,128)(2,1)} fusion(bf16[32,2,80,128]{3,2,1,0:T(8,128)(2,1)} %param.20, s32[1024]{0:T(1024)S(1)} %pad_clamp_fusion.2), kind=kCustom, calls=%fused_computation.5 | custom fusion | bytes 2621568 | tf_op jit(solution)/shard_map/gather | solution.py:119
  20.2 0.7 gather_fusion.6
  21.3 1.6 %gather_fusion.1 = bf16[8,2560]{1,0:T(8,128)(2,1)S(1)} fusion(bf16[32,2,2560]{2,1,0:T(2,128)(2,1)} %all-to-all-done, s32[8]{0:T(128)S(1)} %get-tuple-element.18), kind=kCustom, calls=%fused_computation.1 | custom fusion | bytes 81984 | tf_op jit(solution)/shard_map/gather | solution.py:93
  23.0 1.5 %fusion.53 = f32[8,160]{1,0:T(8,128)S(1)} fusion(bf16[2560,160]{0,1:T(8,128)(2,1)} %param.17, bf16[8,2560]{1,0:T(8,128)(2,1)S(1)} %gather_fusion.1, f32[2560]{0:T(1024)S(1)} %convert_element_type.64, f32[8]{0:T(128)S(1)} %add_rsqrt_fusion.1), kind=kOutput, calls=%fused_computation.113 | convolution fusion | flops 6635520 | bytes 875552 | tf_op jit(solution)/shard_map/dot_general | solution.py:106
  24.6 2.5 %fusion.55 = f32[8,640]{1,0:T(8,128)S(1)} fusion(bf16[2560,640]{1,0:T(8,128)(2,1)} %param.16, bf16[8,2560]{1,0:T(8,128)(2,1)S(1)} %gather_fusion.1, f32[2560]{0:T(1024)S(1)} %convert_element_type.64, f32[8]{0:T(128)S(1)} %add_rsqrt_fusion.1), kind=kOutput, calls=%fused_computation.114 | convolution fusion | flops 26296320 | bytes 3348512 | tf_op jit(solution)/shard_map/dot_general | solution.py:97
  27.6 1.8 %select_reduce_fusion.1 = (f32[8,2,4]{2,1,0:T(2,128)S(1)}, f32[8,2,4,4,128]{4,2,3,1,0:T(4,128)S(1)}) fusion(pred[8,4,128]{2,1,0:T(4,128)(4,1)S(1)} %broadcast_compare_fusion, bf16[8,4,2,80,128]{4,3,2,1,0:T(8,128)(2,1)} %bitcast.63, bf16[8,2,4,40]{3,2,1,0:T(4,128)(2,1)S(1)} %bitcast.69, bf16[8,2,4,40]{3,2,1,0:T(4,128)(2,1)S(1)} %bitcast.67), kind=kOutput, calls=%fused_computation.24 | convolution fusion | flops 5361600 | bytes 1456384 | tf_op jit(solution)/shard_map/rhgd,rphdc->rhgpc/dot_general | solution.py:121
  29.7 1.5 %fusion.21 = f32[8,160]{1,0:T(8,128)S(1)} fusion(bf16[2560,160]{0,1:T(8,128)(2,1)} %param.18, bf16[8,2560]{1,0:T(8,128)(2,1)S(1)} %gather_fusion.1, f32[2560]{0:T(1024)S(1)} %convert_element_type.64, f32[8]{0:T(128)S(1)} %add_rsqrt_fusion.1), kind=kOutput, calls=%fused_computation.21 | convolution fusion | flops 6638080 | bytes 875552 | tf_op jit(solution)/shard_map/dot_general | solution.py:112
  31.2 1.8 %fusion.16 = bf16[8,2,4,80]{3,2,1,0:T(4,128)(2,1)S(1)} fusion(bf16[8,4,2,80,128]{4,3,2,1,0:T(8,128)(2,1)} %bitcast.62, f32[8,2,4,4,128]{4,2,3,1,0:T(4,128)S(1)} %get-tuple-element.21, f32[8,2,4]{2,1,0:T(2,128)S(1)} %multiply_maximum_fusion, pred[8,4,128]{2,1,0:T(4,128)(4,1)S(1)} %broadcast_compare_fusion, f32[8,2,4]{2,1,0:T(2,128)S(1)} %get-tuple-element.7, ...), kind=kOutput, calls=%fused_computation.17 | convolution fusion | flops 5328896 | bytes 1462016 | tf_op jit(solution)/shard_map/rhgpc,rphdc->rhgd/dot_general | solution.py:137
  33.7 1.7 %collective-permute-start = (f32[8,2560]{1,0:T(8,128)S(1)}, f32[8,2560]{1,0:T(8,128)S(1)}, u32[]{:S(2)}, u32[]{:S(2)}) collective-permute-start(f32[8,2560]{1,0:T(8,128)S(1)} %fusion.58), channel_id=1, source_target_pairs={{0,1},{1,0},{2,3},{3,2},{4,5},{5,4},{6,7},{7,6},{8,9},{9,8},{10,11... | collective-permute-start | bytes 245768 | tf_op jit(solution)/shard_map/ppermute | solution.py:38
  35.5 2.7 %collective-permute-done = f32[8,2560]{1,0:T(8,128)S(1)} collective-permute-done((f32[8,2560]{1,0:T(8,128)S(1)}, f32[8,2560]{1,0:T(8,128)S(1)}, u32[]{:S(2)}, u32[]{:S(2)}) %collective-permute-start) | collective-permute-done | bytes 81952 | tf_op jit(solution)/shard_map/ppermute | solution.py:38
  38.3 2.6 %collective-permute-start.1 = (f32[8,2560]{1,0:T(8,128)S(1)}, f32[8,2560]{1,0:T(8,128)S(1)}, u32[]{:S(2)}, u32[]{:S(2)}) collective-permute-start(f32[8,2560]{1,0:T(8,128)S(1)} %add.260), channel_id=1, source_target_pairs={{0,2},{1,3},{2,0},{3,1},{4,6},{5,7},{6,4},{7,5},{8,10},{9,11},{10,... | collective-permute-start | bytes 245768 | tf_op jit(solution)/shard_map/ppermute | solution.py:38
  40.9 4.0 %collective-permute-done.1 = f32[8,2560]{1,0:T(8,128)S(1)} collective-permute-done((f32[8,2560]{1,0:T(8,128)S(1)}, f32[8,2560]{1,0:T(8,128)S(1)}, u32[]{:S(2)}, u32[]{:S(2)}) %collective-permute-start.1) | collective-permute-done | bytes 81952 | tf_op jit(solution)/shard_map/ppermute | solution.py:38
  45.0 3.0 %fusion.51 = f32[8,896]{1,0:T(8,128)S(1)} fusion(bf16[2560,896]{1,0:T(8,128)(2,1)} %param.25, f32[8,2560]{1,0:T(8,128)S(1)} %get-tuple-element.6, f32[2560]{0:T(1024)S(1)} %convert_element_type.72, f32[8]{0:T(128)S(1)} %add_rsqrt_fusion), kind=kOutput, calls=%fused_computation.112 | convolution fusion | flops 36761600 | bytes 4708384 | tf_op jit(solution)/shard_map/dot_general | solution.py:148
  48.1 5.3 %fusion.20 = f32[8,2560]{1,0:T(8,128)S(1)} fusion(bf16[896,2560]{1,0:T(8,128)(2,1)} %param.27, bf16[2560,896]{1,0:T(8,128)(2,1)} %param.26, f32[8,896]{1,0:T(8,128)S(1)} %fusion.51, f32[8,2560]{1,0:T(8,128)S(1)} %get-tuple-element.6, f32[2560]{0:T(1024)S(1)} %convert_element_type.72, f32[8]{0:T(128)S(1)} %add_rsqrt_fusion), kind=kOutput, calls=%fused_computation.19 | convolution fusion | flops 73504768 | bytes 9377824 | tf_op jit(solution)/shard_map/dot_general | solution.py:152
  53.4 0.6 collective-permute-start.2
  54.0 0.6 gather_fusion
  54.6 3.3 %collective-permute-done.2 = f32[8,2560]{1,0:T(8,128)} collective-permute-done((f32[8,2560]{1,0:T(8,128)S(1)}, f32[8,2560]{1,0:T(8,128)}, u32[]{:S(2)}, u32[]{:S(2)}) %collective-permute-start.2) | collective-permute-done | bytes 81952 | tf_op jit(solution)/shard_map/ppermute | solution.py:38
  57.9 0.9 %add.265 = f32[8,2560]{1,0:T(8,128)S(1)} add(f32[8,2560]{1,0:T(8,128)S(1)} %fusion.20, f32[8,2560]{1,0:T(8,128)} %collective-permute-done.2) | non-fusion elementwise | flops 20480 | bytes 245760 | tf_op jit(solution)/shard_map/add | solution.py:38
  58.8 1.9 %collective-permute-start.3 = (f32[8,2560]{1,0:T(8,128)S(1)}, f32[8,2560]{1,0:T(8,128)S(1)}, u32[]{:S(2)}, u32[]{:S(2)}) collective-permute-start(f32[8,2560]{1,0:T(8,128)S(1)} %add.265), channel_id=1, source_target_pairs={{0,2},{1,3},{2,0},{3,1},{4,6},{5,7},{6,4},{7,5},{8,10},{9,11},{10,... | collective-permute-start | bytes 245768 | tf_op jit(solution)/shard_map/ppermute | solution.py:38
  60.7 4.4 %collective-permute-done.3 = f32[8,2560]{1,0:T(8,128)S(1)} collective-permute-done((f32[8,2560]{1,0:T(8,128)S(1)}, f32[8,2560]{1,0:T(8,128)S(1)}, u32[]{:S(2)}, u32[]{:S(2)}) %collective-permute-start.3) | collective-permute-done | bytes 81952 | tf_op jit(solution)/shard_map/ppermute | solution.py:38
  65.1 0.6 gather_fusion.7
  65.7 0.7 reshape.452
  66.4 3.6 %all-to-all-start.1 = ((bf16[8,2,2560]{2,1,0:T(2,128)(2,1)}), bf16[8,2,2560]{2,1,0:T(2,128)(2,1)S(1)}, u32[]{:S(2)}, u32[]{:S(2)}) async-start(bf16[8,2,2560]{2,1,0:T(2,128)(2,1)} %reshape.452), calls=%async_computation.1 | async-start | bytes 163840 | tf_op jit(solution)/shard_map/all_to_all | solution.py:162
  70.0 5.1 %all-to-all-done.1 = bf16[8,2,2560]{2,1,0:T(2,128)(2,1)S(1)} async-done(((bf16[8,2,2560]{2,1,0:T(2,128)(2,1)}), bf16[8,2,2560]{2,1,0:T(2,128)(2,1)S(1)}, u32[]{:S(2)}, u32[]{:S(2)}) %all-to-all-start.1) | async-done | bytes 81952 | tf_op jit(solution)/shard_map/all_to_all | solution.py:162
  75.1 0.8 select_reduce_fusion
  (54 shorter events, 3.7 us)
Async XLA Ops:
  0.0 33.2 %copy-start = (bf16[640,2560]{1,0:T(8,128)(2,1)S(1)}, bf16[640,2560]{1,0:T(8,128)(2,1)}, u32[]{:S(2)}) copy-start(bf16[640,2560]{1,0:T(8,128)(2,1)} %param.23) | copy-start | bytes 9830404
  1.8 19.5 %all-to-all-start = ((bf16[32,2,2560]{2,1,0:T(2,128)(2,1)}), bf16[32,2,2560]{2,1,0:T(2,128)(2,1)}, u32[]{:S(2)}, u32[]{:S(2)}) async-start(bf16[32,2,2560]{2,1,0:T(2,128)(2,1)} %broadcast_in_dim.37), calls=%async_computation | async-start | bytes 655360 | tf_op jit(solution)/shard_map/all_to_all | solution.py:75
  29.6 5.8 %copy-start.1 = (bf16[2560]{0:T(1024)(128)(2,1)S(1)}, bf16[2560]{0:T(1024)(128)(2,1)}, u32[]{:S(2)}) copy-start(bf16[2560]{0:T(1024)(128)(2,1)} %param.24) | copy-start | bytes 15364
  33.7 4.5 %collective-permute-start = (f32[8,2560]{1,0:T(8,128)S(1)}, f32[8,2560]{1,0:T(8,128)S(1)}, u32[]{:S(2)}, u32[]{:S(2)}) collective-permute-start(f32[8,2560]{1,0:T(8,128)S(1)} %fusion.58), channel_id=1, source_target_pairs={{0,1},{1,0},{2,3},{3,2},{4,5},{5,4},{6,7},{7,6},{8,9},{9,8},{10,11... | collective-permute-start | bytes 245768 | tf_op jit(solution)/shard_map/ppermute | solution.py:38
  38.3 6.6 %collective-permute-start.1 = (f32[8,2560]{1,0:T(8,128)S(1)}, f32[8,2560]{1,0:T(8,128)S(1)}, u32[]{:S(2)}, u32[]{:S(2)}) collective-permute-start(f32[8,2560]{1,0:T(8,128)S(1)} %add.260), channel_id=1, source_target_pairs={{0,2},{1,3},{2,0},{3,1},{4,6},{5,7},{6,4},{7,5},{8,10},{9,11},{10,... | collective-permute-start | bytes 245768 | tf_op jit(solution)/shard_map/ppermute | solution.py:38
  53.4 4.6 %collective-permute-start.2 = (f32[8,2560]{1,0:T(8,128)S(1)}, f32[8,2560]{1,0:T(8,128)}, u32[]{:S(2)}, u32[]{:S(2)}) collective-permute-start(f32[8,2560]{1,0:T(8,128)S(1)} %fusion.20), channel_id=1, source_target_pairs={{0,1},{1,0},{2,3},{3,2},{4,5},{5,4},{6,7},{7,6},{8,9},{9,8},{10,11... | collective-permute-start | bytes 245768 | tf_op jit(solution)/shard_map/ppermute | solution.py:38
  58.8 6.3 %collective-permute-start.3 = (f32[8,2560]{1,0:T(8,128)S(1)}, f32[8,2560]{1,0:T(8,128)S(1)}, u32[]{:S(2)}, u32[]{:S(2)}) collective-permute-start(f32[8,2560]{1,0:T(8,128)S(1)} %add.265), channel_id=1, source_target_pairs={{0,2},{1,3},{2,0},{3,1},{4,6},{5,7},{6,4},{7,5},{8,10},{9,11},{10,... | collective-permute-start | bytes 245768 | tf_op jit(solution)/shard_map/ppermute | solution.py:38
  66.4 8.7 %all-to-all-start.1 = ((bf16[8,2,2560]{2,1,0:T(2,128)(2,1)}), bf16[8,2,2560]{2,1,0:T(2,128)(2,1)S(1)}, u32[]{:S(2)}, u32[]{:S(2)}) async-start(bf16[8,2,2560]{2,1,0:T(2,128)(2,1)} %reshape.452), calls=%async_computation.1 | async-start | bytes 163840 | tf_op jit(solution)/shard_map/all_to_all | solution.py:162

commit v6 on v5

--- a/solution.py
+++ b/solution.py
@@ -72,11 +72,11 @@
     tp_index = lax.axis_index("tensor")
 
     dev_count = dp_count * tp_count
+    width = residual_in.shape[1]
+    sub = 8
+    packed = residual_in.reshape(rows_loc * sub, width // sub)
     rows_all = lax.all_to_all(
-        jnp.broadcast_to(residual_in[None], (dev_count,) + residual_in.shape),
-        ("dp", "tensor"),
-        0,
-        0,
+        jnp.broadcast_to(packed[None], (dev_count,) + packed.shape), ("dp", "tensor"), 0, 0
     )
 
     request_ids = jnp.arange(total_reqs, dtype=jnp.int32)
@@ -90,7 +90,9 @@
     served = jnp.sum(jnp.where(hits, request_ids[None, :], 0), axis=1)
     served_len = lengths[served]
 
-    rows_srv = rows_all[served // rows_loc, served % rows_loc]
+    sub_rows = (served % rows_loc)[:, None] * sub + jnp.arange(sub, dtype=jnp.int32)[None, :]
+    rows_srv = rows_all[(served // rows_loc)[:, None], sub_rows].reshape(req_loc, width)
+    rows_srv = lax.optimization_barrier(rows_srv)
     scaled_input = norm_rows(rows_srv, norm_gain).astype(jnp.bfloat16)
     query_srv = (
         apply_rotation(

time: 76.6 us -> 77.1 us (level)
  starting transfers between devices: 17.8 us -> 15.9 us
  waiting for transfers between devices: 19.6 us -> 21.5 us
    ppermute x4, waiting for transfers between devices: 14.5 us -> 16.4 us  [tensor_allreduce(): part = part + lax.ppermute(part, 'tensor', pairs)]
    ppermute x4, starting transfers between devices: 6.77 us -> 5.15 us  [tensor_allreduce(): part = part + lax.ppermute(part, 'tensor', pairs)]
    broadcast_in_dim x1 -> x2, local copies, waits for them, and re-layouts: 1.76 us -> 1.75 us  [local(): jnp.broadcast_to(packed[None], (dev_count,) + packed.shape)]
where the time goes in v6:
time: 77.1 us; the launch traced here: 76.5 us
  waiting for transfers between devices  21.5 us (28%)
  matrix products  18.1 us (23%)
  local copies, waits for them, and re-layouts  16.1 us (21%)
  starting transfers between devices  15.9 us (21%)
  other arithmetic  4.68 us (6%)
    ppermute x4, waiting for transfers between devices, tensor_allreduce(): part = part + lax.ppermute(part, 'tensor', pairs)  16.4 us
    all_to_all x1, starting transfers between devices, local(): lax.all_to_all(jnp.broadcast_to(packed[None], (dev_count,) + packed.shape...  7.41 us
    dot_general x1, matrix products, local(): jnp.dot(hidden, w_down, preferred_element_type=jnp.float32)  5.29 us
    ppermute x4, starting transfers between devices, tensor_allreduce(): part = part + lax.ppermute(part, 'tensor', pairs)  5.15 us
    all_to_all x1, waiting for transfers between devices, local(): incoming = lax.all_to_all(outgoing, 'dp', 0, 0)  5.05 us
    all_to_all x1, starting transfers between devices, local(): incoming = lax.all_to_all(outgoing, 'dp', 0, 0)  3.36 us
    gather x1, local copies, waits for them, and re-layouts, local(): key_rows = key_page_pool[page_list]  3.11 us
    gather x1, local copies, waits for them, and re-layouts, local(): value_rows = value_page_pool[page_list]  3.09 us
  transfers between devices with their start and end apart: 6, of which 5 were waited for; matrix products, arithmetic and copies ran while one was open for 17% of the time, Pallas kernels for 0%

profile of v6, /device:TPU:0, one launch (start us, length us, event | category | flops | bytes accessed | tf_op | source)
XLA Modules:
  0.0 76.5 jit_solution(11362192744996368980)
XLA Ops:
  0.0 0.9 %broadcast_in_dim.41 = bf16[16,320]{1,0:T(8,128)(2,1)S(1)} reshape(bf16[2,2560]{1,0:T(2,128)(2,1)} %param.14) | data formatting | bytes 20480 | tf_op jit(solution)/shard_map/broadcast_in_dim | solution.py:79
  0.9 0.8 %broadcast_in_dim.42 = bf16[32,16,320]{2,1,0:T(8,128)(2,1)} broadcast(bf16[16,320]{1,0:T(8,128)(2,1)S(1)} %broadcast_in_dim.41), dimensions={1,2} | broadcast | bytes 337920 | tf_op jit(solution)/shard_map/broadcast_in_dim | solution.py:79
  1.8 7.4 %all-to-all-start = ((bf16[32,16,320]{2,1,0:T(8,128)(2,1)}), bf16[32,16,320]{2,1,0:T(8,128)(2,1)}, u32[]{:S(2)}, u32[]{:S(2)}) async-start(bf16[32,16,320]{2,1,0:T(8,128)(2,1)} %broadcast_in_dim.42), calls=%async_computation | async-start | bytes 786432 | tf_op jit(solution)/shard_map/all_to_all | solution.py:78
  9.2 0.7 iota_add_fusion.2
  10.4 0.7 convert_element_type.64
  11.1 1.3 %gather_fusion.2 = s32[8]{0:T(128)S(1)} fusion(s32[64]{0:T(128)} %param.21, s32[1024]{0:T(1024)S(1)} %pad_clamp_fusion.3), kind=kCustom, calls=%fused_computation.2 | custom fusion | bytes 96 | tf_op jit(solution)/shard_map/gather | solution.py:91
  12.4 0.8 %copy.25 = s32[64,4]{1,0:T(8,128)S(1)} copy(s32[64,4]{0,1:T(4,128)} %param.22) | data formatting | bytes 2048 | tf_op args[8]
  14.0 3.1 %gather_fusion.4 = bf16[32,2,80,128]{3,2,1,0:T(8,128)(2,1)} fusion(bf16[32,2,80,128]{3,2,1,0:T(8,128)(2,1)} %param.19, s32[1024]{0:T(1024)S(1)} %pad_clamp_fusion.2), kind=kCustom, calls=%fused_computation.4 | custom fusion | bytes 2621568 | tf_op jit(solution)/shard_map/gather | solution.py:120
  17.1 3.1 %gather_fusion.5 = bf16[32,2,80,128]{3,2,1,0:T(8,128)(2,1)} fusion(bf16[32,2,80,128]{3,2,1,0:T(8,128)(2,1)} %param.20, s32[1024]{0:T(1024)S(1)} %pad_clamp_fusion.2), kind=kCustom, calls=%fused_computation.5 | custom fusion | bytes 2621568 | tf_op jit(solution)/shard_map/gather | solution.py:121
  20.4 0.7 gather_fusion.6
  21.4 1.9 %gather_fusion.1 = bf16[64,320]{1,0:T(8,128)(2,1)S(1)} fusion(bf16[32,16,320]{2,1,0:T(8,128)(2,1)} %all-to-all-done, s32[64]{0:T(128)S(1)} %reshape.401), kind=kCustom, calls=%fused_computation.1 | custom fusion | bytes 82432 | tf_op jit(solution)/shard_map/gather | solution.py:94
  23.6 1.5 %fusion.53 = f32[8,160]{1,0:T(8,128)S(1)} fusion(bf16[2560,160]{0,1:T(8,128)(2,1)} %param.17, bf16[8,2560]{1,0:T(8,128)(2,1)S(1)} %reshape.388, f32[2560]{0:T(1024)S(1)} %convert_element_type.64, f32[8]{0:T(128)S(1)} %add_rsqrt_fusion.1), kind=kOutput, calls=%fused_computation.112 | convolution fusion | flops 6635520 | bytes 875552 | tf_op jit(solution)/shard_map/dot_general | solution.py:108
  25.1 2.5 %fusion.55 = f32[8,640]{1,0:T(8,128)S(1)} fusion(bf16[2560,640]{1,0:T(8,128)(2,1)} %param.16, bf16[8,2560]{1,0:T(8,128)(2,1)S(1)} %reshape.388, f32[2560]{0:T(1024)S(1)} %convert_element_type.64, f32[8]{0:T(128)S(1)} %add_rsqrt_fusion.1), kind=kOutput, calls=%fused_computation.113 | convolution fusion | flops 26296320 | bytes 3348512 | tf_op jit(solution)/shard_map/dot_general | solution.py:99
  28.2 1.8 %select_reduce_fusion.1 = (f32[8,2,4]{2,1,0:T(2,128)S(1)}, f32[8,2,4,4,128]{4,2,3,1,0:T(4,128)S(1)}) fusion(pred[8,4,128]{2,1,0:T(4,128)(4,1)S(1)} %broadcast_compare_fusion, bf16[8,4,2,80,128]{4,3,2,1,0:T(8,128)(2,1)} %bitcast.49, bf16[8,2,4,40]{3,2,1,0:T(4,128)(2,1)S(1)} %bitcast.55, bf16[8,2,4,40]{3,2,1,0:T(4,128)(2,1)S(1)} %bitcast.53), kind=kOutput, calls=%fused_computation.24 | convolution fusion | flops 5361600 | bytes 1456384 | tf_op jit(solution)/shard_map/rhgd,rphdc->rhgpc/dot_general | solution.py:123
  30.2 1.5 %fusion.21 = f32[8,160]{1,0:T(8,128)S(1)} fusion(bf16[2560,160]{0,1:T(8,128)(2,1)} %param.18, bf16[8,2560]{1,0:T(8,128)(2,1)S(1)} %reshape.388, f32[2560]{0:T(1024)S(1)} %convert_element_type.64, f32[8]{0:T(128)S(1)} %add_rsqrt_fusion.1), kind=kOutput, calls=%fused_computation.21 | convolution fusion | flops 6638080 | bytes 875552 | tf_op jit(solution)/shard_map/dot_general | solution.py:114
  31.8 1.8 %fusion.16 = bf16[8,2,4,80]{3,2,1,0:T(4,128)(2,1)S(1)} fusion(bf16[8,4,2,80,128]{4,3,2,1,0:T(8,128)(2,1)} %bitcast.48, f32[8,2,4,4,128]{4,2,3,1,0:T(4,128)S(1)} %get-tuple-element.21, f32[8,2,4]{2,1,0:T(2,128)S(1)} %multiply_maximum_fusion, pred[8,4,128]{2,1,0:T(4,128)(4,1)S(1)} %broadcast_compare_fusion, f32[8,2,4]{2,1,0:T(2,128)S(1)} %get-tuple-element.7, ...), kind=kOutput, calls=%fused_computation.17 | convolution fusion | flops 5328896 | bytes 1462016 | tf_op jit(solution)/shard_map/rhgpc,rphdc->rhgd/dot_general | solution.py:139
  34.3 1.9 %collective-permute-start = (f32[8,2560]{1,0:T(8,128)S(1)}, f32[8,2560]{1,0:T(8,128)S(1)}, u32[]{:S(2)}, u32[]{:S(2)}) collective-permute-start(f32[8,2560]{1,0:T(8,128)S(1)} %fusion.58), channel_id=1, source_target_pairs={{0,1},{1,0},{2,3},{3,2},{4,5},{5,4},{6,7},{7,6},{8,9},{9,8},{10,11... | collective-permute-start | bytes 245768 | tf_op jit(solution)/shard_map/ppermute | solution.py:38
  36.2 3.1 %collective-permute-done = f32[8,2560]{1,0:T(8,128)S(1)} collective-permute-done((f32[8,2560]{1,0:T(8,128)S(1)}, f32[8,2560]{1,0:T(8,128)S(1)}, u32[]{:S(2)}, u32[]{:S(2)}) %collective-permute-start) | collective-permute-done | bytes 81952 | tf_op jit(solution)/shard_map/ppermute | solution.py:38
  39.4 2.1 %collective-permute-start.1 = (f32[8,2560]{1,0:T(8,128)S(1)}, f32[8,2560]{1,0:T(8,128)S(1)}, u32[]{:S(2)}, u32[]{:S(2)}) collective-permute-start(f32[8,2560]{1,0:T(8,128)S(1)} %add.279), channel_id=1, source_target_pairs={{0,2},{1,3},{2,0},{3,1},{4,6},{5,7},{6,4},{7,5},{8,10},{9,11},{10,... | collective-permute-start | bytes 245768 | tf_op jit(solution)/shard_map/ppermute | solution.py:38
  41.5 4.6 %collective-permute-done.1 = f32[8,2560]{1,0:T(8,128)S(1)} collective-permute-done((f32[8,2560]{1,0:T(8,128)S(1)}, f32[8,2560]{1,0:T(8,128)S(1)}, u32[]{:S(2)}, u32[]{:S(2)}) %collective-permute-start.1) | collective-permute-done | bytes 81952 | tf_op jit(solution)/shard_map/ppermute | solution.py:38
  46.2 3.0 %fusion.51 = f32[8,896]{1,0:T(8,128)S(1)} fusion(bf16[2560,896]{1,0:T(8,128)(2,1)} %param.25, f32[8,2560]{1,0:T(8,128)S(1)} %get-tuple-element.6, f32[2560]{0:T(1024)S(1)} %convert_element_type.72, f32[8]{0:T(128)S(1)} %add_rsqrt_fusion), kind=kOutput, calls=%fused_computation.111 | convolution fusion | flops 36761600 | bytes 4708384 | tf_op jit(solution)/shard_map/dot_general | solution.py:150
  49.3 5.3 %fusion.20 = f32[8,2560]{1,0:T(8,128)S(1)} fusion(bf16[896,2560]{1,0:T(8,128)(2,1)} %param.27, bf16[2560,896]{1,0:T(8,128)(2,1)} %param.26, f32[8,896]{1,0:T(8,128)S(1)} %fusion.51, f32[8,2560]{1,0:T(8,128)S(1)} %get-tuple-element.6, f32[2560]{0:T(1024)S(1)} %convert_element_type.72, f32[8]{0:T(128)S(1)} %add_rsqrt_fusion), kind=kOutput, calls=%fused_computation.19 | convolution fusion | flops 73504768 | bytes 9377824 | tf_op jit(solution)/shard_map/dot_general | solution.py:154
  54.6 0.6 gather_fusion
  55.2 3.9 %collective-permute-done.2 = f32[8,2560]{1,0:T(8,128)} collective-permute-done((f32[8,2560]{1,0:T(8,128)S(1)}, f32[8,2560]{1,0:T(8,128)}, u32[]{:S(2)}, u32[]{:S(2)}) %collective-permute-start.2) | collective-permute-done | bytes 81952 | tf_op jit(solution)/shard_map/ppermute | solution.py:38
  59.1 0.9 %add.284 = f32[8,2560]{1,0:T(8,128)S(1)} add(f32[8,2560]{1,0:T(8,128)S(1)} %fusion.20, f32[8,2560]{1,0:T(8,128)} %collective-permute-done.2) | non-fusion elementwise | flops 20480 | bytes 245760 | tf_op jit(solution)/shard_map/add | solution.py:38
  60.0 1.2 %collective-permute-start.3 = (f32[8,2560]{1,0:T(8,128)S(1)}, f32[8,2560]{1,0:T(8,128)S(1)}, u32[]{:S(2)}, u32[]{:S(2)}) collective-permute-start(f32[8,2560]{1,0:T(8,128)S(1)} %add.284), channel_id=1, source_target_pairs={{0,2},{1,3},{2,0},{3,1},{4,6},{5,7},{6,4},{7,5},{8,10},{9,11},{10,... | collective-permute-start | bytes 245768 | tf_op jit(solution)/shard_map/ppermute | solution.py:38
  61.2 4.8 %collective-permute-done.3 = f32[8,2560]{1,0:T(8,128)S(1)} collective-permute-done((f32[8,2560]{1,0:T(8,128)S(1)}, f32[8,2560]{1,0:T(8,128)S(1)}, u32[]{:S(2)}, u32[]{:S(2)}) %collective-permute-start.3) | collective-permute-done | bytes 81952 | tf_op jit(solution)/shard_map/ppermute | solution.py:38
  66.0 0.6 gather_fusion.7
  66.6 0.7 reshape.448
  67.3 3.4 %all-to-all-start.1 = ((bf16[8,2,2560]{2,1,0:T(2,128)(2,1)}), bf16[8,2,2560]{2,1,0:T(2,128)(2,1)S(1)}, u32[]{:S(2)}, u32[]{:S(2)}) async-start(bf16[8,2,2560]{2,1,0:T(2,128)(2,1)} %reshape.448), calls=%async_computation.1 | async-start | bytes 163840 | tf_op jit(solution)/shard_map/all_to_all | solution.py:164
  70.7 5.0 %all-to-all-done.1 = bf16[8,2,2560]{2,1,0:T(2,128)(2,1)S(1)} async-done(((bf16[8,2,2560]{2,1,0:T(2,128)(2,1)}), bf16[8,2,2560]{2,1,0:T(2,128)(2,1)S(1)}, u32[]{:S(2)}, u32[]{:S(2)}) %all-to-all-start.1) | async-done | bytes 81952 | tf_op jit(solution)/shard_map/all_to_all | solution.py:164
  75.7 0.8 select_reduce_fusion
  (59 shorter events, 4.0 us)
Async XLA Ops:
  0.0 33.7 %copy-start = (bf16[640,2560]{1,0:T(8,128)(2,1)S(1)}, bf16[640,2560]{1,0:T(8,128)(2,1)}, u32[]{:S(2)}) copy-start(bf16[640,2560]{1,0:T(8,128)(2,1)} %param.23) | copy-start | bytes 9830404
  1.8 19.7 %all-to-all-start = ((bf16[32,16,320]{2,1,0:T(8,128)(2,1)}), bf16[32,16,320]{2,1,0:T(8,128)(2,1)}, u32[]{:S(2)}, u32[]{:S(2)}) async-start(bf16[32,16,320]{2,1,0:T(8,128)(2,1)} %broadcast_in_dim.42), calls=%async_computation | async-start | bytes 786432 | tf_op jit(solution)/shard_map/all_to_all | solution.py:78
  30.2 6.0 %copy-start.1 = (bf16[2560]{0:T(1024)(128)(2,1)S(1)}, bf16[2560]{0:T(1024)(128)(2,1)}, u32[]{:S(2)}) copy-start(bf16[2560]{0:T(1024)(128)(2,1)} %param.24) | copy-start | bytes 15364
  34.3 5.1 %collective-permute-start = (f32[8,2560]{1,0:T(8,128)S(1)}, f32[8,2560]{1,0:T(8,128)S(1)}, u32[]{:S(2)}, u32[]{:S(2)}) collective-permute-start(f32[8,2560]{1,0:T(8,128)S(1)} %fusion.58), channel_id=1, source_target_pairs={{0,1},{1,0},{2,3},{3,2},{4,5},{5,4},{6,7},{7,6},{8,9},{9,8},{10,11... | collective-permute-start | bytes 245768 | tf_op jit(solution)/shard_map/ppermute | solution.py:38
  39.4 6.7 %collective-permute-start.1 = (f32[8,2560]{1,0:T(8,128)S(1)}, f32[8,2560]{1,0:T(8,128)S(1)}, u32[]{:S(2)}, u32[]{:S(2)}) collective-permute-start(f32[8,2560]{1,0:T(8,128)S(1)} %add.279), channel_id=1, source_target_pairs={{0,2},{1,3},{2,0},{3,1},{4,6},{5,7},{6,4},{7,5},{8,10},{9,11},{10,... | collective-permute-start | bytes 245768 | tf_op jit(solution)/shard_map/ppermute | solution.py:38
  54.6 4.6 %collective-permute-start.2 = (f32[8,2560]{1,0:T(8,128)S(1)}, f32[8,2560]{1,0:T(8,128)}, u32[]{:S(2)}, u32[]{:S(2)}) collective-permute-start(f32[8,2560]{1,0:T(8,128)S(1)} %fusion.20), channel_id=1, source_target_pairs={{0,1},{1,0},{2,3},{3,2},{4,5},{5,4},{6,7},{7,6},{8,9},{9,8},{10,11... | collective-permute-start | bytes 245768 | tf_op jit(solution)/shard_map/ppermute | solution.py:38
  60.0 6.0 %collective-permute-start.3 = (f32[8,2560]{1,0:T(8,128)S(1)}, f32[8,2560]{1,0:T(8,128)S(1)}, u32[]{:S(2)}, u32[]{:S(2)}) collective-permute-start(f32[8,2560]{1,0:T(8,128)S(1)} %add.284), channel_id=1, source_target_pairs={{0,2},{1,3},{2,0},{3,1},{4,6},{5,7},{6,4},{7,5},{8,10},{9,11},{10,... | collective-permute-start | bytes 245768 | tf_op jit(solution)/shard_map/ppermute | solution.py:38
  67.3 8.4 %all-to-all-start.1 = ((bf16[8,2,2560]{2,1,0:T(2,128)(2,1)}), bf16[8,2,2560]{2,1,0:T(2,128)(2,1)S(1)}, u32[]{:S(2)}, u32[]{:S(2)}) async-start(bf16[8,2,2560]{2,1,0:T(2,128)(2,1)} %reshape.448), calls=%async_computation.1 | async-start | bytes 163840 | tf_op jit(solution)/shard_map/all_to_all | solution.py:164

commit v7 on v5

--- a/solution.py
+++ b/solution.py
@@ -88,7 +88,8 @@
     slots = jnp.arange(req_loc, dtype=jnp.int32)
     hits = (server[None, :] == dp_index) & (round_no[None, :] == slots[:, None])
     served = jnp.sum(jnp.where(hits, request_ids[None, :], 0), axis=1)
-    served_len = lengths[served]
+    served_len = jnp.sum(jnp.where(hits, lengths[None, :], 0), axis=1)
+    served_pages = jnp.sum(jnp.where(hits[:, :, None], page_table[None, :, :], 0), axis=1)
 
     rows_srv = rows_all[served // rows_loc, served % rows_loc]
     scaled_input = norm_rows(rows_srv, norm_gain).astype(jnp.bfloat16)
@@ -114,9 +115,16 @@
         .reshape(req_loc, kv_loc, HEAD_SIZE)
     )
 
-    page_list = page_table[served] - dp_index * pool_size
-    key_rows = key_page_pool[page_list]
-    value_rows = value_page_pool[page_list]
+    page_list = (served_pages - dp_index * pool_size).reshape(-1)
+    page_hot = (
+        page_list[:, None] == jnp.arange(pool_size, dtype=jnp.int32)[None, :]
+    ).astype(key_page_pool.dtype)
+    key_rows = jnp.einsum(
+        "sq,qhdc->shdc", page_hot, key_page_pool, preferred_element_type=jnp.bfloat16
+    ).reshape((req_loc, per_req) + key_page_pool.shape[1:])
+    value_rows = jnp.einsum(
+        "sq,qhdc->shdc", page_hot, value_page_pool, preferred_element_type=jnp.bfloat16
+    ).reshape((req_loc, per_req) + value_page_pool.shape[1:])
     scores = (
         jnp.einsum("rhgd,rphdc->rhgpc", query_srv, key_rows, preferred_element_type=jnp.float32)
         * score_scale
@@ -158,7 +166,10 @@
         + tp_index * rows_loc
         + jnp.arange(rows_loc, dtype=jnp.int32)[None, :]
     ).reshape(-1)
-    outgoing = final[round_no[dest_rows].reshape(dp_count, rows_loc)]
+    dest_round = jnp.sum(
+        jnp.where(request_ids[None, :] == dest_rows[:, None], round_no[None, :], 0), axis=1
+    )
+    outgoing = final[dest_round.reshape(dp_count, rows_loc)]
     incoming = lax.all_to_all(outgoing, "dp", 0, 0)
     mine = dp_index * req_loc + tp_index * rows_loc + jnp.arange(rows_loc, dtype=jnp.int32)
     from_src = jnp.arange(dp_count, dtype=jnp.int32)[:, None] == server[mine][None, :]

time: 76.6 us -> 74.1 us (0.967)
  local copies, waits for them, and re-layouts: 15.6 us -> 6.01 us
  waiting for transfers between devices: 19.6 us -> 25.1 us
  matrix products: 18.1 us -> 22.1 us
  starting transfers between devices: 17.8 us -> 13.9 us
  other arithmetic: 4.59 us -> 6.24 us
    gather x7 -> x2, local copies, waits for them, and re-layouts: 9.97 us -> 1.26 us  [local(): outgoing = final[dest_round.reshape(dp_count, rows_loc)]]
    dot_general x0 -> x2, matrix products: none -> 4.87 us  [the longest x1 3.15 us: local(): jnp.einsum('sq,qhdc->shdc', page_hot, key_page_pool, preferred_element_ty...]
    ppermute x4, starting transfers between devices: 6.77 us -> 3.1 us  [tensor_allreduce(): part = part + lax.ppermute(part, 'tensor', pairs)]
    ppermute x4, waiting for transfers between devices: 14.5 us -> 18.1 us  [tensor_allreduce(): part = part + lax.ppermute(part, 'tensor', pairs)]
    all_to_all x1, waiting for transfers between devices: 0.01 us -> 1.96 us  [local(): lax.all_to_all(jnp.broadcast_to(residual_in[None], (dev_count,) + residua...]
    reduce_sum x1 -> x3, other arithmetic: 0.12 us -> 1.81 us  [the longest x1 0.83 us: local(): jnp.sum(jnp.where(hits[:, :, None], page_table[None, :, :], 0), axis=1)]
    dot_general x1, matrix products: 1.48 us -> 0.34 us  [local(): jnp.dot(scaled_input, value_weight, preferred_element_type=jnp.float32)]
    unnamed x5 -> x8, local copies, waits for them, and re-layouts: 0.79 us -> 0.02 us
  transfers between devices with their start and end apart: 6 -> 6, of which waited for: 5 -> 6; matrix products, arithmetic and copies ran while one was open for 17% -> 13% of each run, Pallas kernels for 0% -> 0%
where the time goes in v7:
time: 74.1 us; the launch traced here: 73.5 us
  waiting for transfers between devices  25.1 us (34%)
  matrix products  22.1 us (30%)
  starting transfers between devices  13.9 us (19%)
  other arithmetic  6.24 us (8%)
  local copies, waits for them, and re-layouts  6.01 us (8%)
    ppermute x4, waiting for transfers between devices, tensor_allreduce(): part = part + lax.ppermute(part, 'tensor', pairs)  18.1 us
    all_to_all x1, starting transfers between devices, local(): lax.all_to_all(jnp.broadcast_to(residual_in[None], (dev_count,) + residua...  7.41 us
    dot_general x1, matrix products, local(): jnp.dot(hidden, w_down, preferred_element_type=jnp.float32)  5.29 us
    all_to_all x1, waiting for transfers between devices, local(): incoming = lax.all_to_all(outgoing, 'dp', 0, 0)  5.02 us
    all_to_all x1, starting transfers between devices, local(): incoming = lax.all_to_all(outgoing, 'dp', 0, 0)  3.36 us
    dot_general x1, matrix products, local(): jnp.einsum('sq,qhdc->shdc', page_hot, key_page_pool, preferred_element_ty...  3.15 us
    ppermute x4, starting transfers between devices, tensor_allreduce(): part = part + lax.ppermute(part, 'tensor', pairs)  3.1 us
    dot_general x1, matrix products, local(): gate_act = jnp.dot(normed_mlp, w_gate, preferred_element_type=jnp.float32)  3.05 us
  transfers between devices with their start and end apart: 6, of which 6 were waited for; matrix products, arithmetic and copies ran while one was open for 13% of the time, Pallas kernels for 0%

profile of v7, /device:TPU:0, one launch (start us, length us, event | category | flops | bytes accessed | tf_op | source)
XLA Modules:
  0.0 73.5 jit_solution(17733901841270737196)
XLA Ops:
  0.0 1.8 %broadcast_in_dim.79 = bf16[32,2,2560]{2,1,0:T(2,128)(2,1)} broadcast(bf16[2,2560]{1,0:T(2,128)(2,1)} %param.14), dimensions={1,2} | broadcast | bytes 337920 | tf_op jit(solution)/shard_map/broadcast_in_dim | solution.py:76
  1.8 7.4 %all-to-all-start = ((bf16[32,2,2560]{2,1,0:T(2,128)(2,1)}), bf16[32,2,2560]{2,1,0:T(2,128)(2,1)}, u32[]{:S(2)}, u32[]{:S(2)}) async-start(bf16[32,2,2560]{2,1,0:T(2,128)(2,1)} %broadcast_in_dim.79), calls=%async_computation | async-start | bytes 655360 | tf_op jit(solution)/shard_map/all_to_all | solution.py:75
  9.2 0.7 iota_add_fusion.2
  10.1 0.8 %select_reduce_fusion.4 = (s32[8]{0:T(128)S(1)}, s32[8]{0:T(128)S(1)}) fusion(s32[64]{0:T(128)} %param.21, s32[64]{0:T(128)S(1)} %get-tuple-element.13, pred[64]{0:T(512)(128)(4,1)S(1)} %get-tuple-element.11), kind=kLoop, calls=%fused_computation.69 | loop fusion | flops 3056 | bytes 640 | tf_op jit(solution)/shard_map/reduce_sum | solution.py:91
  11.4 0.8 %select_reduce_fusion.2 = s32[8,4]{0,1:T(4,128)S(1)} fusion(s32[64,4]{0,1:T(4,128)} %param.22, pred[8,64]{1,0:T(8,128)(4,1)S(1)} %fusion.47), kind=kLoop, calls=%fused_computation.48 | loop fusion | flops 4064 | bytes 1664 | tf_op jit(solution)/shard_map/reduce_sum | solution.py:92
  12.4 0.7 convert_element_type.65
  13.3 3.2 %fusion.6 = bf16[32,2,80,128]{3,0,2,1:T(8,128)(2,1)} fusion(bf16[32,2,80,128]{3,2,1,0:T(8,128)(2,1)} %param.19, s32[32]{0:T(128)S(1)} %sub.54), kind=kOutput, calls=%fused_computation.9 | convolution fusion | flops 41944064 | bytes 2621568 | tf_op jit(solution)/shard_map/sq,qhdc->shdc/dot_general | solution.py:122
  16.5 1.7 %fusion.2 = bf16[32,2,80,128]{3,0,2,1:T(8,128)(2,1)} fusion(bf16[32,2,80,128]{3,2,1,0:T(8,128)(2,1)S(1)} %copy-done.1, s32[32]{0:T(128)S(1)} %sub.54), kind=kOutput, calls=%fused_computation.5 | convolution fusion | flops 41944064 | bytes 2621568 | tf_op jit(solution)/shard_map/sq,qhdc->shdc/dot_general | solution.py:125
  18.2 2.0 %all-to-all-done = bf16[32,2,2560]{2,1,0:T(2,128)(2,1)} async-done(((bf16[32,2,2560]{2,1,0:T(2,128)(2,1)}), bf16[32,2,2560]{2,1,0:T(2,128)(2,1)}, u32[]{:S(2)}, u32[]{:S(2)}) %all-to-all-start) | async-done | bytes 327712 | tf_op jit(solution)/shard_map/all_to_all | solution.py:75
  20.2 1.6 %gather_fusion.1 = bf16[8,2560]{1,0:T(8,128)(2,1)S(1)} fusion(bf16[32,2,2560]{2,1,0:T(2,128)(2,1)} %all-to-all-done, s32[8]{0:T(128)S(1)} %fusion.55), kind=kCustom, calls=%fused_computation.1 | custom fusion | bytes 81984 | tf_op jit(solution)/shard_map/gather | solution.py:94
  21.9 1.5 %fusion.60 = f32[8,160]{1,0:T(8,128)S(1)} fusion(bf16[2560,160]{0,1:T(8,128)(2,1)} %param.17, bf16[8,2560]{1,0:T(8,128)(2,1)S(1)} %gather_fusion.1, f32[2560]{0:T(1024)S(1)} %convert_element_type.65, f32[8]{0:T(128)S(1)} %add_rsqrt_fusion.1), kind=kOutput, calls=%fused_computation.112 | convolution fusion | flops 6635520 | bytes 875552 | tf_op jit(solution)/shard_map/dot_general | solution.py:107
  23.5 2.5 %fusion.62 = f32[8,640]{1,0:T(8,128)S(1)} fusion(bf16[2560,640]{1,0:T(8,128)(2,1)} %param.16, bf16[8,2560]{1,0:T(8,128)(2,1)S(1)} %gather_fusion.1, f32[2560]{0:T(1024)S(1)} %convert_element_type.65, f32[8]{0:T(128)S(1)} %add_rsqrt_fusion.1), kind=kOutput, calls=%fused_computation.113 | convolution fusion | flops 26296320 | bytes 3348512 | tf_op jit(solution)/shard_map/dot_general | solution.py:98
  26.5 1.9 %select_reduce_fusion.1 = (f32[8,2,4]{2,1,0:T(2,128)S(1)}, f32[8,2,4,4,128]{4,2,3,1,0:T(4,128)S(1)}) fusion(pred[8,4,128]{2,1,0:T(4,128)(4,1)S(1)} %broadcast_compare_fusion, bf16[8,4,2,80,128]{4,1,0,3,2:T(4,128)(2,1)} %bitcast.60, bf16[8,2,4,40]{3,2,1,0:T(4,128)(2,1)S(1)} %bitcast.66, bf16[8,2,4,40]{3,2,1,0:T(4,128)(2,1)S(1)} %bitcast.64), kind=kOutput, calls=%fused_computation.23 | convolution fusion | flops 5361600 | bytes 1456384 | tf_op jit(solution)/shard_map/rhgd,rphdc->rhgpc/dot_general | solution.py:129
  28.7 0.3 fusion.25
  29.1 1.9 %fusion.20 = bf16[8,2,4,80]{3,2,1,0:T(4,128)(2,1)S(1)} fusion(bf16[8,4,2,80,128]{4,1,0,3,2:T(4,128)(2,1)} %bitcast.59, f32[8,2,4,4,128]{4,2,3,1,0:T(4,128)S(1)} %get-tuple-element.21, f32[8,2,4]{2,1,0:T(2,128)S(1)} %multiply_maximum_fusion, pred[8,4,128]{2,1,0:T(4,128)(4,1)S(1)} %broadcast_compare_fusion, f32[8,2,4]{2,1,0:T(2,128)S(1)} %get-tuple-element.9, ...), kind=kOutput, calls=%fused_computation.16 | convolution fusion | flops 5328896 | bytes 1462016 | tf_op jit(solution)/shard_map/rhgpc,rphdc->rhgd/dot_general | solution.py:145
  31.2 0.5 fusion.65
  31.7 1.7 %collective-permute-start = (f32[8,2560]{1,0:T(8,128)S(1)}, f32[8,2560]{1,0:T(8,128)S(1)}, u32[]{:S(2)}, u32[]{:S(2)}) collective-permute-start(f32[8,2560]{1,0:T(8,128)S(1)} %fusion.65), channel_id=1, source_target_pairs={{0,1},{1,0},{2,3},{3,2},{4,5},{5,4},{6,7},{7,6},{8,9},{9,8},{10,11... | collective-permute-start | bytes 245768 | tf_op jit(solution)/shard_map/ppermute | solution.py:38
  33.5 3.4 %collective-permute-done = f32[8,2560]{1,0:T(8,128)S(1)} collective-permute-done((f32[8,2560]{1,0:T(8,128)S(1)}, f32[8,2560]{1,0:T(8,128)S(1)}, u32[]{:S(2)}, u32[]{:S(2)}) %collective-permute-start) | collective-permute-done | bytes 81952 | tf_op jit(solution)/shard_map/ppermute | solution.py:38
  36.9 1.0 %collective-permute-start.1 = (f32[8,2560]{1,0:T(8,128)S(1)}, f32[8,2560]{1,0:T(8,128)S(1)}, u32[]{:S(2)}, u32[]{:S(2)}) collective-permute-start(f32[8,2560]{1,0:T(8,128)S(1)} %add.222), channel_id=1, source_target_pairs={{0,2},{1,3},{2,0},{3,1},{4,6},{5,7},{6,4},{7,5},{8,10},{9,11},{10,... | collective-permute-start | bytes 245768 | tf_op jit(solution)/shard_map/ppermute | solution.py:38
  37.9 5.3 %collective-permute-done.1 = f32[8,2560]{1,0:T(8,128)S(1)} collective-permute-done((f32[8,2560]{1,0:T(8,128)S(1)}, f32[8,2560]{1,0:T(8,128)S(1)}, u32[]{:S(2)}, u32[]{:S(2)}) %collective-permute-start.1) | collective-permute-done | bytes 81952 | tf_op jit(solution)/shard_map/ppermute | solution.py:38
  43.3 3.0 %fusion.58 = f32[8,896]{1,0:T(8,128)S(1)} fusion(bf16[2560,896]{1,0:T(8,128)(2,1)} %param.25, f32[8,2560]{1,0:T(8,128)S(1)} %get-tuple-element.8, f32[2560]{0:T(1024)S(1)} %convert_element_type.73, f32[8]{0:T(128)S(1)} %add_rsqrt_fusion), kind=kOutput, calls=%fused_computation.111 | convolution fusion | flops 36761600 | bytes 4708384 | tf_op jit(solution)/shard_map/dot_general | solution.py:156
  46.4 5.3 %fusion.24 = f32[8,2560]{1,0:T(8,128)S(1)} fusion(bf16[896,2560]{1,0:T(8,128)(2,1)} %param.27, bf16[2560,896]{1,0:T(8,128)(2,1)} %param.26, f32[8,896]{1,0:T(8,128)S(1)} %fusion.58, f32[8,2560]{1,0:T(8,128)S(1)} %get-tuple-element.8, f32[2560]{0:T(1024)S(1)} %convert_element_type.73, f32[8]{0:T(128)S(1)} %add_rsqrt_fusion), kind=kOutput, calls=%fused_computation.18 | convolution fusion | flops 73504768 | bytes 9377824 | tf_op jit(solution)/shard_map/dot_general | solution.py:160
  51.7 0.2 collective-permute-start.2
  51.9 0.6 gather_fusion
  52.5 3.7 %collective-permute-done.2 = f32[8,2560]{1,0:T(8,128)} collective-permute-done((f32[8,2560]{1,0:T(8,128)S(1)}, f32[8,2560]{1,0:T(8,128)}, u32[]{:S(2)}, u32[]{:S(2)}) %collective-permute-start.2) | collective-permute-done | bytes 81952 | tf_op jit(solution)/shard_map/ppermute | solution.py:38
  56.2 0.9 %add.227 = f32[8,2560]{1,0:T(8,128)S(1)} add(f32[8,2560]{1,0:T(8,128)S(1)} %fusion.24, f32[8,2560]{1,0:T(8,128)} %collective-permute-done.2) | non-fusion elementwise | flops 20480 | bytes 245760 | tf_op jit(solution)/shard_map/add | solution.py:38
  57.3 5.8 %collective-permute-done.3 = f32[8,2560]{1,0:T(8,128)S(1)} collective-permute-done((f32[8,2560]{1,0:T(8,128)S(1)}, f32[8,2560]{1,0:T(8,128)S(1)}, u32[]{:S(2)}, u32[]{:S(2)}) %collective-permute-start.3) | collective-permute-done | bytes 81952 | tf_op jit(solution)/shard_map/ppermute | solution.py:38
  63.1 0.6 gather_fusion.2
  63.7 0.7 reshape.417
  64.3 3.4 %all-to-all-start.1 = ((bf16[8,2,2560]{2,1,0:T(2,128)(2,1)}), bf16[8,2,2560]{2,1,0:T(2,128)(2,1)S(1)}, u32[]{:S(2)}, u32[]{:S(2)}) async-start(bf16[8,2,2560]{2,1,0:T(2,128)(2,1)} %reshape.417), calls=%async_computation.1 | async-start | bytes 163840 | tf_op jit(solution)/shard_map/all_to_all | solution.py:173
  67.7 5.0 %all-to-all-done.1 = bf16[8,2,2560]{2,1,0:T(2,128)(2,1)S(1)} async-done(((bf16[8,2,2560]{2,1,0:T(2,128)(2,1)}), bf16[8,2,2560]{2,1,0:T(2,128)(2,1)S(1)}, u32[]{:S(2)}, u32[]{:S(2)}) %all-to-all-start.1) | async-done | bytes 81952 | tf_op jit(solution)/shard_map/all_to_all | solution.py:173
  72.7 0.8 %select_reduce_fusion = bf16[2,2560]{1,0:T(2,128)(2,1)} fusion(bf16[8,2,2560]{2,1,0:T(2,128)(2,1)S(1)} %all-to-all-done.1, pred[8,2]{1,0:T(8,128)(4,1)S(1)} %iota_compare_fusion.3), kind=kLoop, calls=%fused_computation.21 | loop fusion | flops 117760 | bytes 92176 | tf_op jit(solution)/shard_map/reduce_sum | solution.py:177
  (51 shorter events, 2.7 us)
Async XLA Ops:
  0.0 31.1 %copy-start = (bf16[640,2560]{1,0:T(8,128)(2,1)S(1)}, bf16[640,2560]{1,0:T(8,128)(2,1)}, u32[]{:S(2)}) copy-start(bf16[640,2560]{1,0:T(8,128)(2,1)} %param.23) | copy-start | bytes 9830404
  1.8 18.4 %all-to-all-start = ((bf16[32,2,2560]{2,1,0:T(2,128)(2,1)}), bf16[32,2,2560]{2,1,0:T(2,128)(2,1)}, u32[]{:S(2)}, u32[]{:S(2)}) async-start(bf16[32,2,2560]{2,1,0:T(2,128)(2,1)} %broadcast_in_dim.79), calls=%async_computation | async-start | bytes 655360 | tf_op jit(solution)/shard_map/all_to_all | solution.py:75
  13.3 3.2 %copy-start.1 = (bf16[32,2,80,128]{3,2,1,0:T(8,128)(2,1)S(1)}, bf16[32,2,80,128]{3,2,1,0:T(8,128)(2,1)}, u32[]{:S(2)}) copy-start(bf16[32,2,80,128]{3,2,1,0:T(8,128)(2,1)} %param.20) | copy-start | bytes 3932164
  26.1 2.6 %copy-start.2 = (bf16[2560,160]{0,1:T(8,128)(2,1)S(1)}, bf16[2560,160]{0,1:T(8,128)(2,1)}, u32[]{:S(2)}) copy-start(bf16[2560,160]{0,1:T(8,128)(2,1)} %param.18) | copy-start | bytes 2457604
  31.1 2.3 %copy-start.3 = (bf16[2560]{0:T(1024)(128)(2,1)S(1)}, bf16[2560]{0:T(1024)(128)(2,1)}, u32[]{:S(2)}) copy-start(bf16[2560]{0:T(1024)(128)(2,1)} %param.24) | copy-start | bytes 15364
  31.7 5.2 %collective-permute-start = (f32[8,2560]{1,0:T(8,128)S(1)}, f32[8,2560]{1,0:T(8,128)S(1)}, u32[]{:S(2)}, u32[]{:S(2)}) collective-permute-start(f32[8,2560]{1,0:T(8,128)S(1)} %fusion.65), channel_id=1, source_target_pairs={{0,1},{1,0},{2,3},{3,2},{4,5},{5,4},{6,7},{7,6},{8,9},{9,8},{10,11... | collective-permute-start | bytes 245768 | tf_op jit(solution)/shard_map/ppermute | solution.py:38
  36.9 6.3 %collective-permute-start.1 = (f32[8,2560]{1,0:T(8,128)S(1)}, f32[8,2560]{1,0:T(8,128)S(1)}, u32[]{:S(2)}, u32[]{:S(2)}) collective-permute-start(f32[8,2560]{1,0:T(8,128)S(1)} %add.222), channel_id=1, source_target_pairs={{0,2},{1,3},{2,0},{3,1},{4,6},{5,7},{6,4},{7,5},{8,10},{9,11},{10,... | collective-permute-start | bytes 245768 | tf_op jit(solution)/shard_map/ppermute | solution.py:38
  51.7 4.6 %collective-permute-start.2 = (f32[8,2560]{1,0:T(8,128)S(1)}, f32[8,2560]{1,0:T(8,128)}, u32[]{:S(2)}, u32[]{:S(2)}) collective-permute-start(f32[8,2560]{1,0:T(8,128)S(1)} %fusion.24), channel_id=1, source_target_pairs={{0,1},{1,0},{2,3},{3,2},{4,5},{5,4},{6,7},{7,6},{8,9},{9,8},{10,11... | collective-permute-start | bytes 245768 | tf_op jit(solution)/shard_map/ppermute | solution.py:38
  57.1 5.9 %collective-permute-start.3 = (f32[8,2560]{1,0:T(8,128)S(1)}, f32[8,2560]{1,0:T(8,128)S(1)}, u32[]{:S(2)}, u32[]{:S(2)}) collective-permute-start(f32[8,2560]{1,0:T(8,128)S(1)} %add.227), channel_id=1, source_target_pairs={{0,2},{1,3},{2,0},{3,1},{4,6},{5,7},{6,4},{7,5},{8,10},{9,11},{10,... | collective-permute-start | bytes 245768 | tf_op jit(solution)/shard_map/ppermute | solution.py:38
  64.3 8.4 %all-to-all-start.1 = ((bf16[8,2,2560]{2,1,0:T(2,128)(2,1)}), bf16[8,2,2560]{2,1,0:T(2,128)(2,1)S(1)}, u32[]{:S(2)}, u32[]{:S(2)}) async-start(bf16[8,2,2560]{2,1,0:T(2,128)(2,1)} %reshape.417), calls=%async_computation.1 | async-start | bytes 163840 | tf_op jit(solution)/shard_map/all_to_all | solution.py:173

commit v8 on v7

--- a/solution.py
+++ b/solution.py
@@ -169,7 +169,10 @@
     dest_round = jnp.sum(
         jnp.where(request_ids[None, :] == dest_rows[:, None], round_no[None, :], 0), axis=1
     )
-    outgoing = final[dest_round.reshape(dp_count, rows_loc)]
+    send_hot = dest_round.reshape(dp_count, rows_loc)[:, :, None] == slots[None, None, :]
+    outgoing = jnp.sum(
+        jnp.where(send_hot[:, :, :, None], final.astype(jnp.float32)[None, None], 0.0), axis=2
+    ).astype(jnp.bfloat16)
     incoming = lax.all_to_all(outgoing, "dp", 0, 0)
     mine = dp_index * req_loc + tp_index * rows_loc + jnp.arange(rows_loc, dtype=jnp.int32)
     from_src = jnp.arange(dp_count, dtype=jnp.int32)[:, None] == server[mine][None, :]

time: 74.1 us -> 76.7 us (1.035)
  other arithmetic: 6.24 us -> 9.82 us
  local copies, waits for them, and re-layouts: 6.01 us -> 4.67 us
    gather x2 -> x0, local copies, waits for them, and re-layouts: 1.26 us -> none  [local(): outgoing = final[dest_round.reshape(dp_count, rows_loc)]]
    reduce_sum x0 -> x1, other arithmetic: none -> 1.12 us  [local(): jnp.sum(jnp.where(send_hot[:, :, :, None], final.astype(jnp.float32)[None...]
    convert_element_type x1, other arithmetic: 0.01 us -> 0.9 us  [local(): final.astype(jnp.float32)[None, None]]
    reduce_sum x2, other arithmetic: 0.28 us -> 1.16 us  [norm_rows(): jnp.mean(value_rows * value_rows, axis=-1, keepdims=True) + 1e-05]
where the time goes in v8:
time: 76.7 us; the launch traced here: 76 us
  waiting for transfers between devices  25.4 us (33%)
  matrix products  22.1 us (29%)
  starting transfers between devices  13.8 us (18%)
  other arithmetic  9.82 us (13%)
  local copies, waits for them, and re-layouts  4.67 us (6%)
    ppermute x4, waiting for transfers between devices, tensor_allreduce(): part = part + lax.ppermute(part, 'tensor', pairs)  18.1 us
    all_to_all x1, starting transfers between devices, local(): lax.all_to_all(jnp.broadcast_to(residual_in[None], (dev_count,) + residua...  7.41 us
    dot_general x1, matrix products, local(): jnp.dot(hidden, w_down, preferred_element_type=jnp.float32)  5.29 us
    all_to_all x1, waiting for transfers between devices, local(): incoming = lax.all_to_all(outgoing, 'dp', 0, 0)  5.02 us
    all_to_all x1, starting transfers between devices, local(): incoming = lax.all_to_all(outgoing, 'dp', 0, 0)  3.36 us
    dot_general x1, matrix products, local(): jnp.einsum('sq,qhdc->shdc', page_hot, key_page_pool, preferred_element_ty...  3.15 us
    dot_general x1, matrix products, local(): gate_act = jnp.dot(normed_mlp, w_gate, preferred_element_type=jnp.float32)  3.05 us
    ppermute x4, starting transfers between devices, tensor_allreduce(): part = part + lax.ppermute(part, 'tensor', pairs)  3.04 us
  transfers between devices with their start and end apart: 6, of which 6 were waited for; matrix products, arithmetic and copies ran while one was open for 13% of the time, Pallas kernels for 0%

profile of v8, /device:TPU:0, one launch (start us, length us, event | category | flops | bytes accessed | tf_op | source)
XLA Modules:
  0.0 76.0 jit_solution(7005143844105622447)
XLA Ops:
  0.0 1.8 %broadcast_in_dim.102 = bf16[32,2,2560]{2,1,0:T(2,128)(2,1)} broadcast(bf16[2,2560]{1,0:T(2,128)(2,1)} %param.14), dimensions={1,2} | broadcast | bytes 337920 | tf_op jit(solution)/shard_map/broadcast_in_dim | solution.py:76
  1.8 7.4 %all-to-all-start = ((bf16[32,2,2560]{2,1,0:T(2,128)(2,1)}), bf16[32,2,2560]{2,1,0:T(2,128)(2,1)}, u32[]{:S(2)}, u32[]{:S(2)}) async-start(bf16[32,2,2560]{2,1,0:T(2,128)(2,1)} %broadcast_in_dim.102), calls=%async_computation | async-start | bytes 655360 | tf_op jit(solution)/shard_map/all_to_all | solution.py:75
  9.2 0.7 iota_add_fusion.2
  10.1 0.8 %select_reduce_fusion.5 = (s32[8]{0:T(128)S(1)}, s32[8]{0:T(128)S(1)}) fusion(s32[64]{0:T(128)} %param.21, s32[64]{0:T(128)S(1)} %get-tuple-element.13, pred[64]{0:T(512)(128)(4,1)S(1)} %get-tuple-element.11), kind=kLoop, calls=%fused_computation.68 | loop fusion | flops 3056 | bytes 640 | tf_op jit(solution)/shard_map/reduce_sum | solution.py:91
  11.3 0.8 %select_reduce_fusion.3 = s32[8,4]{0,1:T(4,128)S(1)} fusion(s32[64,4]{0,1:T(4,128)} %param.22, pred[8,64]{1,0:T(8,128)(4,1)S(1)} %fusion.48), kind=kLoop, calls=%fused_computation.49 | loop fusion | flops 4064 | bytes 1664 | tf_op jit(solution)/shard_map/reduce_sum | solution.py:92
  12.1 0.7 convert_element_type.71
  13.1 3.1 %fusion.6 = bf16[32,2,80,128]{3,0,2,1:T(8,128)(2,1)} fusion(bf16[32,2,80,128]{3,2,1,0:T(8,128)(2,1)} %param.19, s32[32]{0:T(128)S(1)} %sub.54), kind=kOutput, calls=%fused_computation.8 | convolution fusion | flops 41944064 | bytes 2621568 | tf_op jit(solution)/shard_map/sq,qhdc->shdc/dot_general | solution.py:122
  16.2 1.7 %fusion.2 = bf16[32,2,80,128]{3,0,2,1:T(8,128)(2,1)} fusion(bf16[32,2,80,128]{3,2,1,0:T(8,128)(2,1)S(1)} %copy-done.1, s32[32]{0:T(128)S(1)} %sub.54), kind=kOutput, calls=%fused_computation.4 | convolution fusion | flops 41944064 | bytes 2621568 | tf_op jit(solution)/shard_map/sq,qhdc->shdc/dot_general | solution.py:125
  17.9 2.2 %all-to-all-done = bf16[32,2,2560]{2,1,0:T(2,128)(2,1)} async-done(((bf16[32,2,2560]{2,1,0:T(2,128)(2,1)}), bf16[32,2,2560]{2,1,0:T(2,128)(2,1)}, u32[]{:S(2)}, u32[]{:S(2)}) %all-to-all-start) | async-done | bytes 327712 | tf_op jit(solution)/shard_map/all_to_all | solution.py:75
  20.2 1.6 %gather_fusion.1 = bf16[8,2560]{1,0:T(8,128)(2,1)S(1)} fusion(bf16[32,2,2560]{2,1,0:T(2,128)(2,1)} %all-to-all-done, s32[8]{0:T(128)S(1)} %fusion.56), kind=kCustom, calls=%fused_computation.1 | custom fusion | bytes 81984 | tf_op jit(solution)/shard_map/gather | solution.py:94
  21.9 1.5 %fusion.61 = f32[8,160]{1,0:T(8,128)S(1)} fusion(bf16[2560,160]{0,1:T(8,128)(2,1)} %param.17, bf16[8,2560]{1,0:T(8,128)(2,1)S(1)} %gather_fusion.1, f32[2560]{0:T(1024)S(1)} %convert_element_type.71, f32[8]{0:T(128)S(1)} %add_rsqrt_fusion.1), kind=kOutput, calls=%fused_computation.112 | convolution fusion | flops 6635520 | bytes 875552 | tf_op jit(solution)/shard_map/dot_general | solution.py:107
  23.5 2.5 %fusion.63 = f32[8,640]{1,0:T(8,128)S(1)} fusion(bf16[2560,640]{1,0:T(8,128)(2,1)} %param.16, bf16[8,2560]{1,0:T(8,128)(2,1)S(1)} %gather_fusion.1, f32[2560]{0:T(1024)S(1)} %convert_element_type.71, f32[8]{0:T(128)S(1)} %add_rsqrt_fusion.1), kind=kOutput, calls=%fused_computation.113 | convolution fusion | flops 26296320 | bytes 3348512 | tf_op jit(solution)/shard_map/dot_general | solution.py:98
  26.5 1.9 %select_reduce_fusion.2 = (f32[8,2,4]{2,1,0:T(2,128)S(1)}, f32[8,2,4,4,128]{4,2,3,1,0:T(4,128)S(1)}) fusion(pred[8,4,128]{2,1,0:T(4,128)(4,1)S(1)} %broadcast_compare_fusion, bf16[8,4,2,80,128]{4,1,0,3,2:T(4,128)(2,1)} %bitcast.58, bf16[8,2,4,40]{3,2,1,0:T(4,128)(2,1)S(1)} %bitcast.64, bf16[8,2,4,40]{3,2,1,0:T(4,128)(2,1)S(1)} %bitcast.62), kind=kOutput, calls=%fused_computation.23 | convolution fusion | flops 5361600 | bytes 1456384 | tf_op jit(solution)/shard_map/rhgd,rphdc->rhgpc/dot_general | solution.py:129
  29.1 1.9 %fusion.20 = bf16[8,2,4,80]{3,2,1,0:T(4,128)(2,1)S(1)} fusion(bf16[8,4,2,80,128]{4,1,0,3,2:T(4,128)(2,1)} %bitcast.57, f32[8,2,4,4,128]{4,2,3,1,0:T(4,128)S(1)} %get-tuple-element.21, f32[8,2,4]{2,1,0:T(2,128)S(1)} %multiply_maximum_fusion, pred[8,4,128]{2,1,0:T(4,128)(4,1)S(1)} %broadcast_compare_fusion, f32[8,2,4]{2,1,0:T(2,128)S(1)} %get-tuple-element.9, ...), kind=kOutput, calls=%fused_computation.16 | convolution fusion | flops 5328896 | bytes 1462016 | tf_op jit(solution)/shard_map/rhgpc,rphdc->rhgd/dot_general | solution.py:145
  31.2 0.5 fusion.66
  31.7 1.7 %collective-permute-start = (f32[8,2560]{1,0:T(8,128)S(1)}, f32[8,2560]{1,0:T(8,128)}, u32[]{:S(2)}, u32[]{:S(2)}) collective-permute-start(f32[8,2560]{1,0:T(8,128)S(1)} %fusion.66), channel_id=1, source_target_pairs={{0,1},{1,0},{2,3},{3,2},{4,5},{5,4},{6,7},{7,6},{8,9},{9,8},{10,11... | collective-permute-start | bytes 245768 | tf_op jit(solution)/shard_map/ppermute | solution.py:38
  33.7 3.3 %collective-permute-done = f32[8,2560]{1,0:T(8,128)} collective-permute-done((f32[8,2560]{1,0:T(8,128)S(1)}, f32[8,2560]{1,0:T(8,128)}, u32[]{:S(2)}, u32[]{:S(2)}) %collective-permute-start) | collective-permute-done | bytes 81952 | tf_op jit(solution)/shard_map/ppermute | solution.py:38
  37.0 0.9 %add.218 = f32[8,2560]{1,0:T(8,128)S(1)} add(f32[8,2560]{1,0:T(8,128)S(1)} %fusion.66, f32[8,2560]{1,0:T(8,128)} %collective-permute-done) | non-fusion elementwise | flops 20480 | bytes 245760 | tf_op jit(solution)/shard_map/add | solution.py:38
  37.9 1.0 %collective-permute-start.1 = (f32[8,2560]{1,0:T(8,128)S(1)}, f32[8,2560]{1,0:T(8,128)}, u32[]{:S(2)}, u32[]{:S(2)}) collective-permute-start(f32[8,2560]{1,0:T(8,128)S(1)} %add.218), channel_id=1, source_target_pairs={{0,2},{1,3},{2,0},{3,1},{4,6},{5,7},{6,4},{7,5},{8,10},{9,11},{10,... | collective-permute-start | bytes 245768 | tf_op jit(solution)/shard_map/ppermute | solution.py:38
  39.0 5.3 %collective-permute-done.1 = f32[8,2560]{1,0:T(8,128)} collective-permute-done((f32[8,2560]{1,0:T(8,128)S(1)}, f32[8,2560]{1,0:T(8,128)}, u32[]{:S(2)}, u32[]{:S(2)}) %collective-permute-start.1) | collective-permute-done | bytes 81952 | tf_op jit(solution)/shard_map/ppermute | solution.py:38
  44.3 1.0 %multiply_reduce_fusion = (f32[8]{0:T(128)S(1)}, f32[8,2560]{1,0:T(8,128)S(1)}) fusion(f32[8,2560]{1,0:T(8,128)S(1)} %add.218, f32[8,2560]{1,0:T(8,128)} %collective-permute-done.1, bf16[8,2560]{1,0:T(8,128)(2,1)S(1)} %gather_fusion.1), kind=kLoop, calls=%fused_computation.33 | loop fusion | flops 102392 | bytes 286752 | tf_op jit(solution)/shard_map/reduce_sum | solution.py:13
  45.3 3.0 %fusion.59 = f32[8,896]{1,0:T(8,128)S(1)} fusion(bf16[2560,896]{1,0:T(8,128)(2,1)} %param.25, f32[8,2560]{1,0:T(8,128)S(1)} %get-tuple-element.8, f32[2560]{0:T(1024)S(1)} %convert_element_type.79, f32[8]{0:T(128)S(1)} %add_rsqrt_fusion), kind=kOutput, calls=%fused_computation.111 | convolution fusion | flops 36761600 | bytes 4708384 | tf_op jit(solution)/shard_map/dot_general | solution.py:156
  48.3 5.3 %fusion.24 = f32[8,2560]{1,0:T(8,128)S(1)} fusion(bf16[896,2560]{1,0:T(8,128)(2,1)} %param.27, bf16[2560,896]{1,0:T(8,128)(2,1)} %param.26, f32[8,896]{1,0:T(8,128)S(1)} %fusion.59, f32[8,2560]{1,0:T(8,128)S(1)} %get-tuple-element.8, f32[2560]{0:T(1024)S(1)} %convert_element_type.79, f32[8]{0:T(128)S(1)} %add_rsqrt_fusion), kind=kOutput, calls=%fused_computation.18 | convolution fusion | flops 73504768 | bytes 9377824 | tf_op jit(solution)/shard_map/dot_general | solution.py:160
  53.9 4.2 %collective-permute-done.2 = f32[8,2560]{1,0:T(8,128)S(1)} collective-permute-done((f32[8,2560]{1,0:T(8,128)S(1)}, f32[8,2560]{1,0:T(8,128)S(1)}, u32[]{:S(2)}, u32[]{:S(2)}) %collective-permute-start.2) | collective-permute-done | bytes 81952 | tf_op jit(solution)/shard_map/ppermute | solution.py:38
  58.1 0.6 add.223
  58.8 0.6 gather_fusion
  59.5 5.3 %collective-permute-done.3 = f32[8,2560]{1,0:T(8,128)S(1)} collective-permute-done((f32[8,2560]{1,0:T(8,128)}, f32[8,2560]{1,0:T(8,128)S(1)}, u32[]{:S(2)}, u32[]{:S(2)}) %collective-permute-start.3) | collective-permute-done | bytes 81952 | tf_op jit(solution)/shard_map/ppermute | solution.py:38
  64.8 0.9 %fusion.33 = f32[8,2560]{1,0:T(8,128)S(1)} fusion(f32[8,2560]{1,0:T(8,128)S(1)} %get-tuple-element.8, f32[8,2560]{1,0:T(8,128)} %add.223, f32[8,2560]{1,0:T(8,128)S(1)} %collective-permute-done.3), kind=kLoop, calls=%fused_computation.37 | loop fusion | flops 81920 | bytes 327680 | tf_op jit(solution)/shard_map/convert_element_type | solution.py:174
  65.7 1.1 %select_reduce_fusion = bf16[8,2,2560]{2,1,0:T(2,128)(2,1)} fusion(f32[8,2560]{1,0:T(8,128)S(1)} %fusion.33, pred[8,2,8]{2,1,0:T(4,128)(4,1)S(1)} %iota_compare_fusion.1), kind=kLoop, calls=%fused_computation.10 | loop fusion | flops 614400 | bytes 163968 | tf_op jit(solution)/shard_map/reduce_sum | solution.py:173
  66.8 3.4 %all-to-all-start.1 = ((bf16[8,2,2560]{2,1,0:T(2,128)(2,1)}), bf16[8,2,2560]{2,1,0:T(2,128)(2,1)S(1)}, u32[]{:S(2)}, u32[]{:S(2)}) async-start(bf16[8,2,2560]{2,1,0:T(2,128)(2,1)} %select_reduce_fusion), calls=%async_computation.1 | async-start | bytes 163840 | tf_op jit(solution)/shard_map/all_to_all | solution.py:176
  70.2 5.0 %all-to-all-done.1 = bf16[8,2,2560]{2,1,0:T(2,128)(2,1)S(1)} async-done(((bf16[8,2,2560]{2,1,0:T(2,128)(2,1)}), bf16[8,2,2560]{2,1,0:T(2,128)(2,1)S(1)}, u32[]{:S(2)}, u32[]{:S(2)}) %all-to-all-start.1) | async-done | bytes 81952 | tf_op jit(solution)/shard_map/all_to_all | solution.py:176
  75.2 0.8 select_reduce_fusion.1
  (48 shorter events, 3.0 us)
Async XLA Ops:
  0.0 31.1 %copy-start = (bf16[640,2560]{1,0:T(8,128)(2,1)S(1)}, bf16[640,2560]{1,0:T(8,128)(2,1)}, u32[]{:S(2)}) copy-start(bf16[640,2560]{1,0:T(8,128)(2,1)} %param.23) | copy-start | bytes 9830404
  1.8 18.4 %all-to-all-start = ((bf16[32,2,2560]{2,1,0:T(2,128)(2,1)}), bf16[32,2,2560]{2,1,0:T(2,128)(2,1)}, u32[]{:S(2)}, u32[]{:S(2)}) async-start(bf16[32,2,2560]{2,1,0:T(2,128)(2,1)} %broadcast_in_dim.102), calls=%async_computation | async-start | bytes 655360 | tf_op jit(solution)/shard_map/all_to_all | solution.py:75
  13.1 3.2 %copy-start.1 = (bf16[32,2,80,128]{3,2,1,0:T(8,128)(2,1)S(1)}, bf16[32,2,80,128]{3,2,1,0:T(8,128)(2,1)}, u32[]{:S(2)}) copy-start(bf16[32,2,80,128]{3,2,1,0:T(8,128)(2,1)} %param.20) | copy-start | bytes 3932164
  26.1 2.6 %copy-start.2 = (bf16[2560,160]{0,1:T(8,128)(2,1)S(1)}, bf16[2560,160]{0,1:T(8,128)(2,1)}, u32[]{:S(2)}) copy-start(bf16[2560,160]{0,1:T(8,128)(2,1)} %param.18) | copy-start | bytes 2457604
  31.1 7.8 %copy-start.3 = (bf16[2560]{0:T(1024)(128)(2,1)S(1)}, bf16[2560]{0:T(1024)(128)(2,1)}, u32[]{:S(2)}) copy-start(bf16[2560]{0:T(1024)(128)(2,1)} %param.24) | copy-start | bytes 15364
  31.7 5.3 %collective-permute-start = (f32[8,2560]{1,0:T(8,128)S(1)}, f32[8,2560]{1,0:T(8,128)}, u32[]{:S(2)}, u32[]{:S(2)}) collective-permute-start(f32[8,2560]{1,0:T(8,128)S(1)} %fusion.66), channel_id=1, source_target_pairs={{0,1},{1,0},{2,3},{3,2},{4,5},{5,4},{6,7},{7,6},{8,9},{9,8},{10,11... | collective-permute-start | bytes 245768 | tf_op jit(solution)/shard_map/ppermute | solution.py:38
  37.9 6.4 %collective-permute-start.1 = (f32[8,2560]{1,0:T(8,128)S(1)}, f32[8,2560]{1,0:T(8,128)}, u32[]{:S(2)}, u32[]{:S(2)}) collective-permute-start(f32[8,2560]{1,0:T(8,128)S(1)} %add.218), channel_id=1, source_target_pairs={{0,2},{1,3},{2,0},{3,1},{4,6},{5,7},{6,4},{7,5},{8,10},{9,11},{10,... | collective-permute-start | bytes 245768 | tf_op jit(solution)/shard_map/ppermute | solution.py:38
  53.6 4.5 %collective-permute-start.2 = (f32[8,2560]{1,0:T(8,128)S(1)}, f32[8,2560]{1,0:T(8,128)S(1)}, u32[]{:S(2)}, u32[]{:S(2)}) collective-permute-start(f32[8,2560]{1,0:T(8,128)S(1)} %fusion.24), channel_id=1, source_target_pairs={{0,1},{1,0},{2,3},{3,2},{4,5},{5,4},{6,7},{7,6},{8,9},{9,8},{10,11... | collective-permute-start | bytes 245768 | tf_op jit(solution)/shard_map/ppermute | solution.py:38
  58.7 6.1 %collective-permute-start.3 = (f32[8,2560]{1,0:T(8,128)}, f32[8,2560]{1,0:T(8,128)S(1)}, u32[]{:S(2)}, u32[]{:S(2)}) collective-permute-start(f32[8,2560]{1,0:T(8,128)} %add.223), channel_id=1, source_target_pairs={{0,2},{1,3},{2,0},{3,1},{4,6},{5,7},{6,4},{7,5},{8,10},{9,11},{10,... | collective-permute-start | bytes 245768 | tf_op jit(solution)/shard_map/ppermute | solution.py:38
  66.8 8.4 %all-to-all-start.1 = ((bf16[8,2,2560]{2,1,0:T(2,128)(2,1)}), bf16[8,2,2560]{2,1,0:T(2,128)(2,1)S(1)}, u32[]{:S(2)}, u32[]{:S(2)}) async-start(bf16[8,2,2560]{2,1,0:T(2,128)(2,1)} %select_reduce_fusion), calls=%async_computation.1 | async-start | bytes 163840 | tf_op jit(solution)/shard_map/all_to_all | solution.py:176

commit v9 on v7

--- a/solution.py
+++ b/solution.py
@@ -32,10 +32,14 @@
 
 
 def tensor_allreduce(part, tp_count):
+    def shifted(value, k):
+        return lax.ppermute(value, "tensor", [(i, (i + k) % tp_count) for i in range(tp_count)])
+
+    if tp_count == 4:
+        return (part + shifted(part, 2)) + (shifted(part, 1) + shifted(part, 3))
     step = 1
     while step < tp_count:
-        pairs = [(i, i ^ step) for i in range(tp_count)]
-        part = part + lax.ppermute(part, "tensor", pairs)
+        part = part + lax.ppermute(part, "tensor", [(i, i ^ step) for i in range(tp_count)])
         step *= 2
     return part
 

time: 74.1 us -> 71.9 us (0.970)
  waiting for transfers between devices: 25.1 us -> 13.1 us
  starting transfers between devices: 13.9 us -> 22.4 us
  other arithmetic: 6.24 us -> 7.02 us
    ppermute x4 -> x6, waiting for transfers between devices: 18.1 us -> 6.84 us  [shifted(): lax.ppermute(value, 'tensor', [(i, (i + k) % tp_count) for i in range(tp_...]
    ppermute x4 -> x6, starting transfers between devices: 3.1 us -> 11.5 us  [shifted(): lax.ppermute(value, 'tensor', [(i, (i + k) % tp_count) for i in range(tp_...]
    reduce_sum x2, other arithmetic: 0.28 us -> 1.24 us  [norm_rows(): jnp.mean(value_rows * value_rows, axis=-1, keepdims=True) + 1e-05]
    add x2 -> x0, other arithmetic: 0.91 us -> none  [tensor_allreduce(): part = part + lax.ppermute(part, 'tensor', pairs)]
    all_to_all x1, waiting for transfers between devices: 1.96 us -> 1.15 us  [local(): lax.all_to_all(jnp.broadcast_to(residual_in[None], (dev_count,) + residua...]
  transfers between devices with their start and end apart: 6 -> 8, of which waited for: 6 -> 6; matrix products, arithmetic and copies ran while one was open for 13% -> 15% of each run, Pallas kernels for 0% -> 0%
where the time goes in v9:
time: 71.9 us; the launch traced here: 71.2 us
  starting transfers between devices  22.4 us (31%)
  matrix products  22.1 us (31%)
  waiting for transfers between devices  13.1 us (18%)
  other arithmetic  7.02 us (10%)
  local copies, waits for them, and re-layouts  6.51 us (9%)
    ppermute x6, starting transfers between devices, shifted(): lax.ppermute(value, 'tensor', [(i, (i + k) % tp_count) for i in range(tp_...  11.5 us
    all_to_all x1, starting transfers between devices, local(): lax.all_to_all(jnp.broadcast_to(residual_in[None], (dev_count,) + residua...  7.41 us
    ppermute x6, waiting for transfers between devices, shifted(): lax.ppermute(value, 'tensor', [(i, (i + k) % tp_count) for i in range(tp_...  6.84 us
    dot_general x1, matrix products, local(): jnp.dot(hidden, w_down, preferred_element_type=jnp.float32)  5.29 us
    all_to_all x1, waiting for transfers between devices, local(): incoming = lax.all_to_all(outgoing, 'dp', 0, 0)  5.1 us
    all_to_all x1, starting transfers between devices, local(): incoming = lax.all_to_all(outgoing, 'dp', 0, 0)  3.43 us
    dot_general x1, matrix products, local(): jnp.einsum('sq,qhdc->shdc', page_hot, key_page_pool, preferred_element_ty...  3.15 us
    dot_general x1, matrix products, local(): gate_act = jnp.dot(normed_mlp, w_gate, preferred_element_type=jnp.float32)  3.05 us
  transfers between devices with their start and end apart: 8, of which 6 were waited for; matrix products, arithmetic and copies ran while one was open for 15% of the time, Pallas kernels for 0%

profile of v9, /device:TPU:0, one launch (start us, length us, event | category | flops | bytes accessed | tf_op | source)
XLA Modules:
  0.0 71.2 jit_solution(11546214236739938402)
XLA Ops:
  0.0 1.8 %broadcast_in_dim.79 = bf16[32,2,2560]{2,1,0:T(2,128)(2,1)} broadcast(bf16[2,2560]{1,0:T(2,128)(2,1)} %param.14), dimensions={1,2} | broadcast | bytes 337920 | tf_op jit(solution)/shard_map/broadcast_in_dim | solution.py:80
  1.8 7.4 %all-to-all-start = ((bf16[32,2,2560]{2,1,0:T(2,128)(2,1)}), bf16[32,2,2560]{2,1,0:T(2,128)(2,1)}, u32[]{:S(2)}, u32[]{:S(2)}) async-start(bf16[32,2,2560]{2,1,0:T(2,128)(2,1)} %broadcast_in_dim.79), calls=%async_computation | async-start | bytes 655360 | tf_op jit(solution)/shard_map/all_to_all | solution.py:79
  9.2 0.7 iota_add_fusion.2
  10.1 0.8 %select_reduce_fusion.4 = (s32[8]{0:T(128)S(1)}, s32[8]{0:T(128)S(1)}) fusion(s32[64]{0:T(128)} %param.21, s32[64]{0:T(128)S(1)} %get-tuple-element.13, pred[64]{0:T(512)(128)(4,1)S(1)} %get-tuple-element.11), kind=kLoop, calls=%fused_computation.69 | loop fusion | flops 3056 | bytes 640 | tf_op jit(solution)/shard_map/reduce_sum | solution.py:95
  11.6 0.8 %select_reduce_fusion.2 = s32[8,4]{0,1:T(4,128)S(1)} fusion(s32[64,4]{0,1:T(4,128)} %param.22, pred[8,64]{1,0:T(8,128)(4,1)S(1)} %fusion.47), kind=kLoop, calls=%fused_computation.48 | loop fusion | flops 4064 | bytes 1664 | tf_op jit(solution)/shard_map/reduce_sum | solution.py:96
  12.5 0.7 convert_element_type.65
  13.4 0.7 convert_element_type.73
  14.1 3.1 %fusion.6 = bf16[32,2,80,128]{3,0,2,1:T(8,128)(2,1)} fusion(bf16[32,2,80,128]{3,2,1,0:T(8,128)(2,1)} %param.19, s32[32]{0:T(128)S(1)} %sub.54), kind=kOutput, calls=%fused_computation.9 | convolution fusion | flops 41944064 | bytes 2621568 | tf_op jit(solution)/shard_map/sq,qhdc->shdc/dot_general | solution.py:126
  17.3 1.7 %fusion.2 = bf16[32,2,80,128]{3,0,2,1:T(8,128)(2,1)} fusion(bf16[32,2,80,128]{3,2,1,0:T(8,128)(2,1)S(1)} %copy-done.1, s32[32]{0:T(128)S(1)} %sub.54), kind=kOutput, calls=%fused_computation.5 | convolution fusion | flops 41944064 | bytes 2621568 | tf_op jit(solution)/shard_map/sq,qhdc->shdc/dot_general | solution.py:129
  19.0 1.2 %all-to-all-done = bf16[32,2,2560]{2,1,0:T(2,128)(2,1)} async-done(((bf16[32,2,2560]{2,1,0:T(2,128)(2,1)}), bf16[32,2,2560]{2,1,0:T(2,128)(2,1)}, u32[]{:S(2)}, u32[]{:S(2)}) %all-to-all-start) | async-done | bytes 327712 | tf_op jit(solution)/shard_map/all_to_all | solution.py:79
  20.2 1.6 %gather_fusion.1 = bf16[8,2560]{1,0:T(8,128)(2,1)S(1)} fusion(bf16[32,2,2560]{2,1,0:T(2,128)(2,1)} %all-to-all-done, s32[8]{0:T(128)S(1)} %fusion.55), kind=kCustom, calls=%fused_computation.1 | custom fusion | bytes 81984 | tf_op jit(solution)/shard_map/gather | solution.py:98
  21.9 1.5 %fusion.60 = f32[8,160]{1,0:T(8,128)S(1)} fusion(bf16[2560,160]{0,1:T(8,128)(2,1)} %param.17, bf16[8,2560]{1,0:T(8,128)(2,1)S(1)} %gather_fusion.1, f32[2560]{0:T(1024)S(1)} %convert_element_type.65, f32[8]{0:T(128)S(1)} %add_rsqrt_fusion.1), kind=kOutput, calls=%fused_computation.112 | convolution fusion | flops 6635520 | bytes 875552 | tf_op jit(solution)/shard_map/dot_general | solution.py:111
  23.5 2.5 %fusion.62 = f32[8,640]{1,0:T(8,128)S(1)} fusion(bf16[2560,640]{1,0:T(8,128)(2,1)} %param.16, bf16[8,2560]{1,0:T(8,128)(2,1)S(1)} %gather_fusion.1, f32[2560]{0:T(1024)S(1)} %convert_element_type.65, f32[8]{0:T(128)S(1)} %add_rsqrt_fusion.1), kind=kOutput, calls=%fused_computation.113 | convolution fusion | flops 26296320 | bytes 3348512 | tf_op jit(solution)/shard_map/dot_general | solution.py:102
  26.5 1.9 %select_reduce_fusion.1 = (f32[8,2,4]{2,1,0:T(2,128)S(1)}, f32[8,2,4,4,128]{4,2,3,1,0:T(4,128)S(1)}) fusion(pred[8,4,128]{2,1,0:T(4,128)(4,1)S(1)} %broadcast_compare_fusion, bf16[8,4,2,80,128]{4,1,0,3,2:T(4,128)(2,1)} %bitcast.60, bf16[8,2,4,40]{3,2,1,0:T(4,128)(2,1)S(1)} %bitcast.66, bf16[8,2,4,40]{3,2,1,0:T(4,128)(2,1)S(1)} %bitcast.64), kind=kOutput, calls=%fused_computation.23 | convolution fusion | flops 5361600 | bytes 1456384 | tf_op jit(solution)/shard_map/rhgd,rphdc->rhgpc/dot_general | solution.py:133
  29.1 1.9 %fusion.20 = bf16[8,2,4,80]{3,2,1,0:T(4,128)(2,1)S(1)} fusion(bf16[8,4,2,80,128]{4,1,0,3,2:T(4,128)(2,1)} %bitcast.59, f32[8,2,4,4,128]{4,2,3,1,0:T(4,128)S(1)} %get-tuple-element.21, f32[8,2,4]{2,1,0:T(2,128)S(1)} %multiply_maximum_fusion, pred[8,4,128]{2,1,0:T(4,128)(4,1)S(1)} %broadcast_compare_fusion, f32[8,2,4]{2,1,0:T(2,128)S(1)} %get-tuple-element.9, ...), kind=kOutput, calls=%fused_computation.16 | convolution fusion | flops 5328896 | bytes 1462016 | tf_op jit(solution)/shard_map/rhgpc,rphdc->rhgd/dot_general | solution.py:149
  31.1 0.5 fusion.65
  31.7 1.5 %collective-permute-start = (f32[8,2560]{1,0:T(8,128)S(1)}, f32[8,2560]{1,0:T(8,128)S(1)}, u32[]{:S(2)}, u32[]{:S(2)}) collective-permute-start(f32[8,2560]{1,0:T(8,128)S(1)} %fusion.65), channel_id=1, source_target_pairs={{0,2},{1,3},{2,0},{3,1},{4,6},{5,7},{6,4},{7,5},{8,10},{9,11},{10,... | collective-permute-start | bytes 245768 | tf_op jit(solution)/shard_map/ppermute | solution.py:36
  33.1 1.5 %collective-permute-start.1 = (f32[8,2560]{1,0:T(8,128)S(1)}, f32[8,2560]{1,0:T(8,128)}, u32[]{:S(2)}, u32[]{:S(2)}) collective-permute-start(f32[8,2560]{1,0:T(8,128)S(1)} %fusion.65), channel_id=1, source_target_pairs={{0,1},{1,2},{2,3},{3,0},{4,5},{5,6},{6,7},{7,4},{8,9},{9,10},{10,1... | collective-permute-start | bytes 245768 | tf_op jit(solution)/shard_map/ppermute | solution.py:36
  34.7 2.3 %collective-permute-start.2 = (f32[8,2560]{1,0:T(8,128)S(1)}, f32[8,2560]{1,0:T(8,128)}, u32[]{:S(2)}, u32[]{:S(2)}) collective-permute-start(f32[8,2560]{1,0:T(8,128)S(1)} %fusion.65), channel_id=1, source_target_pairs={{0,3},{1,0},{2,1},{3,2},{4,7},{5,4},{6,5},{7,6},{8,11},{9,8},{10,9... | collective-permute-start | bytes 245768 | tf_op jit(solution)/shard_map/ppermute | solution.py:36
  37.0 0.6 gather_fusion
  37.6 3.0 %collective-permute-done = f32[8,2560]{1,0:T(8,128)S(1)} collective-permute-done((f32[8,2560]{1,0:T(8,128)S(1)}, f32[8,2560]{1,0:T(8,128)S(1)}, u32[]{:S(2)}, u32[]{:S(2)}) %collective-permute-start) | collective-permute-done | bytes 81952 | tf_op jit(solution)/shard_map/ppermute | solution.py:36
  41.6 1.1 %multiply_reduce_fusion = (f32[8]{0:T(128)S(1)}, f32[8,2560]{1,0:T(8,128)S(1)}) fusion(f32[8,2560]{1,0:T(8,128)} %collective-permute-done.1, f32[8,2560]{1,0:T(8,128)} %collective-permute-done.2, f32[8,2560]{1,0:T(8,128)S(1)} %fusion.65, f32[8,2560]{1,0:T(8,128)} %copy-done.3, bf16[8,2560]{1,0:T(8,128)(2,1)S(1)} %gather_fusion.1), kind=kLoop, calls=%fused_computation.33 | loop fusion | flops 143352 | bytes 450592 | tf_op jit(solution)/shard_map/reduce_sum | solution.py:13
  42.7 3.0 %fusion.58 = f32[8,896]{1,0:T(8,128)S(1)} fusion(bf16[2560,896]{1,0:T(8,128)(2,1)} %param.25, f32[8,2560]{1,0:T(8,128)S(1)} %get-tuple-element.8, f32[2560]{0:T(1024)S(1)} %convert_element_type.73, f32[8]{0:T(128)S(1)} %add_rsqrt_fusion), kind=kOutput, calls=%fused_computation.111 | convolution fusion | flops 36761600 | bytes 4708384 | tf_op jit(solution)/shard_map/dot_general | solution.py:160
  45.7 5.3 %fusion.24 = f32[8,2560]{1,0:T(8,128)S(1)} fusion(bf16[896,2560]{1,0:T(8,128)(2,1)} %param.27, bf16[2560,896]{1,0:T(8,128)(2,1)} %param.26, f32[8,896]{1,0:T(8,128)S(1)} %fusion.58, f32[8,2560]{1,0:T(8,128)S(1)} %get-tuple-element.8, f32[2560]{0:T(1024)S(1)} %convert_element_type.73, f32[8]{0:T(128)S(1)} %add_rsqrt_fusion), kind=kOutput, calls=%fused_computation.18 | convolution fusion | flops 73504768 | bytes 9377824 | tf_op jit(solution)/shard_map/dot_general | solution.py:164
  51.0 2.4 %collective-permute-start.3 = (f32[8,2560]{1,0:T(8,128)S(1)}, f32[8,2560]{1,0:T(8,128)S(1)}, u32[]{:S(2)}, u32[]{:S(2)}) collective-permute-start(f32[8,2560]{1,0:T(8,128)S(1)} %fusion.24), channel_id=1, source_target_pairs={{0,2},{1,3},{2,0},{3,1},{4,6},{5,7},{6,4},{7,5},{8,10},{9,11},{10,... | collective-permute-start | bytes 245768 | tf_op jit(solution)/shard_map/ppermute | solution.py:36
  53.5 3.7 %collective-permute-start.5 = (f32[8,2560]{1,0:T(8,128)S(1)}, f32[8,2560]{1,0:T(8,128)S(1)}, u32[]{:S(2)}, u32[]{:S(2)}) collective-permute-start(f32[8,2560]{1,0:T(8,128)S(1)} %fusion.24), channel_id=1, source_target_pairs={{0,3},{1,0},{2,1},{3,2},{4,7},{5,4},{6,5},{7,6},{8,11},{9,8},{10,9... | collective-permute-start | bytes 245768 | tf_op jit(solution)/shard_map/ppermute | solution.py:36
  57.3 3.4 %collective-permute-done.3 = f32[8,2560]{1,0:T(8,128)S(1)} collective-permute-done((f32[8,2560]{1,0:T(8,128)S(1)}, f32[8,2560]{1,0:T(8,128)S(1)}, u32[]{:S(2)}, u32[]{:S(2)}) %collective-permute-start.3) | collective-permute-done | bytes 81952 | tf_op jit(solution)/shard_map/ppermute | solution.py:36
  60.7 0.6 gather_fusion.2
  61.3 0.7 reshape.417
  61.9 3.4 %all-to-all-start.1 = ((bf16[8,2,2560]{2,1,0:T(2,128)(2,1)}), bf16[8,2,2560]{2,1,0:T(2,128)(2,1)S(1)}, u32[]{:S(2)}, u32[]{:S(2)}) async-start(bf16[8,2,2560]{2,1,0:T(2,128)(2,1)} %reshape.417), calls=%async_computation.1 | async-start | bytes 163840 | tf_op jit(solution)/shard_map/all_to_all | solution.py:177
  65.4 5.1 %all-to-all-done.1 = bf16[8,2,2560]{2,1,0:T(2,128)(2,1)S(1)} async-done(((bf16[8,2,2560]{2,1,0:T(2,128)(2,1)}), bf16[8,2,2560]{2,1,0:T(2,128)(2,1)S(1)}, u32[]{:S(2)}, u32[]{:S(2)}) %all-to-all-start.1) | async-done | bytes 81952 | tf_op jit(solution)/shard_map/all_to_all | solution.py:177
  70.5 0.8 %select_reduce_fusion = bf16[2,2560]{1,0:T(2,128)(2,1)} fusion(bf16[8,2,2560]{2,1,0:T(2,128)(2,1)S(1)} %all-to-all-done.1, pred[8,2]{1,0:T(8,128)(4,1)S(1)} %iota_compare_fusion.3), kind=kLoop, calls=%fused_computation.21 | loop fusion | flops 117760 | bytes 92176 | tf_op jit(solution)/shard_map/reduce_sum | solution.py:181
  (53 shorter events, 3.8 us)
Async XLA Ops:
  0.0 31.1 %copy-start = (bf16[640,2560]{1,0:T(8,128)(2,1)S(1)}, bf16[640,2560]{1,0:T(8,128)(2,1)}, u32[]{:S(2)}) copy-start(bf16[640,2560]{1,0:T(8,128)(2,1)} %param.23) | copy-start | bytes 9830404
  1.8 18.4 %all-to-all-start = ((bf16[32,2,2560]{2,1,0:T(2,128)(2,1)}), bf16[32,2,2560]{2,1,0:T(2,128)(2,1)}, u32[]{:S(2)}, u32[]{:S(2)}) async-start(bf16[32,2,2560]{2,1,0:T(2,128)(2,1)} %broadcast_in_dim.79), calls=%async_computation | async-start | bytes 655360 | tf_op jit(solution)/shard_map/all_to_all | solution.py:79
  14.1 3.2 %copy-start.1 = (bf16[32,2,80,128]{3,2,1,0:T(8,128)(2,1)S(1)}, bf16[32,2,80,128]{3,2,1,0:T(8,128)(2,1)}, u32[]{:S(2)}) copy-start(bf16[32,2,80,128]{3,2,1,0:T(8,128)(2,1)} %param.20) | copy-start | bytes 3932164
  26.1 2.6 %copy-start.2 = (bf16[2560,160]{0,1:T(8,128)(2,1)S(1)}, bf16[2560,160]{0,1:T(8,128)(2,1)}, u32[]{:S(2)}) copy-start(bf16[2560,160]{0,1:T(8,128)(2,1)} %param.18) | copy-start | bytes 2457604
  31.7 8.9 %collective-permute-start = (f32[8,2560]{1,0:T(8,128)S(1)}, f32[8,2560]{1,0:T(8,128)S(1)}, u32[]{:S(2)}, u32[]{:S(2)}) collective-permute-start(f32[8,2560]{1,0:T(8,128)S(1)} %fusion.65), channel_id=1, source_target_pairs={{0,2},{1,3},{2,0},{3,1},{4,6},{5,7},{6,4},{7,5},{8,10},{9,11},{10,... | collective-permute-start | bytes 245768 | tf_op jit(solution)/shard_map/ppermute | solution.py:36
  33.1 7.6 %collective-permute-start.1 = (f32[8,2560]{1,0:T(8,128)S(1)}, f32[8,2560]{1,0:T(8,128)}, u32[]{:S(2)}, u32[]{:S(2)}) collective-permute-start(f32[8,2560]{1,0:T(8,128)S(1)} %fusion.65), channel_id=1, source_target_pairs={{0,1},{1,2},{2,3},{3,0},{4,5},{5,6},{6,7},{7,4},{8,9},{9,10},{10,1... | collective-permute-start | bytes 245768 | tf_op jit(solution)/shard_map/ppermute | solution.py:36
  34.7 6.9 %collective-permute-start.2 = (f32[8,2560]{1,0:T(8,128)S(1)}, f32[8,2560]{1,0:T(8,128)}, u32[]{:S(2)}, u32[]{:S(2)}) collective-permute-start(f32[8,2560]{1,0:T(8,128)S(1)} %fusion.65), channel_id=1, source_target_pairs={{0,3},{1,0},{2,1},{3,2},{4,7},{5,4},{6,5},{7,6},{8,11},{9,8},{10,9... | collective-permute-start | bytes 245768 | tf_op jit(solution)/shard_map/ppermute | solution.py:36
  40.6 0.6 copy-start.3
  51.0 9.6 %collective-permute-start.3 = (f32[8,2560]{1,0:T(8,128)S(1)}, f32[8,2560]{1,0:T(8,128)S(1)}, u32[]{:S(2)}, u32[]{:S(2)}) collective-permute-start(f32[8,2560]{1,0:T(8,128)S(1)} %fusion.24), channel_id=1, source_target_pairs={{0,2},{1,3},{2,0},{3,1},{4,6},{5,7},{6,4},{7,5},{8,10},{9,11},{10,... | collective-permute-start | bytes 245768 | tf_op jit(solution)/shard_map/ppermute | solution.py:36
  53.4 7.2 %collective-permute-start.4 = (f32[8,2560]{1,0:T(8,128)S(1)}, f32[8,2560]{1,0:T(8,128)S(1)}, u32[]{:S(2)}, u32[]{:S(2)}) collective-permute-start(f32[8,2560]{1,0:T(8,128)S(1)} %fusion.24), channel_id=1, source_target_pairs={{0,1},{1,2},{2,3},{3,0},{4,5},{5,6},{6,7},{7,4},{8,9},{9,10},{10,1... | collective-permute-start | bytes 245768 | tf_op jit(solution)/shard_map/ppermute | solution.py:36
  53.5 7.1 %collective-permute-start.5 = (f32[8,2560]{1,0:T(8,128)S(1)}, f32[8,2560]{1,0:T(8,128)S(1)}, u32[]{:S(2)}, u32[]{:S(2)}) collective-permute-start(f32[8,2560]{1,0:T(8,128)S(1)} %fusion.24), channel_id=1, source_target_pairs={{0,3},{1,0},{2,1},{3,2},{4,7},{5,4},{6,5},{7,6},{8,11},{9,8},{10,9... | collective-permute-start | bytes 245768 | tf_op jit(solution)/shard_map/ppermute | solution.py:36
  61.9 8.5 %all-to-all-start.1 = ((bf16[8,2,2560]{2,1,0:T(2,128)(2,1)}), bf16[8,2,2560]{2,1,0:T(2,128)(2,1)S(1)}, u32[]{:S(2)}, u32[]{:S(2)}) async-start(bf16[8,2,2560]{2,1,0:T(2,128)(2,1)} %reshape.417), calls=%async_computation.1 | async-start | bytes 163840 | tf_op jit(solution)/shard_map/all_to_all | solution.py:177

commit v10 on v9

--- a/solution.py
+++ b/solution.py
@@ -95,7 +95,16 @@
     served_len = jnp.sum(jnp.where(hits, lengths[None, :], 0), axis=1)
     served_pages = jnp.sum(jnp.where(hits[:, :, None], page_table[None, :, :], 0), axis=1)
 
-    rows_srv = rows_all[served // rows_loc, served % rows_loc]
+    width = residual_in.shape[1]
+    rows_srv = jnp.concatenate(
+        [
+            lax.dynamic_slice(
+                rows_all, (served[i] // rows_loc, served[i] % rows_loc, 0), (1, 1, width)
+            ).reshape(1, width)
+            for i in range(req_loc)
+        ],
+        axis=0,
+    )
     scaled_input = norm_rows(rows_srv, norm_gain).astype(jnp.bfloat16)
     query_srv = (
         apply_rotation(
@@ -173,7 +182,18 @@
     dest_round = jnp.sum(
         jnp.where(request_ids[None, :] == dest_rows[:, None], round_no[None, :], 0), axis=1
     )
-    outgoing = final[dest_round.reshape(dp_count, rows_loc)]
+    outgoing = jnp.stack(
+        [
+            jnp.concatenate(
+                [
+                    lax.dynamic_slice(final, (dest_round[d * rows_loc + j], 0), (1, width))
+                    for j in range(rows_loc)
+                ],
+                axis=0,
+            )
+            for d in range(dp_count)
+        ]
+    )
     incoming = lax.all_to_all(outgoing, "dp", 0, 0)
     mine = dp_index * req_loc + tp_index * rows_loc + jnp.arange(rows_loc, dtype=jnp.int32)
     from_src = jnp.arange(dp_count, dtype=jnp.int32)[:, None] == server[mine][None, :]

time: 71.9 us -> 126 us (1.75)
  between operations: 0.17 us -> 50.4 us
  other arithmetic: 7.02 us -> 10.6 us
  starting transfers between devices: 22.4 us -> 24.2 us
    unnamed x0 -> x7, other arithmetic: none -> 4.36 us
    gather x3 -> x0, local copies, waits for them, and re-layouts: 2.86 us -> none  [the longest x1 1.6 us: local(): rows_srv = rows_all[served // rows_loc, served % rows_loc]]
    ppermute x6, starting transfers between devices: 11.5 us -> 13.2 us  [shifted(): lax.ppermute(value, 'tensor', [(i, (i + k) % tp_count) for i in range(tp_...]
    slice x0 -> x2, local copies, waits for them, and re-layouts: none -> 1.4 us  [the longest x1 0.71 us: local(): dest_round[d * rows_loc + j]]
    convert_element_type x2, other arithmetic: 1.39 us -> 0.01 us  [norm_rows(): gain.astype(jnp.float32)]
    dot_general x1, matrix products: 1.9 us -> 0.57 us  [local(): jnp.einsum('rhgpc,rphdc->rhgd', weights, value_rows.astype(jnp.float32))]
  transfers between devices with their start and end apart: 8 -> 8, of which waited for: 6 -> 7; matrix products, arithmetic and copies ran while one was open for 15% -> 8% of each run, Pallas kernels for 0% -> 0%
where the time goes in v10:
time: 126 us; the launch traced here: 125 us
  between operations  50.4 us (40%)
  starting transfers between devices  24.2 us (19%)
  matrix products  21.9 us (17%)
  waiting for transfers between devices  12 us (10%)
  other arithmetic  10.6 us (8%)
  local copies, waits for them, and re-layouts  5.67 us (4%)
    ppermute x6, starting transfers between devices, shifted(): lax.ppermute(value, 'tensor', [(i, (i + k) % tp_count) for i in range(tp_...  13.2 us
    all_to_all x1, starting transfers between devices, local(): lax.all_to_all(jnp.broadcast_to(residual_in[None], (dev_count,) + residua...  7.42 us
    ppermute x6, waiting for transfers between devices, shifted(): lax.ppermute(value, 'tensor', [(i, (i + k) % tp_count) for i in range(tp_...  6.91 us
    dot_general x1, matrix products, local(): jnp.dot(hidden, w_down, preferred_element_type=jnp.float32)  5.29 us
    all_to_all x1, waiting for transfers between devices, local(): incoming = lax.all_to_all(outgoing, 'dp', 0, 0)  5.1 us
    unnamed x7, other arithmetic  4.36 us
    all_to_all x1, starting transfers between devices, local(): incoming = lax.all_to_all(outgoing, 'dp', 0, 0)  3.64 us
    dot_general x1, matrix products, local(): jnp.einsum('sq,qhdc->shdc', page_hot, key_page_pool, preferred_element_ty...  3.15 us
  transfers between devices with their start and end apart: 8, of which 7 were waited for; matrix products, arithmetic and copies ran while one was open for 8% of the time, Pallas kernels for 0%

profile of v10, /device:TPU:0, one launch (start us, length us, event | category | flops | bytes accessed | tf_op | source)
XLA Modules:
  0.0 124.8 jit_solution(15096566257424201610)
XLA Ops:
  0.0 1.8 %broadcast_in_dim.79 = bf16[32,2,2560]{2,1,0:T(2,128)(2,1)} broadcast(bf16[2,2560]{1,0:T(2,128)(2,1)} %param.14), dimensions={1,2} | broadcast | bytes 337920 | tf_op jit(solution)/shard_map/broadcast_in_dim | solution.py:80
  1.8 7.4 %all-to-all-start = ((bf16[32,2,2560]{2,1,0:T(2,128)(2,1)}), bf16[32,2,2560]{2,1,0:T(2,128)(2,1)}, u32[]{:S(2)}, u32[]{:S(2)}) async-start(bf16[32,2,2560]{2,1,0:T(2,128)(2,1)} %broadcast_in_dim.79), calls=%async_computation | async-start | bytes 655360 | tf_op jit(solution)/shard_map/all_to_all | solution.py:79
  9.2 0.7 iota_add_fusion.2
  10.1 0.8 select_reduce_fusion.4
  11.4 0.7 fusion.59
  12.2 0.8 select_reduce_fusion.2
  13.1 0.7 fusion.60
  64.2 3.1 %fusion.6 = bf16[32,2,80,128]{3,0,2,1:T(8,128)(2,1)} fusion(bf16[32,2,80,128]{3,2,1,0:T(8,128)(2,1)} %param.19, s32[32]{0:T(128)S(1)} %sub.82), kind=kOutput, calls=%fused_computation.7 | convolution fusion | flops 41944064 | bytes 2621568 | tf_op jit(solution)/shard_map/sq,qhdc->shdc/dot_general | solution.py:135
  67.3 1.7 %fusion.2 = bf16[32,2,80,128]{3,0,2,1:T(8,128)(2,1)} fusion(bf16[32,2,80,128]{3,2,1,0:T(8,128)(2,1)S(1)} %copy-done.1, s32[32]{0:T(128)S(1)} %sub.82), kind=kOutput, calls=%fused_computation.3 | convolution fusion | flops 41944064 | bytes 2621568 | tf_op jit(solution)/shard_map/sq,qhdc->shdc/dot_general | solution.py:138
  69.0 0.9 dynamic-slice_bitcast_fusion
  70.2 1.5 %fusion.25 = f32[8,160]{1,0:T(8,128)S(1)} fusion(bf16[2560,160]{0,1:T(8,128)(2,1)} %param.18, bf16[8,2560]{1,0:T(8,128)(2,1)S(1)} %concatenate.40, f32[2560]{0:T(1024)S(1)} %convert_element_type.65, f32[8]{0:T(128)S(1)} %add_rsqrt_fusion.1), kind=kOutput, calls=%fused_computation.18 | convolution fusion | flops 6638080 | bytes 875552 | tf_op jit(solution)/shard_map/dot_general | solution.py:126
  71.8 1.5 %fusion.54 = f32[8,160]{1,0:T(8,128)S(1)} fusion(bf16[2560,160]{0,1:T(8,128)(2,1)} %param.17, bf16[8,2560]{1,0:T(8,128)(2,1)S(1)} %concatenate.40, f32[2560]{0:T(1024)S(1)} %convert_element_type.65, f32[8]{0:T(128)S(1)} %add_rsqrt_fusion.1), kind=kOutput, calls=%fused_computation.134 | convolution fusion | flops 6635520 | bytes 875552 | tf_op jit(solution)/shard_map/dot_general | solution.py:120
  73.4 2.5 %fusion.56 = f32[8,640]{1,0:T(8,128)S(1)} fusion(bf16[2560,640]{1,0:T(8,128)(2,1)} %param.16, bf16[8,2560]{1,0:T(8,128)(2,1)S(1)} %concatenate.40, f32[2560]{0:T(1024)S(1)} %convert_element_type.65, f32[8]{0:T(128)S(1)} %add_rsqrt_fusion.1), kind=kOutput, calls=%fused_computation.135 | convolution fusion | flops 26296320 | bytes 3348512 | tf_op jit(solution)/shard_map/dot_general | solution.py:111
  76.4 1.9 %select_reduce_fusion.1 = (f32[8,2,4]{2,1,0:T(2,128)S(1)}, f32[8,2,4,4,128]{4,2,3,1,0:T(4,128)S(1)}) fusion(pred[8,4,128]{2,1,0:T(4,128)(4,1)S(1)} %broadcast_compare_fusion, bf16[8,4,2,80,128]{4,1,0,3,2:T(4,128)(2,1)} %bitcast.113, bf16[8,2,4,40]{3,2,1,0:T(4,128)(2,1)S(1)} %bitcast.119, bf16[8,2,4,40]{3,2,1,0:T(4,128)(2,1)S(1)} %bitcast.117), kind=kOutput, calls=%fused_computation.21 | convolution fusion | flops 5361600 | bytes 1456384 | tf_op jit(solution)/shard_map/rhgd,rphdc->rhgpc/dot_general | solution.py:142
  79.8 2.6 %collective-permute-start = (f32[8,2560]{1,0:T(8,128)S(1)}, f32[8,2560]{1,0:T(8,128)S(1)}, u32[]{:S(2)}, u32[]{:S(2)}) collective-permute-start(f32[8,2560]{1,0:T(8,128)S(1)} %fusion.61), channel_id=1, source_target_pairs={{0,2},{1,3},{2,0},{3,1},{4,6},{5,7},{6,4},{7,5},{8,10},{9,11},{10,... | collective-permute-start | bytes 245768 | tf_op jit(solution)/shard_map/ppermute | solution.py:36
  82.5 1.5 %collective-permute-start.1 = (f32[8,2560]{1,0:T(8,128)S(1)}, f32[8,2560]{1,0:T(8,128)S(1)}, u32[]{:S(2)}, u32[]{:S(2)}) collective-permute-start(f32[8,2560]{1,0:T(8,128)S(1)} %fusion.61), channel_id=1, source_target_pairs={{0,1},{1,2},{2,3},{3,0},{4,5},{5,6},{6,7},{7,4},{8,9},{9,10},{10,1... | collective-permute-start | bytes 245768 | tf_op jit(solution)/shard_map/ppermute | solution.py:36
  84.0 2.3 %collective-permute-start.2 = (f32[8,2560]{1,0:T(8,128)S(1)}, f32[8,2560]{1,0:T(8,128)S(1)}, u32[]{:S(2)}, u32[]{:S(2)}) collective-permute-start(f32[8,2560]{1,0:T(8,128)S(1)} %fusion.61), channel_id=1, source_target_pairs={{0,3},{1,0},{2,1},{3,2},{4,7},{5,4},{6,5},{7,6},{8,11},{9,8},{10,9... | collective-permute-start | bytes 245768 | tf_op jit(solution)/shard_map/ppermute | solution.py:36
  86.3 2.8 %collective-permute-done = f32[8,2560]{1,0:T(8,128)S(1)} collective-permute-done((f32[8,2560]{1,0:T(8,128)S(1)}, f32[8,2560]{1,0:T(8,128)S(1)}, u32[]{:S(2)}, u32[]{:S(2)}) %collective-permute-start) | collective-permute-done | bytes 81952 | tf_op jit(solution)/shard_map/ppermute | solution.py:36
  89.4 0.8 collective-permute-done.2
  90.4 3.0 %fusion.52 = f32[8,896]{1,0:T(8,128)S(1)} fusion(bf16[2560,896]{1,0:T(8,128)(2,1)} %param.25, f32[8,2560]{1,0:T(8,128)S(1)} %get-tuple-element.8, f32[2560]{0:T(1024)S(1)} %convert_element_type.73, f32[8]{0:T(128)S(1)} %add_rsqrt_fusion), kind=kOutput, calls=%fused_computation.133 | convolution fusion | flops 36761600 | bytes 4708384 | tf_op jit(solution)/shard_map/dot_general | solution.py:169
  93.4 5.3 %fusion.24 = f32[8,2560]{1,0:T(8,128)S(1)} fusion(bf16[896,2560]{1,0:T(8,128)(2,1)} %param.27, bf16[2560,896]{1,0:T(8,128)(2,1)} %param.26, f32[8,896]{1,0:T(8,128)S(1)} %fusion.52, f32[8,2560]{1,0:T(8,128)S(1)} %get-tuple-element.8, f32[2560]{0:T(1024)S(1)} %convert_element_type.73, f32[8]{0:T(128)S(1)} %add_rsqrt_fusion), kind=kOutput, calls=%fused_computation.16 | convolution fusion | flops 73504768 | bytes 9377824 | tf_op jit(solution)/shard_map/dot_general | solution.py:173
  98.7 2.9 %collective-permute-start.3 = (f32[8,2560]{1,0:T(8,128)S(1)}, f32[8,2560]{1,0:T(8,128)}, u32[]{:S(2)}, u32[]{:S(2)}) collective-permute-start(f32[8,2560]{1,0:T(8,128)S(1)} %fusion.24), channel_id=1, source_target_pairs={{0,2},{1,3},{2,0},{3,1},{4,6},{5,7},{6,4},{7,5},{8,10},{9,11},{10,... | collective-permute-start | bytes 245768 | tf_op jit(solution)/shard_map/ppermute | solution.py:36
  101.6 3.8 %collective-permute-start.5 = (f32[8,2560]{1,0:T(8,128)S(1)}, f32[8,2560]{1,0:T(8,128)}, u32[]{:S(2)}, u32[]{:S(2)}) collective-permute-start(f32[8,2560]{1,0:T(8,128)S(1)} %fusion.24), channel_id=1, source_target_pairs={{0,3},{1,0},{2,1},{3,2},{4,7},{5,4},{6,5},{7,6},{8,11},{9,8},{10,9... | collective-permute-start | bytes 245768 | tf_op jit(solution)/shard_map/ppermute | solution.py:36
  105.4 0.6 gather_fusion
  106.1 1.4 %collective-permute-done.3 = f32[8,2560]{1,0:T(8,128)} collective-permute-done((f32[8,2560]{1,0:T(8,128)S(1)}, f32[8,2560]{1,0:T(8,128)}, u32[]{:S(2)}, u32[]{:S(2)}) %collective-permute-start.3) | collective-permute-done | bytes 81952 | tf_op jit(solution)/shard_map/ppermute | solution.py:36
  107.5 1.1 collective-permute-done.4
  109.1 1.0 add_convert_fusion
  111.6 0.6 constant_dynamic-update-slice_fusion.5
  114.0 0.6 constant_dynamic-update-slice_fusion.1
  115.3 3.6 %all-to-all-start.1 = ((bf16[8,2,2560]{2,1,0:T(2,128)(2,1)}), bf16[8,2,2560]{2,1,0:T(2,128)(2,1)S(1)}, u32[]{:S(2)}, u32[]{:S(2)}) async-start(bf16[8,2,2560]{2,1,0:T(2,128)(2,1)} %constant_dynamic-update-slice_fusion), calls=%async_computation.1 | async-start | bytes 163840 | tf_op jit(solution)/shard_map/all_to_all | solution.py:197
  118.9 5.1 %all-to-all-done.1 = bf16[8,2,2560]{2,1,0:T(2,128)(2,1)S(1)} async-done(((bf16[8,2,2560]{2,1,0:T(2,128)(2,1)}), bf16[8,2,2560]{2,1,0:T(2,128)(2,1)S(1)}, u32[]{:S(2)}, u32[]{:S(2)}) %all-to-all-start.1) | async-done | bytes 81952 | tf_op jit(solution)/shard_map/all_to_all | solution.py:197
  124.0 0.8 select_reduce_fusion
  (60 shorter events, 8.4 us)
Async XLA Ops:
  0.0 79.3 %copy-start = (bf16[640,2560]{1,0:T(8,128)(2,1)S(1)}, bf16[640,2560]{1,0:T(8,128)(2,1)}, u32[]{:S(2)}) copy-start(bf16[640,2560]{1,0:T(8,128)(2,1)} %param.23) | copy-start | bytes 9830404
  0.0 53.9 %copy-start.3 = (bf16[2560]{0:T(1024)(128)(2,1)S(1)}, bf16[2560]{0:T(1024)(128)(2,1)}, u32[]{:S(2)}) copy-start(bf16[2560]{0:T(1024)(128)(2,1)} %param.15) | copy-start | bytes 15364
  0.0 54.1 %copy-start.4 = (bf16[2560]{0:T(1024)(128)(2,1)S(1)}, bf16[2560]{0:T(1024)(128)(2,1)}, u32[]{:S(2)}) copy-start(bf16[2560]{0:T(1024)(128)(2,1)} %param.24) | copy-start | bytes 15364
  1.8 67.3 %all-to-all-start = ((bf16[32,2,2560]{2,1,0:T(2,128)(2,1)}), bf16[32,2,2560]{2,1,0:T(2,128)(2,1)}, u32[]{:S(2)}, u32[]{:S(2)}) async-start(bf16[32,2,2560]{2,1,0:T(2,128)(2,1)} %broadcast_in_dim.79), calls=%async_computation | async-start | bytes 655360 | tf_op jit(solution)/shard_map/all_to_all | solution.py:79
  64.1 3.2 %copy-start.1 = (bf16[32,2,80,128]{3,2,1,0:T(8,128)(2,1)S(1)}, bf16[32,2,80,128]{3,2,1,0:T(8,128)(2,1)}, u32[]{:S(2)}) copy-start(bf16[32,2,80,128]{3,2,1,0:T(8,128)(2,1)} %param.20) | copy-start | bytes 3932164
  76.0 2.6 %copy-start.2 = (bf16[32,2,80,128]{3,0,2,1:T(8,128)(2,1)S(1)}, bf16[32,2,80,128]{3,0,2,1:T(8,128)(2,1)}, u32[]{:S(2)}) copy-start(bf16[32,2,80,128]{3,0,2,1:T(8,128)(2,1)} %fusion.2) | copy-start | bytes 3932164
  79.8 9.3 %collective-permute-start = (f32[8,2560]{1,0:T(8,128)S(1)}, f32[8,2560]{1,0:T(8,128)S(1)}, u32[]{:S(2)}, u32[]{:S(2)}) collective-permute-start(f32[8,2560]{1,0:T(8,128)S(1)} %fusion.61), channel_id=1, source_target_pairs={{0,2},{1,3},{2,0},{3,1},{4,6},{5,7},{6,4},{7,5},{8,10},{9,11},{10,... | collective-permute-start | bytes 245768 | tf_op jit(solution)/shard_map/ppermute | solution.py:36
  82.5 6.9 %collective-permute-start.1 = (f32[8,2560]{1,0:T(8,128)S(1)}, f32[8,2560]{1,0:T(8,128)S(1)}, u32[]{:S(2)}, u32[]{:S(2)}) collective-permute-start(f32[8,2560]{1,0:T(8,128)S(1)} %fusion.61), channel_id=1, source_target_pairs={{0,1},{1,2},{2,3},{3,0},{4,5},{5,6},{6,7},{7,4},{8,9},{9,10},{10,1... | collective-permute-start | bytes 245768 | tf_op jit(solution)/shard_map/ppermute | solution.py:36
  84.0 6.2 %collective-permute-start.2 = (f32[8,2560]{1,0:T(8,128)S(1)}, f32[8,2560]{1,0:T(8,128)S(1)}, u32[]{:S(2)}, u32[]{:S(2)}) collective-permute-start(f32[8,2560]{1,0:T(8,128)S(1)} %fusion.61), channel_id=1, source_target_pairs={{0,3},{1,0},{2,1},{3,2},{4,7},{5,4},{6,5},{7,6},{8,11},{9,8},{10,9... | collective-permute-start | bytes 245768 | tf_op jit(solution)/shard_map/ppermute | solution.py:36
  98.7 8.8 %collective-permute-start.3 = (f32[8,2560]{1,0:T(8,128)S(1)}, f32[8,2560]{1,0:T(8,128)}, u32[]{:S(2)}, u32[]{:S(2)}) collective-permute-start(f32[8,2560]{1,0:T(8,128)S(1)} %fusion.24), channel_id=1, source_target_pairs={{0,2},{1,3},{2,0},{3,1},{4,6},{5,7},{6,4},{7,5},{8,10},{9,11},{10,... | collective-permute-start | bytes 245768 | tf_op jit(solution)/shard_map/ppermute | solution.py:36
  101.6 6.9 %collective-permute-start.4 = (f32[8,2560]{1,0:T(8,128)S(1)}, f32[8,2560]{1,0:T(8,128)}, u32[]{:S(2)}, u32[]{:S(2)}) collective-permute-start(f32[8,2560]{1,0:T(8,128)S(1)} %fusion.24), channel_id=1, source_target_pairs={{0,1},{1,2},{2,3},{3,0},{4,5},{5,6},{6,7},{7,4},{8,9},{9,10},{10,1... | collective-permute-start | bytes 245768 | tf_op jit(solution)/shard_map/ppermute | solution.py:36
  101.6 7.4 %collective-permute-start.5 = (f32[8,2560]{1,0:T(8,128)S(1)}, f32[8,2560]{1,0:T(8,128)}, u32[]{:S(2)}, u32[]{:S(2)}) collective-permute-start(f32[8,2560]{1,0:T(8,128)S(1)} %fusion.24), channel_id=1, source_target_pairs={{0,3},{1,0},{2,1},{3,2},{4,7},{5,4},{6,5},{7,6},{8,11},{9,8},{10,9... | collective-permute-start | bytes 245768 | tf_op jit(solution)/shard_map/ppermute | solution.py:36
  115.3 8.7 %all-to-all-start.1 = ((bf16[8,2,2560]{2,1,0:T(2,128)(2,1)}), bf16[8,2,2560]{2,1,0:T(2,128)(2,1)S(1)}, u32[]{:S(2)}, u32[]{:S(2)}) async-start(bf16[8,2,2560]{2,1,0:T(2,128)(2,1)} %constant_dynamic-update-slice_fusion), calls=%async_computation.1 | async-start | bytes 163840 | tf_op jit(solution)/shard_map/all_to_all | solution.py:197

commit v11 on v9

--- a/solution.py
+++ b/solution.py
@@ -75,12 +75,8 @@
     dp_index = lax.axis_index("dp")
     tp_index = lax.axis_index("tensor")
 
-    dev_count = dp_count * tp_count
-    rows_all = lax.all_to_all(
-        jnp.broadcast_to(residual_in[None], (dev_count,) + residual_in.shape),
-        ("dp", "tensor"),
-        0,
-        0,
+    rows_dp = lax.all_to_all(
+        jnp.broadcast_to(residual_in[None], (dp_count,) + residual_in.shape), "dp", 0, 0
     )
 
     request_ids = jnp.arange(total_reqs, dtype=jnp.int32)
@@ -95,7 +91,10 @@
     served_len = jnp.sum(jnp.where(hits, lengths[None, :], 0), axis=1)
     served_pages = jnp.sum(jnp.where(hits[:, :, None], page_table[None, :, :], 0), axis=1)
 
-    rows_srv = rows_all[served // rows_loc, served % rows_loc]
+    owner_tp = (served % req_loc) // rows_loc
+    held = rows_dp[served // req_loc, served % rows_loc]
+    held = jnp.where((owner_tp == tp_index)[:, None], held, jnp.zeros_like(held))
+    rows_srv = tensor_allreduce(held, tp_count)
     scaled_input = norm_rows(rows_srv, norm_gain).astype(jnp.bfloat16)
     query_srv = (
         apply_rotation(

time: 71.9 us -> 73.6 us (1.024)
  starting transfers between devices: 22.4 us -> 26 us
  local copies, waits for them, and re-layouts: 6.51 us -> 5.45 us
    ppermute x6 -> x9, starting transfers between devices: 11.5 us -> 16.9 us  [shifted(): lax.ppermute(value, 'tensor', [(i, (i + k) % tp_count) for i in range(tp_...]
    all_to_all x1, starting transfers between devices: 7.41 us -> 5.17 us  [local(): lax.all_to_all(jnp.broadcast_to(residual_in[None], (dp_count,) + residual...]
    all_to_all x1, waiting for transfers between devices: 1.15 us -> 0.01 us  [local(): lax.all_to_all(jnp.broadcast_to(residual_in[None], (dp_count,) + residual...]
    gather x1, local copies, waits for them, and re-layouts: 1.6 us -> 0.63 us  [local(): held = rows_dp[served // req_loc, served % rows_loc]]
    convert_element_type x2, other arithmetic: 1.39 us -> 0.6 us  [norm_rows(): gain.astype(jnp.float32)]
    ppermute x6 -> x9, waiting for transfers between devices: 6.84 us -> 7.31 us  [shifted(): lax.ppermute(value, 'tensor', [(i, (i + k) % tp_count) for i in range(tp_...]
  transfers between devices with their start and end apart: 8 -> 11, of which waited for: 6 -> 6; matrix products, arithmetic and copies ran while one was open for 15% -> 14% of each run, Pallas kernels for 0% -> 0%
where the time goes in v11:
time: 73.6 us; the launch traced here: 73 us
  starting transfers between devices  26 us (35%)
  matrix products  22.1 us (30%)
  waiting for transfers between devices  12.4 us (17%)
  other arithmetic  6.9 us (9%)
  local copies, waits for them, and re-layouts  5.45 us (7%)
    ppermute x9, starting transfers between devices, shifted(): lax.ppermute(value, 'tensor', [(i, (i + k) % tp_count) for i in range(tp_...  16.9 us
    ppermute x9, waiting for transfers between devices, shifted(): lax.ppermute(value, 'tensor', [(i, (i + k) % tp_count) for i in range(tp_...  7.31 us
    dot_general x1, matrix products, local(): jnp.dot(hidden, w_down, preferred_element_type=jnp.float32)  5.29 us
    all_to_all x1, starting transfers between devices, local(): lax.all_to_all(jnp.broadcast_to(residual_in[None], (dp_count,) + residual...  5.17 us
    all_to_all x1, waiting for transfers between devices, local(): incoming = lax.all_to_all(outgoing, 'dp', 0, 0)  5.1 us
    all_to_all x1, starting transfers between devices, local(): incoming = lax.all_to_all(outgoing, 'dp', 0, 0)  3.88 us
    dot_general x1, matrix products, local(): jnp.einsum('sq,qhdc->shdc', page_hot, key_page_pool, preferred_element_ty...  3.16 us
    dot_general x1, matrix products, local(): gate_act = jnp.dot(normed_mlp, w_gate, preferred_element_type=jnp.float32)  3.04 us
  transfers between devices with their start and end apart: 11, of which 6 were waited for; matrix products, arithmetic and copies ran while one was open for 14% of the time, Pallas kernels for 0%

profile of v11, /device:TPU:0, one launch (start us, length us, event | category | flops | bytes accessed | tf_op | source)
XLA Modules:
  0.0 73.0 jit_solution(16758680904245880021)
XLA Ops:
  0.0 1.5 %broadcast_in_dim.92 = bf16[8,2,2560]{2,1,0:T(2,128)(2,1)} broadcast(bf16[2,2560]{1,0:T(2,128)(2,1)} %param.14), dimensions={1,2} | broadcast | bytes 92160 | tf_op jit(solution)/shard_map/broadcast_in_dim | solution.py:79
  1.5 5.2 %all-to-all-start = ((bf16[8,2,2560]{2,1,0:T(2,128)(2,1)}), bf16[8,2,2560]{2,1,0:T(2,128)(2,1)S(1)}, u32[]{:S(2)}, u32[]{:S(2)}) async-start(bf16[8,2,2560]{2,1,0:T(2,128)(2,1)} %broadcast_in_dim.92), calls=%async_computation | async-start | bytes 163840 | tf_op jit(solution)/shard_map/all_to_all | solution.py:78
  6.7 0.7 iota_add_fusion.2
  7.6 0.8 %select_reduce_fusion.4 = (s32[8]{0:T(128)S(1)}, s32[8]{0:T(128)S(1)}) fusion(s32[64]{0:T(128)} %param.21, s32[64]{0:T(128)S(1)} %get-tuple-element.15, pred[64]{0:T(512)(128)(4,1)S(1)} %get-tuple-element.13), kind=kLoop, calls=%fused_computation.71 | loop fusion | flops 3056 | bytes 640 | tf_op jit(solution)/shard_map/reduce_sum | solution.py:91
  8.4 0.8 %select_reduce_fusion.2 = s32[8,4]{0,1:T(4,128)S(1)} fusion(s32[64,4]{0,1:T(4,128)} %param.22, pred[8,64]{1,0:T(8,128)(4,1)S(1)} %fusion.47), kind=kLoop, calls=%fused_computation.50 | loop fusion | flops 4064 | bytes 1664 | tf_op jit(solution)/shard_map/reduce_sum | solution.py:92
  9.6 3.2 %fusion.6 = bf16[32,2,80,128]{3,0,2,1:T(8,128)(2,1)} fusion(bf16[32,2,80,128]{3,2,1,0:T(8,128)(2,1)} %param.19, s32[32]{0:T(128)S(1)} %sub.58), kind=kOutput, calls=%fused_computation.9 | convolution fusion | flops 41944064 | bytes 2621568 | tf_op jit(solution)/shard_map/sq,qhdc->shdc/dot_general | solution.py:125
  12.8 1.7 %fusion.2 = bf16[32,2,80,128]{3,0,2,1:T(8,128)(2,1)} fusion(bf16[32,2,80,128]{3,2,1,0:T(8,128)(2,1)S(1)} %copy-done.1, s32[32]{0:T(128)S(1)} %sub.58), kind=kOutput, calls=%fused_computation.5 | convolution fusion | flops 41944064 | bytes 2621568 | tf_op jit(solution)/shard_map/sq,qhdc->shdc/dot_general | solution.py:128
  15.1 0.6 gather_fusion.1
  15.8 2.6 %collective-permute-start = (bf16[8,2560]{1,0:T(8,128)(2,1)S(1)}, bf16[8,2560]{1,0:T(8,128)(2,1)S(1)}, u32[]{:S(2)}, u32[]{:S(2)}) collective-permute-start(bf16[8,2560]{1,0:T(8,128)(2,1)S(1)} %broadcast_select_fusion), channel_id=1, source_target_pairs={{0,2},{1,3},{2,0},{3,1},{4,6},{5,7},{6,4},{7,5},{8,10},{9,11},{10,... | collective-permute-start | bytes 122888 | tf_op jit(solution)/shard_map/ppermute | solution.py:36
  18.4 1.6 %collective-permute-start.1 = (bf16[8,2560]{1,0:T(8,128)(2,1)S(1)}, bf16[8,2560]{1,0:T(8,128)(2,1)S(1)}, u32[]{:S(2)}, u32[]{:S(2)}) collective-permute-start(bf16[8,2560]{1,0:T(8,128)(2,1)S(1)} %broadcast_select_fusion), channel_id=1, source_target_pairs={{0,1},{1,2},{2,3},{3,0},{4,5},{5,6},{6,7},{7,4},{8,9},{9,10},{10,1... | collective-permute-start | bytes 122888 | tf_op jit(solution)/shard_map/ppermute | solution.py:36
  20.0 2.2 %collective-permute-start.2 = (bf16[8,2560]{1,0:T(8,128)(2,1)S(1)}, bf16[8,2560]{1,0:T(8,128)(2,1)S(1)}, u32[]{:S(2)}, u32[]{:S(2)}) collective-permute-start(bf16[8,2560]{1,0:T(8,128)(2,1)S(1)} %broadcast_select_fusion), channel_id=1, source_target_pairs={{0,3},{1,0},{2,1},{3,2},{4,7},{5,4},{6,5},{7,6},{8,11},{9,8},{10,9... | collective-permute-start | bytes 122888 | tf_op jit(solution)/shard_map/ppermute | solution.py:36
  23.4 0.9 %collective-permute-done.1 = bf16[8,2560]{1,0:T(8,128)(2,1)S(1)} collective-permute-done((bf16[8,2560]{1,0:T(8,128)(2,1)S(1)}, bf16[8,2560]{1,0:T(8,128)(2,1)S(1)}, u32[]{:S(2)}, u32[]{:S(2)}) %collective-permute-start.1) | collective-permute-done | bytes 40992 | tf_op jit(solution)/shard_map/ppermute | solution.py:36
  24.7 1.5 %fusion.62 = f32[8,160]{1,0:T(8,128)S(1)} fusion(bf16[2560,160]{0,1:T(8,128)(2,1)} %param.17, bf16[8,2560]{1,0:T(8,128)(2,1)S(1)} %get-tuple-element.12, f32[2560]{0:T(1024)S(1)} %convert_element_type.65, f32[8]{0:T(128)S(1)} %add_rsqrt_fusion.1), kind=kOutput, calls=%fused_computation.124 | convolution fusion | flops 6635520 | bytes 875552 | tf_op jit(solution)/shard_map/dot_general | solution.py:110
  26.2 2.5 %fusion.64 = f32[8,640]{1,0:T(8,128)S(1)} fusion(bf16[2560,640]{1,0:T(8,128)(2,1)} %param.16, bf16[8,2560]{1,0:T(8,128)(2,1)S(1)} %get-tuple-element.12, f32[2560]{0:T(1024)S(1)} %convert_element_type.65, f32[8]{0:T(128)S(1)} %add_rsqrt_fusion.1), kind=kOutput, calls=%fused_computation.125 | convolution fusion | flops 26296320 | bytes 3348512 | tf_op jit(solution)/shard_map/dot_general | solution.py:101
  29.3 1.9 %select_reduce_fusion.1 = (f32[8,2,4]{2,1,0:T(2,128)S(1)}, f32[8,2,4,4,128]{4,2,3,1,0:T(4,128)S(1)}) fusion(pred[8,4,128]{2,1,0:T(4,128)(4,1)S(1)} %broadcast_compare_fusion, bf16[8,4,2,80,128]{4,1,0,3,2:T(4,128)(2,1)} %bitcast.60, bf16[8,2,4,40]{3,2,1,0:T(4,128)(2,1)S(1)} %bitcast.66, bf16[8,2,4,40]{3,2,1,0:T(4,128)(2,1)S(1)} %bitcast.64), kind=kOutput, calls=%fused_computation.23 | convolution fusion | flops 5361600 | bytes 1456384 | tf_op jit(solution)/shard_map/rhgd,rphdc->rhgpc/dot_general | solution.py:132
  31.9 1.9 %fusion.20 = bf16[8,2,4,80]{3,2,1,0:T(4,128)(2,1)S(1)} fusion(bf16[8,4,2,80,128]{4,1,0,3,2:T(4,128)(2,1)} %bitcast.59, f32[8,2,4,4,128]{4,2,3,1,0:T(4,128)S(1)} %get-tuple-element.23, f32[8,2,4]{2,1,0:T(2,128)S(1)} %multiply_maximum_fusion, pred[8,4,128]{2,1,0:T(4,128)(4,1)S(1)} %broadcast_compare_fusion, f32[8,2,4]{2,1,0:T(2,128)S(1)} %get-tuple-element.9, ...), kind=kOutput, calls=%fused_computation.16 | convolution fusion | flops 5328896 | bytes 1462016 | tf_op jit(solution)/shard_map/rhgpc,rphdc->rhgd/dot_general | solution.py:148
  34.5 0.9 %collective-permute-start.3 = (f32[8,2560]{1,0:T(8,128)S(1)}, f32[8,2560]{1,0:T(8,128)S(1)}, u32[]{:S(2)}, u32[]{:S(2)}) collective-permute-start(f32[8,2560]{1,0:T(8,128)S(1)} %fusion.67), channel_id=1, source_target_pairs={{0,2},{1,3},{2,0},{3,1},{4,6},{5,7},{6,4},{7,5},{8,10},{9,11},{10,... | collective-permute-start | bytes 245768 | tf_op jit(solution)/shard_map/ppermute | solution.py:36
  35.4 3.3 %collective-permute-start.4 = (f32[8,2560]{1,0:T(8,128)S(1)}, f32[8,2560]{1,0:T(8,128)}, u32[]{:S(2)}, u32[]{:S(2)}) collective-permute-start(f32[8,2560]{1,0:T(8,128)S(1)} %fusion.67), channel_id=1, source_target_pairs={{0,1},{1,2},{2,3},{3,0},{4,5},{5,6},{6,7},{7,4},{8,9},{9,10},{10,1... | collective-permute-start | bytes 245768 | tf_op jit(solution)/shard_map/ppermute | solution.py:36
  39.2 0.6 gather_fusion
  39.8 3.2 %collective-permute-done.3 = f32[8,2560]{1,0:T(8,128)S(1)} collective-permute-done((f32[8,2560]{1,0:T(8,128)S(1)}, f32[8,2560]{1,0:T(8,128)S(1)}, u32[]{:S(2)}, u32[]{:S(2)}) %collective-permute-start.3) | collective-permute-done | bytes 81952 | tf_op jit(solution)/shard_map/ppermute | solution.py:36
  43.1 0.6 copy-done.4
  43.8 1.1 %multiply_reduce_fusion = (f32[8]{0:T(128)S(1)}, f32[8,2560]{1,0:T(8,128)S(1)}) fusion(f32[8,2560]{1,0:T(8,128)} %collective-permute-done.4, f32[8,2560]{1,0:T(8,128)} %collective-permute-done.5, f32[8,2560]{1,0:T(8,128)S(1)} %fusion.67, f32[8,2560]{1,0:T(8,128)} %copy-done.4, bf16[8,2560]{1,0:T(8,128)(2,1)S(1)} %get-tuple-element.12), kind=kLoop, calls=%fused_computation.33 | loop fusion | flops 143352 | bytes 450592 | tf_op jit(solution)/shard_map/reduce_sum | solution.py:13
  45.0 3.0 %fusion.60 = f32[8,896]{1,0:T(8,128)S(1)} fusion(bf16[2560,896]{1,0:T(8,128)(2,1)} %param.25, f32[8,2560]{1,0:T(8,128)S(1)} %get-tuple-element.8, f32[2560]{0:T(1024)S(1)} %copy-done.3, f32[8]{0:T(128)S(1)} %add_rsqrt_fusion), kind=kOutput, calls=%fused_computation.123 | convolution fusion | flops 36761600 | bytes 4708384 | tf_op jit(solution)/shard_map/dot_general | solution.py:159
  48.0 5.3 %fusion.24 = f32[8,2560]{1,0:T(8,128)S(1)} fusion(bf16[896,2560]{1,0:T(8,128)(2,1)} %param.27, bf16[2560,896]{1,0:T(8,128)(2,1)} %param.26, f32[8,896]{1,0:T(8,128)S(1)} %fusion.60, f32[8,2560]{1,0:T(8,128)S(1)} %get-tuple-element.8, f32[2560]{0:T(1024)S(1)} %copy-done.3, f32[8]{0:T(128)S(1)} %add_rsqrt_fusion), kind=kOutput, calls=%fused_computation.18 | convolution fusion | flops 73504768 | bytes 9377824 | tf_op jit(solution)/shard_map/dot_general | solution.py:163
  53.3 1.9 %collective-permute-start.6 = (f32[8,2560]{1,0:T(8,128)S(1)}, f32[8,2560]{1,0:T(8,128)S(1)}, u32[]{:S(2)}, u32[]{:S(2)}) collective-permute-start(f32[8,2560]{1,0:T(8,128)S(1)} %fusion.24), channel_id=1, source_target_pairs={{0,2},{1,3},{2,0},{3,1},{4,6},{5,7},{6,4},{7,5},{8,10},{9,11},{10,... | collective-permute-start | bytes 245768 | tf_op jit(solution)/shard_map/ppermute | solution.py:36
  55.2 0.7 %collective-permute-start.7 = (f32[8,2560]{1,0:T(8,128)S(1)}, f32[8,2560]{1,0:T(8,128)S(1)}, u32[]{:S(2)}, u32[]{:S(2)}) collective-permute-start(f32[8,2560]{1,0:T(8,128)S(1)} %fusion.24), channel_id=1, source_target_pairs={{0,1},{1,2},{2,3},{3,0},{4,5},{5,6},{6,7},{7,4},{8,9},{9,10},{10,1... | collective-permute-start | bytes 245768 | tf_op jit(solution)/shard_map/ppermute | solution.py:36
  56.0 3.1 %collective-permute-start.8 = (f32[8,2560]{1,0:T(8,128)S(1)}, f32[8,2560]{1,0:T(8,128)S(1)}, u32[]{:S(2)}, u32[]{:S(2)}) collective-permute-start(f32[8,2560]{1,0:T(8,128)S(1)} %fusion.24), channel_id=1, source_target_pairs={{0,3},{1,0},{2,1},{3,2},{4,7},{5,4},{6,5},{7,6},{8,11},{9,8},{10,9... | collective-permute-start | bytes 245768 | tf_op jit(solution)/shard_map/ppermute | solution.py:36
  59.1 2.9 %collective-permute-done.6 = f32[8,2560]{1,0:T(8,128)S(1)} collective-permute-done((f32[8,2560]{1,0:T(8,128)S(1)}, f32[8,2560]{1,0:T(8,128)S(1)}, u32[]{:S(2)}, u32[]{:S(2)}) %collective-permute-start.6) | collective-permute-done | bytes 81952 | tf_op jit(solution)/shard_map/ppermute | solution.py:36
  62.7 0.7 reshape.454
  63.3 3.9 %all-to-all-start.1 = ((bf16[8,2,2560]{2,1,0:T(2,128)(2,1)}), bf16[8,2,2560]{2,1,0:T(2,128)(2,1)S(1)}, u32[]{:S(2)}, u32[]{:S(2)}) async-start(bf16[8,2,2560]{2,1,0:T(2,128)(2,1)} %reshape.454), calls=%async_computation.1 | async-start | bytes 163840 | tf_op jit(solution)/shard_map/all_to_all | solution.py:176
  67.2 5.1 %all-to-all-done.1 = bf16[8,2,2560]{2,1,0:T(2,128)(2,1)S(1)} async-done(((bf16[8,2,2560]{2,1,0:T(2,128)(2,1)}), bf16[8,2,2560]{2,1,0:T(2,128)(2,1)S(1)}, u32[]{:S(2)}, u32[]{:S(2)}) %all-to-all-start.1) | async-done | bytes 81952 | tf_op jit(solution)/shard_map/all_to_all | solution.py:176
  72.3 0.8 %select_reduce_fusion = bf16[2,2560]{1,0:T(2,128)(2,1)} fusion(bf16[8,2,2560]{2,1,0:T(2,128)(2,1)S(1)} %all-to-all-done.1, pred[8,2]{1,0:T(8,128)(4,1)S(1)} %iota_compare_fusion.3), kind=kLoop, calls=%fused_computation.21 | loop fusion | flops 117760 | bytes 92176 | tf_op jit(solution)/shard_map/reduce_sum | solution.py:180
  (69 shorter events, 6.0 us)
Async XLA Ops:
  0.0 33.9 %copy-start = (bf16[640,2560]{1,0:T(8,128)(2,1)S(1)}, bf16[640,2560]{1,0:T(8,128)(2,1)}, u32[]{:S(2)}) copy-start(bf16[640,2560]{1,0:T(8,128)(2,1)} %param.23) | copy-start | bytes 9830404
  1.5 13.6 %all-to-all-start = ((bf16[8,2,2560]{2,1,0:T(2,128)(2,1)}), bf16[8,2,2560]{2,1,0:T(2,128)(2,1)S(1)}, u32[]{:S(2)}, u32[]{:S(2)}) async-start(bf16[8,2,2560]{2,1,0:T(2,128)(2,1)} %broadcast_in_dim.92), calls=%async_computation | async-start | bytes 163840 | tf_op jit(solution)/shard_map/all_to_all | solution.py:78
  9.6 3.2 %copy-start.1 = (bf16[32,2,80,128]{3,2,1,0:T(8,128)(2,1)S(1)}, bf16[32,2,80,128]{3,2,1,0:T(8,128)(2,1)}, u32[]{:S(2)}) copy-start(bf16[32,2,80,128]{3,2,1,0:T(8,128)(2,1)} %param.20) | copy-start | bytes 3932164
  12.8 10.0 %copy-start.5 = (bf16[2560]{0:T(1024)(128)(2,1)S(1)}, bf16[2560]{0:T(1024)(128)(2,1)}, u32[]{:S(2)}) copy-start(bf16[2560]{0:T(1024)(128)(2,1)} %param.15) | copy-start | bytes 15364
  12.8 10.0 %copy-start.6 = (bf16[2560]{0:T(1024)(128)(2,1)S(1)}, bf16[2560]{0:T(1024)(128)(2,1)}, u32[]{:S(2)}) copy-start(bf16[2560]{0:T(1024)(128)(2,1)} %param.24) | copy-start | bytes 15364
  15.8 7.6 %collective-permute-start = (bf16[8,2560]{1,0:T(8,128)(2,1)S(1)}, bf16[8,2560]{1,0:T(8,128)(2,1)S(1)}, u32[]{:S(2)}, u32[]{:S(2)}) collective-permute-start(bf16[8,2560]{1,0:T(8,128)(2,1)S(1)} %broadcast_select_fusion), channel_id=1, source_target_pairs={{0,2},{1,3},{2,0},{3,1},{4,6},{5,7},{6,4},{7,5},{8,10},{9,11},{10,... | collective-permute-start | bytes 122888 | tf_op jit(solution)/shard_map/ppermute | solution.py:36
  18.4 6.0 %collective-permute-start.1 = (bf16[8,2560]{1,0:T(8,128)(2,1)S(1)}, bf16[8,2560]{1,0:T(8,128)(2,1)S(1)}, u32[]{:S(2)}, u32[]{:S(2)}) collective-permute-start(bf16[8,2560]{1,0:T(8,128)(2,1)S(1)} %broadcast_select_fusion), channel_id=1, source_target_pairs={{0,1},{1,2},{2,3},{3,0},{4,5},{5,6},{6,7},{7,4},{8,9},{9,10},{10,1... | collective-permute-start | bytes 122888 | tf_op jit(solution)/shard_map/ppermute | solution.py:36
  20.0 4.5 %collective-permute-start.2 = (bf16[8,2560]{1,0:T(8,128)(2,1)S(1)}, bf16[8,2560]{1,0:T(8,128)(2,1)S(1)}, u32[]{:S(2)}, u32[]{:S(2)}) collective-permute-start(bf16[8,2560]{1,0:T(8,128)(2,1)S(1)} %broadcast_select_fusion), channel_id=1, source_target_pairs={{0,3},{1,0},{2,1},{3,2},{4,7},{5,4},{6,5},{7,6},{8,11},{9,8},{10,9... | collective-permute-start | bytes 122888 | tf_op jit(solution)/shard_map/ppermute | solution.py:36
  28.8 2.6 %copy-start.2 = (bf16[2560,160]{0,1:T(8,128)(2,1)S(1)}, bf16[2560,160]{0,1:T(8,128)(2,1)}, u32[]{:S(2)}) copy-start(bf16[2560,160]{0,1:T(8,128)(2,1)} %param.18) | copy-start | bytes 2457604
  33.9 5.3 %copy-start.7 = (s32[2]{0:T(128)S(1)}, s32[2]{0:T(128)}, u32[]{:S(2)}) copy-start(s32[2]{0:T(128)} %fusion.50) | copy-start | bytes 28
  33.9 11.0 %copy-start.3 = (f32[2560]{0:T(1024)S(1)}, f32[2560]{0:T(1024)}, u32[]{:S(2)}) copy-start(f32[2560]{0:T(1024)} %convert_element_type.73) | copy-start | bytes 30724
  34.5 8.6 %collective-permute-start.3 = (f32[8,2560]{1,0:T(8,128)S(1)}, f32[8,2560]{1,0:T(8,128)S(1)}, u32[]{:S(2)}, u32[]{:S(2)}) collective-permute-start(f32[8,2560]{1,0:T(8,128)S(1)} %fusion.67), channel_id=1, source_target_pairs={{0,2},{1,3},{2,0},{3,1},{4,6},{5,7},{6,4},{7,5},{8,10},{9,11},{10,... | collective-permute-start | bytes 245768 | tf_op jit(solution)/shard_map/ppermute | solution.py:36
  35.4 7.7 %collective-permute-start.4 = (f32[8,2560]{1,0:T(8,128)S(1)}, f32[8,2560]{1,0:T(8,128)}, u32[]{:S(2)}, u32[]{:S(2)}) collective-permute-start(f32[8,2560]{1,0:T(8,128)S(1)} %fusion.67), channel_id=1, source_target_pairs={{0,1},{1,2},{2,3},{3,0},{4,5},{5,6},{6,7},{7,4},{8,9},{9,10},{10,1... | collective-permute-start | bytes 245768 | tf_op jit(solution)/shard_map/ppermute | solution.py:36
  38.6 5.2 %collective-permute-start.5 = (f32[8,2560]{1,0:T(8,128)S(1)}, f32[8,2560]{1,0:T(8,128)}, u32[]{:S(2)}, u32[]{:S(2)}) collective-permute-start(f32[8,2560]{1,0:T(8,128)S(1)} %fusion.67), channel_id=1, source_target_pairs={{0,3},{1,0},{2,1},{3,2},{4,7},{5,4},{6,5},{7,6},{8,11},{9,8},{10,9... | collective-permute-start | bytes 245768 | tf_op jit(solution)/shard_map/ppermute | solution.py:36
  43.1 0.6 copy-start.4
  53.3 8.7 %collective-permute-start.6 = (f32[8,2560]{1,0:T(8,128)S(1)}, f32[8,2560]{1,0:T(8,128)S(1)}, u32[]{:S(2)}, u32[]{:S(2)}) collective-permute-start(f32[8,2560]{1,0:T(8,128)S(1)} %fusion.24), channel_id=1, source_target_pairs={{0,2},{1,3},{2,0},{3,1},{4,6},{5,7},{6,4},{7,5},{8,10},{9,11},{10,... | collective-permute-start | bytes 245768 | tf_op jit(solution)/shard_map/ppermute | solution.py:36
  55.2 6.8 %collective-permute-start.7 = (f32[8,2560]{1,0:T(8,128)S(1)}, f32[8,2560]{1,0:T(8,128)S(1)}, u32[]{:S(2)}, u32[]{:S(2)}) collective-permute-start(f32[8,2560]{1,0:T(8,128)S(1)} %fusion.24), channel_id=1, source_target_pairs={{0,1},{1,2},{2,3},{3,0},{4,5},{5,6},{6,7},{7,4},{8,9},{9,10},{10,1... | collective-permute-start | bytes 245768 | tf_op jit(solution)/shard_map/ppermute | solution.py:36
  56.0 6.0 %collective-permute-start.8 = (f32[8,2560]{1,0:T(8,128)S(1)}, f32[8,2560]{1,0:T(8,128)S(1)}, u32[]{:S(2)}, u32[]{:S(2)}) collective-permute-start(f32[8,2560]{1,0:T(8,128)S(1)} %fusion.24), channel_id=1, source_target_pairs={{0,3},{1,0},{2,1},{3,2},{4,7},{5,4},{6,5},{7,6},{8,11},{9,8},{10,9... | collective-permute-start | bytes 245768 | tf_op jit(solution)/shard_map/ppermute | solution.py:36
  63.3 9.0 %all-to-all-start.1 = ((bf16[8,2,2560]{2,1,0:T(2,128)(2,1)}), bf16[8,2,2560]{2,1,0:T(2,128)(2,1)S(1)}, u32[]{:S(2)}, u32[]{:S(2)}) async-start(bf16[8,2,2560]{2,1,0:T(2,128)(2,1)} %reshape.454), calls=%async_computation.1 | async-start | bytes 163840 | tf_op jit(solution)/shard_map/all_to_all | solution.py:176

commit v12 on v11

--- a/solution.py
+++ b/solution.py
@@ -94,6 +94,7 @@
     owner_tp = (served % req_loc) // rows_loc
     held = rows_dp[served // req_loc, served % rows_loc]
     held = jnp.where((owner_tp == tp_index)[:, None], held, jnp.zeros_like(held))
+    held, served_pages = lax.optimization_barrier((held, served_pages))
     rows_srv = tensor_allreduce(held, tp_count)
     scaled_input = norm_rows(rows_srv, norm_gain).astype(jnp.bfloat16)
     query_srv = (

time: 73.6 us -> 70.7 us (0.961)
  starting transfers between devices: 26 us -> 24 us
  matrix products: 22.1 us -> 20.9 us
    ppermute x9, starting transfers between devices: 16.9 us -> 14.9 us  [shifted(): lax.ppermute(value, 'tensor', [(i, (i + k) % tp_count) for i in range(tp_...]
    dot_general x1, matrix products: 1.48 us -> 0.34 us  [local(): jnp.dot(scaled_input, key_weight, preferred_element_type=jnp.float32)]
    convert_element_type x2, other arithmetic: 0.6 us -> 1.4 us  [norm_rows(): gain.astype(jnp.float32)]
  transfers between devices with their start and end apart: 11 -> 11, of which waited for: 6 -> 4; matrix products, arithmetic and copies ran while one was open for 14% -> 15% of each run, Pallas kernels for 0% -> 0%
where the time goes in v12:
time: 70.7 us; the launch traced here: 70.1 us
  starting transfers between devices  24 us (34%)
  matrix products  20.9 us (30%)
  waiting for transfers between devices  12.5 us (18%)
  other arithmetic  7.13 us (10%)
  local copies, waits for them, and re-layouts  5.43 us (8%)
    ppermute x9, starting transfers between devices, shifted(): lax.ppermute(value, 'tensor', [(i, (i + k) % tp_count) for i in range(tp_...  14.9 us
    ppermute x9, waiting for transfers between devices, shifted(): lax.ppermute(value, 'tensor', [(i, (i + k) % tp_count) for i in range(tp_...  7.1 us
    dot_general x1, matrix products, local(): jnp.dot(hidden, w_down, preferred_element_type=jnp.float32)  5.29 us
    all_to_all x1, starting transfers between devices, local(): lax.all_to_all(jnp.broadcast_to(residual_in[None], (dp_count,) + residual...  5.17 us
    all_to_all x1, waiting for transfers between devices, local(): incoming = lax.all_to_all(outgoing, 'dp', 0, 0)  5.1 us
    all_to_all x1, starting transfers between devices, local(): incoming = lax.all_to_all(outgoing, 'dp', 0, 0)  3.86 us
    dot_general x1, matrix products, local(): jnp.einsum('sq,qhdc->shdc', page_hot, key_page_pool, preferred_element_ty...  3.15 us
    dot_general x1, matrix products, local(): gate_act = jnp.dot(normed_mlp, w_gate, preferred_element_type=jnp.float32)  3.05 us
  transfers between devices with their start and end apart: 11, of which 4 were waited for; matrix products, arithmetic and copies ran while one was open for 15% of the time, Pallas kernels for 0%

profile of v12, /device:TPU:0, one launch (start us, length us, event | category | flops | bytes accessed | tf_op | source)
XLA Modules:
  0.0 70.1 jit_solution(3135501798119700087)
XLA Ops:
  0.0 1.5 %broadcast_in_dim.92 = bf16[8,2,2560]{2,1,0:T(2,128)(2,1)} broadcast(bf16[2,2560]{1,0:T(2,128)(2,1)} %param.14), dimensions={1,2} | broadcast | bytes 92160 | tf_op jit(solution)/shard_map/broadcast_in_dim | solution.py:79
  1.5 5.2 %all-to-all-start = ((bf16[8,2,2560]{2,1,0:T(2,128)(2,1)}), bf16[8,2,2560]{2,1,0:T(2,128)(2,1)S(1)}, u32[]{:S(2)}, u32[]{:S(2)}) async-start(bf16[8,2,2560]{2,1,0:T(2,128)(2,1)} %broadcast_in_dim.92), calls=%async_computation | async-start | bytes 163840 | tf_op jit(solution)/shard_map/all_to_all | solution.py:78
  6.7 0.7 iota_add_fusion.2
  7.6 0.8 %select_reduce_fusion.4 = (s32[8]{0:T(128)S(1)}, s32[8]{0:T(128)S(1)}) fusion(s32[64]{0:T(128)} %param.21, s32[64]{0:T(128)S(1)} %get-tuple-element.19, pred[64]{0:T(512)(128)(4,1)S(1)} %get-tuple-element.17), kind=kLoop, calls=%fused_computation.71 | loop fusion | flops 3056 | bytes 640 | tf_op jit(solution)/shard_map/reduce_sum | solution.py:91
  8.4 0.7 convert_element_type.65
  9.3 0.7 convert_element_type.73
  10.5 0.8 %select_reduce_fusion.2 = s32[8,4]{0,1:T(4,128)S(1)} fusion(s32[64,4]{0,1:T(4,128)} %param.22, pred[8,64]{1,0:T(8,128)(4,1)S(1)} %fusion.47), kind=kLoop, calls=%fused_computation.50 | loop fusion | flops 4064 | bytes 1664 | tf_op jit(solution)/shard_map/reduce_sum | solution.py:92
  11.8 0.6 gather_fusion.1
  12.5 2.6 %collective-permute-start = (bf16[8,2560]{1,0:T(8,128)(2,1)S(1)}, bf16[8,2560]{1,0:T(8,128)(2,1)S(1)}, u32[]{:S(2)}, u32[]{:S(2)}) collective-permute-start(bf16[8,2560]{1,0:T(8,128)(2,1)S(1)} %broadcast_select_fusion), channel_id=1, source_target_pairs={{0,2},{1,3},{2,0},{3,1},{4,6},{5,7},{6,4},{7,5},{8,10},{9,11},{10,... | collective-permute-start | bytes 122888 | tf_op jit(solution)/shard_map/ppermute | solution.py:36
  15.1 1.6 %collective-permute-start.1 = (bf16[8,2560]{1,0:T(8,128)(2,1)S(1)}, bf16[8,2560]{1,0:T(8,128)(2,1)S(1)}, u32[]{:S(2)}, u32[]{:S(2)}) collective-permute-start(bf16[8,2560]{1,0:T(8,128)(2,1)S(1)} %broadcast_select_fusion), channel_id=1, source_target_pairs={{0,1},{1,2},{2,3},{3,0},{4,5},{5,6},{6,7},{7,4},{8,9},{9,10},{10,1... | collective-permute-start | bytes 122888 | tf_op jit(solution)/shard_map/ppermute | solution.py:36
  16.7 2.2 %collective-permute-start.2 = (bf16[8,2560]{1,0:T(8,128)(2,1)S(1)}, bf16[8,2560]{1,0:T(8,128)(2,1)S(1)}, u32[]{:S(2)}, u32[]{:S(2)}) collective-permute-start(bf16[8,2560]{1,0:T(8,128)(2,1)S(1)} %broadcast_select_fusion), channel_id=1, source_target_pairs={{0,3},{1,0},{2,1},{3,2},{4,7},{5,4},{6,5},{7,6},{8,11},{9,8},{10,9... | collective-permute-start | bytes 122888 | tf_op jit(solution)/shard_map/ppermute | solution.py:36
  19.1 3.1 %fusion.6 = bf16[32,2,80,128]{3,0,2,1:T(8,128)(2,1)} fusion(bf16[32,2,80,128]{3,2,1,0:T(8,128)(2,1)} %param.19, s32[32]{0:T(128)S(1)} %eq.108), kind=kOutput, calls=%fused_computation.9 | convolution fusion | flops 41944064 | bytes 2621568 | tf_op jit(solution)/shard_map/sq,qhdc->shdc/dot_general | solution.py:126
  22.3 1.7 %fusion.2 = bf16[32,2,80,128]{3,0,2,1:T(8,128)(2,1)} fusion(bf16[32,2,80,128]{3,2,1,0:T(8,128)(2,1)S(1)} %copy-done.1, s32[32]{0:T(128)S(1)} %eq.108), kind=kOutput, calls=%fused_computation.5 | convolution fusion | flops 41944064 | bytes 2621568 | tf_op jit(solution)/shard_map/sq,qhdc->shdc/dot_general | solution.py:129
  24.6 2.5 %fusion.64 = f32[8,640]{1,0:T(8,128)S(1)} fusion(bf16[2560,640]{1,0:T(8,128)(2,1)} %param.16, bf16[8,2560]{1,0:T(8,128)(2,1)S(1)} %get-tuple-element.16, f32[2560]{0:T(1024)S(1)} %convert_element_type.65, f32[8]{0:T(128)S(1)} %add_rsqrt_fusion.1), kind=kOutput, calls=%fused_computation.125 | convolution fusion | flops 26296320 | bytes 3348512 | tf_op jit(solution)/shard_map/dot_general | solution.py:102
  27.6 1.9 %select_reduce_fusion.1 = (f32[8,2,4]{2,1,0:T(2,128)S(1)}, f32[8,2,4,4,128]{4,2,3,1,0:T(4,128)S(1)}) fusion(pred[8,4,128]{2,1,0:T(4,128)(4,1)S(1)} %broadcast_compare_fusion, bf16[8,4,2,80,128]{4,1,0,3,2:T(4,128)(2,1)} %bitcast.60, bf16[8,2,4,40]{3,2,1,0:T(4,128)(2,1)S(1)} %bitcast.66, bf16[8,2,4,40]{3,2,1,0:T(4,128)(2,1)S(1)} %bitcast.64), kind=kOutput, calls=%fused_computation.23 | convolution fusion | flops 5361600 | bytes 1456384 | tf_op jit(solution)/shard_map/rhgd,rphdc->rhgpc/dot_general | solution.py:133
  30.2 1.9 %fusion.20 = bf16[8,2,4,80]{3,2,1,0:T(4,128)(2,1)S(1)} fusion(bf16[8,4,2,80,128]{4,1,0,3,2:T(4,128)(2,1)} %bitcast.59, f32[8,2,4,4,128]{4,2,3,1,0:T(4,128)S(1)} %get-tuple-element.27, f32[8,2,4]{2,1,0:T(2,128)S(1)} %multiply_maximum_fusion, pred[8,4,128]{2,1,0:T(4,128)(4,1)S(1)} %broadcast_compare_fusion, f32[8,2,4]{2,1,0:T(2,128)S(1)} %get-tuple-element.13, ...), kind=kOutput, calls=%fused_computation.16 | convolution fusion | flops 5328896 | bytes 1462016 | tf_op jit(solution)/shard_map/rhgpc,rphdc->rhgd/dot_general | solution.py:149
  32.8 1.3 %collective-permute-start.4 = (f32[8,2560]{1,0:T(8,128)S(1)}, f32[8,2560]{1,0:T(8,128)}, u32[]{:S(2)}, u32[]{:S(2)}) collective-permute-start(f32[8,2560]{1,0:T(8,128)S(1)} %fusion.67), channel_id=1, source_target_pairs={{0,1},{1,2},{2,3},{3,0},{4,5},{5,6},{6,7},{7,4},{8,9},{9,10},{10,1... | collective-permute-start | bytes 245768 | tf_op jit(solution)/shard_map/ppermute | solution.py:36
  34.1 2.5 %collective-permute-start.5 = (f32[8,2560]{1,0:T(8,128)S(1)}, f32[8,2560]{1,0:T(8,128)}, u32[]{:S(2)}, u32[]{:S(2)}) collective-permute-start(f32[8,2560]{1,0:T(8,128)S(1)} %fusion.67), channel_id=1, source_target_pairs={{0,3},{1,0},{2,1},{3,2},{4,7},{5,4},{6,5},{7,6},{8,11},{9,8},{10,9... | collective-permute-start | bytes 245768 | tf_op jit(solution)/shard_map/ppermute | solution.py:36
  36.6 0.6 gather_fusion
  37.3 3.7 %collective-permute-done.3 = f32[8,2560]{1,0:T(8,128)S(1)} collective-permute-done((f32[8,2560]{1,0:T(8,128)S(1)}, f32[8,2560]{1,0:T(8,128)S(1)}, u32[]{:S(2)}, u32[]{:S(2)}) %collective-permute-start.3) | collective-permute-done | bytes 81952 | tf_op jit(solution)/shard_map/ppermute | solution.py:36
  41.0 0.6 copy-done.4
  41.6 1.1 %multiply_reduce_fusion = (f32[8]{0:T(128)S(1)}, f32[8,2560]{1,0:T(8,128)S(1)}) fusion(f32[8,2560]{1,0:T(8,128)} %collective-permute-done.4, f32[8,2560]{1,0:T(8,128)} %collective-permute-done.5, f32[8,2560]{1,0:T(8,128)S(1)} %fusion.67, f32[8,2560]{1,0:T(8,128)} %copy-done.4, bf16[8,2560]{1,0:T(8,128)(2,1)S(1)} %get-tuple-element.16), kind=kLoop, calls=%fused_computation.33 | loop fusion | flops 143352 | bytes 450592 | tf_op jit(solution)/shard_map/reduce_sum | solution.py:13
  42.7 3.0 %fusion.60 = f32[8,896]{1,0:T(8,128)S(1)} fusion(bf16[2560,896]{1,0:T(8,128)(2,1)} %param.25, f32[8,2560]{1,0:T(8,128)S(1)} %get-tuple-element.12, f32[2560]{0:T(1024)S(1)} %convert_element_type.73, f32[8]{0:T(128)S(1)} %add_rsqrt_fusion), kind=kOutput, calls=%fused_computation.123 | convolution fusion | flops 36761600 | bytes 4708384 | tf_op jit(solution)/shard_map/dot_general | solution.py:160
  45.8 5.3 %fusion.24 = f32[8,2560]{1,0:T(8,128)S(1)} fusion(bf16[896,2560]{1,0:T(8,128)(2,1)} %param.27, bf16[2560,896]{1,0:T(8,128)(2,1)} %param.26, f32[8,896]{1,0:T(8,128)S(1)} %fusion.60, f32[8,2560]{1,0:T(8,128)S(1)} %get-tuple-element.12, f32[2560]{0:T(1024)S(1)} %convert_element_type.73, f32[8]{0:T(128)S(1)} %add_rsqrt_fusion), kind=kOutput, calls=%fused_computation.18 | convolution fusion | flops 73504768 | bytes 9377824 | tf_op jit(solution)/shard_map/dot_general | solution.py:164
  51.1 0.9 %collective-permute-start.6 = (f32[8,2560]{1,0:T(8,128)S(1)}, f32[8,2560]{1,0:T(8,128)S(1)}, u32[]{:S(2)}, u32[]{:S(2)}) collective-permute-start(f32[8,2560]{1,0:T(8,128)S(1)} %fusion.24), channel_id=1, source_target_pairs={{0,2},{1,3},{2,0},{3,1},{4,6},{5,7},{6,4},{7,5},{8,10},{9,11},{10,... | collective-permute-start | bytes 245768 | tf_op jit(solution)/shard_map/ppermute | solution.py:36
  51.9 1.2 %collective-permute-start.7 = (f32[8,2560]{1,0:T(8,128)S(1)}, f32[8,2560]{1,0:T(8,128)S(1)}, u32[]{:S(2)}, u32[]{:S(2)}) collective-permute-start(f32[8,2560]{1,0:T(8,128)S(1)} %fusion.24), channel_id=1, source_target_pairs={{0,1},{1,2},{2,3},{3,0},{4,5},{5,6},{6,7},{7,4},{8,9},{9,10},{10,1... | collective-permute-start | bytes 245768 | tf_op jit(solution)/shard_map/ppermute | solution.py:36
  53.1 2.6 %collective-permute-start.8 = (f32[8,2560]{1,0:T(8,128)S(1)}, f32[8,2560]{1,0:T(8,128)S(1)}, u32[]{:S(2)}, u32[]{:S(2)}) collective-permute-start(f32[8,2560]{1,0:T(8,128)S(1)} %fusion.24), channel_id=1, source_target_pairs={{0,3},{1,0},{2,1},{3,2},{4,7},{5,4},{6,5},{7,6},{8,11},{9,8},{10,9... | collective-permute-start | bytes 245768 | tf_op jit(solution)/shard_map/ppermute | solution.py:36
  55.8 3.4 %collective-permute-done.6 = f32[8,2560]{1,0:T(8,128)S(1)} collective-permute-done((f32[8,2560]{1,0:T(8,128)S(1)}, f32[8,2560]{1,0:T(8,128)S(1)}, u32[]{:S(2)}, u32[]{:S(2)}) %collective-permute-start.6) | collective-permute-done | bytes 81952 | tf_op jit(solution)/shard_map/ppermute | solution.py:36
  59.8 0.7 reshape.448
  60.4 3.9 %all-to-all-start.1 = ((bf16[8,2,2560]{2,1,0:T(2,128)(2,1)}), bf16[8,2,2560]{2,1,0:T(2,128)(2,1)S(1)}, u32[]{:S(2)}, u32[]{:S(2)}) async-start(bf16[8,2,2560]{2,1,0:T(2,128)(2,1)} %reshape.448), calls=%async_computation.1 | async-start | bytes 163840 | tf_op jit(solution)/shard_map/all_to_all | solution.py:177
  64.3 5.1 %all-to-all-done.1 = bf16[8,2,2560]{2,1,0:T(2,128)(2,1)S(1)} async-done(((bf16[8,2,2560]{2,1,0:T(2,128)(2,1)}), bf16[8,2,2560]{2,1,0:T(2,128)(2,1)S(1)}, u32[]{:S(2)}, u32[]{:S(2)}) %all-to-all-start.1) | async-done | bytes 81952 | tf_op jit(solution)/shard_map/all_to_all | solution.py:177
  69.4 0.8 %select_reduce_fusion = bf16[2,2560]{1,0:T(2,128)(2,1)} fusion(bf16[8,2,2560]{2,1,0:T(2,128)(2,1)S(1)} %all-to-all-done.1, pred[8,2]{1,0:T(8,128)(4,1)S(1)} %iota_compare_fusion.3), kind=kLoop, calls=%fused_computation.21 | loop fusion | flops 117760 | bytes 92176 | tf_op jit(solution)/shard_map/reduce_sum | solution.py:181
  (63 shorter events, 4.7 us)
Async XLA Ops:
  0.0 32.2 %copy-start = (bf16[640,2560]{1,0:T(8,128)(2,1)S(1)}, bf16[640,2560]{1,0:T(8,128)(2,1)}, u32[]{:S(2)}) copy-start(bf16[640,2560]{1,0:T(8,128)(2,1)} %param.23) | copy-start | bytes 9830404
  1.5 10.3 %all-to-all-start = ((bf16[8,2,2560]{2,1,0:T(2,128)(2,1)}), bf16[8,2,2560]{2,1,0:T(2,128)(2,1)S(1)}, u32[]{:S(2)}, u32[]{:S(2)}) async-start(bf16[8,2,2560]{2,1,0:T(2,128)(2,1)} %broadcast_in_dim.92), calls=%async_computation | async-start | bytes 163840 | tf_op jit(solution)/shard_map/all_to_all | solution.py:78
  12.5 11.5 %collective-permute-start = (bf16[8,2560]{1,0:T(8,128)(2,1)S(1)}, bf16[8,2560]{1,0:T(8,128)(2,1)S(1)}, u32[]{:S(2)}, u32[]{:S(2)}) collective-permute-start(bf16[8,2560]{1,0:T(8,128)(2,1)S(1)} %broadcast_select_fusion), channel_id=1, source_target_pairs={{0,2},{1,3},{2,0},{3,1},{4,6},{5,7},{6,4},{7,5},{8,10},{9,11},{10,... | collective-permute-start | bytes 122888 | tf_op jit(solution)/shard_map/ppermute | solution.py:36
  15.1 8.9 %collective-permute-start.1 = (bf16[8,2560]{1,0:T(8,128)(2,1)S(1)}, bf16[8,2560]{1,0:T(8,128)(2,1)S(1)}, u32[]{:S(2)}, u32[]{:S(2)}) collective-permute-start(bf16[8,2560]{1,0:T(8,128)(2,1)S(1)} %broadcast_select_fusion), channel_id=1, source_target_pairs={{0,1},{1,2},{2,3},{3,0},{4,5},{5,6},{6,7},{7,4},{8,9},{9,10},{10,1... | collective-permute-start | bytes 122888 | tf_op jit(solution)/shard_map/ppermute | solution.py:36
  16.7 7.3 %collective-permute-start.2 = (bf16[8,2560]{1,0:T(8,128)(2,1)S(1)}, bf16[8,2560]{1,0:T(8,128)(2,1)S(1)}, u32[]{:S(2)}, u32[]{:S(2)}) collective-permute-start(bf16[8,2560]{1,0:T(8,128)(2,1)S(1)} %broadcast_select_fusion), channel_id=1, source_target_pairs={{0,3},{1,0},{2,1},{3,2},{4,7},{5,4},{6,5},{7,6},{8,11},{9,8},{10,9... | collective-permute-start | bytes 122888 | tf_op jit(solution)/shard_map/ppermute | solution.py:36
  19.1 3.2 %copy-start.1 = (bf16[32,2,80,128]{3,2,1,0:T(8,128)(2,1)S(1)}, bf16[32,2,80,128]{3,2,1,0:T(8,128)(2,1)}, u32[]{:S(2)}) copy-start(bf16[32,2,80,128]{3,2,1,0:T(8,128)(2,1)} %param.20) | copy-start | bytes 3932164
  22.2 1.9 %copy-start.2 = (bf16[2560,160]{0,1:T(8,128)(2,1)S(1)}, bf16[2560,160]{0,1:T(8,128)(2,1)}, u32[]{:S(2)}) copy-start(bf16[2560,160]{0,1:T(8,128)(2,1)} %param.17) | copy-start | bytes 2457604
  27.1 2.6 %copy-start.3 = (bf16[2560,160]{0,1:T(8,128)(2,1)S(1)}, bf16[2560,160]{0,1:T(8,128)(2,1)}, u32[]{:S(2)}) copy-start(bf16[2560,160]{0,1:T(8,128)(2,1)} %param.18) | copy-start | bytes 2457604
  32.8 8.2 %collective-permute-start.3 = (f32[8,2560]{1,0:T(8,128)S(1)}, f32[8,2560]{1,0:T(8,128)S(1)}, u32[]{:S(2)}, u32[]{:S(2)}) collective-permute-start(f32[8,2560]{1,0:T(8,128)S(1)} %fusion.67), channel_id=1, source_target_pairs={{0,2},{1,3},{2,0},{3,1},{4,6},{5,7},{6,4},{7,5},{8,10},{9,11},{10,... | collective-permute-start | bytes 245768 | tf_op jit(solution)/shard_map/ppermute | solution.py:36
  32.8 8.2 %collective-permute-start.4 = (f32[8,2560]{1,0:T(8,128)S(1)}, f32[8,2560]{1,0:T(8,128)}, u32[]{:S(2)}, u32[]{:S(2)}) collective-permute-start(f32[8,2560]{1,0:T(8,128)S(1)} %fusion.67), channel_id=1, source_target_pairs={{0,1},{1,2},{2,3},{3,0},{4,5},{5,6},{6,7},{7,4},{8,9},{9,10},{10,1... | collective-permute-start | bytes 245768 | tf_op jit(solution)/shard_map/ppermute | solution.py:36
  34.1 7.5 %collective-permute-start.5 = (f32[8,2560]{1,0:T(8,128)S(1)}, f32[8,2560]{1,0:T(8,128)}, u32[]{:S(2)}, u32[]{:S(2)}) collective-permute-start(f32[8,2560]{1,0:T(8,128)S(1)} %fusion.67), channel_id=1, source_target_pairs={{0,3},{1,0},{2,1},{3,2},{4,7},{5,4},{6,5},{7,6},{8,11},{9,8},{10,9... | collective-permute-start | bytes 245768 | tf_op jit(solution)/shard_map/ppermute | solution.py:36
  41.0 0.6 copy-start.4
  51.1 8.0 %collective-permute-start.6 = (f32[8,2560]{1,0:T(8,128)S(1)}, f32[8,2560]{1,0:T(8,128)S(1)}, u32[]{:S(2)}, u32[]{:S(2)}) collective-permute-start(f32[8,2560]{1,0:T(8,128)S(1)} %fusion.24), channel_id=1, source_target_pairs={{0,2},{1,3},{2,0},{3,1},{4,6},{5,7},{6,4},{7,5},{8,10},{9,11},{10,... | collective-permute-start | bytes 245768 | tf_op jit(solution)/shard_map/ppermute | solution.py:36
  51.9 7.2 %collective-permute-start.7 = (f32[8,2560]{1,0:T(8,128)S(1)}, f32[8,2560]{1,0:T(8,128)S(1)}, u32[]{:S(2)}, u32[]{:S(2)}) collective-permute-start(f32[8,2560]{1,0:T(8,128)S(1)} %fusion.24), channel_id=1, source_target_pairs={{0,1},{1,2},{2,3},{3,0},{4,5},{5,6},{6,7},{7,4},{8,9},{9,10},{10,1... | collective-permute-start | bytes 245768 | tf_op jit(solution)/shard_map/ppermute | solution.py:36
  53.1 6.0 %collective-permute-start.8 = (f32[8,2560]{1,0:T(8,128)S(1)}, f32[8,2560]{1,0:T(8,128)S(1)}, u32[]{:S(2)}, u32[]{:S(2)}) collective-permute-start(f32[8,2560]{1,0:T(8,128)S(1)} %fusion.24), channel_id=1, source_target_pairs={{0,3},{1,0},{2,1},{3,2},{4,7},{5,4},{6,5},{7,6},{8,11},{9,8},{10,9... | collective-permute-start | bytes 245768 | tf_op jit(solution)/shard_map/ppermute | solution.py:36
  60.4 9.0 %all-to-all-start.1 = ((bf16[8,2,2560]{2,1,0:T(2,128)(2,1)}), bf16[8,2,2560]{2,1,0:T(2,128)(2,1)S(1)}, u32[]{:S(2)}, u32[]{:S(2)}) async-start(bf16[8,2,2560]{2,1,0:T(2,128)(2,1)} %reshape.448), calls=%async_computation.1 | async-start | bytes 163840 | tf_op jit(solution)/shard_map/all_to_all | solution.py:177

commit v13 on v11

--- a/solution.py
+++ b/solution.py
@@ -118,25 +118,25 @@
         .reshape(req_loc, kv_loc, HEAD_SIZE)
     )
 
-    page_list = (served_pages - dp_index * pool_size).reshape(-1)
-    page_hot = (
-        page_list[:, None] == jnp.arange(pool_size, dtype=jnp.int32)[None, :]
-    ).astype(key_page_pool.dtype)
-    key_rows = jnp.einsum(
-        "sq,qhdc->shdc", page_hot, key_page_pool, preferred_element_type=jnp.bfloat16
-    ).reshape((req_loc, per_req) + key_page_pool.shape[1:])
-    value_rows = jnp.einsum(
-        "sq,qhdc->shdc", page_hot, value_page_pool, preferred_element_type=jnp.bfloat16
-    ).reshape((req_loc, per_req) + value_page_pool.shape[1:])
+    page_loc = served_pages - dp_index * pool_size
+    pool_ids = jnp.arange(pool_size, dtype=jnp.int32)
+    match = page_loc[:, :, None] == pool_ids[None, None, :]
+    page_start = jnp.arange(per_req, dtype=jnp.int32)[None, :, None] * page_len
+    offset = jnp.where(
+        jnp.any(match, axis=1),
+        jnp.sum(jnp.where(match, page_start, 0), axis=1),
+        per_req * page_len,
+    )
+    valid_pos = (
+        offset[:, :, None] + jnp.arange(page_len, dtype=jnp.int32)[None, None, :]
+        < served_len[:, None, None]
+    )[:, None, None, :, :]
     scores = (
-        jnp.einsum("rhgd,rphdc->rhgpc", query_srv, key_rows, preferred_element_type=jnp.float32)
+        jnp.einsum(
+            "rhgd,qhdc->rhgqc", query_srv, key_page_pool, preferred_element_type=jnp.float32
+        )
         * score_scale
     )
-    positions = (
-        jnp.arange(per_req, dtype=jnp.int32)[:, None] * page_len
-        + jnp.arange(page_len, dtype=jnp.int32)[None, :]
-    )
-    valid_pos = (positions[None, :, :] < served_len[:, None, None])[:, None, None, :, :]
     own_score = (
         jnp.einsum("rhgd,rhd->rhg", query_srv, key_srv, preferred_element_type=jnp.float32)
         * score_scale
@@ -145,7 +145,7 @@
     weights = jnp.where(valid_pos, jnp.exp(scores - best[..., None, None]), 0.0)
     own_weight = jnp.exp(own_score - best)
     numer = (
-        jnp.einsum("rhgpc,rphdc->rhgd", weights, value_rows.astype(jnp.float32))
+        jnp.einsum("rhgqc,qhdc->rhgd", weights, value_page_pool.astype(jnp.float32))
         + own_weight[..., None] * value_srv.astype(jnp.float32)[:, :, None, :]
     )
     denom = jnp.sum(weights, axis=(-2, -1)) + own_weight

time: 73.6 us -> 71.4 us (0.970)
  matrix products: 22.1 us -> 17.3 us
  other arithmetic: 6.9 us -> 8.31 us
  local copies, waits for them, and re-layouts: 5.45 us -> 6.42 us
    dot_general x4 -> x2, matrix products: 8.71 us -> 3.99 us  [the longest x1 2.19 us: local(): jnp.einsum('rhgqc,qhdc->rhgd', weights, value_page_pool.astype(jnp.float32))]
    all_to_all x1, waiting for transfers between devices: 0.01 us -> 1.55 us  [local(): lax.all_to_all(jnp.broadcast_to(residual_in[None], (dp_count,) + residual...]
    unnamed x16 -> x8, local copies, waits for them, and re-layouts: 0.66 us -> 1.61 us
    convert_element_type x2, other arithmetic: 0.6 us -> 1.39 us  [norm_rows(): gain.astype(jnp.float32)]
    reduce_sum x2, other arithmetic: 1.31 us -> 2.09 us  [norm_rows(): jnp.mean(value_rows * value_rows, axis=-1, keepdims=True) + 1e-05]
    ppermute x9, waiting for transfers between devices: 7.31 us -> 6.54 us  [shifted(): lax.ppermute(value, 'tensor', [(i, (i + k) % tp_count) for i in range(tp_...]
  transfers between devices with their start and end apart: 11 -> 11, of which waited for: 6 -> 9; matrix products, arithmetic and copies ran while one was open for 14% -> 8% of each run, Pallas kernels for 0% -> 0%
where the time goes in v13:
time: 71.4 us; the launch traced here: 70.7 us
  starting transfers between devices  25.4 us (36%)
  matrix products  17.3 us (24%)
  waiting for transfers between devices  13.1 us (18%)
  other arithmetic  8.31 us (12%)
  local copies, waits for them, and re-layouts  6.42 us (9%)
    ppermute x9, starting transfers between devices, shifted(): lax.ppermute(value, 'tensor', [(i, (i + k) % tp_count) for i in range(tp_...  16.8 us
    ppermute x9, waiting for transfers between devices, shifted(): lax.ppermute(value, 'tensor', [(i, (i + k) % tp_count) for i in range(tp_...  6.54 us
    dot_general x1, matrix products, local(): jnp.dot(hidden, w_down, preferred_element_type=jnp.float32)  5.29 us
    all_to_all x1, starting transfers between devices, local(): lax.all_to_all(jnp.broadcast_to(residual_in[None], (dp_count,) + residual...  5.17 us
    all_to_all x1, waiting for transfers between devices, local(): incoming = lax.all_to_all(outgoing, 'dp', 0, 0)  5.02 us
    all_to_all x1, starting transfers between devices, local(): incoming = lax.all_to_all(outgoing, 'dp', 0, 0)  3.36 us
    dot_general x1, matrix products, local(): gate_act = jnp.dot(normed_mlp, w_gate, preferred_element_type=jnp.float32)  3.05 us
    dot_general x1, matrix products, local(): jnp.dot(scaled_input, w_query, preferred_element_type=jnp.float32)  2.51 us
  transfers between devices with their start and end apart: 11, of which 9 were waited for; matrix products, arithmetic and copies ran while one was open for 8% of the time, Pallas kernels for 0%

profile of v13, /device:TPU:0, one launch (start us, length us, event | category | flops | bytes accessed | tf_op | source)
XLA Modules:
  0.0 70.7 jit_solution(11911109177196418813)
XLA Ops:
  0.0 1.5 %broadcast_in_dim.161 = bf16[8,2,2560]{2,1,0:T(2,128)(2,1)} broadcast(bf16[2,2560]{1,0:T(2,128)(2,1)} %param.14), dimensions={1,2} | broadcast | bytes 92160 | tf_op jit(solution)/shard_map/broadcast_in_dim | solution.py:79
  1.5 5.2 %all-to-all-start = ((bf16[8,2,2560]{2,1,0:T(2,128)(2,1)}), bf16[8,2,2560]{2,1,0:T(2,128)(2,1)S(1)}, u32[]{:S(2)}, u32[]{:S(2)}) async-start(bf16[8,2,2560]{2,1,0:T(2,128)(2,1)} %broadcast_in_dim.161), calls=%async_computation | async-start | bytes 163840 | tf_op jit(solution)/shard_map/all_to_all | solution.py:78
  6.7 0.7 iota_add_fusion.1
  7.6 0.8 %select_reduce_fusion.5 = (s32[8]{0:T(128)S(1)}, s32[8]{0:T(128)S(1)}) fusion(s32[64]{0:T(128)} %param.21, s32[64]{0:T(128)S(1)} %get-tuple-element.15, pred[64]{0:T(512)(128)(4,1)S(1)} %get-tuple-element.13), kind=kLoop, calls=%fused_computation.67 | loop fusion | flops 3056 | bytes 640 | tf_op jit(solution)/shard_map/reduce_sum | solution.py:91
  8.4 0.8 %select_reduce_fusion.3 = s32[8,4]{0,1:T(4,128)S(1)} fusion(s32[64,4]{0,1:T(4,128)} %param.22, pred[8,64]{1,0:T(8,128)(4,1)S(1)} %fusion.37), kind=kLoop, calls=%fused_computation.49 | loop fusion | flops 4064 | bytes 1664 | tf_op jit(solution)/shard_map/reduce_sum | solution.py:92
  10.2 1.6 %all-to-all-done = bf16[8,2,2560]{2,1,0:T(2,128)(2,1)S(1)} async-done(((bf16[8,2,2560]{2,1,0:T(2,128)(2,1)}), bf16[8,2,2560]{2,1,0:T(2,128)(2,1)S(1)}, u32[]{:S(2)}, u32[]{:S(2)}) %all-to-all-start) | async-done | bytes 81952 | tf_op jit(solution)/shard_map/all_to_all | solution.py:78
  12.5 2.6 %collective-permute-start = (bf16[8,2560]{1,0:T(8,128)(2,1)S(1)}, bf16[8,2560]{1,0:T(8,128)(2,1)S(1)}, u32[]{:S(2)}, u32[]{:S(2)}) collective-permute-start(bf16[8,2560]{1,0:T(8,128)(2,1)S(1)} %broadcast_select_fusion), channel_id=1, source_target_pairs={{0,2},{1,3},{2,0},{3,1},{4,6},{5,7},{6,4},{7,5},{8,10},{9,11},{10,... | collective-permute-start | bytes 122888 | tf_op jit(solution)/shard_map/ppermute | solution.py:36
  15.1 1.6 %collective-permute-start.1 = (bf16[8,2560]{1,0:T(8,128)(2,1)S(1)}, bf16[8,2560]{1,0:T(8,128)(2,1)S(1)}, u32[]{:S(2)}, u32[]{:S(2)}) collective-permute-start(bf16[8,2560]{1,0:T(8,128)(2,1)S(1)} %broadcast_select_fusion), channel_id=1, source_target_pairs={{0,1},{1,2},{2,3},{3,0},{4,5},{5,6},{6,7},{7,4},{8,9},{9,10},{10,1... | collective-permute-start | bytes 122888 | tf_op jit(solution)/shard_map/ppermute | solution.py:36
  16.7 2.2 %collective-permute-start.2 = (bf16[8,2560]{1,0:T(8,128)(2,1)S(1)}, bf16[8,2560]{1,0:T(8,128)(2,1)}, u32[]{:S(2)}, u32[]{:S(2)}) collective-permute-start(bf16[8,2560]{1,0:T(8,128)(2,1)S(1)} %broadcast_select_fusion), channel_id=1, source_target_pairs={{0,3},{1,0},{2,1},{3,2},{4,7},{5,4},{6,5},{7,6},{8,11},{9,8},{10,9... | collective-permute-start | bytes 122888 | tf_op jit(solution)/shard_map/ppermute | solution.py:36
  18.9 0.7 convert_element_type.64
  19.6 0.7 convert_element_type.72
  21.2 1.0 %fusion.23 = (f32[8]{0:T(128)S(1)}, bf16[8,2560]{1,0:T(8,128)(2,1)S(1)}) fusion(bf16[8,2560]{1,0:T(8,128)(2,1)S(1)} %collective-permute-done.1, bf16[8,2560]{1,0:T(8,128)(2,1)} %collective-permute-done.2, bf16[8,2560]{1,0:T(8,128)(2,1)S(1)} %collective-permute-done, bf16[8,2560]{1,0:T(8,128)(2,1)S(1)} %gather_fusion.1, pred[8]{0:T(512)(128)(4,1)S(1)} %fusion.48), kind=kLoop, calls=%fused_computation.28 | loop fusion | flops 143352 | bytes 204840 | tf_op jit(solution)/shard_map/reduce_sum | solution.py:13
  22.2 1.5 %fusion.53 = f32[8,160]{1,0:T(8,128)S(1)} fusion(bf16[2560,160]{0,1:T(8,128)(2,1)} %param.17, bf16[8,2560]{1,0:T(8,128)(2,1)S(1)} %get-tuple-element.12, f32[2560]{0:T(1024)S(1)} %convert_element_type.64, f32[8]{0:T(128)S(1)} %add_rsqrt_fusion.1), kind=kOutput, calls=%fused_computation.121 | convolution fusion | flops 6635520 | bytes 875552 | tf_op jit(solution)/shard_map/dot_general | solution.py:110
  23.8 2.5 %fusion.55 = f32[8,640]{1,0:T(8,128)S(1)} fusion(bf16[2560,640]{1,0:T(8,128)(2,1)} %param.16, bf16[8,2560]{1,0:T(8,128)(2,1)S(1)} %get-tuple-element.12, f32[2560]{0:T(1024)S(1)} %convert_element_type.64, f32[8]{0:T(128)S(1)} %add_rsqrt_fusion.1), kind=kOutput, calls=%fused_computation.122 | convolution fusion | flops 26296320 | bytes 3348512 | tf_op jit(solution)/shard_map/dot_general | solution.py:101
  27.0 1.8 %select_reduce_fusion = (f32[8,2,4]{0,2,1:T(4,128)S(1)}, f32[8,2,4,32,128]{4,0,3,2,1:T(8,128)S(1)}) fusion(pred[8,32,128]{2,0,1:T(8,128)(4,1)S(1)} %add_compare_fusion, bf16[8,2,4,80]{3,0,2,1:T(8,128)(2,1)S(1)} %pad_maximum_fusion, bf16[32,2,80,128]{3,2,1,0:T(8,128)(2,1)} %param.19), kind=kOutput, calls=%fused_computation.18 | convolution fusion | flops 42729408 | bytes 2402560 | tf_op jit(solution)/shard_map/rhgd,qhdc->rhgqc/dot_general | solution.py:135
  28.8 1.0 %copy-done.1 = f32[8,2,4,32,128]{4,0,3,2,1:T(8,128)} copy-done((f32[8,2,4,32,128]{4,0,3,2,1:T(8,128)}, f32[8,2,4,32,128]{4,0,3,2,1:T(8,128)S(1)}, u32[]{:S(2)}) %copy-start.1) | copy-done | bytes 1048600
  30.6 2.2 %fusion.13 = bf16[8,2,4,80]{3,0,2,1:T(8,128)(2,1)S(1)} fusion(f32[8,2,4,32,128]{4,0,3,2,1:T(8,128)} %copy-done.1, f32[8,2,4]{0,2,1:T(4,128)S(1)} %fusion.38, pred[8,32,128]{2,0,1:T(8,128)(4,1)S(1)} %add_compare_fusion, f32[8,2,4]{0,2,1:T(4,128)S(1)} %get-tuple-element.9, f32[8,2,80]{2,0,1:T(8,128)S(1)} %copy.33, f32[8,2,4]{0,2,1:T(4,128)S(1)} %get-tuple-element.10, ...), kind=kOutput, calls=%fused_computation.12 | convolution fusion | flops 42487808 | bytes 2408192 | tf_op jit(solution)/shard_map/rhgqc,qhdc->rhgd/dot_general | solution.py:148
  33.4 0.8 %collective-permute-start.3 = (f32[8,2560]{1,0:T(8,128)S(1)}, f32[8,2560]{1,0:T(8,128)S(1)}, u32[]{:S(2)}, u32[]{:S(2)}) collective-permute-start(f32[8,2560]{1,0:T(8,128)S(1)} %fusion.58), channel_id=1, source_target_pairs={{0,2},{1,3},{2,0},{3,1},{4,6},{5,7},{6,4},{7,5},{8,10},{9,11},{10,... | collective-permute-start | bytes 245768 | tf_op jit(solution)/shard_map/ppermute | solution.py:36
  34.2 3.4 %collective-permute-start.4 = (f32[8,2560]{1,0:T(8,128)S(1)}, f32[8,2560]{1,0:T(8,128)}, u32[]{:S(2)}, u32[]{:S(2)}) collective-permute-start(f32[8,2560]{1,0:T(8,128)S(1)} %fusion.58), channel_id=1, source_target_pairs={{0,1},{1,2},{2,3},{3,0},{4,5},{5,6},{6,7},{7,4},{8,9},{9,10},{10,1... | collective-permute-start | bytes 245768 | tf_op jit(solution)/shard_map/ppermute | solution.py:36
  38.7 2.5 %collective-permute-done.3 = f32[8,2560]{1,0:T(8,128)S(1)} collective-permute-done((f32[8,2560]{1,0:T(8,128)S(1)}, f32[8,2560]{1,0:T(8,128)S(1)}, u32[]{:S(2)}, u32[]{:S(2)}) %collective-permute-start.3) | collective-permute-done | bytes 81952 | tf_op jit(solution)/shard_map/ppermute | solution.py:36
  42.2 1.1 %multiply_reduce_fusion = (f32[8]{0:T(128)S(1)}, f32[8,2560]{1,0:T(8,128)S(1)}) fusion(f32[8,2560]{1,0:T(8,128)} %collective-permute-done.4, f32[8,2560]{1,0:T(8,128)} %collective-permute-done.5, f32[8,2560]{1,0:T(8,128)S(1)} %fusion.58, f32[8,2560]{1,0:T(8,128)} %copy-done.3, bf16[8,2560]{1,0:T(8,128)(2,1)S(1)} %get-tuple-element.12), kind=kLoop, calls=%fused_computation.33 | loop fusion | flops 143352 | bytes 450592 | tf_op jit(solution)/shard_map/reduce_sum | solution.py:13
  43.3 3.0 %fusion.51 = f32[8,896]{1,0:T(8,128)S(1)} fusion(bf16[2560,896]{1,0:T(8,128)(2,1)} %param.25, f32[8,2560]{1,0:T(8,128)S(1)} %get-tuple-element.8, f32[2560]{0:T(1024)S(1)} %convert_element_type.72, f32[8]{0:T(128)S(1)} %add_rsqrt_fusion), kind=kOutput, calls=%fused_computation.120 | convolution fusion | flops 36761600 | bytes 4708384 | tf_op jit(solution)/shard_map/dot_general | solution.py:159
  46.3 5.3 %fusion.17 = f32[8,2560]{1,0:T(8,128)S(1)} fusion(bf16[896,2560]{1,0:T(8,128)(2,1)} %param.27, bf16[2560,896]{1,0:T(8,128)(2,1)} %param.26, f32[8,896]{1,0:T(8,128)S(1)} %fusion.51, f32[8,2560]{1,0:T(8,128)S(1)} %get-tuple-element.8, f32[2560]{0:T(1024)S(1)} %convert_element_type.72, f32[8]{0:T(128)S(1)} %add_rsqrt_fusion), kind=kOutput, calls=%fused_computation.14 | convolution fusion | flops 73504768 | bytes 9377824 | tf_op jit(solution)/shard_map/dot_general | solution.py:163
  51.6 2.0 %collective-permute-start.6 = (f32[8,2560]{1,0:T(8,128)S(1)}, f32[8,2560]{1,0:T(8,128)S(1)}, u32[]{:S(2)}, u32[]{:S(2)}) collective-permute-start(f32[8,2560]{1,0:T(8,128)S(1)} %fusion.17), channel_id=1, source_target_pairs={{0,2},{1,3},{2,0},{3,1},{4,6},{5,7},{6,4},{7,5},{8,10},{9,11},{10,... | collective-permute-start | bytes 245768 | tf_op jit(solution)/shard_map/ppermute | solution.py:36
  53.6 1.4 %collective-permute-start.7 = (f32[8,2560]{1,0:T(8,128)S(1)}, f32[8,2560]{1,0:T(8,128)S(1)}, u32[]{:S(2)}, u32[]{:S(2)}) collective-permute-start(f32[8,2560]{1,0:T(8,128)S(1)} %fusion.17), channel_id=1, source_target_pairs={{0,1},{1,2},{2,3},{3,0},{4,5},{5,6},{6,7},{7,4},{8,9},{9,10},{10,1... | collective-permute-start | bytes 245768 | tf_op jit(solution)/shard_map/ppermute | solution.py:36
  55.0 2.4 %collective-permute-start.8 = (f32[8,2560]{1,0:T(8,128)S(1)}, f32[8,2560]{1,0:T(8,128)S(1)}, u32[]{:S(2)}, u32[]{:S(2)}) collective-permute-start(f32[8,2560]{1,0:T(8,128)S(1)} %fusion.17), channel_id=1, source_target_pairs={{0,3},{1,0},{2,1},{3,2},{4,7},{5,4},{6,5},{7,6},{8,11},{9,8},{10,9... | collective-permute-start | bytes 245768 | tf_op jit(solution)/shard_map/ppermute | solution.py:36
  57.4 1.1 %collective-permute-done.6 = f32[8,2560]{1,0:T(8,128)S(1)} collective-permute-done((f32[8,2560]{1,0:T(8,128)S(1)}, f32[8,2560]{1,0:T(8,128)S(1)}, u32[]{:S(2)}, u32[]{:S(2)}) %collective-permute-start.6) | collective-permute-done | bytes 81952 | tf_op jit(solution)/shard_map/ppermute | solution.py:36
  58.5 1.5 %collective-permute-done.7 = f32[8,2560]{1,0:T(8,128)S(1)} collective-permute-done((f32[8,2560]{1,0:T(8,128)S(1)}, f32[8,2560]{1,0:T(8,128)S(1)}, u32[]{:S(2)}, u32[]{:S(2)}) %collective-permute-start.7) | collective-permute-done | bytes 81952 | tf_op jit(solution)/shard_map/ppermute | solution.py:36
  60.9 0.7 reshape.431
  61.6 3.4 %all-to-all-start.1 = ((bf16[8,2,2560]{2,1,0:T(2,128)(2,1)}), bf16[8,2,2560]{2,1,0:T(2,128)(2,1)S(1)}, u32[]{:S(2)}, u32[]{:S(2)}) async-start(bf16[8,2,2560]{2,1,0:T(2,128)(2,1)} %reshape.431), calls=%async_computation.1 | async-start | bytes 163840 | tf_op jit(solution)/shard_map/all_to_all | solution.py:176
  65.0 5.0 %all-to-all-done.1 = bf16[8,2,2560]{2,1,0:T(2,128)(2,1)S(1)} async-done(((bf16[8,2,2560]{2,1,0:T(2,128)(2,1)}), bf16[8,2,2560]{2,1,0:T(2,128)(2,1)S(1)}, u32[]{:S(2)}, u32[]{:S(2)}) %all-to-all-start.1) | async-done | bytes 81952 | tf_op jit(solution)/shard_map/all_to_all | solution.py:176
  70.0 0.8 %select_reduce_fusion.1 = bf16[2,2560]{1,0:T(2,128)(2,1)} fusion(bf16[8,2,2560]{2,1,0:T(2,128)(2,1)S(1)} %all-to-all-done.1, pred[8,2]{1,0:T(8,128)(4,1)S(1)} %iota_compare_fusion.3), kind=kLoop, calls=%fused_computation.23 | loop fusion | flops 117760 | bytes 92176 | tf_op jit(solution)/shard_map/reduce_sum | solution.py:180
  (66 shorter events, 8.0 us)
Async XLA Ops:
  0.0 32.9 %copy-start = (bf16[640,2560]{1,0:T(8,128)(2,1)S(1)}, bf16[640,2560]{1,0:T(8,128)(2,1)}, u32[]{:S(2)}) copy-start(bf16[640,2560]{1,0:T(8,128)(2,1)} %param.23) | copy-start | bytes 9830404
  1.5 10.3 %all-to-all-start = ((bf16[8,2,2560]{2,1,0:T(2,128)(2,1)}), bf16[8,2,2560]{2,1,0:T(2,128)(2,1)S(1)}, u32[]{:S(2)}, u32[]{:S(2)}) async-start(bf16[8,2,2560]{2,1,0:T(2,128)(2,1)} %broadcast_in_dim.161), calls=%async_computation | async-start | bytes 163840 | tf_op jit(solution)/shard_map/all_to_all | solution.py:78
  12.5 7.9 %collective-permute-start = (bf16[8,2560]{1,0:T(8,128)(2,1)S(1)}, bf16[8,2560]{1,0:T(8,128)(2,1)S(1)}, u32[]{:S(2)}, u32[]{:S(2)}) collective-permute-start(bf16[8,2560]{1,0:T(8,128)(2,1)S(1)} %broadcast_select_fusion), channel_id=1, source_target_pairs={{0,2},{1,3},{2,0},{3,1},{4,6},{5,7},{6,4},{7,5},{8,10},{9,11},{10,... | collective-permute-start | bytes 122888 | tf_op jit(solution)/shard_map/ppermute | solution.py:36
  15.1 5.9 %collective-permute-start.1 = (bf16[8,2560]{1,0:T(8,128)(2,1)S(1)}, bf16[8,2560]{1,0:T(8,128)(2,1)S(1)}, u32[]{:S(2)}, u32[]{:S(2)}) collective-permute-start(bf16[8,2560]{1,0:T(8,128)(2,1)S(1)} %broadcast_select_fusion), channel_id=1, source_target_pairs={{0,1},{1,2},{2,3},{3,0},{4,5},{5,6},{6,7},{7,4},{8,9},{9,10},{10,1... | collective-permute-start | bytes 122888 | tf_op jit(solution)/shard_map/ppermute | solution.py:36
  16.7 4.5 %collective-permute-start.2 = (bf16[8,2560]{1,0:T(8,128)(2,1)S(1)}, bf16[8,2560]{1,0:T(8,128)(2,1)}, u32[]{:S(2)}, u32[]{:S(2)}) collective-permute-start(bf16[8,2560]{1,0:T(8,128)(2,1)S(1)} %broadcast_select_fusion), channel_id=1, source_target_pairs={{0,3},{1,0},{2,1},{3,2},{4,7},{5,4},{6,5},{7,6},{8,11},{9,8},{10,9... | collective-permute-start | bytes 122888 | tf_op jit(solution)/shard_map/ppermute | solution.py:36
  27.0 3.2 %copy-start.2 = (bf16[2560,160]{0,1:T(8,128)(2,1)S(1)}, bf16[2560,160]{0,1:T(8,128)(2,1)}, u32[]{:S(2)}) copy-start(bf16[2560,160]{0,1:T(8,128)(2,1)} %param.18) | copy-start | bytes 2457604
  28.8 1.0 %copy-start.1 = (f32[8,2,4,32,128]{4,0,3,2,1:T(8,128)}, f32[8,2,4,32,128]{4,0,3,2,1:T(8,128)S(1)}, u32[]{:S(2)}) copy-start(f32[8,2,4,32,128]{4,0,3,2,1:T(8,128)S(1)} %get-tuple-element.23) | copy-start | bytes 3145732
  33.4 7.7 %collective-permute-start.3 = (f32[8,2560]{1,0:T(8,128)S(1)}, f32[8,2560]{1,0:T(8,128)S(1)}, u32[]{:S(2)}, u32[]{:S(2)}) collective-permute-start(f32[8,2560]{1,0:T(8,128)S(1)} %fusion.58), channel_id=1, source_target_pairs={{0,2},{1,3},{2,0},{3,1},{4,6},{5,7},{6,4},{7,5},{8,10},{9,11},{10,... | collective-permute-start | bytes 245768 | tf_op jit(solution)/shard_map/ppermute | solution.py:36
  34.2 7.0 %collective-permute-start.4 = (f32[8,2560]{1,0:T(8,128)S(1)}, f32[8,2560]{1,0:T(8,128)}, u32[]{:S(2)}, u32[]{:S(2)}) collective-permute-start(f32[8,2560]{1,0:T(8,128)S(1)} %fusion.58), channel_id=1, source_target_pairs={{0,1},{1,2},{2,3},{3,0},{4,5},{5,6},{6,7},{7,4},{8,9},{9,10},{10,1... | collective-permute-start | bytes 245768 | tf_op jit(solution)/shard_map/ppermute | solution.py:36
  37.6 4.5 %collective-permute-start.5 = (f32[8,2560]{1,0:T(8,128)S(1)}, f32[8,2560]{1,0:T(8,128)}, u32[]{:S(2)}, u32[]{:S(2)}) collective-permute-start(f32[8,2560]{1,0:T(8,128)S(1)} %fusion.58), channel_id=1, source_target_pairs={{0,3},{1,0},{2,1},{3,2},{4,7},{5,4},{6,5},{7,6},{8,11},{9,8},{10,9... | collective-permute-start | bytes 245768 | tf_op jit(solution)/shard_map/ppermute | solution.py:36
  41.2 0.6 copy-start.3
  51.6 6.9 %collective-permute-start.6 = (f32[8,2560]{1,0:T(8,128)S(1)}, f32[8,2560]{1,0:T(8,128)S(1)}, u32[]{:S(2)}, u32[]{:S(2)}) collective-permute-start(f32[8,2560]{1,0:T(8,128)S(1)} %fusion.17), channel_id=1, source_target_pairs={{0,2},{1,3},{2,0},{3,1},{4,6},{5,7},{6,4},{7,5},{8,10},{9,11},{10,... | collective-permute-start | bytes 245768 | tf_op jit(solution)/shard_map/ppermute | solution.py:36
  53.6 6.4 %collective-permute-start.7 = (f32[8,2560]{1,0:T(8,128)S(1)}, f32[8,2560]{1,0:T(8,128)S(1)}, u32[]{:S(2)}, u32[]{:S(2)}) collective-permute-start(f32[8,2560]{1,0:T(8,128)S(1)} %fusion.17), channel_id=1, source_target_pairs={{0,1},{1,2},{2,3},{3,0},{4,5},{5,6},{6,7},{7,4},{8,9},{9,10},{10,1... | collective-permute-start | bytes 245768 | tf_op jit(solution)/shard_map/ppermute | solution.py:36
  55.0 5.3 %collective-permute-start.8 = (f32[8,2560]{1,0:T(8,128)S(1)}, f32[8,2560]{1,0:T(8,128)S(1)}, u32[]{:S(2)}, u32[]{:S(2)}) collective-permute-start(f32[8,2560]{1,0:T(8,128)S(1)} %fusion.17), channel_id=1, source_target_pairs={{0,3},{1,0},{2,1},{3,2},{4,7},{5,4},{6,5},{7,6},{8,11},{9,8},{10,9... | collective-permute-start | bytes 245768 | tf_op jit(solution)/shard_map/ppermute | solution.py:36
  61.6 8.4 %all-to-all-start.1 = ((bf16[8,2,2560]{2,1,0:T(2,128)(2,1)}), bf16[8,2,2560]{2,1,0:T(2,128)(2,1)S(1)}, u32[]{:S(2)}, u32[]{:S(2)}) async-start(bf16[8,2,2560]{2,1,0:T(2,128)(2,1)} %reshape.431), calls=%async_computation.1 | async-start | bytes 163840 | tf_op jit(solution)/shard_map/all_to_all | solution.py:176

commit v14 on v12

--- a/solution.py
+++ b/solution.py
@@ -94,6 +94,7 @@
     owner_tp = (served % req_loc) // rows_loc
     held = rows_dp[served // req_loc, served % rows_loc]
     held = jnp.where((owner_tp == tp_index)[:, None], held, jnp.zeros_like(held))
+    early_pages = served_pages
     held, served_pages = lax.optimization_barrier((held, served_pages))
     rows_srv = tensor_allreduce(held, tp_count)
     scaled_input = norm_rows(rows_srv, norm_gain).astype(jnp.bfloat16)
@@ -126,8 +127,12 @@
     key_rows = jnp.einsum(
         "sq,qhdc->shdc", page_hot, key_page_pool, preferred_element_type=jnp.bfloat16
     ).reshape((req_loc, per_req) + key_page_pool.shape[1:])
+    early_hot = (
+        (early_pages - dp_index * pool_size).reshape(-1)[:, None]
+        == jnp.arange(pool_size, dtype=jnp.int32)[None, :]
+    ).astype(value_page_pool.dtype)
     value_rows = jnp.einsum(
-        "sq,qhdc->shdc", page_hot, value_page_pool, preferred_element_type=jnp.bfloat16
+        "sq,qhdc->shdc", early_hot, value_page_pool, preferred_element_type=jnp.bfloat16
     ).reshape((req_loc, per_req) + value_page_pool.shape[1:])
     scores = (
         jnp.einsum("rhgd,rphdc->rhgpc", query_srv, key_rows, preferred_element_type=jnp.float32)

time: 70.7 us -> 72.3 us (1.023)
  matrix products: 20.9 us -> 22.2 us
    dot_general x1, matrix products: 1.72 us -> 3.03 us  [local(): jnp.einsum('sq,qhdc->shdc', early_hot, value_page_pool, preferred_element...]
  transfers between devices with their start and end apart: 11 -> 11, of which waited for: 4 -> 4; matrix products, arithmetic and copies ran while one was open for 15% -> 17% of each run, Pallas kernels for 0% -> 0%
where the time goes in v14:
time: 72.3 us; the launch traced here: 71.6 us
  starting transfers between devices  24.1 us (33%)
  matrix products  22.2 us (31%)
  waiting for transfers between devices  12.5 us (17%)
  other arithmetic  7.14 us (10%)
  local copies, waits for them, and re-layouts  5.59 us (8%)
    ppermute x9, starting transfers between devices, shifted(): lax.ppermute(value, 'tensor', [(i, (i + k) % tp_count) for i in range(tp_...  15.5 us
    ppermute x9, waiting for transfers between devices, shifted(): lax.ppermute(value, 'tensor', [(i, (i + k) % tp_count) for i in range(tp_...  7.45 us
    dot_general x1, matrix products, local(): jnp.dot(hidden, w_down, preferred_element_type=jnp.float32)  5.29 us
    all_to_all x1, starting transfers between devices, local(): lax.all_to_all(jnp.broadcast_to(residual_in[None], (dp_count,) + residual...  5.17 us
    all_to_all x1, waiting for transfers between devices, local(): incoming = lax.all_to_all(outgoing, 'dp', 0, 0)  5.02 us
    all_to_all x1, starting transfers between devices, local(): incoming = lax.all_to_all(outgoing, 'dp', 0, 0)  3.36 us
    dot_general x1, matrix products, local(): jnp.einsum('sq,qhdc->shdc', page_hot, key_page_pool, preferred_element_ty...  3.12 us
    dot_general x1, matrix products, local(): gate_act = jnp.dot(normed_mlp, w_gate, preferred_element_type=jnp.float32)  3.05 us
  transfers between devices with their start and end apart: 11, of which 4 were waited for; matrix products, arithmetic and copies ran while one was open for 17% of the time, Pallas kernels for 0%

profile of v14, /device:TPU:0, one launch (start us, length us, event | category | flops | bytes accessed | tf_op | source)
XLA Modules:
  0.0 71.6 jit_solution(10458016611626466305)
XLA Ops:
  0.0 1.5 %broadcast_in_dim.92 = bf16[8,2,2560]{2,1,0:T(2,128)(2,1)} broadcast(bf16[2,2560]{1,0:T(2,128)(2,1)} %param.14), dimensions={1,2} | broadcast | bytes 92160 | tf_op jit(solution)/shard_map/broadcast_in_dim | solution.py:79
  1.5 5.2 %all-to-all-start = ((bf16[8,2,2560]{2,1,0:T(2,128)(2,1)}), bf16[8,2,2560]{2,1,0:T(2,128)(2,1)S(1)}, u32[]{:S(2)}, u32[]{:S(2)}) async-start(bf16[8,2,2560]{2,1,0:T(2,128)(2,1)} %broadcast_in_dim.92), calls=%async_computation | async-start | bytes 163840 | tf_op jit(solution)/shard_map/all_to_all | solution.py:78
  6.7 0.7 iota_add_fusion.2
  7.6 0.8 %select_reduce_fusion.4 = (s32[8]{0:T(128)S(1)}, s32[8]{0:T(128)S(1)}) fusion(s32[64]{0:T(128)} %param.21, s32[64]{0:T(128)S(1)} %get-tuple-element.19, pred[64]{0:T(512)(128)(4,1)S(1)} %get-tuple-element.17), kind=kLoop, calls=%fused_computation.73 | loop fusion | flops 3056 | bytes 640 | tf_op jit(solution)/shard_map/reduce_sum | solution.py:91
  8.5 0.7 convert_element_type.66
  9.3 0.8 %select_reduce_fusion.2 = s32[8,4]{0,1:T(4,128)S(1)} fusion(s32[64,4]{0,1:T(4,128)} %param.22, pred[8,64]{1,0:T(8,128)(4,1)S(1)} %fusion.48), kind=kLoop, calls=%fused_computation.51 | loop fusion | flops 4064 | bytes 1664 | tf_op jit(solution)/shard_map/reduce_sum | solution.py:92
  10.3 0.7 convert_element_type.74
  11.6 3.0 %fusion.2 = bf16[32,2,80,128]{3,0,2,1:T(8,128)(2,1)} fusion(bf16[32,2,80,128]{3,2,1,0:T(8,128)(2,1)} %param.20, s32[32]{0:T(128)S(1)} %sub.66), kind=kOutput, calls=%fused_computation.5 | convolution fusion | flops 41944064 | bytes 2621568 | tf_op jit(solution)/shard_map/sq,qhdc->shdc/dot_general | solution.py:134
  14.7 0.6 gather_fusion.1
  15.4 2.6 %collective-permute-start = (bf16[8,2560]{1,0:T(8,128)(2,1)S(1)}, bf16[8,2560]{1,0:T(8,128)(2,1)S(1)}, u32[]{:S(2)}, u32[]{:S(2)}) collective-permute-start(bf16[8,2560]{1,0:T(8,128)(2,1)S(1)} %broadcast_select_fusion), channel_id=1, source_target_pairs={{0,2},{1,3},{2,0},{3,1},{4,6},{5,7},{6,4},{7,5},{8,10},{9,11},{10,... | collective-permute-start | bytes 122888 | tf_op jit(solution)/shard_map/ppermute | solution.py:36
  18.0 1.6 %collective-permute-start.1 = (bf16[8,2560]{1,0:T(8,128)(2,1)S(1)}, bf16[8,2560]{1,0:T(8,128)(2,1)S(1)}, u32[]{:S(2)}, u32[]{:S(2)}) collective-permute-start(bf16[8,2560]{1,0:T(8,128)(2,1)S(1)} %broadcast_select_fusion), channel_id=1, source_target_pairs={{0,1},{1,2},{2,3},{3,0},{4,5},{5,6},{6,7},{7,4},{8,9},{9,10},{10,1... | collective-permute-start | bytes 122888 | tf_op jit(solution)/shard_map/ppermute | solution.py:36
  19.6 2.2 %collective-permute-start.2 = (bf16[8,2560]{1,0:T(8,128)(2,1)S(1)}, bf16[8,2560]{1,0:T(8,128)(2,1)S(1)}, u32[]{:S(2)}, u32[]{:S(2)}) collective-permute-start(bf16[8,2560]{1,0:T(8,128)(2,1)S(1)} %broadcast_select_fusion), channel_id=1, source_target_pairs={{0,3},{1,0},{2,1},{3,2},{4,7},{5,4},{6,5},{7,6},{8,11},{9,8},{10,9... | collective-permute-start | bytes 122888 | tf_op jit(solution)/shard_map/ppermute | solution.py:36
  22.0 3.1 %fusion.6 = bf16[32,2,80,128]{3,0,2,1:T(8,128)(2,1)} fusion(bf16[32,2,80,128]{3,2,1,0:T(8,128)(2,1)} %param.19, s32[32]{0:T(128)S(1)} %eq.121), kind=kOutput, calls=%fused_computation.9 | convolution fusion | flops 41944064 | bytes 2621568 | tf_op jit(solution)/shard_map/sq,qhdc->shdc/dot_general | solution.py:127
  25.7 2.5 %fusion.65 = f32[8,640]{1,0:T(8,128)S(1)} fusion(bf16[2560,640]{1,0:T(8,128)(2,1)} %param.16, bf16[8,2560]{1,0:T(8,128)(2,1)S(1)} %get-tuple-element.16, f32[2560]{0:T(1024)S(1)} %convert_element_type.66, f32[8]{0:T(128)S(1)} %add_rsqrt_fusion.1), kind=kOutput, calls=%fused_computation.128 | convolution fusion | flops 26296320 | bytes 3348512 | tf_op jit(solution)/shard_map/dot_general | solution.py:103
  28.8 1.9 %select_reduce_fusion.1 = (f32[8,2,4]{2,1,0:T(2,128)S(1)}, f32[8,2,4,4,128]{4,2,3,1,0:T(4,128)S(1)}) fusion(pred[8,4,128]{2,1,0:T(4,128)(4,1)S(1)} %broadcast_compare_fusion, bf16[8,4,2,80,128]{4,1,0,3,2:T(4,128)(2,1)} %bitcast.64, bf16[8,2,4,40]{3,2,1,0:T(4,128)(2,1)S(1)} %bitcast.70, bf16[8,2,4,40]{3,2,1,0:T(4,128)(2,1)S(1)} %bitcast.68), kind=kOutput, calls=%fused_computation.23 | convolution fusion | flops 5361600 | bytes 1456384 | tf_op jit(solution)/shard_map/rhgd,rphdc->rhgpc/dot_general | solution.py:138
  31.4 1.9 %fusion.20 = bf16[8,2,4,80]{3,2,1,0:T(4,128)(2,1)S(1)} fusion(bf16[8,4,2,80,128]{4,1,0,3,2:T(4,128)(2,1)} %bitcast.63, f32[8,2,4,4,128]{4,2,3,1,0:T(4,128)S(1)} %get-tuple-element.27, f32[8,2,4]{2,1,0:T(2,128)S(1)} %multiply_maximum_fusion, pred[8,4,128]{2,1,0:T(4,128)(4,1)S(1)} %broadcast_compare_fusion, f32[8,2,4]{2,1,0:T(2,128)S(1)} %get-tuple-element.13, ...), kind=kOutput, calls=%fused_computation.16 | convolution fusion | flops 5328896 | bytes 1462016 | tf_op jit(solution)/shard_map/rhgpc,rphdc->rhgd/dot_general | solution.py:154
  33.9 3.1 %collective-permute-start.4 = (f32[8,2560]{1,0:T(8,128)S(1)}, f32[8,2560]{1,0:T(8,128)}, u32[]{:S(2)}, u32[]{:S(2)}) collective-permute-start(f32[8,2560]{1,0:T(8,128)S(1)} %fusion.68), channel_id=1, source_target_pairs={{0,1},{1,2},{2,3},{3,0},{4,5},{5,6},{6,7},{7,4},{8,9},{9,10},{10,1... | collective-permute-start | bytes 245768 | tf_op jit(solution)/shard_map/ppermute | solution.py:36
  37.0 0.8 %collective-permute-start.5 = (f32[8,2560]{1,0:T(8,128)S(1)}, f32[8,2560]{1,0:T(8,128)}, u32[]{:S(2)}, u32[]{:S(2)}) collective-permute-start(f32[8,2560]{1,0:T(8,128)S(1)} %fusion.68), channel_id=1, source_target_pairs={{0,3},{1,0},{2,1},{3,2},{4,7},{5,4},{6,5},{7,6},{8,11},{9,8},{10,9... | collective-permute-start | bytes 245768 | tf_op jit(solution)/shard_map/ppermute | solution.py:36
  37.8 0.6 gather_fusion
  38.4 4.0 %collective-permute-done.3 = f32[8,2560]{1,0:T(8,128)S(1)} collective-permute-done((f32[8,2560]{1,0:T(8,128)S(1)}, f32[8,2560]{1,0:T(8,128)S(1)}, u32[]{:S(2)}, u32[]{:S(2)}) %collective-permute-start.3) | collective-permute-done | bytes 81952 | tf_op jit(solution)/shard_map/ppermute | solution.py:36
  42.4 0.6 copy-done.3
  43.0 1.1 %multiply_reduce_fusion = (f32[8]{0:T(128)S(1)}, f32[8,2560]{1,0:T(8,128)S(1)}) fusion(f32[8,2560]{1,0:T(8,128)} %collective-permute-done.4, f32[8,2560]{1,0:T(8,128)} %collective-permute-done.5, f32[8,2560]{1,0:T(8,128)S(1)} %fusion.68, f32[8,2560]{1,0:T(8,128)} %copy-done.3, bf16[8,2560]{1,0:T(8,128)(2,1)S(1)} %get-tuple-element.16), kind=kLoop, calls=%fused_computation.33 | loop fusion | flops 143352 | bytes 450592 | tf_op jit(solution)/shard_map/reduce_sum | solution.py:13
  44.2 3.0 %fusion.61 = f32[8,896]{1,0:T(8,128)S(1)} fusion(bf16[2560,896]{1,0:T(8,128)(2,1)} %param.25, f32[8,2560]{1,0:T(8,128)S(1)} %get-tuple-element.12, f32[2560]{0:T(1024)S(1)} %convert_element_type.74, f32[8]{0:T(128)S(1)} %add_rsqrt_fusion), kind=kOutput, calls=%fused_computation.126 | convolution fusion | flops 36761600 | bytes 4708384 | tf_op jit(solution)/shard_map/dot_general | solution.py:165
  47.2 5.3 %fusion.24 = f32[8,2560]{1,0:T(8,128)S(1)} fusion(bf16[896,2560]{1,0:T(8,128)(2,1)} %param.27, bf16[2560,896]{1,0:T(8,128)(2,1)} %param.26, f32[8,896]{1,0:T(8,128)S(1)} %fusion.61, f32[8,2560]{1,0:T(8,128)S(1)} %get-tuple-element.12, f32[2560]{0:T(1024)S(1)} %convert_element_type.74, f32[8]{0:T(128)S(1)} %add_rsqrt_fusion), kind=kOutput, calls=%fused_computation.18 | convolution fusion | flops 73504768 | bytes 9377824 | tf_op jit(solution)/shard_map/dot_general | solution.py:169
  52.5 1.4 %collective-permute-start.6 = (f32[8,2560]{1,0:T(8,128)S(1)}, f32[8,2560]{1,0:T(8,128)S(1)}, u32[]{:S(2)}, u32[]{:S(2)}) collective-permute-start(f32[8,2560]{1,0:T(8,128)S(1)} %fusion.24), channel_id=1, source_target_pairs={{0,2},{1,3},{2,0},{3,1},{4,6},{5,7},{6,4},{7,5},{8,10},{9,11},{10,... | collective-permute-start | bytes 245768 | tf_op jit(solution)/shard_map/ppermute | solution.py:36
  53.9 1.1 %collective-permute-start.7 = (f32[8,2560]{1,0:T(8,128)S(1)}, f32[8,2560]{1,0:T(8,128)S(1)}, u32[]{:S(2)}, u32[]{:S(2)}) collective-permute-start(f32[8,2560]{1,0:T(8,128)S(1)} %fusion.24), channel_id=1, source_target_pairs={{0,1},{1,2},{2,3},{3,0},{4,5},{5,6},{6,7},{7,4},{8,9},{9,10},{10,1... | collective-permute-start | bytes 245768 | tf_op jit(solution)/shard_map/ppermute | solution.py:36
  55.1 2.7 %collective-permute-start.8 = (f32[8,2560]{1,0:T(8,128)S(1)}, f32[8,2560]{1,0:T(8,128)S(1)}, u32[]{:S(2)}, u32[]{:S(2)}) collective-permute-start(f32[8,2560]{1,0:T(8,128)S(1)} %fusion.24), channel_id=1, source_target_pairs={{0,3},{1,0},{2,1},{3,2},{4,7},{5,4},{6,5},{7,6},{8,11},{9,8},{10,9... | collective-permute-start | bytes 245768 | tf_op jit(solution)/shard_map/ppermute | solution.py:36
  57.8 3.2 %collective-permute-done.6 = f32[8,2560]{1,0:T(8,128)S(1)} collective-permute-done((f32[8,2560]{1,0:T(8,128)S(1)}, f32[8,2560]{1,0:T(8,128)S(1)}, u32[]{:S(2)}, u32[]{:S(2)}) %collective-permute-start.6) | collective-permute-done | bytes 81952 | tf_op jit(solution)/shard_map/ppermute | solution.py:36
  61.8 0.7 reshape.455
  62.5 3.4 %all-to-all-start.1 = ((bf16[8,2,2560]{2,1,0:T(2,128)(2,1)}), bf16[8,2,2560]{2,1,0:T(2,128)(2,1)S(1)}, u32[]{:S(2)}, u32[]{:S(2)}) async-start(bf16[8,2,2560]{2,1,0:T(2,128)(2,1)} %reshape.455), calls=%async_computation.1 | async-start | bytes 163840 | tf_op jit(solution)/shard_map/all_to_all | solution.py:182
  65.9 5.0 %all-to-all-done.1 = bf16[8,2,2560]{2,1,0:T(2,128)(2,1)S(1)} async-done(((bf16[8,2,2560]{2,1,0:T(2,128)(2,1)}), bf16[8,2,2560]{2,1,0:T(2,128)(2,1)S(1)}, u32[]{:S(2)}, u32[]{:S(2)}) %all-to-all-start.1) | async-done | bytes 81952 | tf_op jit(solution)/shard_map/all_to_all | solution.py:182
  70.9 0.8 %select_reduce_fusion = bf16[2,2560]{1,0:T(2,128)(2,1)} fusion(bf16[8,2,2560]{2,1,0:T(2,128)(2,1)S(1)} %all-to-all-done.1, pred[8,2]{1,0:T(8,128)(4,1)S(1)} %iota_compare_fusion.4), kind=kLoop, calls=%fused_computation.21 | loop fusion | flops 117760 | bytes 92176 | tf_op jit(solution)/shard_map/reduce_sum | solution.py:186
  (64 shorter events, 4.8 us)
Async XLA Ops:
  0.0 33.4 %copy-start = (bf16[640,2560]{1,0:T(8,128)(2,1)S(1)}, bf16[640,2560]{1,0:T(8,128)(2,1)}, u32[]{:S(2)}) copy-start(bf16[640,2560]{1,0:T(8,128)(2,1)} %param.23) | copy-start | bytes 9830404
  1.5 13.2 %all-to-all-start = ((bf16[8,2,2560]{2,1,0:T(2,128)(2,1)}), bf16[8,2,2560]{2,1,0:T(2,128)(2,1)S(1)}, u32[]{:S(2)}, u32[]{:S(2)}) async-start(bf16[8,2,2560]{2,1,0:T(2,128)(2,1)} %broadcast_in_dim.92), calls=%async_computation | async-start | bytes 163840 | tf_op jit(solution)/shard_map/all_to_all | solution.py:78
  15.4 9.7 %collective-permute-start = (bf16[8,2560]{1,0:T(8,128)(2,1)S(1)}, bf16[8,2560]{1,0:T(8,128)(2,1)S(1)}, u32[]{:S(2)}, u32[]{:S(2)}) collective-permute-start(bf16[8,2560]{1,0:T(8,128)(2,1)S(1)} %broadcast_select_fusion), channel_id=1, source_target_pairs={{0,2},{1,3},{2,0},{3,1},{4,6},{5,7},{6,4},{7,5},{8,10},{9,11},{10,... | collective-permute-start | bytes 122888 | tf_op jit(solution)/shard_map/ppermute | solution.py:36
  18.0 7.1 %collective-permute-start.1 = (bf16[8,2560]{1,0:T(8,128)(2,1)S(1)}, bf16[8,2560]{1,0:T(8,128)(2,1)S(1)}, u32[]{:S(2)}, u32[]{:S(2)}) collective-permute-start(bf16[8,2560]{1,0:T(8,128)(2,1)S(1)} %broadcast_select_fusion), channel_id=1, source_target_pairs={{0,1},{1,2},{2,3},{3,0},{4,5},{5,6},{6,7},{7,4},{8,9},{9,10},{10,1... | collective-permute-start | bytes 122888 | tf_op jit(solution)/shard_map/ppermute | solution.py:36
  19.6 5.5 %collective-permute-start.2 = (bf16[8,2560]{1,0:T(8,128)(2,1)S(1)}, bf16[8,2560]{1,0:T(8,128)(2,1)S(1)}, u32[]{:S(2)}, u32[]{:S(2)}) collective-permute-start(bf16[8,2560]{1,0:T(8,128)(2,1)S(1)} %broadcast_select_fusion), channel_id=1, source_target_pairs={{0,3},{1,0},{2,1},{3,2},{4,7},{5,4},{6,5},{7,6},{8,11},{9,8},{10,9... | collective-permute-start | bytes 122888 | tf_op jit(solution)/shard_map/ppermute | solution.py:36
  22.0 3.3 %copy-start.1 = (bf16[2560,160]{0,1:T(8,128)(2,1)S(1)}, bf16[2560,160]{0,1:T(8,128)(2,1)}, u32[]{:S(2)}) copy-start(bf16[2560,160]{0,1:T(8,128)(2,1)} %param.17) | copy-start | bytes 2457604
  28.3 2.6 %copy-start.2 = (bf16[2560,160]{0,1:T(8,128)(2,1)S(1)}, bf16[2560,160]{0,1:T(8,128)(2,1)}, u32[]{:S(2)}) copy-start(bf16[2560,160]{0,1:T(8,128)(2,1)} %param.18) | copy-start | bytes 2457604
  33.9 8.5 %collective-permute-start.3 = (f32[8,2560]{1,0:T(8,128)S(1)}, f32[8,2560]{1,0:T(8,128)S(1)}, u32[]{:S(2)}, u32[]{:S(2)}) collective-permute-start(f32[8,2560]{1,0:T(8,128)S(1)} %fusion.68), channel_id=1, source_target_pairs={{0,2},{1,3},{2,0},{3,1},{4,6},{5,7},{6,4},{7,5},{8,10},{9,11},{10,... | collective-permute-start | bytes 245768 | tf_op jit(solution)/shard_map/ppermute | solution.py:36
  33.9 8.5 %collective-permute-start.4 = (f32[8,2560]{1,0:T(8,128)S(1)}, f32[8,2560]{1,0:T(8,128)}, u32[]{:S(2)}, u32[]{:S(2)}) collective-permute-start(f32[8,2560]{1,0:T(8,128)S(1)} %fusion.68), channel_id=1, source_target_pairs={{0,1},{1,2},{2,3},{3,0},{4,5},{5,6},{6,7},{7,4},{8,9},{9,10},{10,1... | collective-permute-start | bytes 245768 | tf_op jit(solution)/shard_map/ppermute | solution.py:36
  37.0 6.1 %collective-permute-start.5 = (f32[8,2560]{1,0:T(8,128)S(1)}, f32[8,2560]{1,0:T(8,128)}, u32[]{:S(2)}, u32[]{:S(2)}) collective-permute-start(f32[8,2560]{1,0:T(8,128)S(1)} %fusion.68), channel_id=1, source_target_pairs={{0,3},{1,0},{2,1},{3,2},{4,7},{5,4},{6,5},{7,6},{8,11},{9,8},{10,9... | collective-permute-start | bytes 245768 | tf_op jit(solution)/shard_map/ppermute | solution.py:36
  42.4 0.6 copy-start.3
  52.5 8.4 %collective-permute-start.6 = (f32[8,2560]{1,0:T(8,128)S(1)}, f32[8,2560]{1,0:T(8,128)S(1)}, u32[]{:S(2)}, u32[]{:S(2)}) collective-permute-start(f32[8,2560]{1,0:T(8,128)S(1)} %fusion.24), channel_id=1, source_target_pairs={{0,2},{1,3},{2,0},{3,1},{4,6},{5,7},{6,4},{7,5},{8,10},{9,11},{10,... | collective-permute-start | bytes 245768 | tf_op jit(solution)/shard_map/ppermute | solution.py:36
  53.9 7.0 %collective-permute-start.7 = (f32[8,2560]{1,0:T(8,128)S(1)}, f32[8,2560]{1,0:T(8,128)S(1)}, u32[]{:S(2)}, u32[]{:S(2)}) collective-permute-start(f32[8,2560]{1,0:T(8,128)S(1)} %fusion.24), channel_id=1, source_target_pairs={{0,1},{1,2},{2,3},{3,0},{4,5},{5,6},{6,7},{7,4},{8,9},{9,10},{10,1... | collective-permute-start | bytes 245768 | tf_op jit(solution)/shard_map/ppermute | solution.py:36
  55.1 6.1 %collective-permute-start.8 = (f32[8,2560]{1,0:T(8,128)S(1)}, f32[8,2560]{1,0:T(8,128)S(1)}, u32[]{:S(2)}, u32[]{:S(2)}) collective-permute-start(f32[8,2560]{1,0:T(8,128)S(1)} %fusion.24), channel_id=1, source_target_pairs={{0,3},{1,0},{2,1},{3,2},{4,7},{5,4},{6,5},{7,6},{8,11},{9,8},{10,9... | collective-permute-start | bytes 245768 | tf_op jit(solution)/shard_map/ppermute | solution.py:36
  62.5 8.4 %all-to-all-start.1 = ((bf16[8,2,2560]{2,1,0:T(2,128)(2,1)}), bf16[8,2,2560]{2,1,0:T(2,128)(2,1)S(1)}, u32[]{:S(2)}, u32[]{:S(2)}) async-start(bf16[8,2,2560]{2,1,0:T(2,128)(2,1)} %reshape.455), calls=%async_computation.1 | async-start | bytes 163840 | tf_op jit(solution)/shard_map/all_to_all | solution.py:182

commit v15 on v12

--- a/solution.py
+++ b/solution.py
@@ -95,7 +95,13 @@
     held = rows_dp[served // req_loc, served % rows_loc]
     held = jnp.where((owner_tp == tp_index)[:, None], held, jnp.zeros_like(held))
     held, served_pages = lax.optimization_barrier((held, served_pages))
-    rows_srv = tensor_allreduce(held, tp_count)
+    rows_srv = held
+    step = 1
+    while step < tp_count:
+        rows_srv = rows_srv + lax.ppermute(
+            rows_srv, "tensor", [(i, i ^ step) for i in range(tp_count)]
+        )
+        step *= 2
     scaled_input = norm_rows(rows_srv, norm_gain).astype(jnp.bfloat16)
     query_srv = (
         apply_rotation(

time: 70.7 us -> 70.8 us (level)
    ppermute x9 -> x6, starting transfers between devices: 14.9 us -> 10.7 us  [shifted(): lax.ppermute(value, 'tensor', [(i, (i + k) % tp_count) for i in range(tp_...]
    ppermute x0 -> x2, starting transfers between devices: none -> 4.23 us  [local(): lax.ppermute(rows_srv, 'tensor', [(i, i ^ step) for i in range(tp_count)])]
    ppermute x9 -> x6, waiting for transfers between devices: 7.1 us -> 6.03 us  [shifted(): lax.ppermute(value, 'tensor', [(i, (i + k) % tp_count) for i in range(tp_...]
    ppermute x0 -> x2, waiting for transfers between devices: none -> 1.03 us  [local(): lax.ppermute(rows_srv, 'tensor', [(i, i ^ step) for i in range(tp_count)])]
  transfers between devices with their start and end apart: 11 -> 10, of which waited for: 4 -> 9; matrix products, arithmetic and copies ran while one was open for 15% -> 15% of each run, Pallas kernels for 0% -> 0%
where the time goes in v15:
time: 70.8 us; the launch traced here: 70.2 us
  starting transfers between devices  24 us (34%)
  matrix products  20.9 us (30%)
  waiting for transfers between devices  12.5 us (18%)
  other arithmetic  7.23 us (10%)
  local copies, waits for them, and re-layouts  5.44 us (8%)
    ppermute x6, starting transfers between devices, shifted(): lax.ppermute(value, 'tensor', [(i, (i + k) % tp_count) for i in range(tp_...  10.7 us
    ppermute x6, waiting for transfers between devices, shifted(): lax.ppermute(value, 'tensor', [(i, (i + k) % tp_count) for i in range(tp_...  6.03 us
    dot_general x1, matrix products, local(): jnp.dot(hidden, w_down, preferred_element_type=jnp.float32)  5.29 us
    all_to_all x1, starting transfers between devices, local(): lax.all_to_all(jnp.broadcast_to(residual_in[None], (dp_count,) + residual...  5.17 us
    all_to_all x1, waiting for transfers between devices, local(): incoming = lax.all_to_all(outgoing, 'dp', 0, 0)  5.1 us
    ppermute x2, starting transfers between devices, local(): lax.ppermute(rows_srv, 'tensor', [(i, i ^ step) for i in range(tp_count)])  4.23 us
    all_to_all x1, starting transfers between devices, local(): incoming = lax.all_to_all(outgoing, 'dp', 0, 0)  3.89 us
    dot_general x1, matrix products, local(): jnp.einsum('sq,qhdc->shdc', page_hot, key_page_pool, preferred_element_ty...  3.15 us
  transfers between devices with their start and end apart: 10, of which 9 were waited for; matrix products, arithmetic and copies ran while one was open for 15% of the time, Pallas kernels for 0%

profile of v15, /device:TPU:0, one launch (start us, length us, event | category | flops | bytes accessed | tf_op | source)
XLA Modules:
  0.0 70.2 jit_solution(1196872490795056182)
XLA Ops:
  0.0 1.5 %broadcast_in_dim.92 = bf16[8,2,2560]{2,1,0:T(2,128)(2,1)} broadcast(bf16[2,2560]{1,0:T(2,128)(2,1)} %param.14), dimensions={1,2} | broadcast | bytes 92160 | tf_op jit(solution)/shard_map/broadcast_in_dim | solution.py:79
  1.5 5.2 %all-to-all-start = ((bf16[8,2,2560]{2,1,0:T(2,128)(2,1)}), bf16[8,2,2560]{2,1,0:T(2,128)(2,1)S(1)}, u32[]{:S(2)}, u32[]{:S(2)}) async-start(bf16[8,2,2560]{2,1,0:T(2,128)(2,1)} %broadcast_in_dim.92), calls=%async_computation | async-start | bytes 163840 | tf_op jit(solution)/shard_map/all_to_all | solution.py:78
  6.7 0.7 iota_add_fusion.2
  7.6 0.8 %select_reduce_fusion.4 = (s32[8]{0:T(128)S(1)}, s32[8]{0:T(128)S(1)}) fusion(s32[64]{0:T(128)} %param.21, s32[64]{0:T(128)S(1)} %get-tuple-element.17, pred[64]{0:T(512)(128)(4,1)S(1)} %get-tuple-element.15), kind=kLoop, calls=%fused_computation.70 | loop fusion | flops 3056 | bytes 640 | tf_op jit(solution)/shard_map/reduce_sum | solution.py:91
  8.5 0.7 convert_element_type.65
  9.3 0.7 convert_element_type.73
  10.5 0.8 %select_reduce_fusion.2 = s32[8,4]{0,1:T(4,128)S(1)} fusion(s32[64,4]{0,1:T(4,128)} %param.22, pred[8,64]{1,0:T(8,128)(4,1)S(1)} %fusion.47), kind=kLoop, calls=%fused_computation.49 | loop fusion | flops 4064 | bytes 1664 | tf_op jit(solution)/shard_map/reduce_sum | solution.py:92
  12.5 1.6 %collective-permute-start = (bf16[8,2560]{1,0:T(8,128)(2,1)S(1)}, bf16[8,2560]{1,0:T(8,128)(2,1)S(1)}, u32[]{:S(2)}, u32[]{:S(2)}) collective-permute-start(bf16[8,2560]{1,0:T(8,128)(2,1)S(1)} %broadcast_select_fusion), channel_id=1, source_target_pairs={{0,1},{1,0},{2,3},{3,2},{4,5},{5,4},{6,7},{7,6},{8,9},{9,8},{10,11... | collective-permute-start | bytes 122888 | tf_op jit(solution)/shard_map/ppermute | solution.py:101
  14.3 3.1 %fusion.6 = bf16[32,2,80,128]{3,0,2,1:T(8,128)(2,1)} fusion(bf16[32,2,80,128]{3,2,1,0:T(8,128)(2,1)} %param.19, s32[32]{0:T(128)S(1)} %eq.108), kind=kOutput, calls=%fused_computation.9 | convolution fusion | flops 41944064 | bytes 2621568 | tf_op jit(solution)/shard_map/sq,qhdc->shdc/dot_general | solution.py:132
  17.4 2.7 %collective-permute-start.1 = (bf16[8,2560]{1,0:T(8,128)(2,1)S(1)}, bf16[8,2560]{1,0:T(8,128)(2,1)S(1)}, u32[]{:S(2)}, u32[]{:S(2)}) collective-permute-start(bf16[8,2560]{1,0:T(8,128)(2,1)S(1)} %add.240), channel_id=1, source_target_pairs={{0,2},{1,3},{2,0},{3,1},{4,6},{5,7},{6,4},{7,5},{8,10},{9,11},{10,... | collective-permute-start | bytes 122888 | tf_op jit(solution)/shard_map/ppermute | solution.py:101
  20.1 1.7 %fusion.2 = bf16[32,2,80,128]{3,0,2,1:T(8,128)(2,1)} fusion(bf16[32,2,80,128]{3,2,1,0:T(8,128)(2,1)S(1)} %copy-done.1, s32[32]{0:T(128)S(1)} %eq.108), kind=kOutput, calls=%fused_computation.5 | convolution fusion | flops 41944064 | bytes 2621568 | tf_op jit(solution)/shard_map/sq,qhdc->shdc/dot_general | solution.py:135
  21.8 1.0 %collective-permute-done.1 = bf16[8,2560]{1,0:T(8,128)(2,1)S(1)} collective-permute-done((bf16[8,2560]{1,0:T(8,128)(2,1)S(1)}, bf16[8,2560]{1,0:T(8,128)(2,1)S(1)}, u32[]{:S(2)}, u32[]{:S(2)}) %collective-permute-start.1) | collective-permute-done | bytes 40992 | tf_op jit(solution)/shard_map/ppermute | solution.py:101
  23.5 2.5 %fusion.62 = f32[8,640]{1,0:T(8,128)S(1)} fusion(bf16[8,2560]{1,0:T(8,128)(2,1)S(1)} %fusion.29, bf16[2560,640]{1,0:T(8,128)(2,1)} %param.16), kind=kOutput, calls=%fused_computation.124 | convolution fusion | flops 26214400 | bytes 3338240 | tf_op jit(solution)/shard_map/dot_general | solution.py:108
  26.5 1.9 %select_reduce_fusion.1 = (f32[8,2,4]{2,1,0:T(2,128)S(1)}, f32[8,2,4,4,128]{4,2,3,1,0:T(4,128)S(1)}) fusion(pred[8,4,128]{2,1,0:T(4,128)(4,1)S(1)} %broadcast_compare_fusion, bf16[8,4,2,80,128]{4,1,0,3,2:T(4,128)(2,1)} %bitcast.63, bf16[8,2,4,40]{3,2,1,0:T(4,128)(2,1)S(1)} %bitcast.69, bf16[8,2,4,40]{3,2,1,0:T(4,128)(2,1)S(1)} %bitcast.67), kind=kOutput, calls=%fused_computation.23 | convolution fusion | flops 5361600 | bytes 1456384 | tf_op jit(solution)/shard_map/rhgd,rphdc->rhgpc/dot_general | solution.py:139
  29.7 2.0 %fusion.20 = bf16[8,2,4,80]{3,2,1,0:T(4,128)(2,1)S(1)} fusion(bf16[8,4,2,80,128]{4,1,0,3,2:T(4,128)(2,1)} %bitcast.62, f32[8,2,4,4,128]{4,2,3,1,0:T(4,128)} %copy-done.4, f32[8,2,4]{2,1,0:T(2,128)S(1)} %multiply_maximum_fusion, pred[8,4,128]{2,1,0:T(4,128)(4,1)S(1)} %broadcast_compare_fusion, f32[8,2,4]{2,1,0:T(2,128)S(1)} %get-tuple-element.13, ...), kind=kOutput, calls=%fused_computation.16 | convolution fusion | flops 5328896 | bytes 1462016 | tf_op jit(solution)/shard_map/rhgpc,rphdc->rhgd/dot_general | solution.py:155
  32.3 2.2 %collective-permute-start.2 = (f32[8,2560]{1,0:T(8,128)S(1)}, f32[8,2560]{1,0:T(8,128)S(1)}, u32[]{:S(2)}, u32[]{:S(2)}) collective-permute-start(f32[8,2560]{1,0:T(8,128)S(1)} %fusion.64), channel_id=1, source_target_pairs={{0,2},{1,3},{2,0},{3,1},{4,6},{5,7},{6,4},{7,5},{8,10},{9,11},{10,... | collective-permute-start | bytes 245768 | tf_op jit(solution)/shard_map/ppermute | solution.py:36
  34.5 0.8 %collective-permute-start.3 = (f32[8,2560]{1,0:T(8,128)S(1)}, f32[8,2560]{1,0:T(8,128)}, u32[]{:S(2)}, u32[]{:S(2)}) collective-permute-start(f32[8,2560]{1,0:T(8,128)S(1)} %fusion.64), channel_id=1, source_target_pairs={{0,1},{1,2},{2,3},{3,0},{4,5},{5,6},{6,7},{7,4},{8,9},{9,10},{10,1... | collective-permute-start | bytes 245768 | tf_op jit(solution)/shard_map/ppermute | solution.py:36
  35.3 3.0 %collective-permute-start.4 = (f32[8,2560]{1,0:T(8,128)S(1)}, f32[8,2560]{1,0:T(8,128)}, u32[]{:S(2)}, u32[]{:S(2)}) collective-permute-start(f32[8,2560]{1,0:T(8,128)S(1)} %fusion.64), channel_id=1, source_target_pairs={{0,3},{1,0},{2,1},{3,2},{4,7},{5,4},{6,5},{7,6},{8,11},{9,8},{10,9... | collective-permute-start | bytes 245768 | tf_op jit(solution)/shard_map/ppermute | solution.py:36
  39.0 0.7 %collective-permute-done.2 = f32[8,2560]{1,0:T(8,128)S(1)} collective-permute-done((f32[8,2560]{1,0:T(8,128)S(1)}, f32[8,2560]{1,0:T(8,128)S(1)}, u32[]{:S(2)}, u32[]{:S(2)}) %collective-permute-start.2) | collective-permute-done | bytes 81952 | tf_op jit(solution)/shard_map/ppermute | solution.py:36
  39.7 1.3 %collective-permute-done.3 = f32[8,2560]{1,0:T(8,128)} collective-permute-done((f32[8,2560]{1,0:T(8,128)S(1)}, f32[8,2560]{1,0:T(8,128)}, u32[]{:S(2)}, u32[]{:S(2)}) %collective-permute-start.3) | collective-permute-done | bytes 81952 | tf_op jit(solution)/shard_map/ppermute | solution.py:36
  41.4 1.1 %multiply_reduce_fusion = (f32[8]{0:T(128)S(1)}, f32[8,2560]{1,0:T(8,128)S(1)}) fusion(f32[8,2560]{1,0:T(8,128)} %collective-permute-done.3, f32[8,2560]{1,0:T(8,128)} %collective-permute-done.4, f32[8,2560]{1,0:T(8,128)S(1)} %fusion.64, f32[8,2560]{1,0:T(8,128)} %copy-done.5, bf16[8,2560]{1,0:T(8,128)(2,1)S(1)} %add.240, ...), kind=kLoop, calls=%fused_computation.33 | loop fusion | flops 163832 | bytes 491552 | tf_op jit(solution)/shard_map/reduce_sum | solution.py:13
  42.6 3.0 %fusion.60 = f32[8,896]{1,0:T(8,128)S(1)} fusion(bf16[2560,896]{1,0:T(8,128)(2,1)} %param.25, f32[8,2560]{1,0:T(8,128)S(1)} %get-tuple-element.12, f32[2560]{0:T(1024)S(1)} %convert_element_type.73, f32[8]{0:T(128)S(1)} %add_rsqrt_fusion), kind=kOutput, calls=%fused_computation.122 | convolution fusion | flops 36761600 | bytes 4708384 | tf_op jit(solution)/shard_map/dot_general | solution.py:166
  45.6 5.3 %fusion.24 = f32[8,2560]{1,0:T(8,128)S(1)} fusion(bf16[896,2560]{1,0:T(8,128)(2,1)} %param.27, bf16[2560,896]{1,0:T(8,128)(2,1)} %param.26, f32[8,896]{1,0:T(8,128)S(1)} %fusion.60, f32[8,2560]{1,0:T(8,128)S(1)} %get-tuple-element.12, f32[2560]{0:T(1024)S(1)} %convert_element_type.73, f32[8]{0:T(128)S(1)} %add_rsqrt_fusion), kind=kOutput, calls=%fused_computation.18 | convolution fusion | flops 73504768 | bytes 9377824 | tf_op jit(solution)/shard_map/dot_general | solution.py:170
  50.9 0.8 %collective-permute-start.5 = (f32[8,2560]{1,0:T(8,128)S(1)}, f32[8,2560]{1,0:T(8,128)S(1)}, u32[]{:S(2)}, u32[]{:S(2)}) collective-permute-start(f32[8,2560]{1,0:T(8,128)S(1)} %fusion.24), channel_id=1, source_target_pairs={{0,2},{1,3},{2,0},{3,1},{4,6},{5,7},{6,4},{7,5},{8,10},{9,11},{10,... | collective-permute-start | bytes 245768 | tf_op jit(solution)/shard_map/ppermute | solution.py:36
  51.7 2.9 %collective-permute-start.6 = (f32[8,2560]{1,0:T(8,128)S(1)}, f32[8,2560]{1,0:T(8,128)S(1)}, u32[]{:S(2)}, u32[]{:S(2)}) collective-permute-start(f32[8,2560]{1,0:T(8,128)S(1)} %fusion.24), channel_id=1, source_target_pairs={{0,1},{1,2},{2,3},{3,0},{4,5},{5,6},{6,7},{7,4},{8,9},{9,10},{10,1... | collective-permute-start | bytes 245768 | tf_op jit(solution)/shard_map/ppermute | solution.py:36
  54.7 0.9 %collective-permute-start.7 = (f32[8,2560]{1,0:T(8,128)S(1)}, f32[8,2560]{1,0:T(8,128)S(1)}, u32[]{:S(2)}, u32[]{:S(2)}) collective-permute-start(f32[8,2560]{1,0:T(8,128)S(1)} %fusion.24), channel_id=1, source_target_pairs={{0,3},{1,0},{2,1},{3,2},{4,7},{5,4},{6,5},{7,6},{8,11},{9,8},{10,9... | collective-permute-start | bytes 245768 | tf_op jit(solution)/shard_map/ppermute | solution.py:36
  55.6 1.6 %collective-permute-done.5 = f32[8,2560]{1,0:T(8,128)S(1)} collective-permute-done((f32[8,2560]{1,0:T(8,128)S(1)}, f32[8,2560]{1,0:T(8,128)S(1)}, u32[]{:S(2)}, u32[]{:S(2)}) %collective-permute-start.5) | collective-permute-done | bytes 81952 | tf_op jit(solution)/shard_map/ppermute | solution.py:36
  57.2 0.9 %collective-permute-done.6 = f32[8,2560]{1,0:T(8,128)S(1)} collective-permute-done((f32[8,2560]{1,0:T(8,128)S(1)}, f32[8,2560]{1,0:T(8,128)S(1)}, u32[]{:S(2)}, u32[]{:S(2)}) %collective-permute-start.6) | collective-permute-done | bytes 81952 | tf_op jit(solution)/shard_map/ppermute | solution.py:36
  58.1 1.1 %collective-permute-done.7 = f32[8,2560]{1,0:T(8,128)S(1)} collective-permute-done((f32[8,2560]{1,0:T(8,128)S(1)}, f32[8,2560]{1,0:T(8,128)S(1)}, u32[]{:S(2)}, u32[]{:S(2)}) %collective-permute-start.7) | collective-permute-done | bytes 81952 | tf_op jit(solution)/shard_map/ppermute | solution.py:36
  60.4 3.9 %all-to-all-start.1 = ((bf16[8,2,2560]{2,1,0:T(2,128)(2,1)}), bf16[8,2,2560]{2,1,0:T(2,128)(2,1)S(1)}, u32[]{:S(2)}, u32[]{:S(2)}) async-start(bf16[8,2,2560]{2,1,0:T(2,128)(2,1)} %reshape.448), calls=%async_computation.1 | async-start | bytes 163840 | tf_op jit(solution)/shard_map/all_to_all | solution.py:183
  64.3 5.1 %all-to-all-done.1 = bf16[8,2,2560]{2,1,0:T(2,128)(2,1)S(1)} async-done(((bf16[8,2,2560]{2,1,0:T(2,128)(2,1)}), bf16[8,2,2560]{2,1,0:T(2,128)(2,1)S(1)}, u32[]{:S(2)}, u32[]{:S(2)}) %all-to-all-start.1) | async-done | bytes 81952 | tf_op jit(solution)/shard_map/all_to_all | solution.py:183
  69.4 0.8 %select_reduce_fusion = bf16[2,2560]{1,0:T(2,128)(2,1)} fusion(bf16[8,2,2560]{2,1,0:T(2,128)(2,1)S(1)} %all-to-all-done.1, pred[8,2]{1,0:T(8,128)(4,1)S(1)} %iota_compare_fusion.3), kind=kLoop, calls=%fused_computation.21 | loop fusion | flops 117760 | bytes 92176 | tf_op jit(solution)/shard_map/reduce_sum | solution.py:187
  (65 shorter events, 7.7 us)
Async XLA Ops:
  0.0 31.8 %copy-start = (bf16[640,2560]{1,0:T(8,128)(2,1)S(1)}, bf16[640,2560]{1,0:T(8,128)(2,1)}, u32[]{:S(2)}) copy-start(bf16[640,2560]{1,0:T(8,128)(2,1)} %param.23) | copy-start | bytes 9830404
  1.5 10.3 %all-to-all-start = ((bf16[8,2,2560]{2,1,0:T(2,128)(2,1)}), bf16[8,2,2560]{2,1,0:T(2,128)(2,1)S(1)}, u32[]{:S(2)}, u32[]{:S(2)}) async-start(bf16[8,2,2560]{2,1,0:T(2,128)(2,1)} %broadcast_in_dim.92), calls=%async_computation | async-start | bytes 163840 | tf_op jit(solution)/shard_map/all_to_all | solution.py:78
  12.5 4.9 %collective-permute-start = (bf16[8,2560]{1,0:T(8,128)(2,1)S(1)}, bf16[8,2560]{1,0:T(8,128)(2,1)S(1)}, u32[]{:S(2)}, u32[]{:S(2)}) collective-permute-start(bf16[8,2560]{1,0:T(8,128)(2,1)S(1)} %broadcast_select_fusion), channel_id=1, source_target_pairs={{0,1},{1,0},{2,3},{3,2},{4,5},{5,4},{6,7},{7,6},{8,9},{9,8},{10,11... | collective-permute-start | bytes 122888 | tf_op jit(solution)/shard_map/ppermute | solution.py:101
  14.3 5.8 %copy-start.1 = (bf16[32,2,80,128]{3,2,1,0:T(8,128)(2,1)S(1)}, bf16[32,2,80,128]{3,2,1,0:T(8,128)(2,1)}, u32[]{:S(2)}) copy-start(bf16[32,2,80,128]{3,2,1,0:T(8,128)(2,1)} %param.20) | copy-start | bytes 3932164
  17.4 5.6 %copy-start.2 = (bf16[2560,160]{0,1:T(8,128)(2,1)S(1)}, bf16[2560,160]{0,1:T(8,128)(2,1)}, u32[]{:S(2)}) copy-start(bf16[2560,160]{0,1:T(8,128)(2,1)} %param.17) | copy-start | bytes 2457604
  17.4 5.4 %collective-permute-start.1 = (bf16[8,2560]{1,0:T(8,128)(2,1)S(1)}, bf16[8,2560]{1,0:T(8,128)(2,1)S(1)}, u32[]{:S(2)}, u32[]{:S(2)}) collective-permute-start(bf16[8,2560]{1,0:T(8,128)(2,1)S(1)} %add.240), channel_id=1, source_target_pairs={{0,2},{1,3},{2,0},{3,1},{4,6},{5,7},{6,4},{7,5},{8,10},{9,11},{10,... | collective-permute-start | bytes 122888 | tf_op jit(solution)/shard_map/ppermute | solution.py:101
  26.0 3.3 %copy-start.3 = (bf16[2560,160]{0,1:T(8,128)(2,1)S(1)}, bf16[2560,160]{0,1:T(8,128)(2,1)}, u32[]{:S(2)}) copy-start(bf16[2560,160]{0,1:T(8,128)(2,1)} %param.18) | copy-start | bytes 2457604
  28.4 0.6 copy-start.4
  32.3 7.4 %collective-permute-start.2 = (f32[8,2560]{1,0:T(8,128)S(1)}, f32[8,2560]{1,0:T(8,128)S(1)}, u32[]{:S(2)}, u32[]{:S(2)}) collective-permute-start(f32[8,2560]{1,0:T(8,128)S(1)} %fusion.64), channel_id=1, source_target_pairs={{0,2},{1,3},{2,0},{3,1},{4,6},{5,7},{6,4},{7,5},{8,10},{9,11},{10,... | collective-permute-start | bytes 245768 | tf_op jit(solution)/shard_map/ppermute | solution.py:36
  34.5 6.5 %collective-permute-start.3 = (f32[8,2560]{1,0:T(8,128)S(1)}, f32[8,2560]{1,0:T(8,128)}, u32[]{:S(2)}, u32[]{:S(2)}) collective-permute-start(f32[8,2560]{1,0:T(8,128)S(1)} %fusion.64), channel_id=1, source_target_pairs={{0,1},{1,2},{2,3},{3,0},{4,5},{5,6},{6,7},{7,4},{8,9},{9,10},{10,1... | collective-permute-start | bytes 245768 | tf_op jit(solution)/shard_map/ppermute | solution.py:36
  35.3 6.1 %collective-permute-start.4 = (f32[8,2560]{1,0:T(8,128)S(1)}, f32[8,2560]{1,0:T(8,128)}, u32[]{:S(2)}, u32[]{:S(2)}) collective-permute-start(f32[8,2560]{1,0:T(8,128)S(1)} %fusion.64), channel_id=1, source_target_pairs={{0,3},{1,0},{2,1},{3,2},{4,7},{5,4},{6,5},{7,6},{8,11},{9,8},{10,9... | collective-permute-start | bytes 245768 | tf_op jit(solution)/shard_map/ppermute | solution.py:36
  39.7 1.3 %copy-start.5 = (f32[8,2560]{1,0:T(8,128)}, f32[8,2560]{1,0:T(8,128)S(1)}, u32[]{:S(2)}) copy-start(f32[8,2560]{1,0:T(8,128)S(1)} %collective-permute-done.2) | copy-start | bytes 245764
  50.9 6.3 %collective-permute-start.5 = (f32[8,2560]{1,0:T(8,128)S(1)}, f32[8,2560]{1,0:T(8,128)S(1)}, u32[]{:S(2)}, u32[]{:S(2)}) collective-permute-start(f32[8,2560]{1,0:T(8,128)S(1)} %fusion.24), channel_id=1, source_target_pairs={{0,2},{1,3},{2,0},{3,1},{4,6},{5,7},{6,4},{7,5},{8,10},{9,11},{10,... | collective-permute-start | bytes 245768 | tf_op jit(solution)/shard_map/ppermute | solution.py:36
  51.7 6.3 %collective-permute-start.6 = (f32[8,2560]{1,0:T(8,128)S(1)}, f32[8,2560]{1,0:T(8,128)S(1)}, u32[]{:S(2)}, u32[]{:S(2)}) collective-permute-start(f32[8,2560]{1,0:T(8,128)S(1)} %fusion.24), channel_id=1, source_target_pairs={{0,1},{1,2},{2,3},{3,0},{4,5},{5,6},{6,7},{7,4},{8,9},{9,10},{10,1... | collective-permute-start | bytes 245768 | tf_op jit(solution)/shard_map/ppermute | solution.py:36
  54.7 4.4 %collective-permute-start.7 = (f32[8,2560]{1,0:T(8,128)S(1)}, f32[8,2560]{1,0:T(8,128)S(1)}, u32[]{:S(2)}, u32[]{:S(2)}) collective-permute-start(f32[8,2560]{1,0:T(8,128)S(1)} %fusion.24), channel_id=1, source_target_pairs={{0,3},{1,0},{2,1},{3,2},{4,7},{5,4},{6,5},{7,6},{8,11},{9,8},{10,9... | collective-permute-start | bytes 245768 | tf_op jit(solution)/shard_map/ppermute | solution.py:36
  60.4 9.0 %all-to-all-start.1 = ((bf16[8,2,2560]{2,1,0:T(2,128)(2,1)}), bf16[8,2,2560]{2,1,0:T(2,128)(2,1)S(1)}, u32[]{:S(2)}, u32[]{:S(2)}) async-start(bf16[8,2,2560]{2,1,0:T(2,128)(2,1)} %reshape.448), calls=%async_computation.1 | async-start | bytes 163840 | tf_op jit(solution)/shard_map/all_to_all | solution.py:183

commit v16 on v12

--- a/solution.py
+++ b/solution.py
@@ -75,8 +75,11 @@
     dp_index = lax.axis_index("dp")
     tp_index = lax.axis_index("tensor")
 
+    width = residual_in.shape[1]
+    sub = 8
+    packed = residual_in.reshape(rows_loc * sub, width // sub)
     rows_dp = lax.all_to_all(
-        jnp.broadcast_to(residual_in[None], (dp_count,) + residual_in.shape), "dp", 0, 0
+        jnp.broadcast_to(packed[None], (dp_count,) + packed.shape), "dp", 0, 0
     )
 
     request_ids = jnp.arange(total_reqs, dtype=jnp.int32)
@@ -92,7 +95,8 @@
     served_pages = jnp.sum(jnp.where(hits[:, :, None], page_table[None, :, :], 0), axis=1)
 
     owner_tp = (served % req_loc) // rows_loc
-    held = rows_dp[served // req_loc, served % rows_loc]
+    sub_rows = (served % rows_loc)[:, None] * sub + jnp.arange(sub, dtype=jnp.int32)[None, :]
+    held = rows_dp[(served // req_loc)[:, None], sub_rows].reshape(req_loc, width)
     held = jnp.where((owner_tp == tp_index)[:, None], held, jnp.zeros_like(held))
     held, served_pages = lax.optimization_barrier((held, served_pages))
     rows_srv = tensor_allreduce(held, tp_count)

time: 70.7 us -> 71.3 us (level)
    broadcast_in_dim x1 -> x2, local copies, waits for them, and re-layouts: 1.52 us -> 1.57 us  [local(): jnp.broadcast_to(packed[None], (dp_count,) + packed.shape)]
where the time goes in v16:
time: 71.3 us; the launch traced here: 70.7 us
  starting transfers between devices  23.6 us (33%)
  matrix products  20.9 us (29%)
  waiting for transfers between devices  12.9 us (18%)
  other arithmetic  7.21 us (10%)
  local copies, waits for them, and re-layouts  5.93 us (8%)
    ppermute x9, starting transfers between devices, shifted(): lax.ppermute(value, 'tensor', [(i, (i + k) % tp_count) for i in range(tp_...  14.9 us
    ppermute x9, waiting for transfers between devices, shifted(): lax.ppermute(value, 'tensor', [(i, (i + k) % tp_count) for i in range(tp_...  7.55 us
    dot_general x1, matrix products, local(): jnp.dot(hidden, w_down, preferred_element_type=jnp.float32)  5.29 us
    all_to_all x1, starting transfers between devices, local(): lax.all_to_all(jnp.broadcast_to(packed[None], (dp_count,) + packed.shape)...  5.17 us
    all_to_all x1, waiting for transfers between devices, local(): incoming = lax.all_to_all(outgoing, 'dp', 0, 0)  5.1 us
    all_to_all x1, starting transfers between devices, local(): incoming = lax.all_to_all(outgoing, 'dp', 0, 0)  3.5 us
    dot_general x1, matrix products, local(): jnp.einsum('sq,qhdc->shdc', page_hot, key_page_pool, preferred_element_ty...  3.15 us
    dot_general x1, matrix products, local(): gate_act = jnp.dot(normed_mlp, w_gate, preferred_element_type=jnp.float32)  3.05 us
  transfers between devices with their start and end apart: 11, of which 4 were waited for; matrix products, arithmetic and copies ran while one was open for 15% of the time, Pallas kernels for 0%

profile of v16, /device:TPU:0, one launch (start us, length us, event | category | flops | bytes accessed | tf_op | source)
XLA Modules:
  0.0 70.7 jit_solution(1631428626091960056)
XLA Ops:
  0.0 0.9 %broadcast_in_dim.96 = bf16[16,320]{1,0:T(8,128)(2,1)S(1)} reshape(bf16[2,2560]{1,0:T(2,128)(2,1)} %param.14) | data formatting | bytes 20480 | tf_op jit(solution)/shard_map/broadcast_in_dim | solution.py:82
  0.9 0.6 broadcast_in_dim.97
  1.6 5.2 %all-to-all-start = ((bf16[8,16,320]{2,1,0:T(8,128)(2,1)}), bf16[8,16,320]{2,1,0:T(8,128)(2,1)S(1)}, u32[]{:S(2)}, u32[]{:S(2)}) async-start(bf16[8,16,320]{2,1,0:T(8,128)(2,1)} %broadcast_in_dim.97), calls=%async_computation | async-start | bytes 196608 | tf_op jit(solution)/shard_map/all_to_all | solution.py:81
  6.7 0.7 iota_add_fusion.2
  7.6 0.8 %select_reduce_fusion.4 = (s32[8]{0:T(128)S(1)}, s32[8]{0:T(128)S(1)}) fusion(s32[64]{0:T(128)} %param.21, s32[64]{0:T(128)S(1)} %get-tuple-element.19, pred[64]{0:T(512)(128)(4,1)S(1)} %get-tuple-element.17), kind=kLoop, calls=%fused_computation.75 | loop fusion | flops 3056 | bytes 640 | tf_op jit(solution)/shard_map/reduce_sum | solution.py:94
  8.7 0.7 convert_element_type.65
  9.5 0.7 convert_element_type.73
  10.7 0.8 %select_reduce_fusion.2 = s32[8,4]{0,1:T(4,128)S(1)} fusion(s32[64,4]{0,1:T(4,128)} %param.22, pred[8,64]{1,0:T(8,128)(4,1)S(1)} %fusion.50), kind=kLoop, calls=%fused_computation.50 | loop fusion | flops 4064 | bytes 1664 | tf_op jit(solution)/shard_map/reduce_sum | solution.py:95
  11.9 0.9 %gather_fusion.1 = bf16[64,320]{1,0:T(8,128)(2,1)S(1)} fusion(bf16[8,16,320]{2,1,0:T(8,128)(2,1)S(1)} %all-to-all-done, s32[64]{0:T(128)S(1)} %reshape.427), kind=kCustom, calls=%fused_computation.1 | custom fusion | bytes 82432 | tf_op jit(solution)/shard_map/gather | solution.py:99
  13.0 2.6 %collective-permute-start = (bf16[8,2560]{1,0:T(8,128)(2,1)S(1)}, bf16[8,2560]{1,0:T(8,128)(2,1)S(1)}, u32[]{:S(2)}, u32[]{:S(2)}) collective-permute-start(bf16[8,2560]{1,0:T(8,128)(2,1)S(1)} %broadcast_select_fusion), channel_id=1, source_target_pairs={{0,2},{1,3},{2,0},{3,1},{4,6},{5,7},{6,4},{7,5},{8,10},{9,11},{10,... | collective-permute-start | bytes 122888 | tf_op jit(solution)/shard_map/ppermute | solution.py:36
  15.6 1.6 %collective-permute-start.1 = (bf16[8,2560]{1,0:T(8,128)(2,1)S(1)}, bf16[8,2560]{1,0:T(8,128)(2,1)S(1)}, u32[]{:S(2)}, u32[]{:S(2)}) collective-permute-start(bf16[8,2560]{1,0:T(8,128)(2,1)S(1)} %broadcast_select_fusion), channel_id=1, source_target_pairs={{0,1},{1,2},{2,3},{3,0},{4,5},{5,6},{6,7},{7,4},{8,9},{9,10},{10,1... | collective-permute-start | bytes 122888 | tf_op jit(solution)/shard_map/ppermute | solution.py:36
  17.2 2.2 %collective-permute-start.2 = (bf16[8,2560]{1,0:T(8,128)(2,1)S(1)}, bf16[8,2560]{1,0:T(8,128)(2,1)S(1)}, u32[]{:S(2)}, u32[]{:S(2)}) collective-permute-start(bf16[8,2560]{1,0:T(8,128)(2,1)S(1)} %broadcast_select_fusion), channel_id=1, source_target_pairs={{0,3},{1,0},{2,1},{3,2},{4,7},{5,4},{6,5},{7,6},{8,11},{9,8},{10,9... | collective-permute-start | bytes 122888 | tf_op jit(solution)/shard_map/ppermute | solution.py:36
  19.6 3.1 %fusion.6 = bf16[32,2,80,128]{3,0,2,1:T(8,128)(2,1)} fusion(bf16[32,2,80,128]{3,2,1,0:T(8,128)(2,1)} %param.19, s32[32]{0:T(128)S(1)} %eq.108), kind=kOutput, calls=%fused_computation.9 | convolution fusion | flops 41944064 | bytes 2621568 | tf_op jit(solution)/shard_map/sq,qhdc->shdc/dot_general | solution.py:130
  22.8 1.7 %fusion.2 = bf16[32,2,80,128]{3,0,2,1:T(8,128)(2,1)} fusion(bf16[32,2,80,128]{3,2,1,0:T(8,128)(2,1)S(1)} %copy-done.1, s32[32]{0:T(128)S(1)} %eq.108), kind=kOutput, calls=%fused_computation.5 | convolution fusion | flops 41944064 | bytes 2621568 | tf_op jit(solution)/shard_map/sq,qhdc->shdc/dot_general | solution.py:133
  25.1 2.5 %fusion.63 = f32[8,640]{1,0:T(8,128)S(1)} fusion(bf16[2560,640]{1,0:T(8,128)(2,1)} %param.16, bf16[8,2560]{1,0:T(8,128)(2,1)S(1)} %get-tuple-element.16, f32[2560]{0:T(1024)S(1)} %convert_element_type.65, f32[8]{0:T(128)S(1)} %add_rsqrt_fusion.1), kind=kOutput, calls=%fused_computation.122 | convolution fusion | flops 26296320 | bytes 3348512 | tf_op jit(solution)/shard_map/dot_general | solution.py:106
  28.1 1.9 %select_reduce_fusion.1 = (f32[8,2,4]{2,1,0:T(2,128)S(1)}, f32[8,2,4,4,128]{4,2,3,1,0:T(4,128)S(1)}) fusion(pred[8,4,128]{2,1,0:T(4,128)(4,1)S(1)} %broadcast_compare_fusion, bf16[8,4,2,80,128]{4,1,0,3,2:T(4,128)(2,1)} %bitcast.45, bf16[8,2,4,40]{3,2,1,0:T(4,128)(2,1)S(1)} %bitcast.51, bf16[8,2,4,40]{3,2,1,0:T(4,128)(2,1)S(1)} %bitcast.49), kind=kOutput, calls=%fused_computation.23 | convolution fusion | flops 5361600 | bytes 1456384 | tf_op jit(solution)/shard_map/rhgd,rphdc->rhgpc/dot_general | solution.py:137
  30.7 1.9 %fusion.20 = bf16[8,2,4,80]{3,2,1,0:T(4,128)(2,1)S(1)} fusion(bf16[8,4,2,80,128]{4,1,0,3,2:T(4,128)(2,1)} %bitcast.44, f32[8,2,4,4,128]{4,2,3,1,0:T(4,128)S(1)} %get-tuple-element.29, f32[8,2,4]{2,1,0:T(2,128)S(1)} %multiply_maximum_fusion, pred[8,4,128]{2,1,0:T(4,128)(4,1)S(1)} %broadcast_compare_fusion, f32[8,2,4]{2,1,0:T(2,128)S(1)} %get-tuple-element.13, ...), kind=kOutput, calls=%fused_computation.16 | convolution fusion | flops 5328896 | bytes 1462016 | tf_op jit(solution)/shard_map/rhgpc,rphdc->rhgd/dot_general | solution.py:153
  33.3 1.3 %collective-permute-start.4 = (f32[8,2560]{1,0:T(8,128)S(1)}, f32[8,2560]{1,0:T(8,128)}, u32[]{:S(2)}, u32[]{:S(2)}) collective-permute-start(f32[8,2560]{1,0:T(8,128)S(1)} %fusion.66), channel_id=1, source_target_pairs={{0,1},{1,2},{2,3},{3,0},{4,5},{5,6},{6,7},{7,4},{8,9},{9,10},{10,1... | collective-permute-start | bytes 245768 | tf_op jit(solution)/shard_map/ppermute | solution.py:36
  34.6 2.5 %collective-permute-start.5 = (f32[8,2560]{1,0:T(8,128)S(1)}, f32[8,2560]{1,0:T(8,128)}, u32[]{:S(2)}, u32[]{:S(2)}) collective-permute-start(f32[8,2560]{1,0:T(8,128)S(1)} %fusion.66), channel_id=1, source_target_pairs={{0,3},{1,0},{2,1},{3,2},{4,7},{5,4},{6,5},{7,6},{8,11},{9,8},{10,9... | collective-permute-start | bytes 245768 | tf_op jit(solution)/shard_map/ppermute | solution.py:36
  37.1 0.6 gather_fusion
  37.8 3.7 %collective-permute-done.3 = f32[8,2560]{1,0:T(8,128)S(1)} collective-permute-done((f32[8,2560]{1,0:T(8,128)S(1)}, f32[8,2560]{1,0:T(8,128)S(1)}, u32[]{:S(2)}, u32[]{:S(2)}) %collective-permute-start.3) | collective-permute-done | bytes 81952 | tf_op jit(solution)/shard_map/ppermute | solution.py:36
  42.2 1.1 %multiply_reduce_fusion = (f32[8]{0:T(128)S(1)}, f32[8,2560]{1,0:T(8,128)S(1)}) fusion(f32[8,2560]{1,0:T(8,128)} %collective-permute-done.4, f32[8,2560]{1,0:T(8,128)} %collective-permute-done.5, f32[8,2560]{1,0:T(8,128)S(1)} %fusion.66, f32[8,2560]{1,0:T(8,128)} %copy-done.4, bf16[8,2560]{1,0:T(8,128)(2,1)S(1)} %get-tuple-element.16), kind=kLoop, calls=%fused_computation.33 | loop fusion | flops 143352 | bytes 450592 | tf_op jit(solution)/shard_map/reduce_sum | solution.py:13
  43.3 3.0 %fusion.59 = f32[8,896]{1,0:T(8,128)S(1)} fusion(bf16[2560,896]{1,0:T(8,128)(2,1)} %param.25, f32[8,2560]{1,0:T(8,128)S(1)} %get-tuple-element.12, f32[2560]{0:T(1024)S(1)} %convert_element_type.73, f32[8]{0:T(128)S(1)} %add_rsqrt_fusion), kind=kOutput, calls=%fused_computation.120 | convolution fusion | flops 36761600 | bytes 4708384 | tf_op jit(solution)/shard_map/dot_general | solution.py:164
  46.3 5.3 %fusion.24 = f32[8,2560]{1,0:T(8,128)S(1)} fusion(bf16[896,2560]{1,0:T(8,128)(2,1)} %param.27, bf16[2560,896]{1,0:T(8,128)(2,1)} %param.26, f32[8,896]{1,0:T(8,128)S(1)} %fusion.59, f32[8,2560]{1,0:T(8,128)S(1)} %get-tuple-element.12, f32[2560]{0:T(1024)S(1)} %convert_element_type.73, f32[8]{0:T(128)S(1)} %add_rsqrt_fusion), kind=kOutput, calls=%fused_computation.18 | convolution fusion | flops 73504768 | bytes 9377824 | tf_op jit(solution)/shard_map/dot_general | solution.py:168
  51.6 0.8 %collective-permute-start.6 = (f32[8,2560]{1,0:T(8,128)S(1)}, f32[8,2560]{1,0:T(8,128)S(1)}, u32[]{:S(2)}, u32[]{:S(2)}) collective-permute-start(f32[8,2560]{1,0:T(8,128)S(1)} %fusion.24), channel_id=1, source_target_pairs={{0,2},{1,3},{2,0},{3,1},{4,6},{5,7},{6,4},{7,5},{8,10},{9,11},{10,... | collective-permute-start | bytes 245768 | tf_op jit(solution)/shard_map/ppermute | solution.py:36
  52.4 1.2 %collective-permute-start.7 = (f32[8,2560]{1,0:T(8,128)S(1)}, f32[8,2560]{1,0:T(8,128)S(1)}, u32[]{:S(2)}, u32[]{:S(2)}) collective-permute-start(f32[8,2560]{1,0:T(8,128)S(1)} %fusion.24), channel_id=1, source_target_pairs={{0,1},{1,2},{2,3},{3,0},{4,5},{5,6},{6,7},{7,4},{8,9},{9,10},{10,1... | collective-permute-start | bytes 245768 | tf_op jit(solution)/shard_map/ppermute | solution.py:36
  53.6 2.6 %collective-permute-start.8 = (f32[8,2560]{1,0:T(8,128)S(1)}, f32[8,2560]{1,0:T(8,128)S(1)}, u32[]{:S(2)}, u32[]{:S(2)}) collective-permute-start(f32[8,2560]{1,0:T(8,128)S(1)} %fusion.24), channel_id=1, source_target_pairs={{0,3},{1,0},{2,1},{3,2},{4,7},{5,4},{6,5},{7,6},{8,11},{9,8},{10,9... | collective-permute-start | bytes 245768 | tf_op jit(solution)/shard_map/ppermute | solution.py:36
  56.3 3.8 %collective-permute-done.6 = f32[8,2560]{1,0:T(8,128)S(1)} collective-permute-done((f32[8,2560]{1,0:T(8,128)S(1)}, f32[8,2560]{1,0:T(8,128)S(1)}, u32[]{:S(2)}, u32[]{:S(2)}) %collective-permute-start.6) | collective-permute-done | bytes 81952 | tf_op jit(solution)/shard_map/ppermute | solution.py:36
  60.7 0.7 reshape.434
  61.4 3.5 %all-to-all-start.1 = ((bf16[8,2,2560]{2,1,0:T(2,128)(2,1)}), bf16[8,2,2560]{2,1,0:T(2,128)(2,1)S(1)}, u32[]{:S(2)}, u32[]{:S(2)}) async-start(bf16[8,2,2560]{2,1,0:T(2,128)(2,1)} %reshape.434), calls=%async_computation.1 | async-start | bytes 163840 | tf_op jit(solution)/shard_map/all_to_all | solution.py:181
  64.9 5.1 %all-to-all-done.1 = bf16[8,2,2560]{2,1,0:T(2,128)(2,1)S(1)} async-done(((bf16[8,2,2560]{2,1,0:T(2,128)(2,1)}), bf16[8,2,2560]{2,1,0:T(2,128)(2,1)S(1)}, u32[]{:S(2)}, u32[]{:S(2)}) %all-to-all-start.1) | async-done | bytes 81952 | tf_op jit(solution)/shard_map/all_to_all | solution.py:181
  70.0 0.8 %select_reduce_fusion = bf16[2,2560]{1,0:T(2,128)(2,1)} fusion(bf16[8,2,2560]{2,1,0:T(2,128)(2,1)S(1)} %all-to-all-done.1, pred[8,2]{1,0:T(8,128)(4,1)S(1)} %iota_compare_fusion.3), kind=kLoop, calls=%fused_computation.21 | loop fusion | flops 117760 | bytes 92176 | tf_op jit(solution)/shard_map/reduce_sum | solution.py:185
  (67 shorter events, 5.5 us)
Async XLA Ops:
  0.0 32.7 %copy-start = (bf16[640,2560]{1,0:T(8,128)(2,1)S(1)}, bf16[640,2560]{1,0:T(8,128)(2,1)}, u32[]{:S(2)}) copy-start(bf16[640,2560]{1,0:T(8,128)(2,1)} %param.23) | copy-start | bytes 9830404
  1.6 10.4 %all-to-all-start = ((bf16[8,16,320]{2,1,0:T(8,128)(2,1)}), bf16[8,16,320]{2,1,0:T(8,128)(2,1)S(1)}, u32[]{:S(2)}, u32[]{:S(2)}) async-start(bf16[8,16,320]{2,1,0:T(8,128)(2,1)} %broadcast_in_dim.97), calls=%async_computation | async-start | bytes 196608 | tf_op jit(solution)/shard_map/all_to_all | solution.py:81
  13.0 11.5 %collective-permute-start = (bf16[8,2560]{1,0:T(8,128)(2,1)S(1)}, bf16[8,2560]{1,0:T(8,128)(2,1)S(1)}, u32[]{:S(2)}, u32[]{:S(2)}) collective-permute-start(bf16[8,2560]{1,0:T(8,128)(2,1)S(1)} %broadcast_select_fusion), channel_id=1, source_target_pairs={{0,2},{1,3},{2,0},{3,1},{4,6},{5,7},{6,4},{7,5},{8,10},{9,11},{10,... | collective-permute-start | bytes 122888 | tf_op jit(solution)/shard_map/ppermute | solution.py:36
  15.6 8.9 %collective-permute-start.1 = (bf16[8,2560]{1,0:T(8,128)(2,1)S(1)}, bf16[8,2560]{1,0:T(8,128)(2,1)S(1)}, u32[]{:S(2)}, u32[]{:S(2)}) collective-permute-start(bf16[8,2560]{1,0:T(8,128)(2,1)S(1)} %broadcast_select_fusion), channel_id=1, source_target_pairs={{0,1},{1,2},{2,3},{3,0},{4,5},{5,6},{6,7},{7,4},{8,9},{9,10},{10,1... | collective-permute-start | bytes 122888 | tf_op jit(solution)/shard_map/ppermute | solution.py:36
  17.2 7.3 %collective-permute-start.2 = (bf16[8,2560]{1,0:T(8,128)(2,1)S(1)}, bf16[8,2560]{1,0:T(8,128)(2,1)S(1)}, u32[]{:S(2)}, u32[]{:S(2)}) collective-permute-start(bf16[8,2560]{1,0:T(8,128)(2,1)S(1)} %broadcast_select_fusion), channel_id=1, source_target_pairs={{0,3},{1,0},{2,1},{3,2},{4,7},{5,4},{6,5},{7,6},{8,11},{9,8},{10,9... | collective-permute-start | bytes 122888 | tf_op jit(solution)/shard_map/ppermute | solution.py:36
  19.6 3.2 %copy-start.1 = (bf16[32,2,80,128]{3,2,1,0:T(8,128)(2,1)S(1)}, bf16[32,2,80,128]{3,2,1,0:T(8,128)(2,1)}, u32[]{:S(2)}) copy-start(bf16[32,2,80,128]{3,2,1,0:T(8,128)(2,1)} %param.20) | copy-start | bytes 3932164
  22.8 1.9 %copy-start.2 = (bf16[2560,160]{0,1:T(8,128)(2,1)S(1)}, bf16[2560,160]{0,1:T(8,128)(2,1)}, u32[]{:S(2)}) copy-start(bf16[2560,160]{0,1:T(8,128)(2,1)} %param.17) | copy-start | bytes 2457604
  27.7 2.6 %copy-start.3 = (bf16[2560,160]{0,1:T(8,128)(2,1)S(1)}, bf16[2560,160]{0,1:T(8,128)(2,1)}, u32[]{:S(2)}) copy-start(bf16[2560,160]{0,1:T(8,128)(2,1)} %param.18) | copy-start | bytes 2457604
  33.3 8.2 %collective-permute-start.3 = (f32[8,2560]{1,0:T(8,128)S(1)}, f32[8,2560]{1,0:T(8,128)S(1)}, u32[]{:S(2)}, u32[]{:S(2)}) collective-permute-start(f32[8,2560]{1,0:T(8,128)S(1)} %fusion.66), channel_id=1, source_target_pairs={{0,2},{1,3},{2,0},{3,1},{4,6},{5,7},{6,4},{7,5},{8,10},{9,11},{10,... | collective-permute-start | bytes 245768 | tf_op jit(solution)/shard_map/ppermute | solution.py:36
  33.3 8.2 %collective-permute-start.4 = (f32[8,2560]{1,0:T(8,128)S(1)}, f32[8,2560]{1,0:T(8,128)}, u32[]{:S(2)}, u32[]{:S(2)}) collective-permute-start(f32[8,2560]{1,0:T(8,128)S(1)} %fusion.66), channel_id=1, source_target_pairs={{0,1},{1,2},{2,3},{3,0},{4,5},{5,6},{6,7},{7,4},{8,9},{9,10},{10,1... | collective-permute-start | bytes 245768 | tf_op jit(solution)/shard_map/ppermute | solution.py:36
  34.6 7.6 %collective-permute-start.5 = (f32[8,2560]{1,0:T(8,128)S(1)}, f32[8,2560]{1,0:T(8,128)}, u32[]{:S(2)}, u32[]{:S(2)}) collective-permute-start(f32[8,2560]{1,0:T(8,128)S(1)} %fusion.66), channel_id=1, source_target_pairs={{0,3},{1,0},{2,1},{3,2},{4,7},{5,4},{6,5},{7,6},{8,11},{9,8},{10,9... | collective-permute-start | bytes 245768 | tf_op jit(solution)/shard_map/ppermute | solution.py:36
  41.5 0.6 copy-start.4
  51.6 8.5 %collective-permute-start.6 = (f32[8,2560]{1,0:T(8,128)S(1)}, f32[8,2560]{1,0:T(8,128)S(1)}, u32[]{:S(2)}, u32[]{:S(2)}) collective-permute-start(f32[8,2560]{1,0:T(8,128)S(1)} %fusion.24), channel_id=1, source_target_pairs={{0,2},{1,3},{2,0},{3,1},{4,6},{5,7},{6,4},{7,5},{8,10},{9,11},{10,... | collective-permute-start | bytes 245768 | tf_op jit(solution)/shard_map/ppermute | solution.py:36
  52.4 7.6 %collective-permute-start.7 = (f32[8,2560]{1,0:T(8,128)S(1)}, f32[8,2560]{1,0:T(8,128)S(1)}, u32[]{:S(2)}, u32[]{:S(2)}) collective-permute-start(f32[8,2560]{1,0:T(8,128)S(1)} %fusion.24), channel_id=1, source_target_pairs={{0,1},{1,2},{2,3},{3,0},{4,5},{5,6},{6,7},{7,4},{8,9},{9,10},{10,1... | collective-permute-start | bytes 245768 | tf_op jit(solution)/shard_map/ppermute | solution.py:36
  53.6 6.4 %collective-permute-start.8 = (f32[8,2560]{1,0:T(8,128)S(1)}, f32[8,2560]{1,0:T(8,128)S(1)}, u32[]{:S(2)}, u32[]{:S(2)}) collective-permute-start(f32[8,2560]{1,0:T(8,128)S(1)} %fusion.24), channel_id=1, source_target_pairs={{0,3},{1,0},{2,1},{3,2},{4,7},{5,4},{6,5},{7,6},{8,11},{9,8},{10,9... | collective-permute-start | bytes 245768 | tf_op jit(solution)/shard_map/ppermute | solution.py:36
  61.4 8.6 %all-to-all-start.1 = ((bf16[8,2,2560]{2,1,0:T(2,128)(2,1)}), bf16[8,2,2560]{2,1,0:T(2,128)(2,1)S(1)}, u32[]{:S(2)}, u32[]{:S(2)}) async-start(bf16[8,2,2560]{2,1,0:T(2,128)(2,1)} %reshape.434), calls=%async_computation.1 | async-start | bytes 163840 | tf_op jit(solution)/shard_map/all_to_all | solution.py:181

commit v17 on v12

--- a/solution.py
+++ b/solution.py
@@ -170,15 +170,13 @@
         + tp_index * rows_loc
         + jnp.arange(rows_loc, dtype=jnp.int32)[None, :]
     ).reshape(-1)
-    dest_round = jnp.sum(
-        jnp.where(request_ids[None, :] == dest_rows[:, None], round_no[None, :], 0), axis=1
-    )
-    outgoing = final[dest_round.reshape(dp_count, rows_loc)]
-    incoming = lax.all_to_all(outgoing, "dp", 0, 0)
+    gathered = lax.all_gather(final, "dp")
     mine = dp_index * req_loc + tp_index * rows_loc + jnp.arange(rows_loc, dtype=jnp.int32)
-    from_src = jnp.arange(dp_count, dtype=jnp.int32)[:, None] == server[mine][None, :]
-    picked = jnp.where(from_src[:, :, None], incoming.astype(jnp.float32), 0.0)
-    return jnp.sum(picked, axis=0).astype(jnp.bfloat16)
+    own_hot = (jnp.arange(dp_count, dtype=jnp.int32)[None, :, None] == server[mine][:, None, None]) & (
+        slots[None, None, :] == round_no[mine][:, None, None]
+    )
+    picked = jnp.where(own_hot[..., None], gathered.astype(jnp.float32)[None], 0.0)
+    return jnp.sum(picked, axis=(1, 2)).astype(jnp.bfloat16)
 
 
 def solution(mesh):

time: 70.7 us -> 68.4 us (0.967)
  blocking collectives: 0 us -> 9.25 us
  starting transfers between devices: 24 us -> 20.1 us
  waiting for transfers between devices: 12.5 us -> 8.86 us
  other arithmetic: 7.13 us -> 4.74 us
  local copies, waits for them, and re-layouts: 5.43 us -> 3.96 us
    all_gather x0 -> x1, blocking collectives: none -> 9.25 us  [local(): gathered = lax.all_gather(final, 'dp')]
    all_to_all x1 -> x0, waiting for transfers between devices: 5.1 us -> none  [local(): incoming = lax.all_to_all(outgoing, 'dp', 0, 0)]
    all_to_all x1 -> x0, starting transfers between devices: 3.86 us -> none  [local(): incoming = lax.all_to_all(outgoing, 'dp', 0, 0)]
    reduce_sum x2, other arithmetic: 1.25 us -> 0.29 us  [norm_rows(): jnp.mean(value_rows * value_rows, axis=-1, keepdims=True) + 1e-05]
    ppermute x9, waiting for transfers between devices: 7.1 us -> 7.93 us  [shifted(): lax.ppermute(value, 'tensor', [(i, (i + k) % tp_count) for i in range(tp_...]
    gather x3 -> x2, local copies, waits for them, and re-layouts: 1.9 us -> 1.28 us  [the longest x1 0.64 us: local(): round_no[mine][:, None, None]]
  transfers between devices with their start and end apart: 11 -> 10, of which waited for: 4 -> 4; matrix products, arithmetic and copies ran while one was open for 15% -> 14% of each run, Pallas kernels for 0% -> 0%
where the time goes in v17:
time: 68.4 us; the launch traced here: 68 us
  matrix products  21 us (31%)
  starting transfers between devices  20.1 us (29%)
  blocking collectives  9.25 us (14%)
  waiting for transfers between devices  8.86 us (13%)
  other arithmetic  4.74 us (7%)
  local copies, waits for them, and re-layouts  3.96 us (6%)
    ppermute x9, starting transfers between devices, shifted(): lax.ppermute(value, 'tensor', [(i, (i + k) % tp_count) for i in range(tp_...  14.9 us
    all_gather x1, blocking collectives, local(): gathered = lax.all_gather(final, 'dp')  9.25 us
    ppermute x9, waiting for transfers between devices, shifted(): lax.ppermute(value, 'tensor', [(i, (i + k) % tp_count) for i in range(tp_...  7.93 us
    dot_general x1, matrix products, local(): jnp.dot(hidden, w_down, preferred_element_type=jnp.float32)  5.29 us
    all_to_all x1, starting transfers between devices, local(): lax.all_to_all(jnp.broadcast_to(residual_in[None], (dp_count,) + residual...  5.17 us
    dot_general x1, matrix products, local(): jnp.einsum('sq,qhdc->shdc', page_hot, key_page_pool, preferred_element_ty...  3.16 us
    dot_general x1, matrix products, local(): gate_act = jnp.dot(normed_mlp, w_gate, preferred_element_type=jnp.float32)  3.05 us
    dot_general x1, matrix products, local(): jnp.dot(scaled_input, w_query, preferred_element_type=jnp.float32)  2.51 us
  transfers between devices with their start and end apart: 10, of which 4 were waited for; matrix products, arithmetic and copies ran while one was open for 14% of the time, Pallas kernels for 0%

profile of v17, /device:TPU:0, one launch (start us, length us, event | category | flops | bytes accessed | tf_op | source)
XLA Modules:
  0.0 68.0 jit_solution(14111398498550648785)
XLA Ops:
  0.0 1.5 %broadcast_in_dim.85 = bf16[8,2,2560]{2,1,0:T(2,128)(2,1)} broadcast(bf16[2,2560]{1,0:T(2,128)(2,1)} %param.14), dimensions={1,2} | broadcast | bytes 92160 | tf_op jit(solution)/shard_map/broadcast_in_dim | solution.py:79
  1.5 5.2 %all-to-all-start = ((bf16[8,2,2560]{2,1,0:T(2,128)(2,1)}), bf16[8,2,2560]{2,1,0:T(2,128)(2,1)S(1)}, u32[]{:S(2)}, u32[]{:S(2)}) async-start(bf16[8,2,2560]{2,1,0:T(2,128)(2,1)} %broadcast_in_dim.85), calls=%async_computation | async-start | bytes 163840 | tf_op jit(solution)/shard_map/all_to_all | solution.py:78
  6.7 0.7 iota_add_fusion.1
  7.6 0.8 %select_reduce_fusion.3 = (s32[8]{0:T(128)S(1)}, s32[8]{0:T(128)S(1)}) fusion(s32[64]{0:T(128)} %param.21, s32[64]{0:T(128)S(1)} %get-tuple-element.19, pred[64]{0:T(512)(128)(4,1)S(1)} %get-tuple-element.17), kind=kLoop, calls=%fused_computation.67 | loop fusion | flops 3056 | bytes 640 | tf_op jit(solution)/shard_map/reduce_sum | solution.py:91
  8.5 0.7 %convert_element_type.65 = f32[2560]{0:T(1024)S(1)} convert(bf16[2560]{0:T(1024)(128)(2,1)} %param.15) | non-fusion elementwise | flops 2560 | bytes 15360 | tf_op jit(solution)/shard_map/convert_element_type | solution.py:14
  9.3 0.6 gather_fusion.1
  10.0 0.6 gather_fusion
  10.9 0.9 %all-to-all-done = bf16[8,2,2560]{2,1,0:T(2,128)(2,1)S(1)} async-done(((bf16[8,2,2560]{2,1,0:T(2,128)(2,1)}), bf16[8,2,2560]{2,1,0:T(2,128)(2,1)S(1)}, u32[]{:S(2)}, u32[]{:S(2)}) %all-to-all-start) | async-done | bytes 81952 | tf_op jit(solution)/shard_map/all_to_all | solution.py:78
  11.8 0.6 gather_fusion.2
  12.5 2.6 %collective-permute-start = (bf16[8,2560]{1,0:T(8,128)(2,1)S(1)}, bf16[8,2560]{1,0:T(8,128)(2,1)S(1)}, u32[]{:S(2)}, u32[]{:S(2)}) collective-permute-start(bf16[8,2560]{1,0:T(8,128)(2,1)S(1)} %broadcast_select_fusion), channel_id=1, source_target_pairs={{0,2},{1,3},{2,0},{3,1},{4,6},{5,7},{6,4},{7,5},{8,10},{9,11},{10,... | collective-permute-start | bytes 122888 | tf_op jit(solution)/shard_map/ppermute | solution.py:36
  15.1 1.6 %collective-permute-start.1 = (bf16[8,2560]{1,0:T(8,128)(2,1)S(1)}, bf16[8,2560]{1,0:T(8,128)(2,1)S(1)}, u32[]{:S(2)}, u32[]{:S(2)}) collective-permute-start(bf16[8,2560]{1,0:T(8,128)(2,1)S(1)} %broadcast_select_fusion), channel_id=1, source_target_pairs={{0,1},{1,2},{2,3},{3,0},{4,5},{5,6},{6,7},{7,4},{8,9},{9,10},{10,1... | collective-permute-start | bytes 122888 | tf_op jit(solution)/shard_map/ppermute | solution.py:36
  16.7 2.2 %collective-permute-start.2 = (bf16[8,2560]{1,0:T(8,128)(2,1)S(1)}, bf16[8,2560]{1,0:T(8,128)(2,1)S(1)}, u32[]{:S(2)}, u32[]{:S(2)}) collective-permute-start(bf16[8,2560]{1,0:T(8,128)(2,1)S(1)} %broadcast_select_fusion), channel_id=1, source_target_pairs={{0,3},{1,0},{2,1},{3,2},{4,7},{5,4},{6,5},{7,6},{8,11},{9,8},{10,9... | collective-permute-start | bytes 122888 | tf_op jit(solution)/shard_map/ppermute | solution.py:36
  19.1 3.2 %fusion.6 = bf16[32,2,80,128]{3,0,2,1:T(8,128)(2,1)} fusion(bf16[32,2,80,128]{3,2,1,0:T(8,128)(2,1)} %param.19, s32[32]{0:T(128)S(1)} %eq.117), kind=kOutput, calls=%fused_computation.9 | convolution fusion | flops 41944064 | bytes 2621568 | tf_op jit(solution)/shard_map/sq,qhdc->shdc/dot_general | solution.py:126
  22.3 1.7 %fusion.2 = bf16[32,2,80,128]{3,0,2,1:T(8,128)(2,1)} fusion(bf16[32,2,80,128]{3,2,1,0:T(8,128)(2,1)S(1)} %copy-done.1, s32[32]{0:T(128)S(1)} %eq.117), kind=kOutput, calls=%fused_computation.5 | convolution fusion | flops 41944064 | bytes 2621568 | tf_op jit(solution)/shard_map/sq,qhdc->shdc/dot_general | solution.py:129
  24.2 0.3 fusion.62
  24.6 2.5 %fusion.64 = f32[8,640]{1,0:T(8,128)S(1)} fusion(bf16[2560,640]{1,0:T(8,128)(2,1)} %param.16, bf16[8,2560]{1,0:T(8,128)(2,1)S(1)} %get-tuple-element.16, f32[2560]{0:T(1024)S(1)} %convert_element_type.65, f32[8]{0:T(128)S(1)} %add_rsqrt_fusion.1), kind=kOutput, calls=%fused_computation.122 | convolution fusion | flops 26296320 | bytes 3348512 | tf_op jit(solution)/shard_map/dot_general | solution.py:102
  27.7 1.9 %select_reduce_fusion.1 = (f32[8,2,4]{2,1,0:T(2,128)S(1)}, f32[8,2,4,4,128]{4,2,3,1,0:T(4,128)S(1)}) fusion(pred[8,4,128]{2,1,0:T(4,128)(4,1)S(1)} %broadcast_compare_fusion, bf16[8,4,2,80,128]{4,1,0,3,2:T(4,128)(2,1)} %bitcast.61, bf16[8,2,4,40]{3,2,1,0:T(4,128)(2,1)S(1)} %bitcast.67, bf16[8,2,4,40]{3,2,1,0:T(4,128)(2,1)S(1)} %bitcast.65), kind=kOutput, calls=%fused_computation.24 | convolution fusion | flops 5361600 | bytes 1456384 | tf_op jit(solution)/shard_map/rhgd,rphdc->rhgpc/dot_general | solution.py:133
  29.8 0.3 fusion.25
  30.3 1.9 %fusion.20 = bf16[8,2,4,80]{3,2,1,0:T(4,128)(2,1)S(1)} fusion(bf16[8,4,2,80,128]{4,1,0,3,2:T(4,128)(2,1)} %bitcast.60, f32[8,2,4,4,128]{4,2,3,1,0:T(4,128)S(1)} %get-tuple-element.27, f32[8,2,4]{2,1,0:T(2,128)S(1)} %multiply_maximum_fusion, pred[8,4,128]{2,1,0:T(4,128)(4,1)S(1)} %broadcast_compare_fusion, f32[8,2,4]{2,1,0:T(2,128)S(1)} %get-tuple-element.13, ...), kind=kOutput, calls=%fused_computation.17 | convolution fusion | flops 5328896 | bytes 1462016 | tf_op jit(solution)/shard_map/rhgpc,rphdc->rhgd/dot_general | solution.py:149
  32.3 0.5 fusion.67
  32.8 1.3 %collective-permute-start.4 = (f32[8,2560]{1,0:T(8,128)S(1)}, f32[8,2560]{1,0:T(8,128)S(1)}, u32[]{:S(2)}, u32[]{:S(2)}) collective-permute-start(f32[8,2560]{1,0:T(8,128)S(1)} %fusion.67), channel_id=1, source_target_pairs={{0,1},{1,2},{2,3},{3,0},{4,5},{5,6},{6,7},{7,4},{8,9},{9,10},{10,1... | collective-permute-start | bytes 245768 | tf_op jit(solution)/shard_map/ppermute | solution.py:36
  34.1 2.6 %collective-permute-start.5 = (f32[8,2560]{1,0:T(8,128)S(1)}, f32[8,2560]{1,0:T(8,128)S(1)}, u32[]{:S(2)}, u32[]{:S(2)}) collective-permute-start(f32[8,2560]{1,0:T(8,128)S(1)} %fusion.67), channel_id=1, source_target_pairs={{0,3},{1,0},{2,1},{3,2},{4,7},{5,4},{6,5},{7,6},{8,11},{9,8},{10,9... | collective-permute-start | bytes 245768 | tf_op jit(solution)/shard_map/ppermute | solution.py:36
  36.7 3.7 %collective-permute-done.3 = f32[8,2560]{1,0:T(8,128)S(1)} collective-permute-done((f32[8,2560]{1,0:T(8,128)S(1)}, f32[8,2560]{1,0:T(8,128)S(1)}, u32[]{:S(2)}, u32[]{:S(2)}) %collective-permute-start.3) | collective-permute-done | bytes 81952 | tf_op jit(solution)/shard_map/ppermute | solution.py:36
  40.6 3.0 %fusion.60 = f32[8,896]{1,0:T(8,128)S(1)} fusion(bf16[2560,896]{1,0:T(8,128)(2,1)} %param.25, f32[8,2560]{1,0:T(8,128)S(1)} %get-tuple-element.12, f32[2560]{0:T(1024)S(1)} %convert_element_type.73, f32[8]{0:T(128)S(1)} %add_rsqrt_fusion), kind=kOutput, calls=%fused_computation.120 | convolution fusion | flops 36761600 | bytes 4708384 | tf_op jit(solution)/shard_map/dot_general | solution.py:160
  43.6 5.3 %fusion.24 = f32[8,2560]{1,0:T(8,128)S(1)} fusion(bf16[896,2560]{1,0:T(8,128)(2,1)} %param.27, bf16[2560,896]{1,0:T(8,128)(2,1)} %param.26, f32[8,896]{1,0:T(8,128)S(1)} %fusion.60, f32[8,2560]{1,0:T(8,128)S(1)} %get-tuple-element.12, f32[2560]{0:T(1024)S(1)} %convert_element_type.73, f32[8]{0:T(128)S(1)} %add_rsqrt_fusion), kind=kOutput, calls=%fused_computation.19 | convolution fusion | flops 73504768 | bytes 9377824 | tf_op jit(solution)/shard_map/dot_general | solution.py:164
  48.9 0.8 %collective-permute-start.6 = (f32[8,2560]{1,0:T(8,128)S(1)}, f32[8,2560]{1,0:T(8,128)S(1)}, u32[]{:S(2)}, u32[]{:S(2)}) collective-permute-start(f32[8,2560]{1,0:T(8,128)S(1)} %fusion.24), channel_id=1, source_target_pairs={{0,2},{1,3},{2,0},{3,1},{4,6},{5,7},{6,4},{7,5},{8,10},{9,11},{10,... | collective-permute-start | bytes 245768 | tf_op jit(solution)/shard_map/ppermute | solution.py:36
  49.7 2.3 %collective-permute-start.7 = (f32[8,2560]{1,0:T(8,128)S(1)}, f32[8,2560]{1,0:T(8,128)S(1)}, u32[]{:S(2)}, u32[]{:S(2)}) collective-permute-start(f32[8,2560]{1,0:T(8,128)S(1)} %fusion.24), channel_id=1, source_target_pairs={{0,1},{1,2},{2,3},{3,0},{4,5},{5,6},{6,7},{7,4},{8,9},{9,10},{10,1... | collective-permute-start | bytes 245768 | tf_op jit(solution)/shard_map/ppermute | solution.py:36
  52.1 1.5 %collective-permute-start.8 = (f32[8,2560]{1,0:T(8,128)S(1)}, f32[8,2560]{1,0:T(8,128)S(1)}, u32[]{:S(2)}, u32[]{:S(2)}) collective-permute-start(f32[8,2560]{1,0:T(8,128)S(1)} %fusion.24), channel_id=1, source_target_pairs={{0,3},{1,0},{2,1},{3,2},{4,7},{5,4},{6,5},{7,6},{8,11},{9,8},{10,9... | collective-permute-start | bytes 245768 | tf_op jit(solution)/shard_map/ppermute | solution.py:36
  53.6 3.8 %collective-permute-done.6 = f32[8,2560]{1,0:T(8,128)S(1)} collective-permute-done((f32[8,2560]{1,0:T(8,128)S(1)}, f32[8,2560]{1,0:T(8,128)S(1)}, u32[]{:S(2)}, u32[]{:S(2)}) %collective-permute-start.6) | collective-permute-done | bytes 81952 | tf_op jit(solution)/shard_map/ppermute | solution.py:36
  57.5 0.4 collective-permute-done.8
  57.9 9.2 %all-gather = bf16[64,2560]{1,0:T(8,128)(2,1)S(1)} all-gather(bf16[8,2560]{1,0:T(8,128)(2,1)S(1)} %add_convert_fusion), channel_id=2, replica_groups=mesh['dp'=8,'tensor'=4] {'dp'}, dimensions={0}, use_global_device_ids=true | all-gather | bytes 368640 | tf_op jit(solution)/shard_map/all_gather | solution.py:173
  67.2 0.8 %select_reduce_fusion = bf16[2,2560]{1,0:T(2,128)(2,1)} fusion(f32[8,8,2560]{2,1,0:T(8,128)S(1)} %bitcast_convert_fusion, pred[2,8,8]{2,1,0:T(8,128)(4,1)S(1)} %broadcast_and_fusion), kind=kLoop, calls=%fused_computation.11 | loop fusion | flops 650240 | bytes 665728 | tf_op jit(solution)/shard_map/reduce_sum | solution.py:179
  (57 shorter events, 2.5 us)
Async XLA Ops:
  0.0 32.3 %copy-start = (bf16[640,2560]{1,0:T(8,128)(2,1)S(1)}, bf16[640,2560]{1,0:T(8,128)(2,1)}, u32[]{:S(2)}) copy-start(bf16[640,2560]{1,0:T(8,128)(2,1)} %param.23) | copy-start | bytes 9830404
  0.0 10.7 %copy-start.5 = (s32[64,4]{0,1:T(4,128)S(1)}, s32[64,4]{0,1:T(4,128)}, u32[]{:S(2)}) copy-start(s32[64,4]{0,1:T(4,128)} %param.22) | copy-start | bytes 3076
  1.5 10.3 %all-to-all-start = ((bf16[8,2,2560]{2,1,0:T(2,128)(2,1)}), bf16[8,2,2560]{2,1,0:T(2,128)(2,1)S(1)}, u32[]{:S(2)}, u32[]{:S(2)}) async-start(bf16[8,2,2560]{2,1,0:T(2,128)(2,1)} %broadcast_in_dim.85), calls=%async_computation | async-start | bytes 163840 | tf_op jit(solution)/shard_map/all_to_all | solution.py:78
  12.5 11.5 %collective-permute-start = (bf16[8,2560]{1,0:T(8,128)(2,1)S(1)}, bf16[8,2560]{1,0:T(8,128)(2,1)S(1)}, u32[]{:S(2)}, u32[]{:S(2)}) collective-permute-start(bf16[8,2560]{1,0:T(8,128)(2,1)S(1)} %broadcast_select_fusion), channel_id=1, source_target_pairs={{0,2},{1,3},{2,0},{3,1},{4,6},{5,7},{6,4},{7,5},{8,10},{9,11},{10,... | collective-permute-start | bytes 122888 | tf_op jit(solution)/shard_map/ppermute | solution.py:36
  15.1 8.9 %collective-permute-start.1 = (bf16[8,2560]{1,0:T(8,128)(2,1)S(1)}, bf16[8,2560]{1,0:T(8,128)(2,1)S(1)}, u32[]{:S(2)}, u32[]{:S(2)}) collective-permute-start(bf16[8,2560]{1,0:T(8,128)(2,1)S(1)} %broadcast_select_fusion), channel_id=1, source_target_pairs={{0,1},{1,2},{2,3},{3,0},{4,5},{5,6},{6,7},{7,4},{8,9},{9,10},{10,1... | collective-permute-start | bytes 122888 | tf_op jit(solution)/shard_map/ppermute | solution.py:36
  16.7 7.3 %collective-permute-start.2 = (bf16[8,2560]{1,0:T(8,128)(2,1)S(1)}, bf16[8,2560]{1,0:T(8,128)(2,1)S(1)}, u32[]{:S(2)}, u32[]{:S(2)}) collective-permute-start(bf16[8,2560]{1,0:T(8,128)(2,1)S(1)} %broadcast_select_fusion), channel_id=1, source_target_pairs={{0,3},{1,0},{2,1},{3,2},{4,7},{5,4},{6,5},{7,6},{8,11},{9,8},{10,9... | collective-permute-start | bytes 122888 | tf_op jit(solution)/shard_map/ppermute | solution.py:36
  19.1 3.2 %copy-start.1 = (bf16[32,2,80,128]{3,2,1,0:T(8,128)(2,1)S(1)}, bf16[32,2,80,128]{3,2,1,0:T(8,128)(2,1)}, u32[]{:S(2)}) copy-start(bf16[32,2,80,128]{3,2,1,0:T(8,128)(2,1)} %param.20) | copy-start | bytes 3932164
  22.3 1.9 %copy-start.2 = (bf16[2560,160]{0,1:T(8,128)(2,1)S(1)}, bf16[2560,160]{0,1:T(8,128)(2,1)}, u32[]{:S(2)}) copy-start(bf16[2560,160]{0,1:T(8,128)(2,1)} %param.17) | copy-start | bytes 2457604
  27.2 2.6 %copy-start.3 = (bf16[2560,160]{0,1:T(8,128)(2,1)S(1)}, bf16[2560,160]{0,1:T(8,128)(2,1)}, u32[]{:S(2)}) copy-start(bf16[2560,160]{0,1:T(8,128)(2,1)} %param.18) | copy-start | bytes 2457604
  32.3 4.5 %copy-start.4 = (bf16[2560]{0:T(1024)(128)(2,1)S(1)}, bf16[2560]{0:T(1024)(128)(2,1)}, u32[]{:S(2)}) copy-start(bf16[2560]{0:T(1024)(128)(2,1)} %param.24) | copy-start | bytes 15364
  32.8 7.6 %collective-permute-start.3 = (f32[8,2560]{1,0:T(8,128)S(1)}, f32[8,2560]{1,0:T(8,128)S(1)}, u32[]{:S(2)}, u32[]{:S(2)}) collective-permute-start(f32[8,2560]{1,0:T(8,128)S(1)} %fusion.67), channel_id=1, source_target_pairs={{0,2},{1,3},{2,0},{3,1},{4,6},{5,7},{6,4},{7,5},{8,10},{9,11},{10,... | collective-permute-start | bytes 245768 | tf_op jit(solution)/shard_map/ppermute | solution.py:36
  32.8 7.6 %collective-permute-start.4 = (f32[8,2560]{1,0:T(8,128)S(1)}, f32[8,2560]{1,0:T(8,128)S(1)}, u32[]{:S(2)}, u32[]{:S(2)}) collective-permute-start(f32[8,2560]{1,0:T(8,128)S(1)} %fusion.67), channel_id=1, source_target_pairs={{0,1},{1,2},{2,3},{3,0},{4,5},{5,6},{6,7},{7,4},{8,9},{9,10},{10,1... | collective-permute-start | bytes 245768 | tf_op jit(solution)/shard_map/ppermute | solution.py:36
  34.1 6.3 %collective-permute-start.5 = (f32[8,2560]{1,0:T(8,128)S(1)}, f32[8,2560]{1,0:T(8,128)S(1)}, u32[]{:S(2)}, u32[]{:S(2)}) collective-permute-start(f32[8,2560]{1,0:T(8,128)S(1)} %fusion.67), channel_id=1, source_target_pairs={{0,3},{1,0},{2,1},{3,2},{4,7},{5,4},{6,5},{7,6},{8,11},{9,8},{10,9... | collective-permute-start | bytes 245768 | tf_op jit(solution)/shard_map/ppermute | solution.py:36
  48.9 8.5 %collective-permute-start.6 = (f32[8,2560]{1,0:T(8,128)S(1)}, f32[8,2560]{1,0:T(8,128)S(1)}, u32[]{:S(2)}, u32[]{:S(2)}) collective-permute-start(f32[8,2560]{1,0:T(8,128)S(1)} %fusion.24), channel_id=1, source_target_pairs={{0,2},{1,3},{2,0},{3,1},{4,6},{5,7},{6,4},{7,5},{8,10},{9,11},{10,... | collective-permute-start | bytes 245768 | tf_op jit(solution)/shard_map/ppermute | solution.py:36
  49.7 7.7 %collective-permute-start.7 = (f32[8,2560]{1,0:T(8,128)S(1)}, f32[8,2560]{1,0:T(8,128)S(1)}, u32[]{:S(2)}, u32[]{:S(2)}) collective-permute-start(f32[8,2560]{1,0:T(8,128)S(1)} %fusion.24), channel_id=1, source_target_pairs={{0,1},{1,2},{2,3},{3,0},{4,5},{5,6},{6,7},{7,4},{8,9},{9,10},{10,1... | collective-permute-start | bytes 245768 | tf_op jit(solution)/shard_map/ppermute | solution.py:36
  52.1 5.8 %collective-permute-start.8 = (f32[8,2560]{1,0:T(8,128)S(1)}, f32[8,2560]{1,0:T(8,128)S(1)}, u32[]{:S(2)}, u32[]{:S(2)}) collective-permute-start(f32[8,2560]{1,0:T(8,128)S(1)} %fusion.24), channel_id=1, source_target_pairs={{0,3},{1,0},{2,1},{3,2},{4,7},{5,4},{6,5},{7,6},{8,11},{9,8},{10,9... | collective-permute-start | bytes 245768 | tf_op jit(solution)/shard_map/ppermute | solution.py:36

commit v18 on v17

--- a/solution.py
+++ b/solution.py
@@ -75,9 +75,7 @@
     dp_index = lax.axis_index("dp")
     tp_index = lax.axis_index("tensor")
 
-    rows_dp = lax.all_to_all(
-        jnp.broadcast_to(residual_in[None], (dp_count,) + residual_in.shape), "dp", 0, 0
-    )
+    rows_dp = lax.all_gather(residual_in, "dp")
 
     request_ids = jnp.arange(total_reqs, dtype=jnp.int32)
     ranking = lengths * total_reqs + request_ids

time: 68.4 us -> 74.7 us (1.092)
  blocking collectives: 9.25 us -> 20.2 us
  starting transfers between devices: 20.1 us -> 15.2 us
  local copies, waits for them, and re-layouts: 3.96 us -> 2.43 us
  matrix products: 21 us -> 22.1 us
  other arithmetic: 4.74 us -> 5.66 us
    all_gather x0 -> x1, blocking collectives: none -> 10.9 us  [local(): rows_dp = lax.all_gather(residual_in, 'dp')]
    all_to_all x1 -> x0, starting transfers between devices: 5.17 us -> none  [local(): lax.all_to_all(jnp.broadcast_to(residual_in[None], (dp_count,) + residual...]
    broadcast_in_dim x1 -> x0, local copies, waits for them, and re-layouts: 1.53 us -> none  [local(): jnp.broadcast_to(residual_in[None], (dp_count,) + residual_in.shape)]
    dot_general x1, matrix products: 0.34 us -> 1.48 us  [local(): jnp.dot(scaled_input, key_weight, preferred_element_type=jnp.float32)]
    all_to_all x1 -> x0, waiting for transfers between devices: 0.93 us -> none  [local(): lax.all_to_all(jnp.broadcast_to(residual_in[None], (dp_count,) + residual...]
    reduce_sum x2, other arithmetic: 0.29 us -> 1.07 us  [norm_rows(): jnp.mean(value_rows * value_rows, axis=-1, keepdims=True) + 1e-05]
  transfers between devices with their start and end apart: 10 -> 9, of which waited for: 4 -> 3; matrix products, arithmetic and copies ran while one was open for 14% -> 9% of each run, Pallas kernels for 0% -> 0%
where the time goes in v18:
time: 74.7 us; the launch traced here: 74.2 us
  matrix products  22.1 us (30%)
  blocking collectives  20.2 us (27%)
  starting transfers between devices  15.2 us (20%)
  waiting for transfers between devices  8.45 us (11%)
  other arithmetic  5.66 us (8%)
  local copies, waits for them, and re-layouts  2.43 us (3%)
    ppermute x9, starting transfers between devices, shifted(): lax.ppermute(value, 'tensor', [(i, (i + k) % tp_count) for i in range(tp_...  15.2 us
    all_gather x1, blocking collectives, local(): rows_dp = lax.all_gather(residual_in, 'dp')  10.9 us
    all_gather x1, blocking collectives, local(): gathered = lax.all_gather(final, 'dp')  9.28 us
    ppermute x9, waiting for transfers between devices, shifted(): lax.ppermute(value, 'tensor', [(i, (i + k) % tp_count) for i in range(tp_...  8.45 us
    dot_general x1, matrix products, local(): jnp.dot(hidden, w_down, preferred_element_type=jnp.float32)  5.29 us
    dot_general x1, matrix products, local(): jnp.einsum('sq,qhdc->shdc', page_hot, key_page_pool, preferred_element_ty...  3.15 us
    dot_general x1, matrix products, local(): gate_act = jnp.dot(normed_mlp, w_gate, preferred_element_type=jnp.float32)  3.05 us
    dot_general x1, matrix products, local(): jnp.dot(scaled_input, w_query, preferred_element_type=jnp.float32)  2.51 us
  transfers between devices with their start and end apart: 9, of which 3 were waited for; matrix products, arithmetic and copies ran while one was open for 9% of the time, Pallas kernels for 0%

profile of v18, /device:TPU:0, one launch (start us, length us, event | category | flops | bytes accessed | tf_op | source)
XLA Modules:
  0.0 74.2 jit_solution(12711172096315294721)
XLA Ops:
  0.0 0.8 %iota_add_fusion.1 = s32[64]{0:T(128)S(1)} fusion(s32[64]{0:T(128)} %param.21), kind=kLoop, calls=%fused_computation.116 | loop fusion | flops 128 | bytes 512 | tf_op jit(solution)/shard_map/add | solution.py:81
  1.0 0.8 %select_reduce_fusion.3 = (s32[8]{0:T(128)S(1)}, s32[8]{0:T(128)S(1)}) fusion(s32[64]{0:T(128)} %param.21, s32[64]{0:T(128)S(1)} %get-tuple-element.19, pred[64]{0:T(512)(128)(4,1)S(1)} %get-tuple-element.17), kind=kLoop, calls=%fused_computation.67 | loop fusion | flops 3056 | bytes 640 | tf_op jit(solution)/shard_map/reduce_sum | solution.py:89
  1.9 10.9 %all-gather.2 = bf16[8,2,2560]{2,1,0:T(2,128)(2,1)S(1)} all-gather(bf16[1,2,2560]{2,1,0:T(2,128)(2,1)} %bitcast.69), channel_id=2, replica_groups=mesh['dp'=8,'tensor'=4] {'dp'}, dimensions={0}, use_global_device_ids=true | all-gather | bytes 92160 | tf_op jit(solution)/shard_map/all_gather | solution.py:78
  12.8 0.6 gather_fusion.2
  13.5 0.8 %select_reduce_fusion.2 = s32[8,4]{0,1:T(4,128)S(1)} fusion(s32[64,4]{0,1:T(4,128)} %param.22, pred[8,64]{1,0:T(8,128)(4,1)S(1)} %fusion.47), kind=kLoop, calls=%fused_computation.51 | loop fusion | flops 4064 | bytes 1664 | tf_op jit(solution)/shard_map/reduce_sum | solution.py:90
  14.3 2.7 %collective-permute-start = (bf16[8,2560]{1,0:T(8,128)(2,1)S(1)}, bf16[8,2560]{1,0:T(8,128)(2,1)S(1)}, u32[]{:S(2)}, u32[]{:S(2)}) collective-permute-start(bf16[8,2560]{1,0:T(8,128)(2,1)S(1)} %broadcast_select_fusion), channel_id=1, source_target_pairs={{0,2},{1,3},{2,0},{3,1},{4,6},{5,7},{6,4},{7,5},{8,10},{9,11},{10,... | collective-permute-start | bytes 122888 | tf_op jit(solution)/shard_map/ppermute | solution.py:36
  16.9 1.6 %collective-permute-start.1 = (bf16[8,2560]{1,0:T(8,128)(2,1)S(1)}, bf16[8,2560]{1,0:T(8,128)(2,1)S(1)}, u32[]{:S(2)}, u32[]{:S(2)}) collective-permute-start(bf16[8,2560]{1,0:T(8,128)(2,1)S(1)} %broadcast_select_fusion), channel_id=1, source_target_pairs={{0,1},{1,2},{2,3},{3,0},{4,5},{5,6},{6,7},{7,4},{8,9},{9,10},{10,1... | collective-permute-start | bytes 122888 | tf_op jit(solution)/shard_map/ppermute | solution.py:36
  18.5 2.2 %collective-permute-start.2 = (bf16[8,2560]{1,0:T(8,128)(2,1)S(1)}, bf16[8,2560]{1,0:T(8,128)(2,1)}, u32[]{:S(2)}, u32[]{:S(2)}) collective-permute-start(bf16[8,2560]{1,0:T(8,128)(2,1)S(1)} %broadcast_select_fusion), channel_id=1, source_target_pairs={{0,3},{1,0},{2,1},{3,2},{4,7},{5,4},{6,5},{7,6},{8,11},{9,8},{10,9... | collective-permute-start | bytes 122888 | tf_op jit(solution)/shard_map/ppermute | solution.py:36
  21.1 3.1 %fusion.6 = bf16[32,2,80,128]{3,0,2,1:T(8,128)(2,1)} fusion(bf16[32,2,80,128]{3,2,1,0:T(8,128)(2,1)} %param.19, s32[32]{0:T(128)S(1)} %eq.117), kind=kOutput, calls=%fused_computation.9 | convolution fusion | flops 41944064 | bytes 2621568 | tf_op jit(solution)/shard_map/sq,qhdc->shdc/dot_general | solution.py:124
  24.3 1.7 %fusion.2 = bf16[32,2,80,128]{3,0,2,1:T(8,128)(2,1)} fusion(bf16[32,2,80,128]{3,2,1,0:T(8,128)(2,1)S(1)} %copy-done.1, s32[32]{0:T(128)S(1)} %eq.117), kind=kOutput, calls=%fused_computation.5 | convolution fusion | flops 41944064 | bytes 2621568 | tf_op jit(solution)/shard_map/sq,qhdc->shdc/dot_general | solution.py:127
  26.2 0.6 gather_fusion.1
  26.8 0.6 gather_fusion
  27.5 0.9 %fusion.27 = (f32[8]{0:T(128)S(1)}, bf16[8,2560]{1,0:T(8,128)(2,1)S(1)}) fusion(bf16[8,2560]{1,0:T(8,128)(2,1)S(1)} %collective-permute-done.1, bf16[8,2560]{1,0:T(8,128)(2,1)} %collective-permute-done.2, bf16[8,2560]{1,0:T(8,128)(2,1)S(1)} %broadcast_select_fusion, bf16[8,2560]{1,0:T(8,128)(2,1)S(1)} %collective-permute-done), kind=kLoop, calls=%fused_computation.29 | loop fusion | flops 122872 | bytes 204832 | tf_op jit(solution)/shard_map/reduce_sum | solution.py:13
  28.4 1.5 %fusion.62 = f32[8,160]{1,0:T(8,128)S(1)} fusion(bf16[2560,160]{0,1:T(8,128)(2,1)} %param.17, bf16[8,2560]{1,0:T(8,128)(2,1)S(1)} %get-tuple-element.16, f32[2560]{0:T(1024)S(1)} %convert_element_type.65, f32[8]{0:T(128)S(1)} %add_rsqrt_fusion.1), kind=kOutput, calls=%fused_computation.121 | convolution fusion | flops 6635520 | bytes 875552 | tf_op jit(solution)/shard_map/dot_general | solution.py:109
  29.9 2.5 %fusion.64 = f32[8,640]{1,0:T(8,128)S(1)} fusion(bf16[2560,640]{1,0:T(8,128)(2,1)} %param.16, bf16[8,2560]{1,0:T(8,128)(2,1)S(1)} %get-tuple-element.16, f32[2560]{0:T(1024)S(1)} %convert_element_type.65, f32[8]{0:T(128)S(1)} %add_rsqrt_fusion.1), kind=kOutput, calls=%fused_computation.122 | convolution fusion | flops 26296320 | bytes 3348512 | tf_op jit(solution)/shard_map/dot_general | solution.py:100
  32.8 0.2 fusion.45
  33.0 1.9 %select_reduce_fusion.1 = (f32[8,2,4]{2,1,0:T(2,128)S(1)}, f32[8,2,4,4,128]{4,2,3,1,0:T(4,128)S(1)}) fusion(pred[8,4,128]{2,1,0:T(4,128)(4,1)S(1)} %broadcast_compare_fusion, bf16[8,4,2,80,128]{4,1,0,3,2:T(4,128)(2,1)} %bitcast.62, bf16[8,2,4,40]{3,2,1,0:T(4,128)(2,1)S(1)} %bitcast.68, bf16[8,2,4,40]{3,2,1,0:T(4,128)(2,1)S(1)} %bitcast.66), kind=kOutput, calls=%fused_computation.24 | convolution fusion | flops 5361600 | bytes 1456384 | tf_op jit(solution)/shard_map/rhgd,rphdc->rhgpc/dot_general | solution.py:131
  34.9 0.2 fusion.26
  35.2 0.3 fusion.25
  35.6 1.9 %fusion.20 = bf16[8,2,4,80]{3,2,1,0:T(4,128)(2,1)S(1)} fusion(bf16[8,4,2,80,128]{4,1,0,3,2:T(4,128)(2,1)} %bitcast.61, f32[8,2,4,4,128]{4,2,3,1,0:T(4,128)S(1)} %get-tuple-element.27, f32[8,2,4]{2,1,0:T(2,128)S(1)} %multiply_maximum_fusion, pred[8,4,128]{2,1,0:T(4,128)(4,1)S(1)} %broadcast_compare_fusion, f32[8,2,4]{2,1,0:T(2,128)S(1)} %get-tuple-element.13, ...), kind=kOutput, calls=%fused_computation.17 | convolution fusion | flops 5328896 | bytes 1462016 | tf_op jit(solution)/shard_map/rhgpc,rphdc->rhgd/dot_general | solution.py:147
  37.6 0.5 fusion.67
  38.2 0.6 collective-permute-start.4
  38.7 3.3 %collective-permute-start.5 = (f32[8,2560]{1,0:T(8,128)S(1)}, f32[8,2560]{1,0:T(8,128)S(1)}, u32[]{:S(2)}, u32[]{:S(2)}) collective-permute-start(f32[8,2560]{1,0:T(8,128)S(1)} %fusion.67), channel_id=1, source_target_pairs={{0,3},{1,0},{2,1},{3,2},{4,7},{5,4},{6,5},{7,6},{8,11},{9,8},{10,9... | collective-permute-start | bytes 245768 | tf_op jit(solution)/shard_map/ppermute | solution.py:36
  42.1 4.3 %collective-permute-done.3 = f32[8,2560]{1,0:T(8,128)S(1)} collective-permute-done((f32[8,2560]{1,0:T(8,128)S(1)}, f32[8,2560]{1,0:T(8,128)S(1)}, u32[]{:S(2)}, u32[]{:S(2)}) %collective-permute-start.3) | collective-permute-done | bytes 81952 | tf_op jit(solution)/shard_map/ppermute | solution.py:36
  46.7 3.0 %fusion.60 = f32[8,896]{1,0:T(8,128)S(1)} fusion(bf16[2560,896]{1,0:T(8,128)(2,1)} %param.25, f32[8,2560]{1,0:T(8,128)S(1)} %get-tuple-element.12, f32[2560]{0:T(1024)S(1)} %convert_element_type.73, f32[8]{0:T(128)S(1)} %add_rsqrt_fusion), kind=kOutput, calls=%fused_computation.120 | convolution fusion | flops 36761600 | bytes 4708384 | tf_op jit(solution)/shard_map/dot_general | solution.py:158
  49.7 5.3 %fusion.24 = f32[8,2560]{1,0:T(8,128)S(1)} fusion(bf16[896,2560]{1,0:T(8,128)(2,1)} %param.27, bf16[2560,896]{1,0:T(8,128)(2,1)} %param.26, f32[8,896]{1,0:T(8,128)S(1)} %fusion.60, f32[8,2560]{1,0:T(8,128)S(1)} %get-tuple-element.12, f32[2560]{0:T(1024)S(1)} %convert_element_type.73, f32[8]{0:T(128)S(1)} %add_rsqrt_fusion), kind=kOutput, calls=%fused_computation.19 | convolution fusion | flops 73504768 | bytes 9377824 | tf_op jit(solution)/shard_map/dot_general | solution.py:162
  55.0 1.1 %collective-permute-start.6 = (f32[8,2560]{1,0:T(8,128)S(1)}, f32[8,2560]{1,0:T(8,128)S(1)}, u32[]{:S(2)}, u32[]{:S(2)}) collective-permute-start(f32[8,2560]{1,0:T(8,128)S(1)} %fusion.24), channel_id=1, source_target_pairs={{0,2},{1,3},{2,0},{3,1},{4,6},{5,7},{6,4},{7,5},{8,10},{9,11},{10,... | collective-permute-start | bytes 245768 | tf_op jit(solution)/shard_map/ppermute | solution.py:36
  56.1 1.3 %collective-permute-start.7 = (f32[8,2560]{1,0:T(8,128)S(1)}, f32[8,2560]{1,0:T(8,128)S(1)}, u32[]{:S(2)}, u32[]{:S(2)}) collective-permute-start(f32[8,2560]{1,0:T(8,128)S(1)} %fusion.24), channel_id=1, source_target_pairs={{0,1},{1,2},{2,3},{3,0},{4,5},{5,6},{6,7},{7,4},{8,9},{9,10},{10,1... | collective-permute-start | bytes 245768 | tf_op jit(solution)/shard_map/ppermute | solution.py:36
  57.4 2.5 %collective-permute-start.8 = (f32[8,2560]{1,0:T(8,128)S(1)}, f32[8,2560]{1,0:T(8,128)S(1)}, u32[]{:S(2)}, u32[]{:S(2)}) collective-permute-start(f32[8,2560]{1,0:T(8,128)S(1)} %fusion.24), channel_id=1, source_target_pairs={{0,3},{1,0},{2,1},{3,2},{4,7},{5,4},{6,5},{7,6},{8,11},{9,8},{10,9... | collective-permute-start | bytes 245768 | tf_op jit(solution)/shard_map/ppermute | solution.py:36
  60.0 4.0 %collective-permute-done.6 = f32[8,2560]{1,0:T(8,128)S(1)} collective-permute-done((f32[8,2560]{1,0:T(8,128)S(1)}, f32[8,2560]{1,0:T(8,128)S(1)}, u32[]{:S(2)}, u32[]{:S(2)}) %collective-permute-start.6) | collective-permute-done | bytes 81952 | tf_op jit(solution)/shard_map/ppermute | solution.py:36
  64.0 9.3 %all-gather.1 = bf16[64,2560]{1,0:T(8,128)(2,1)S(1)} all-gather(bf16[8,2560]{1,0:T(8,128)(2,1)S(1)} %add_convert_fusion), channel_id=3, replica_groups=mesh['dp'=8,'tensor'=4] {'dp'}, dimensions={0}, use_global_device_ids=true | all-gather | bytes 368640 | tf_op jit(solution)/shard_map/all_gather | solution.py:171
  73.4 0.8 %select_reduce_fusion = bf16[2,2560]{1,0:T(2,128)(2,1)} fusion(f32[8,8,2560]{2,1,0:T(8,128)S(1)} %bitcast_convert_fusion, pred[2,8,8]{2,1,0:T(8,128)(4,1)S(1)} %broadcast_and_fusion), kind=kLoop, calls=%fused_computation.11 | loop fusion | flops 650240 | bytes 665728 | tf_op jit(solution)/shard_map/reduce_sum | solution.py:177
  (53 shorter events, 1.9 us)
Async XLA Ops:
  0.0 37.6 %copy-start = (bf16[640,2560]{1,0:T(8,128)(2,1)S(1)}, bf16[640,2560]{1,0:T(8,128)(2,1)}, u32[]{:S(2)}) copy-start(bf16[640,2560]{1,0:T(8,128)(2,1)} %param.23) | copy-start | bytes 9830404
  14.3 13.1 %collective-permute-start = (bf16[8,2560]{1,0:T(8,128)(2,1)S(1)}, bf16[8,2560]{1,0:T(8,128)(2,1)S(1)}, u32[]{:S(2)}, u32[]{:S(2)}) collective-permute-start(bf16[8,2560]{1,0:T(8,128)(2,1)S(1)} %broadcast_select_fusion), channel_id=1, source_target_pairs={{0,2},{1,3},{2,0},{3,1},{4,6},{5,7},{6,4},{7,5},{8,10},{9,11},{10,... | collective-permute-start | bytes 122888 | tf_op jit(solution)/shard_map/ppermute | solution.py:36
  16.9 10.5 %collective-permute-start.1 = (bf16[8,2560]{1,0:T(8,128)(2,1)S(1)}, bf16[8,2560]{1,0:T(8,128)(2,1)S(1)}, u32[]{:S(2)}, u32[]{:S(2)}) collective-permute-start(bf16[8,2560]{1,0:T(8,128)(2,1)S(1)} %broadcast_select_fusion), channel_id=1, source_target_pairs={{0,1},{1,2},{2,3},{3,0},{4,5},{5,6},{6,7},{7,4},{8,9},{9,10},{10,1... | collective-permute-start | bytes 122888 | tf_op jit(solution)/shard_map/ppermute | solution.py:36
  18.5 8.9 %collective-permute-start.2 = (bf16[8,2560]{1,0:T(8,128)(2,1)S(1)}, bf16[8,2560]{1,0:T(8,128)(2,1)}, u32[]{:S(2)}, u32[]{:S(2)}) collective-permute-start(bf16[8,2560]{1,0:T(8,128)(2,1)S(1)} %broadcast_select_fusion), channel_id=1, source_target_pairs={{0,3},{1,0},{2,1},{3,2},{4,7},{5,4},{6,5},{7,6},{8,11},{9,8},{10,9... | collective-permute-start | bytes 122888 | tf_op jit(solution)/shard_map/ppermute | solution.py:36
  21.1 3.2 %copy-start.1 = (bf16[32,2,80,128]{3,2,1,0:T(8,128)(2,1)S(1)}, bf16[32,2,80,128]{3,2,1,0:T(8,128)(2,1)}, u32[]{:S(2)}) copy-start(bf16[32,2,80,128]{3,2,1,0:T(8,128)(2,1)} %param.20) | copy-start | bytes 3932164
  24.3 1.9 %copy-start.3 = (bf16[2560]{0:T(1024)(128)(2,1)S(1)}, bf16[2560]{0:T(1024)(128)(2,1)}, u32[]{:S(2)}) copy-start(bf16[2560]{0:T(1024)(128)(2,1)} %param.15) | copy-start | bytes 15364
  32.5 2.6 %copy-start.2 = (bf16[2560,160]{0,1:T(8,128)(2,1)S(1)}, bf16[2560,160]{0,1:T(8,128)(2,1)}, u32[]{:S(2)}) copy-start(bf16[2560,160]{0,1:T(8,128)(2,1)} %param.18) | copy-start | bytes 2457604
  37.6 4.5 %copy-start.4 = (bf16[2560]{0:T(1024)(128)(2,1)S(1)}, bf16[2560]{0:T(1024)(128)(2,1)}, u32[]{:S(2)}) copy-start(bf16[2560]{0:T(1024)(128)(2,1)} %param.24) | copy-start | bytes 15364
  38.2 8.2 %collective-permute-start.3 = (f32[8,2560]{1,0:T(8,128)S(1)}, f32[8,2560]{1,0:T(8,128)S(1)}, u32[]{:S(2)}, u32[]{:S(2)}) collective-permute-start(f32[8,2560]{1,0:T(8,128)S(1)} %fusion.67), channel_id=1, source_target_pairs={{0,2},{1,3},{2,0},{3,1},{4,6},{5,7},{6,4},{7,5},{8,10},{9,11},{10,... | collective-permute-start | bytes 245768 | tf_op jit(solution)/shard_map/ppermute | solution.py:36
  38.2 8.2 %collective-permute-start.4 = (f32[8,2560]{1,0:T(8,128)S(1)}, f32[8,2560]{1,0:T(8,128)S(1)}, u32[]{:S(2)}, u32[]{:S(2)}) collective-permute-start(f32[8,2560]{1,0:T(8,128)S(1)} %fusion.67), channel_id=1, source_target_pairs={{0,1},{1,2},{2,3},{3,0},{4,5},{5,6},{6,7},{7,4},{8,9},{9,10},{10,1... | collective-permute-start | bytes 245768 | tf_op jit(solution)/shard_map/ppermute | solution.py:36
  38.7 7.8 %collective-permute-start.5 = (f32[8,2560]{1,0:T(8,128)S(1)}, f32[8,2560]{1,0:T(8,128)S(1)}, u32[]{:S(2)}, u32[]{:S(2)}) collective-permute-start(f32[8,2560]{1,0:T(8,128)S(1)} %fusion.67), channel_id=1, source_target_pairs={{0,3},{1,0},{2,1},{3,2},{4,7},{5,4},{6,5},{7,6},{8,11},{9,8},{10,9... | collective-permute-start | bytes 245768 | tf_op jit(solution)/shard_map/ppermute | solution.py:36
  55.0 9.0 %collective-permute-start.6 = (f32[8,2560]{1,0:T(8,128)S(1)}, f32[8,2560]{1,0:T(8,128)S(1)}, u32[]{:S(2)}, u32[]{:S(2)}) collective-permute-start(f32[8,2560]{1,0:T(8,128)S(1)} %fusion.24), channel_id=1, source_target_pairs={{0,2},{1,3},{2,0},{3,1},{4,6},{5,7},{6,4},{7,5},{8,10},{9,11},{10,... | collective-permute-start | bytes 245768 | tf_op jit(solution)/shard_map/ppermute | solution.py:36
  56.1 7.9 %collective-permute-start.7 = (f32[8,2560]{1,0:T(8,128)S(1)}, f32[8,2560]{1,0:T(8,128)S(1)}, u32[]{:S(2)}, u32[]{:S(2)}) collective-permute-start(f32[8,2560]{1,0:T(8,128)S(1)} %fusion.24), channel_id=1, source_target_pairs={{0,1},{1,2},{2,3},{3,0},{4,5},{5,6},{6,7},{7,4},{8,9},{9,10},{10,1... | collective-permute-start | bytes 245768 | tf_op jit(solution)/shard_map/ppermute | solution.py:36
  57.4 6.6 %collective-permute-start.8 = (f32[8,2560]{1,0:T(8,128)S(1)}, f32[8,2560]{1,0:T(8,128)S(1)}, u32[]{:S(2)}, u32[]{:S(2)}) collective-permute-start(f32[8,2560]{1,0:T(8,128)S(1)} %fusion.24), channel_id=1, source_target_pairs={{0,3},{1,0},{2,1},{3,2},{4,7},{5,4},{6,5},{7,6},{8,11},{9,8},{10,9... | collective-permute-start | bytes 245768 | tf_op jit(solution)/shard_map/ppermute | solution.py:36
